TPU v7x, 32 devices: a whole 2x2x4 slice. The times are simulated.
32 devices in a mesh: ctx: 16 (over z, y, x), head: 2 (over core).
Axes of the slice: x: 2, y: 2, z: 4, core: 2. Of those that a mesh axis runs over, the one named last changes fastest.
Arguments:
- queries: bfloat16 [2048, 4096], P('ctx', 'head'), may hold values from -48 to 48
- keys: bfloat16 [2048, 2048], P('ctx', 'head'), may hold values from -6 to 6
- values: bfloat16 [2048, 2048], P('ctx', 'head'), may hold values from -6 to 6
- hidden_in: bfloat16 [2048, 4608], P('ctx', 'head'), may hold values from -6 to 6
- out_weight: bfloat16 [4096, 4608], P('ctx', 'head'), may hold values from -0.09375 to 0.09375
- out_gain: float32 [4608], P('head'), may hold values from 0.1 to 1.9
- reward_weight: float32 [4608], P('head'), may hold values from -0.09375 to 0.09375
- doc_lengths: int32 [16], replicated, may hold values from 1 to 1024, 2048 in all
Outputs:
- hidden_out: bfloat16 [2048, 4608], P('ctx', 'head')
- rewards: float32 [16], replicated
Inputs may be any that keep to these rules, and one draw needn't show every extreme that they name: `doc_lengths`: the lengths sum to 2048; the longest is exactly 1024.
All inputs are finite; a program needn't handle non-finite values.
Results may differ from a plain program's by a relative error of at most 0.005.
Values may be sent and summed in bfloat16 or wider, within the bound.
No kernel may reach another device: no remote copies, remote signals or barrier semaphores. Data moves between devices by JAX's collectives and lax.ppermute only.
A program may use at most 128 MiB of HBM per device.

v0:
```python
import jax
import jax.numpy as jnp
from jax import lax
from jax.sharding import PartitionSpec as P

D = 4608
QUERY_HEADS = 32
KEY_VALUE_HEADS = 16
HEAD_WIDTH = 128
NDOC = 16


soft_cap = 50.0


def storage_positions(rows, tok_dev, n_ctx):
    owner = rows // tok_dev
    offset = rows % tok_dev
    half = tok_dev // 2
    slab = jnp.where(offset < half, owner, 2 * n_ctx - 1 - owner)
    return slab * half + offset % half


def document_of(positions, doc_ends):
    return jnp.sum((positions[:, None] >= doc_ends[None, :]).astype(jnp.int32), axis=1)


def shards(queries, keys, values, hidden_in, out_weight, out_gain, reward_weight, doc_lengths):
    n_ctx = lax.axis_size("ctx")
    device = lax.axis_index("ctx")
    tok_dev = queries.shape[0]
    kv_local = keys.shape[1] // HEAD_WIDTH
    group_repeat = QUERY_HEADS // KEY_VALUE_HEADS
    scale = (D / QUERY_HEADS) ** (-0.5)
    doc_ends = jnp.cumsum(doc_lengths)
    local_rows = device * tok_dev + jnp.arange(tok_dev, dtype=jnp.int32)
    query_pos = storage_positions(local_rows, tok_dev, n_ctx)
    query_doc = document_of(query_pos, doc_ends)
    q_groups = queries.reshape(tok_dev, kv_local, group_repeat, HEAD_WIDTH)
    span = tok_dev * max(1, 2048 // tok_dev)

    def attend_block(state, key_piece, value_piece, start):
        count = key_piece.shape[0]
        key_rows = start + jnp.arange(count, dtype=jnp.int32)
        key_pos = storage_positions(key_rows, tok_dev, n_ctx)
        key_doc = document_of(key_pos, doc_ends)
        visible = (query_doc[:, None] == key_doc[None, :]) & (
            key_pos[None, :] <= query_pos[:, None]
        )

        def compute(carry):
            numerator, denominator = carry
            scores = (
                jnp.einsum(
                    "qgrd,kgd->grqk",
                    q_groups,
                    key_piece.reshape(count, kv_local, HEAD_WIDTH),
                    preferred_element_type=jnp.float32,
                )
                * scale
            )
            scores = soft_cap * jnp.tanh(scores / soft_cap)
            weights = jnp.where(visible[None, None], jnp.exp(scores), 0.0)
            numerator = numerator + jnp.einsum(
                "grqk,kgd->grqd",
                weights.astype(jnp.bfloat16),
                value_piece.reshape(count, kv_local, HEAD_WIDTH),
                preferred_element_type=jnp.float32,
            )
            denominator = denominator + jnp.sum(weights, axis=-1)
            return (numerator, denominator)

        return lax.cond(jnp.any(visible), compute, lambda carry: carry, state)

    def attend(state, key_piece, value_piece, start):
        count = key_piece.shape[0]
        if count <= span:
            return attend_block(state, key_piece, value_piece, start)
        blocks = count // span
        whole = blocks * span
        width = key_piece.shape[1]
        key_blocks = key_piece[:whole].reshape(blocks, span, width)
        value_blocks = value_piece[:whole].reshape(blocks, span, width)
        starts = start + span * jnp.arange(blocks, dtype=jnp.int32)

        def step_fn(carry, item):
            return (attend_block(carry, item[0], item[1], item[2]), None)

        state, _ = lax.scan(step_fn, state, (key_blocks, value_blocks, starts))
        if whole < count:
            state = attend_block(state, key_piece[whole:], value_piece[whole:], start + whole)
        return state

    initial = (
        jnp.zeros((kv_local, group_repeat, tok_dev, HEAD_WIDTH), jnp.float32),
        jnp.zeros((kv_local, group_repeat, tok_dev), jnp.float32),
    )
    numerator, denominator = attend(
        initial,
        lax.all_gather(keys, "ctx", axis=0, tiled=True),
        lax.all_gather(values, "ctx", axis=0, tiled=True),
        jnp.int32(0),
    )
    attended = (numerator / denominator[..., None]).astype(jnp.bfloat16)
    attended = attended.transpose(2, 0, 1, 3).reshape(tok_dev, kv_local * group_repeat * HEAD_WIDTH)
    all_heads = lax.all_gather(attended, "head", axis=1, tiled=True)
    mixed = jnp.dot(
        all_heads,
        lax.all_gather(out_weight, "ctx", axis=0, tiled=True),
        preferred_element_type=jnp.float32,
    )
    squares = lax.psum(jnp.sum(mixed * mixed, axis=1), "head")
    normed = mixed / jnp.sqrt(squares / D + 1e-06)[:, None]
    out32 = hidden_in.astype(jnp.float32) + normed * out_gain[None, :]
    tok_reward = jnp.sum(out32 * reward_weight[None, :], axis=1)
    onehot = (query_doc[:, None] == jnp.arange(NDOC, dtype=jnp.int32)[None, :]).astype(jnp.float32)
    partial_sums = jnp.sum(onehot * tok_reward[:, None], axis=0)
    totals = lax.psum(partial_sums, ("ctx", "head"))
    rewards = totals / jnp.sqrt(doc_lengths.astype(jnp.float32))
    return (out32.astype(jnp.bfloat16), rewards)


def solution(mesh):
    in_specs = (
        P("ctx", "head"),
        P("ctx", "head"),
        P("ctx", "head"),
        P("ctx", "head"),
        P("ctx", "head"),
        P("head"),
        P("head"),
        P(),
    )
    out_specs = (P("ctx", "head"), P())
    return jax.shard_map(shards, mesh=mesh, in_specs=in_specs, out_specs=out_specs, check_vma=False)
```

profile of v0, /device:TPU:0, one launch (start us, length us, event | category | flops | bytes accessed | tf_op | source)
XLA Modules:
  0.0 472.6 jit_solution(5783936691087741869)
XLA Ops:
  7.2 0.7 all-gather.5.cloned.1.call-update
  7.9 0.7 all-gather.7.cloned.1.call-update
  8.7 0.7 copy.26
  9.5 0.1 reduce
  9.7 0.1 convert_reduce_fusion
  9.8 1.9 fusion.26
  12.3 77.3 %all-gather.5.cloned.1.call-done = bf16[2048,1024]{1,0:T(8,128)(2,1)} async-done(((bf16[128,1024]{1,0:T(8,128)(2,1)}), bf16[2048,1024]{1,0:T(8,128)(2,1)}) %all-gather.5.cloned.1.call-update) | async-done | bytes 4194320 | tf_op jit(solution)/shard_map/all_gather | solution.py:100
  89.6 77.5 %all-gather.7.cloned.1.call-done = bf16[2048,1024]{1,0:T(8,128)(2,1)} async-done(((bf16[128,1024]{1,0:T(8,128)(2,1)}), bf16[2048,1024]{1,0:T(8,128)(2,1)}) %all-gather.7.cloned.1.call-update) | async-done | bytes 4194320 | tf_op jit(solution)/shard_map/all_gather | solution.py:101
  167.1 22.7 %conditional.1 = (f32[8,2,128]{2,1,0:T(2,128)S(1)}, f32[8,2,128,128]{2,3,1,0:T(8,128)S(1)}) conditional(s32[]{:T(128)} %convert_element_type.28, () %tuple.16, (pred[128,2048]{0,1:T(8,128)(4,1)S(1)}, bf16[2048,1024]{1,0:T(8,128)(2,1)}, bf16[128,2048]{1,0:T(8,128)(2,1)}, bf16[2048,1024]{1,0:T(8,128)(2,1)}) %tuple.17), branch_computations={%region_4.5_spmd, %region_5.7_spmd} | conditional | flops 2181036032 | bytes 78651440 | solution.py:73
  167.1 1.4 reshape.162
  168.5 3.3 copy.37
  171.8 8.4 %fusion = (f32[8,2,128]{2,1,0:T(2,128)S(1)}, f32[8,2048,128,2]{2,1,3,0:T(8,128)}) fusion(pred[128,2048]{0,1:T(8,128)(4,1)S(1)} %get-tuple-element.9, bf16[128,8,2,128]{3,2,1,0:T(2,128)(2,1)S(1)} %reshape.162, bf16[2048,8,128,1]{2,1,0,3:T(8,128)(2,1)S(1)} %bitcast.23), kind=kOutput, calls=%fused_computation.1 | convolution fusion | flops 1090516992 | bytes 21766144 | tf_op jit(solution)/shard_map/cond/branch_1_fun/qgrd,kgd->grqk/dot_general | solution.py:54
  180.2 1.1 copy.38
  181.3 8.5 %fusion.2 = f32[8,2,128,128]{2,3,1,0:T(8,128)S(1)} fusion(f32[8,2048,128,2]{2,1,3,0:T(8,128)} %get-tuple-element.25, pred[128,2048]{0,1:T(8,128)(4,1)S(1)} %get-tuple-element.9, bf16[2048,8,128,1]{2,1,0,3:T(8,128)(2,1)S(1)} %bitcast.24), kind=kOutput, calls=%fused_computation.3 | convolution fusion | flops 1090519040 | bytes 22282240 | tf_op jit(solution)/shard_map/cond | solution.py:73
  189.8 0.9 divide_convert_fusion
  190.8 0.5 all-gather.11.cloned.1.call-update
  191.4 7.2 %all-gather.9.cloned.1.call-done = bf16[128,4096]{0,1:T(8,128)(2,1)} async-done(((bf16[128,2048]{0,1:T(8,128)(2,1)}), bf16[128,4096]{0,1:T(8,128)(2,1)}) %all-gather.9.cloned.1.call-update) | async-done | bytes 1048592 | tf_op jit(solution)/shard_map/all_gather | solution.py:106
  198.6 215.3 %all-gather.11.cloned.1.call-done = bf16[4096,2304]{1,0:T(8,128)(2,1)} async-done(((bf16[256,2304]{1,0:T(8,128)(2,1)}), bf16[4096,2304]{1,0:T(8,128)(2,1)}) %all-gather.11.cloned.1.call-update) | async-done | bytes 18874384 | tf_op jit(solution)/shard_map/all_gather | solution.py:109
  413.9 9.4 %multiply_reduce_fusion.1 = (f32[128]{0:T(128)S(1)}, f32[128,2304]{1,0:T(8,128)S(1)}) fusion(bf16[128,4096]{0,1:T(8,128)(2,1)} %all-gather.9.cloned.1.call-done, bf16[4096,2304]{1,0:T(8,128)(2,1)} %all-gather.11.cloned.1.call-done), kind=kOutput, calls=%fused_computation.14 | convolution fusion | flops 2416508928 | bytes 21103104 | tf_op jit(solution)/shard_map/dot_general | solution.py:107
  423.3 2.5 psum.14
  425.8 1.2 multiply_reduce_fusion
  427.0 0.1 select_reduce_fusion
  427.1 38.4 %psum.15 = f32[16]{0:T(128)S(1)} all-reduce(f32[16]{0:T(128)S(1)} %select_reduce_fusion), channel_id=1, replica_groups=mesh['ctx'=16,'head'=2] {'ctx','head'}, use_global_device_ids=true, to_apply=%region_11.12 | all-reduce | flops 16 | bytes 128 | tf_op jit(solution)/shard_map/psum | solution.py:118
  465.5 0.5 rsqrt_multiply_fusion
  (20 shorter events, 0.4 us)
Async XLA Ops:
  7.2 82.4 %all-gather.5.cloned.1.call-start = ((), (), s32[]{:S(2)}) async-start(), calls=%async_computation | async-start | bytes 4456448 | tf_op jit(solution)/shard_map/all_gather | solution.py:100
  7.9 159.2 %all-gather.7.cloned.1.call-start = ((), (), s32[]{:S(2)}) async-start(), calls=%async_computation.1 | async-start | bytes 4456448 | tf_op jit(solution)/shard_map/all_gather | solution.py:101
  8.6 189.9 %all-gather.9.cloned.1.call-start = ((), (), s32[]{:S(2)}) async-start(), calls=%async_computation.2 | async-start | bytes 1572864 | tf_op jit(solution)/shard_map/all_gather | solution.py:106
  171.8 8.4 %copy-start = (bf16[2048,1024]{1,0:T(8,128)(2,1)S(1)}, bf16[2048,1024]{1,0:T(8,128)(2,1)}, u32[]{:S(2)}) copy-start(bf16[2048,1024]{1,0:T(8,128)(2,1)} %get-tuple-element.12) | copy-start | bytes 12582916 | tf_op jit(solution)/shard_map/cond
  190.8 223.1 %all-gather.11.cloned.1.call-start = ((), (), s32[]{:S(2)}) async-start(), calls=%async_computation.3 | async-start | bytes 20054016 | tf_op jit(solution)/shard_map/all_gather | solution.py:109
  191.3 234.5 %copy-start.1 = (bf16[128,2304]{1,0:T(8,128)(2,1)S(1)}, bf16[128,2304]{1,0:T(8,128)(2,1)}, u32[]{:S(2)}) copy-start(bf16[128,2304]{1,0:T(8,128)(2,1)} %param.13) | copy-start | bytes 1769476
  191.4 234.5 %copy-start.2 = (f32[2304]{0:T(1024)S(1)}, f32[2304]{0:T(1024)}, u32[]{:S(2)}) copy-start(f32[2304]{0:T(1024)} %param.16) | copy-start | bytes 27652
  191.4 234.5 %copy-start.3 = (f32[2304]{0:T(1024)S(1)}, f32[2304]{0:T(1024)}, u32[]{:S(2)}) copy-start(f32[2304]{0:T(1024)} %param.15) | copy-start | bytes 27652
  191.4 274.2 %copy-start.4 = (s32[16]{0:T(128)S(1)}, s32[16]{0:T(128)}, u32[]{:S(2)}) copy-start(s32[16]{0:T(128)} %param.17) | copy-start | bytes 196
Sparse Core Ops, SparseCore 0:
  10.8 78.7 all-gather.4
  92.3 74.6 all-gather.6
  190.9 7.6 all-gather.8
  201.2 212.6 all-gather.10
where the time goes:
time: 473 us
  waiting for transfers between devices  379 us (80%)
  blocking collectives  40.9 us (9%)
  matrix products  26.4 us (6%)
  between operations  14.5 us (3%)
  local copies, waits for them, and re-layouts  6.53 us (1%)
  other arithmetic  4.96 us (1%)
    all_gather x1, waiting for transfers between devices, shards(): lax.all_gather(out_weight, 'ctx', axis=0, tiled=True)  215 us
    all_gather x1, waiting for transfers between devices, shards(): lax.all_gather(values, 'ctx', axis=0, tiled=True)  77.5 us
    all_gather x1, waiting for transfers between devices, shards(): lax.all_gather(keys, 'ctx', axis=0, tiled=True)  77.3 us
    psum x1, blocking collectives, shards(): totals = lax.psum(partial_sums, ('ctx', 'head'))  38.4 us
  transfers between devices with their start and end apart: 4, of which 4 were waited for; matrix products, arithmetic and copies ran while one was open for 1% of the time, Pallas kernels for 0%

commit v1 on v0

--- a/solution.py
+++ b/solution.py
@@ -1,7 +1,7 @@
 import jax
 import jax.numpy as jnp
 from jax import lax
-from jax.sharding import PartitionSpec as P
+from jax.sharding import Mesh, PartitionSpec as P
 
 D = 4608
 QUERY_HEADS = 32
@@ -11,6 +11,7 @@
 
 
 soft_cap = 50.0
+CTX = ("ca", "cb")
 
 
 def storage_positions(rows, tok_dev, n_ctx):
@@ -26,8 +27,8 @@
 
 
 def shards(queries, keys, values, hidden_in, out_weight, out_gain, reward_weight, doc_lengths):
-    n_ctx = lax.axis_size("ctx")
-    device = lax.axis_index("ctx")
+    n_ctx = lax.axis_size(CTX)
+    device = lax.axis_index(CTX)
     tok_dev = queries.shape[0]
     kv_local = keys.shape[1] // HEAD_WIDTH
     group_repeat = QUERY_HEADS // KEY_VALUE_HEADS
@@ -95,41 +96,34 @@
         jnp.zeros((kv_local, group_repeat, tok_dev, HEAD_WIDTH), jnp.float32),
         jnp.zeros((kv_local, group_repeat, tok_dev), jnp.float32),
     )
-    numerator, denominator = attend(
-        initial,
-        lax.all_gather(keys, "ctx", axis=0, tiled=True),
-        lax.all_gather(values, "ctx", axis=0, tiled=True),
-        jnp.int32(0),
-    )
+    kv_width = keys.shape[1]
+    both = lax.all_gather(jnp.concatenate([keys, values], axis=1), CTX, axis=0, tiled=True)
+    numerator, denominator = attend(initial, both[:, :kv_width], both[:, kv_width:], jnp.int32(0))
     attended = (numerator / denominator[..., None]).astype(jnp.bfloat16)
     attended = attended.transpose(2, 0, 1, 3).reshape(tok_dev, kv_local * group_repeat * HEAD_WIDTH)
     all_heads = lax.all_gather(attended, "head", axis=1, tiled=True)
-    mixed = jnp.dot(
-        all_heads,
-        lax.all_gather(out_weight, "ctx", axis=0, tiled=True),
-        preferred_element_type=jnp.float32,
-    )
+    weight_rows = lax.all_gather(out_weight, "cb", axis=0, tiled=True)
+    regrouped = lax.all_to_all(all_heads, "ca", 1, 0, tiled=True)
+    partial = jnp.dot(regrouped, weight_rows, preferred_element_type=jnp.float32)
+    mixed = lax.psum_scatter(partial, "ca", scatter_dimension=0, tiled=True)
     squares = lax.psum(jnp.sum(mixed * mixed, axis=1), "head")
     normed = mixed / jnp.sqrt(squares / D + 1e-06)[:, None]
     out32 = hidden_in.astype(jnp.float32) + normed * out_gain[None, :]
     tok_reward = jnp.sum(out32 * reward_weight[None, :], axis=1)
     onehot = (query_doc[:, None] == jnp.arange(NDOC, dtype=jnp.int32)[None, :]).astype(jnp.float32)
     partial_sums = jnp.sum(onehot * tok_reward[:, None], axis=0)
-    totals = lax.psum(partial_sums, ("ctx", "head"))
+    totals = lax.psum(partial_sums, CTX + ("head",))
     rewards = totals / jnp.sqrt(doc_lengths.astype(jnp.float32))
     return (out32.astype(jnp.bfloat16), rewards)
 
 
 def solution(mesh):
-    in_specs = (
-        P("ctx", "head"),
-        P("ctx", "head"),
-        P("ctx", "head"),
-        P("ctx", "head"),
-        P("ctx", "head"),
-        P("head"),
-        P("head"),
-        P(),
-    )
-    out_specs = (P("ctx", "head"), P())
-    return jax.shard_map(shards, mesh=mesh, in_specs=in_specs, out_specs=out_specs, check_vma=False)
+    n_ctx, n_head = mesh.devices.shape
+    inner = 1
+    while inner * inner * 4 <= n_ctx:
+        inner *= 2
+    split = Mesh(mesh.devices.reshape(n_ctx // inner, inner, n_head), ("ca", "cb", "head"))
+    rows = P(CTX, "head")
+    in_specs = (rows, rows, rows, rows, rows, P("head"), P("head"), P())
+    out_specs = (rows, P())
+    return jax.shard_map(shards, mesh=split, in_specs=in_specs, out_specs=out_specs, check_vma=False)

time: 473 us -> 399 us (0.84)
  waiting for transfers between devices: 379 us -> 288 us
  local copies, waits for them, and re-layouts: 6.53 us -> 11.7 us
  starting transfers between devices: 0.16 us -> 4.98 us
    all_gather x3 -> x2, waiting for transfers between devices: 370 us -> 195 us  [the longest x1 142 us: shards(): lax.all_gather(jnp.concatenate([keys, values], axis=1), CTX, axis=0, tile...]
    reduce_scatter x0 -> x1, waiting for transfers between devices: none -> 85.4 us  [shards(): mixed = lax.psum_scatter(partial, 'ca', scatter_dimension=0, tiled=True)]
    slice x0 -> x1, local copies, waits for them, and re-layouts: none -> 6.07 us  [shards(): both[:, kv_width:]]
    all_to_all x0 -> x1, starting transfers between devices: none -> 4.85 us  [shards(): regrouped = lax.all_to_all(all_heads, 'ca', 1, 0, tiled=True)]
  transfers between devices with their start and end apart: 4 -> 5, of which waited for: 4 -> 4; matrix products, arithmetic and copies ran while one was open for 1% -> 1% of each run, Pallas kernels for 0% -> 0%
where the time goes in v1:
time: 399 us; the launch traced here: 398 us
  waiting for transfers between devices  288 us (72%)
  blocking collectives  43.2 us (11%)
  matrix products  27 us (7%)
  between operations  14.5 us (4%)
  local copies, waits for them, and re-layouts  11.7 us (3%)
  other arithmetic  8.5 us (2%)
  starting transfers between devices  4.98 us (1%)
    all_gather x1, waiting for transfers between devices, shards(): lax.all_gather(jnp.concatenate([keys, values], axis=1), CTX, axis=0, tile...  142 us
    reduce_scatter x1, waiting for transfers between devices, shards(): mixed = lax.psum_scatter(partial, 'ca', scatter_dimension=0, tiled=True)  85.4 us
    all_gather x1, waiting for transfers between devices, shards(): weight_rows = lax.all_gather(out_weight, 'cb', axis=0, tiled=True)  53 us
    psum x1, blocking collectives, shards(): totals = lax.psum(partial_sums, CTX + ('head',))  40.8 us
    dot_general x1, matrix products, compute(): jnp.einsum('qgrd,kgd->grqk', q_groups, key_piece.reshape(count, kv_local,...  11.8 us
    cond x1, matrix products, attend_block(): return lax.cond(jnp.any(visible), compute, lambda carry: carry, state)  8.62 us
  transfers between devices with their start and end apart: 5, of which 4 were waited for; matrix products, arithmetic and copies ran while one was open for 1% of the time, Pallas kernels for 0%

profile of v1, /device:TPU:0, one launch (start us, length us, event | category | flops | bytes accessed | tf_op | source)
XLA Modules:
  0.0 398.0 jit_solution(5263270378748125020)
XLA Ops:
  7.2 1.1 copy.28
  8.3 1.1 copy.29
  9.5 0.8 pad_maximum_fusion
  10.4 0.7 copy.27
  11.5 1.9 fusion.24
  14.0 142.4 %all-gather.4.cloned.1.call-done = bf16[2048,2048]{0,1:T(8,128)(2,1)} async-done(((bf16[128,2048]{0,1:T(8,128)(2,1)}), bf16[2048,2048]{0,1:T(8,128)(2,1)}) %all-gather.4.cloned.1.call-update) | async-done | bytes 8388624 | tf_op jit(solution)/shard_map/all_gather | solution.py:100
  156.4 26.9 %conditional.1 = (f32[8,2,128]{2,1,0:T(2,128)S(1)}, f32[8,2,128,128]{2,3,1,0:T(8,128)S(1)}) conditional(s32[]{:T(128)} %convert_element_type.28, () %tuple.16, (pred[128,2048]{0,1:T(8,128)(4,1)S(1)}, bf16[2048,2048]{0,1:T(8,128)(2,1)}, bf16[128,2048]{1,0:T(8,128)(2,1)}) %tuple.17), branch_computations={%region_4.5_spmd, %region_5.7_spmd} | conditional | flops 2181036032 | bytes 80748616 | solution.py:74
  156.4 6.1 %fusion.25 = (bf16[2048,1024]{0,1:T(8,128)(2,1)}, bf16[2048,1024]{0,1:T(8,128)(2,1)}) fusion(bf16[2048,2048]{0,1:T(8,128)(2,1)} %get-tuple-element.11), kind=kLoop, calls=%fused_computation.55 | loop fusion | bytes 16777216 | tf_op jit(solution)/shard_map/slice | solution.py:101
  162.4 0.4 reshape.165
  162.8 11.8 %fusion = (f32[8,2,128]{2,1,0:T(2,128)S(1)}, f32[8,2048,128,2]{2,1,3,0:T(8,128)}) fusion(pred[128,2048]{0,1:T(8,128)(4,1)S(1)} %get-tuple-element.10, bf16[2048,8,128,1]{0,2,3,1:T(8,128)(2,1)} %bitcast.30, bf16[128,8,2,128]{3,2,1,0:T(2,128)(2,1)S(1)} %reshape.165), kind=kOutput, calls=%fused_computation.1 | convolution fusion | flops 1090516992 | bytes 21766144 | tf_op jit(solution)/shard_map/cond/branch_1_fun/qgrd,kgd->grqk/dot_general | solution.py:55
  174.6 8.6 %fusion.2 = f32[8,2,128,128]{2,3,1,0:T(8,128)S(1)} fusion(bf16[2048,8,128,1]{0,2,3,1:T(8,128)(2,1)S(1)} %bitcast.29, f32[8,2048,128,2]{2,1,3,0:T(8,128)} %get-tuple-element.27, pred[128,2048]{0,1:T(8,128)(4,1)S(1)} %get-tuple-element.10), kind=kOutput, calls=%fused_computation.3 | convolution fusion | flops 1090519040 | bytes 22282240 | tf_op jit(solution)/shard_map/cond | solution.py:74
  183.2 0.9 divide_convert_fusion
  184.2 0.7 all-gather.8.cloned.1.call-update
  184.9 6.6 %all-gather.6.cloned.1.call-done = bf16[128,4096]{0,1:T(8,128)(2,1)} async-done(((bf16[128,2048]{0,1:T(8,128)(2,1)}), bf16[128,4096]{0,1:T(8,128)(2,1)}) %all-gather.6.cloned.1.call-update) | async-done | bytes 1048592 | tf_op jit(solution)/shard_map/all_gather | solution.py:104
  191.6 2.3 copy.31
  193.9 4.9 %all-to-all-start = ((bf16[128,4,1024]{2,0,1:T(8,128)(2,1)}), bf16[128,4,1024]{2,0,1:T(8,128)(2,1)S(1)}, u32[]{:S(2)}, u32[]{:S(2)}) async-start(bf16[128,4,1024]{2,0,1:T(8,128)(2,1)} %copy.31), calls=%async_computation | async-start | bytes 2097152 | tf_op jit(solution)/shard_map/all_to_all | solution.py:106
  198.7 53.0 %all-gather.8.cloned.1.call-done = bf16[1024,2304]{1,0:T(8,128)(2,1)} async-done(((bf16[256,2304]{1,0:T(8,128)(2,1)}), bf16[1024,2304]{1,0:T(8,128)(2,1)}) %all-gather.8.cloned.1.call-update) | async-done | bytes 4718608 | tf_op jit(solution)/shard_map/all_gather | solution.py:105
  251.7 6.6 %fusion.26 = f32[512,2304]{1,0:T(8,128)} fusion(bf16[512,1024]{1,0:T(8,128)(2,1)S(1)} %bitcast.33, bf16[1024,2304]{1,0:T(8,128)(2,1)} %all-gather.8.cloned.1.call-done), kind=kOutput, calls=%fused_computation.56 | convolution fusion | flops 2415919104 | bytes 10485760 | tf_op jit(solution)/shard_map/dot_general | solution.py:107
  258.3 85.4 %reduce-scatter.2.cloned.1.call-done = f32[128,2304]{1,0:T(8,128)} async-done(((f32[512,2304]{1,0:T(8,128)}), f32[128,2304]{1,0:T(8,128)}) %reduce-scatter.2.cloned.1.call-update) | async-done | bytes 1179664 | tf_op jit(solution)/shard_map/reduce_scatter | solution.py:108
  343.7 1.4 multiply_reduce_fusion.1
  345.2 2.5 psum.14
  347.7 2.4 multiply_reduce_fusion
  350.2 40.8 %psum.15 = f32[16]{0:T(128)S(1)} all-reduce(f32[16]{0:T(128)S(1)} %select_reduce_fusion), channel_id=1, replica_groups=mesh['ca'=4,'cb'=4,'head'=2] {'ca','cb','head'}, use_global_device_ids=true, to_apply=%region_12.13 | all-reduce | flops 16 | bytes 128 | tf_op jit(solution)/shard_map/psum | solution.py:115
  391.0 0.5 rsqrt_multiply_fusion
  (28 shorter events, 0.7 us)
Async XLA Ops:
  7.2 149.2 %all-gather.4.cloned.1.call-start = ((), (), s32[]{:S(2)}) async-start(), calls=%async_computation.2 | async-start | bytes 8912896 | tf_op jit(solution)/shard_map/all_gather | solution.py:100
  10.3 181.3 %all-gather.6.cloned.1.call-start = ((), (), s32[]{:S(2)}) async-start(), calls=%async_computation.3 | async-start | bytes 1572864 | tf_op jit(solution)/shard_map/all_gather | solution.py:104
  156.4 6.1 %copy-start.2 = (bf16[128,2048]{1,0:T(8,128)(2,1)S(1)}, bf16[128,2048]{1,0:T(8,128)(2,1)}, u32[]{:S(2)}) copy-start(bf16[128,2048]{1,0:T(8,128)(2,1)} %get-tuple-element.20) | copy-start | bytes 1572868 | tf_op jit(solution)/shard_map/cond
  162.8 11.8 %copy-start = (bf16[2048,1024]{0,1:T(8,128)(2,1)S(1)}, bf16[2048,1024]{0,1:T(8,128)(2,1)}, u32[]{:S(2)}) copy-start(bf16[2048,1024]{0,1:T(8,128)(2,1)} %get-tuple-element.24) | copy-start | bytes 12582916 | tf_op jit(solution)/shard_map/cond
  184.2 67.5 %all-gather.8.cloned.1.call-start = ((), (), s32[]{:S(2)}) async-start(), calls=%async_computation.4 | async-start | bytes 5898240 | tf_op jit(solution)/shard_map/all_gather | solution.py:105
  193.9 57.8 %all-to-all-start = ((bf16[128,4,1024]{2,0,1:T(8,128)(2,1)}), bf16[128,4,1024]{2,0,1:T(8,128)(2,1)S(1)}, u32[]{:S(2)}, u32[]{:S(2)}) async-start(bf16[128,4,1024]{2,0,1:T(8,128)(2,1)} %copy.31), calls=%async_computation | async-start | bytes 2097152 | tf_op jit(solution)/shard_map/all_to_all | solution.py:106
  198.7 145.0 %reduce-scatter.2.cloned.1.call-start = ((), (), s32[]{:S(2)}) async-start(), calls=%async_computation.5 | async-start | bytes 5898240 | tf_op jit(solution)/shard_map/reduce_scatter | solution.py:108
  258.3 89.3 %copy-start.1 = (bf16[128,2304]{1,0:T(8,128)(2,1)S(1)}, bf16[128,2304]{1,0:T(8,128)(2,1)}, u32[]{:S(2)}) copy-start(bf16[128,2304]{1,0:T(8,128)(2,1)} %param.13) | copy-start | bytes 1769476
  258.3 89.4 %copy-start.3 = (f32[2304]{0:T(1024)S(1)}, f32[2304]{0:T(1024)}, u32[]{:S(2)}) copy-start(f32[2304]{0:T(1024)} %param.16) | copy-start | bytes 27652
  258.3 89.4 %copy-start.4 = (f32[2304]{0:T(1024)S(1)}, f32[2304]{0:T(1024)}, u32[]{:S(2)}) copy-start(f32[2304]{0:T(1024)} %param.15) | copy-start | bytes 27652
  258.3 132.7 %copy-start.5 = (s32[16]{0:T(128)S(1)}, s32[16]{0:T(128)}, u32[]{:S(2)}) copy-start(s32[16]{0:T(128)} %param.17) | copy-start | bytes 196
Sparse Core Ops, SparseCore 0:
  11.3 145.0 all-gather.3
  184.3 7.2 all-gather.5
  193.4 58.2 all-gather.7
  258.5 85.2 reduce-scatter.1

commit v2 on v1

--- a/solution.py
+++ b/solution.py
@@ -96,16 +96,29 @@
         jnp.zeros((kv_local, group_repeat, tok_dev, HEAD_WIDTH), jnp.float32),
         jnp.zeros((kv_local, group_repeat, tok_dev), jnp.float32),
     )
+    outer = lax.axis_size("ca")
+    inner = lax.axis_size("cb")
+    rows_each = out_weight.shape[0]
+    place = lax.axis_index("ca")
+    pieces = [out_weight] + [
+        lax.ppermute(out_weight, "ca", [(i, (i - shift) % outer) for i in range(outer)])
+        for shift in range(1, outer)
+    ]
     kv_width = keys.shape[1]
     both = lax.all_gather(jnp.concatenate([keys, values], axis=1), CTX, axis=0, tiled=True)
+    both, pieces = lax.optimization_barrier((both, pieces))
     numerator, denominator = attend(initial, both[:, :kv_width], both[:, kv_width:], jnp.int32(0))
     attended = (numerator / denominator[..., None]).astype(jnp.bfloat16)
     attended = attended.transpose(2, 0, 1, 3).reshape(tok_dev, kv_local * group_repeat * HEAD_WIDTH)
     all_heads = lax.all_gather(attended, "head", axis=1, tiled=True)
-    weight_rows = lax.all_gather(out_weight, "cb", axis=0, tiled=True)
-    regrouped = lax.all_to_all(all_heads, "ca", 1, 0, tiled=True)
-    partial = jnp.dot(regrouped, weight_rows, preferred_element_type=jnp.float32)
-    mixed = lax.psum_scatter(partial, "ca", scatter_dimension=0, tiled=True)
+    weight_rows = jnp.stack(pieces).reshape(outer * rows_each, out_weight.shape[1])
+    blocks = all_heads.reshape(tok_dev, outer, inner, rows_each).transpose(2, 0, 1, 3)
+    regrouped = lax.all_to_all(blocks, "cb", 0, 0, tiled=True)
+    regrouped = jnp.roll(regrouped.reshape(inner * tok_dev, outer, rows_each), -place, axis=1)
+    partial = jnp.dot(
+        regrouped.reshape(inner * tok_dev, outer * rows_each), weight_rows, preferred_element_type=jnp.float32
+    )
+    mixed = lax.psum_scatter(partial, "cb", scatter_dimension=0, tiled=True)
     squares = lax.psum(jnp.sum(mixed * mixed, axis=1), "head")
     normed = mixed / jnp.sqrt(squares / D + 1e-06)[:, None]
     out32 = hidden_in.astype(jnp.float32) + normed * out_gain[None, :]

time: 399 us -> 397 us (level)
  waiting for transfers between devices: 288 us -> 282 us
  starting transfers between devices: 4.98 us -> 10.1 us
    ppermute x0 -> x3, waiting for transfers between devices: none -> 88.8 us  [shards(): lax.ppermute(out_weight, 'ca', [(i, (i - shift) % outer) for i in range(o...]
    all_gather x1 -> x0, waiting for transfers between devices: 53 us -> none  [shards(): weight_rows = lax.all_gather(out_weight, 'cb', axis=0, tiled=True)]
    all_gather x1, waiting for transfers between devices: 142 us -> 114 us  [shards(): lax.all_gather(jnp.concatenate([keys, values], axis=1), CTX, axis=0, tile...]
    reduce_scatter x1, waiting for transfers between devices: 85.4 us -> 57.4 us  [shards(): mixed = lax.psum_scatter(partial, 'cb', scatter_dimension=0, tiled=True)]
    all_to_all x1, waiting for transfers between devices: 0.01 us -> 14.1 us  [shards(): regrouped = lax.all_to_all(blocks, 'cb', 0, 0, tiled=True)]
    ppermute x0 -> x3, starting transfers between devices: none -> 6.13 us  [shards(): lax.ppermute(out_weight, 'ca', [(i, (i - shift) % outer) for i in range(o...]
  transfers between devices with their start and end apart: 5 -> 7, of which waited for: 4 -> 5; matrix products, arithmetic and copies ran while one was open for 1% -> 1% of each run, Pallas kernels for 0% -> 0%
where the time goes in v2:
time: 397 us; the launch traced here: 396 us
  waiting for transfers between devices  282 us (71%)
  blocking collectives  41.8 us (11%)
  matrix products  27.4 us (7%)
  between operations  14.5 us (4%)
  local copies, waits for them, and re-layouts  12.3 us (3%)
  starting transfers between devices  10.1 us (3%)
  other arithmetic  8.49 us (2%)
    all_gather x1, waiting for transfers between devices, shards(): lax.all_gather(jnp.concatenate([keys, values], axis=1), CTX, axis=0, tile...  114 us
    ppermute x3, waiting for transfers between devices, shards(): lax.ppermute(out_weight, 'ca', [(i, (i - shift) % outer) for i in range(o...  88.8 us
    reduce_scatter x1, waiting for transfers between devices, shards(): mixed = lax.psum_scatter(partial, 'cb', scatter_dimension=0, tiled=True)  57.4 us
    psum x1, blocking collectives, shards(): totals = lax.psum(partial_sums, CTX + ('head',))  39.4 us
    all_to_all x1, waiting for transfers between devices, shards(): regrouped = lax.all_to_all(blocks, 'cb', 0, 0, tiled=True)  14.1 us
    dot_general x1, matrix products, compute(): jnp.einsum('qgrd,kgd->grqk', q_groups, key_piece.reshape(count, kv_local,...  11.8 us
    cond x1, matrix products, attend_block(): return lax.cond(jnp.any(visible), compute, lambda carry: carry, state)  8.61 us
  transfers between devices with their start and end apart: 7, of which 5 were waited for; matrix products, arithmetic and copies ran while one was open for 1% of the time, Pallas kernels for 0%

profile of v2, /device:TPU:0, one launch (start us, length us, event | category | flops | bytes accessed | tf_op | source)
XLA Modules:
  0.0 396.4 jit_solution(3776987094872370002)
XLA Ops:
  7.2 1.1 copy.38
  8.3 1.1 copy.39
  9.5 0.8 pad_maximum_fusion
  10.4 4.1 %collective-permute-start.1 = (bf16[256,2304]{1,0:T(8,128)(2,1)}, bf16[256,2304]{1,0:T(8,128)(2,1)S(1)}, u32[]{:S(2)}, u32[]{:S(2)}) collective-permute-start(bf16[256,2304]{1,0:T(8,128)(2,1)} %param.14), channel_id=1, source_target_pairs={{0,16},{8,24},{16,0},{24,8},{1,17},{9,25},{17,1},{25,9},{2,18},{10... | collective-permute-start | bytes 3538952 | tf_op jit(solution)/shard_map/ppermute | solution.py:104
  14.5 1.3 collective-permute-start
  16.5 0.7 copy.37
  17.6 1.9 fusion.35
  20.1 88.8 %collective-permute-done.1 = bf16[256,2304]{1,0:T(8,128)(2,1)S(1)} collective-permute-done((bf16[256,2304]{1,0:T(8,128)(2,1)}, bf16[256,2304]{1,0:T(8,128)(2,1)S(1)}, u32[]{:S(2)}, u32[]{:S(2)}) %collective-permute-start.1) | collective-permute-done | bytes 1179680 | tf_op jit(solution)/shard_map/ppermute | solution.py:104
  109.0 114.0 %all-gather.3.cloned.1.call-done = bf16[2048,2048]{0,1:T(8,128)(2,1)} async-done(((bf16[128,2048]{0,1:T(8,128)(2,1)}), bf16[2048,2048]{0,1:T(8,128)(2,1)}) %all-gather.3.cloned.1.call-update) | async-done | bytes 8388624 | tf_op jit(solution)/shard_map/all_gather | solution.py:108
  222.9 26.9 %conditional.1 = (f32[8,2,128]{2,1,0:T(2,128)S(1)}, f32[8,2,128,128]{2,3,1,0:T(8,128)S(1)}) conditional(s32[]{:T(128)} %convert_element_type.28, () %tuple.17, (pred[128,2048]{0,1:T(8,128)(4,1)S(1)}, bf16[2048,2048]{0,1:T(8,128)(2,1)}, bf16[128,2048]{1,0:T(8,128)(2,1)}) %tuple.19), branch_computations={%region_4.5_spmd, %region_5.7_spmd} | conditional | flops 2181036032 | bytes 80748616 | solution.py:74
  222.9 6.1 %fusion.36 = (bf16[2048,1024]{0,1:T(8,128)(2,1)}, bf16[2048,1024]{0,1:T(8,128)(2,1)}) fusion(bf16[2048,2048]{0,1:T(8,128)(2,1)} %get-tuple-element.11), kind=kLoop, calls=%fused_computation.68 | loop fusion | bytes 16777216 | tf_op jit(solution)/shard_map/slice | solution.py:110
  229.4 11.8 %fusion = (f32[8,2,128]{2,1,0:T(2,128)S(1)}, f32[8,2048,128,2]{2,1,3,0:T(8,128)}) fusion(pred[128,2048]{0,1:T(8,128)(4,1)S(1)} %get-tuple-element.10, bf16[2048,8,128,1]{0,2,3,1:T(8,128)(2,1)} %bitcast.34, bf16[128,8,2,128]{3,2,1,0:T(2,128)(2,1)S(1)} %reshape.168), kind=kOutput, calls=%fused_computation.1 | convolution fusion | flops 1090516992 | bytes 21766144 | tf_op jit(solution)/shard_map/cond/branch_1_fun/qgrd,kgd->grqk/dot_general | solution.py:55
  241.2 8.6 %fusion.2 = f32[8,2,128,128]{2,3,1,0:T(8,128)S(1)} fusion(bf16[2048,8,128,1]{0,2,3,1:T(8,128)(2,1)S(1)} %bitcast.33, f32[8,2048,128,2]{2,1,3,0:T(8,128)} %get-tuple-element.37, pred[128,2048]{0,1:T(8,128)(4,1)S(1)} %get-tuple-element.10), kind=kOutput, calls=%fused_computation.3 | convolution fusion | flops 1090519040 | bytes 22282240 | tf_op jit(solution)/shard_map/cond | solution.py:74
  249.8 0.9 divide_convert_fusion
  250.8 7.5 %all-gather.5.cloned.1.call-done = bf16[128,4096]{0,1:T(8,128)(2,1)} async-done(((bf16[128,2048]{0,1:T(8,128)(2,1)}), bf16[128,4096]{0,1:T(8,128)(2,1)}) %all-gather.5.cloned.1.call-update) | async-done | bytes 1048592 | tf_op jit(solution)/shard_map/all_gather | solution.py:113
  258.2 2.4 copy.41
  260.6 3.9 all-to-all-start
  264.5 14.1 %all-to-all-done = bf16[4,128,4,256]{1,3,2,0:T(8,128)(2,1)S(1)} async-done(((bf16[4,128,4,256]{1,3,2,0:T(8,128)(2,1)}), bf16[4,128,4,256]{1,3,2,0:T(8,128)(2,1)S(1)}, u32[]{:S(2)}, u32[]{:S(2)}) %all-to-all-start) | async-done | bytes 1048608 | tf_op jit(solution)/shard_map/all_to_all | solution.py:116
  279.1 6.9 %convolution_bitcast_fusion = f32[512,2304]{1,0:T(8,128)} fusion(bf16[1,256,2304]{2,1,0:T(8,128)(2,1)} %bitcast.14, bf16[1,256,2304]{2,1,0:T(8,128)(2,1)} %bitcast.40, bf16[1,256,2304]{2,1,0:T(8,128)(2,1)} %bitcast.41, bf16[1,256,2304]{2,1,0:T(8,128)(2,1)S(1)} %bitcast.39, s32[]{:T(128)S(6)} %select_n.118, bf16[512,4,256]{2,0,1:T(8,128)(2,1)S(1)} %bitcast.37), kind=kOutput, calls=%fused_computation.10 | convolution fusion | flops 2423521280 | bytes 10485764 | tf_op jit(solution)/shard_map/dot_general | solution.py:118
  286.1 57.4 %reduce-scatter.2.cloned.1.call-done = f32[128,2304]{1,0:T(8,128)} async-done(((f32[512,2304]{1,0:T(8,128)}), f32[128,2304]{1,0:T(8,128)}) %reduce-scatter.2.cloned.1.call-update) | async-done | bytes 1179664 | tf_op jit(solution)/shard_map/reduce_scatter | solution.py:121
  343.5 1.4 multiply_reduce_fusion.1
  344.9 2.5 psum.14
  347.4 2.4 multiply_reduce_fusion
  350.0 39.4 %psum.15 = f32[16]{0:T(128)S(1)} all-reduce(f32[16]{0:T(128)S(1)} %select_reduce_fusion), channel_id=1, replica_groups=mesh['ca'=4,'cb'=4,'head'=2] {'ca','cb','head'}, use_global_device_ids=true, to_apply=%region_12.13 | all-reduce | flops 16 | bytes 128 | tf_op jit(solution)/shard_map/psum | solution.py:128
  (38 shorter events, 2.8 us)
Async XLA Ops:
  7.2 215.8 %all-gather.3.cloned.1.call-start = ((), (), s32[]{:S(2)}) async-start(), calls=%async_computation.2 | async-start | bytes 8912896 | tf_op jit(solution)/shard_map/all_gather | solution.py:108
  10.3 247.9 %all-gather.5.cloned.1.call-start = ((), (), s32[]{:S(2)}) async-start(), calls=%async_computation.3 | async-start | bytes 1572864 | tf_op jit(solution)/shard_map/all_gather | solution.py:113
  10.4 98.6 %collective-permute-start.1 = (bf16[256,2304]{1,0:T(8,128)(2,1)}, bf16[256,2304]{1,0:T(8,128)(2,1)S(1)}, u32[]{:S(2)}, u32[]{:S(2)}) collective-permute-start(bf16[256,2304]{1,0:T(8,128)(2,1)} %param.14), channel_id=1, source_target_pairs={{0,16},{8,24},{16,0},{24,8},{1,17},{9,25},{17,1},{25,9},{2,18},{10... | collective-permute-start | bytes 3538952 | tf_op jit(solution)/shard_map/ppermute | solution.py:104
  14.5 94.5 %collective-permute-start = (bf16[256,2304]{1,0:T(8,128)(2,1)}, bf16[256,2304]{1,0:T(8,128)(2,1)S(1)}, u32[]{:S(2)}, u32[]{:S(2)}) collective-permute-start(bf16[256,2304]{1,0:T(8,128)(2,1)} %param.14), channel_id=1, source_target_pairs={{0,24},{8,0},{16,8},{24,16},{1,25},{9,1},{17,9},{25,17},{2,26},{10... | collective-permute-start | bytes 3538952 | tf_op jit(solution)/shard_map/ppermute | solution.py:104
  15.8 93.2 %collective-permute-start.2 = (bf16[256,2304]{1,0:T(8,128)(2,1)}, bf16[256,2304]{1,0:T(8,128)(2,1)}, u32[]{:S(2)}, u32[]{:S(2)}) collective-permute-start(bf16[256,2304]{1,0:T(8,128)(2,1)} %param.14), channel_id=1, source_target_pairs={{0,8},{8,16},{16,24},{24,0},{1,9},{9,17},{17,25},{25,1},{2,10},{10... | collective-permute-start | bytes 3538952 | tf_op jit(solution)/shard_map/ppermute | solution.py:104
  109.0 114.0 %copy-start.7 = (bf16[256,2304]{1,0:T(8,128)(2,1)}, bf16[256,2304]{1,0:T(8,128)(2,1)S(1)}, u32[]{:S(2)}) copy-start(bf16[256,2304]{1,0:T(8,128)(2,1)S(1)} %collective-permute-done.1) | copy-start | bytes 3538948
  109.0 114.0 %copy-start.8 = (bf16[256,2304]{1,0:T(8,128)(2,1)}, bf16[256,2304]{1,0:T(8,128)(2,1)S(1)}, u32[]{:S(2)}) copy-start(bf16[256,2304]{1,0:T(8,128)(2,1)S(1)} %collective-permute-done) | copy-start | bytes 3538948
  222.9 6.1 %copy-start.2 = (bf16[128,2048]{1,0:T(8,128)(2,1)S(1)}, bf16[128,2048]{1,0:T(8,128)(2,1)}, u32[]{:S(2)}) copy-start(bf16[128,2048]{1,0:T(8,128)(2,1)} %get-tuple-element.30) | copy-start | bytes 1572868 | tf_op jit(solution)/shard_map/cond
  229.4 11.8 %copy-start = (bf16[2048,1024]{0,1:T(8,128)(2,1)S(1)}, bf16[2048,1024]{0,1:T(8,128)(2,1)}, u32[]{:S(2)}) copy-start(bf16[2048,1024]{0,1:T(8,128)(2,1)} %get-tuple-element.34) | copy-start | bytes 12582916 | tf_op jit(solution)/shard_map/cond
  249.8 29.3 %copy-start.6 = (bf16[256,2304]{1,0:T(8,128)(2,1)S(1)}, bf16[256,2304]{1,0:T(8,128)(2,1)}, u32[]{:S(2)}) copy-start(bf16[256,2304]{1,0:T(8,128)(2,1)} %param.14) | copy-start | bytes 3538948
  260.6 18.0 %all-to-all-start = ((bf16[4,128,4,256]{1,3,2,0:T(8,128)(2,1)}), bf16[4,128,4,256]{1,3,2,0:T(8,128)(2,1)S(1)}, u32[]{:S(2)}, u32[]{:S(2)}) async-start(bf16[4,128,4,256]{1,3,2,0:T(8,128)(2,1)} %copy.41), calls=%async_computation | async-start | bytes 2097152 | tf_op jit(solution)/shard_map/all_to_all | solution.py:116
  264.5 79.0 %reduce-scatter.2.cloned.1.call-start = ((), (), s32[]{:S(2)}) async-start(), calls=%async_computation.4 | async-start | bytes 5898240 | tf_op jit(solution)/shard_map/reduce_scatter | solution.py:121
  286.1 61.3 %copy-start.1 = (bf16[128,2304]{1,0:T(8,128)(2,1)S(1)}, bf16[128,2304]{1,0:T(8,128)(2,1)}, u32[]{:S(2)}) copy-start(bf16[128,2304]{1,0:T(8,128)(2,1)} %param.13) | copy-start | bytes 1769476
  286.1 61.3 %copy-start.3 = (f32[2304]{0:T(1024)S(1)}, f32[2304]{0:T(1024)}, u32[]{:S(2)}) copy-start(f32[2304]{0:T(1024)} %param.16) | copy-start | bytes 27652
  286.1 61.3 %copy-start.4 = (f32[2304]{0:T(1024)S(1)}, f32[2304]{0:T(1024)}, u32[]{:S(2)}) copy-start(f32[2304]{0:T(1024)} %param.15) | copy-start | bytes 27652
  286.1 103.3 %copy-start.5 = (s32[16]{0:T(128)S(1)}, s32[16]{0:T(128)}, u32[]{:S(2)}) copy-start(s32[16]{0:T(128)} %param.17) | copy-start | bytes 196
Sparse Core Ops, SparseCore 0:
  11.3 211.6 all-gather.2
  250.9 7.2 all-gather.4
  286.2 57.2 reduce-scatter.1

commit v3 on v2

--- a/solution.py
+++ b/solution.py
@@ -24,6 +24,16 @@
 
 def document_of(positions, doc_ends):
     return jnp.sum((positions[:, None] >= doc_ends[None, :]).astype(jnp.int32), axis=1)
+
+
+def butterfly_sum(x, axes):
+    for axis in axes:
+        size = lax.axis_size(axis)
+        bit = 1
+        while bit < size:
+            x = x + lax.ppermute(x, axis, [(i, i ^ bit) for i in range(size)])
+            bit *= 2
+    return x
 
 
 def shards(queries, keys, values, hidden_in, out_weight, out_gain, reward_weight, doc_lengths):
@@ -125,7 +135,7 @@
     tok_reward = jnp.sum(out32 * reward_weight[None, :], axis=1)
     onehot = (query_doc[:, None] == jnp.arange(NDOC, dtype=jnp.int32)[None, :]).astype(jnp.float32)
     partial_sums = jnp.sum(onehot * tok_reward[:, None], axis=0)
-    totals = lax.psum(partial_sums, CTX + ("head",))
+    totals = butterfly_sum(partial_sums, CTX + ("head",))
     rewards = totals / jnp.sqrt(doc_lengths.astype(jnp.float32))
     return (out32.astype(jnp.bfloat16), rewards)
 

time: 397 us -> 374 us (0.942)
  blocking collectives: 41.8 us -> 2.46 us
  waiting for transfers between devices: 282 us -> 291 us
  starting transfers between devices: 10.1 us -> 16.8 us
    psum x1 -> x0, blocking collectives: 39.4 us -> none  [shards(): totals = lax.psum(partial_sums, CTX + ('head',))]
    ppermute x0 -> x5, waiting for transfers between devices: none -> 9.55 us  [butterfly_sum(): x = x + lax.ppermute(x, axis, [(i, i ^ bit) for i in range(size)])]
    ppermute x0 -> x5, starting transfers between devices: none -> 6.69 us  [butterfly_sum(): x = x + lax.ppermute(x, axis, [(i, i ^ bit) for i in range(size)])]
  transfers between devices with their start and end apart: 7 -> 12, of which waited for: 5 -> 10; matrix products, arithmetic and copies ran while one was open for 1% -> 1% of each run, Pallas kernels for 0% -> 0%
where the time goes in v3:
time: 374 us; the launch traced here: 373 us
  waiting for transfers between devices  291 us (78%)
  matrix products  27.3 us (7%)
  starting transfers between devices  16.8 us (4%)
  between operations  14.5 us (4%)
  local copies, waits for them, and re-layouts  12.3 us (3%)
  other arithmetic  8.5 us (2%)
    all_gather x1, waiting for transfers between devices, shards(): lax.all_gather(jnp.concatenate([keys, values], axis=1), CTX, axis=0, tile...  114 us
    ppermute x3, waiting for transfers between devices, shards(): lax.ppermute(out_weight, 'ca', [(i, (i - shift) % outer) for i in range(o...  88.8 us
    reduce_scatter x1, waiting for transfers between devices, shards(): mixed = lax.psum_scatter(partial, 'cb', scatter_dimension=0, tiled=True)  57.4 us
    all_to_all x1, waiting for transfers between devices, shards(): regrouped = lax.all_to_all(blocks, 'cb', 0, 0, tiled=True)  14.1 us
    dot_general x1, matrix products, compute(): jnp.einsum('qgrd,kgd->grqk', q_groups, key_piece.reshape(count, kv_local,...  11.8 us
    ppermute x5, waiting for transfers between devices, butterfly_sum(): x = x + lax.ppermute(x, axis, [(i, i ^ bit) for i in range(size)])  9.55 us
    cond x1, matrix products, attend_block(): return lax.cond(jnp.any(visible), compute, lambda carry: carry, state)  8.61 us
  transfers between devices with their start and end apart: 12, of which 10 were waited for; matrix products, arithmetic and copies ran while one was open for 1% of the time, Pallas kernels for 0%

profile of v3, /device:TPU:0, one launch (start us, length us, event | category | flops | bytes accessed | tf_op | source)
XLA Modules:
  0.0 373.2 jit_solution(11176357874266191357)
XLA Ops:
  10.4 4.1 %collective-permute-start.1 = (bf16[256,2304]{1,0:T(8,128)(2,1)}, bf16[256,2304]{1,0:T(8,128)(2,1)S(1)}, u32[]{:S(2)}, u32[]{:S(2)}) collective-permute-start(bf16[256,2304]{1,0:T(8,128)(2,1)} %param.14), channel_id=1, source_target_pairs={{0,16},{8,24},{16,0},{24,8},{1,17},{9,25},{17,1},{25,9},{2,18},{10... | collective-permute-start | bytes 3538952 | tf_op jit(solution)/shard_map/ppermute | solution.py:114
  17.6 1.9 fusion.35
  20.1 88.8 %collective-permute-done.1 = bf16[256,2304]{1,0:T(8,128)(2,1)S(1)} collective-permute-done((bf16[256,2304]{1,0:T(8,128)(2,1)}, bf16[256,2304]{1,0:T(8,128)(2,1)S(1)}, u32[]{:S(2)}, u32[]{:S(2)}) %collective-permute-start.1) | collective-permute-done | bytes 1179680 | tf_op jit(solution)/shard_map/ppermute | solution.py:114
  109.0 114.0 %all-gather.3.cloned.1.call-done = bf16[2048,2048]{0,1:T(8,128)(2,1)} async-done(((bf16[128,2048]{0,1:T(8,128)(2,1)}), bf16[2048,2048]{0,1:T(8,128)(2,1)}) %all-gather.3.cloned.1.call-update) | async-done | bytes 8388624 | tf_op jit(solution)/shard_map/all_gather | solution.py:118
  222.9 26.9 %conditional.1 = (f32[8,2,128]{2,1,0:T(2,128)S(1)}, f32[8,2,128,128]{2,3,1,0:T(8,128)S(1)}) conditional(s32[]{:T(128)} %convert_element_type.28, () %tuple.17, (pred[128,2048]{0,1:T(8,128)(4,1)S(1)}, bf16[2048,2048]{0,1:T(8,128)(2,1)}, bf16[128,2048]{1,0:T(8,128)(2,1)}) %tuple.19), branch_computations={%region_4.5_spmd, %region_5.7_spmd} | conditional | flops 2181036032 | bytes 80748616 | solution.py:84
  222.9 6.1 %fusion.36 = (bf16[2048,1024]{0,1:T(8,128)(2,1)}, bf16[2048,1024]{0,1:T(8,128)(2,1)}) fusion(bf16[2048,2048]{0,1:T(8,128)(2,1)} %get-tuple-element.11), kind=kLoop, calls=%fused_computation.68 | loop fusion | bytes 16777216 | tf_op jit(solution)/shard_map/slice | solution.py:120
  229.4 11.8 %fusion = (f32[8,2,128]{2,1,0:T(2,128)S(1)}, f32[8,2048,128,2]{2,1,3,0:T(8,128)}) fusion(pred[128,2048]{0,1:T(8,128)(4,1)S(1)} %get-tuple-element.10, bf16[2048,8,128,1]{0,2,3,1:T(8,128)(2,1)} %bitcast.34, bf16[128,8,2,128]{3,2,1,0:T(2,128)(2,1)S(1)} %reshape.168), kind=kOutput, calls=%fused_computation.1 | convolution fusion | flops 1090516992 | bytes 21766144 | tf_op jit(solution)/shard_map/cond/branch_1_fun/qgrd,kgd->grqk/dot_general | solution.py:65
  241.2 8.6 %fusion.2 = f32[8,2,128,128]{2,3,1,0:T(8,128)S(1)} fusion(bf16[2048,8,128,1]{0,2,3,1:T(8,128)(2,1)S(1)} %bitcast.33, f32[8,2048,128,2]{2,1,3,0:T(8,128)} %get-tuple-element.37, pred[128,2048]{0,1:T(8,128)(4,1)S(1)} %get-tuple-element.10), kind=kOutput, calls=%fused_computation.3 | convolution fusion | flops 1090519040 | bytes 22282240 | tf_op jit(solution)/shard_map/cond | solution.py:84
  250.8 7.5 %all-gather.5.cloned.1.call-done = bf16[128,4096]{0,1:T(8,128)(2,1)} async-done(((bf16[128,2048]{0,1:T(8,128)(2,1)}), bf16[128,4096]{0,1:T(8,128)(2,1)}) %all-gather.5.cloned.1.call-update) | async-done | bytes 1048592 | tf_op jit(solution)/shard_map/all_gather | solution.py:123
  258.2 2.3 copy.41
  260.6 3.9 %all-to-all-start = ((bf16[4,128,4,256]{1,3,2,0:T(8,128)(2,1)}), bf16[4,128,4,256]{1,3,2,0:T(8,128)(2,1)S(1)}, u32[]{:S(2)}, u32[]{:S(2)}) async-start(bf16[4,128,4,256]{1,3,2,0:T(8,128)(2,1)} %copy.41), calls=%async_computation | async-start | bytes 2097152 | tf_op jit(solution)/shard_map/all_to_all | solution.py:126
  264.5 14.1 %all-to-all-done = bf16[4,128,4,256]{1,3,2,0:T(8,128)(2,1)S(1)} async-done(((bf16[4,128,4,256]{1,3,2,0:T(8,128)(2,1)}), bf16[4,128,4,256]{1,3,2,0:T(8,128)(2,1)S(1)}, u32[]{:S(2)}, u32[]{:S(2)}) %all-to-all-start) | async-done | bytes 1048608 | tf_op jit(solution)/shard_map/all_to_all | solution.py:126
  279.1 6.9 %convolution_bitcast_fusion = f32[512,2304]{1,0:T(8,128)} fusion(bf16[1,256,2304]{2,1,0:T(8,128)(2,1)} %bitcast.14, bf16[1,256,2304]{2,1,0:T(8,128)(2,1)} %bitcast.40, bf16[1,256,2304]{2,1,0:T(8,128)(2,1)} %bitcast.41, bf16[1,256,2304]{2,1,0:T(8,128)(2,1)S(1)} %bitcast.39, s32[]{:T(128)S(6)} %select_n.118, bf16[512,4,256]{2,0,1:T(8,128)(2,1)S(1)} %bitcast.37), kind=kOutput, calls=%fused_computation.10 | convolution fusion | flops 2423521280 | bytes 10485764 | tf_op jit(solution)/shard_map/dot_general | solution.py:128
  286.1 57.4 %reduce-scatter.2.cloned.1.call-done = f32[128,2304]{1,0:T(8,128)} async-done(((f32[512,2304]{1,0:T(8,128)}), f32[128,2304]{1,0:T(8,128)}) %reduce-scatter.2.cloned.1.call-update) | async-done | bytes 1179664 | tf_op jit(solution)/shard_map/reduce_scatter | solution.py:131
  343.5 1.4 multiply_reduce_fusion.1
  344.9 2.5 psum.7
  347.4 2.4 multiply_reduce_fusion
  349.9 1.6 collective-permute-start.3
  351.5 2.0 collective-permute-done.3
  353.5 2.4 collective-permute-start.4
  356.0 2.0 collective-permute-done.4
  358.0 1.4 collective-permute-start.5
  359.3 2.2 collective-permute-done.5
  362.9 2.2 collective-permute-done.6
  (51 shorter events, 11.3 us)
Async XLA Ops:
  7.2 215.8 %all-gather.3.cloned.1.call-start = ((), (), s32[]{:S(2)}) async-start(), calls=%async_computation.2 | async-start | bytes 8912896 | tf_op jit(solution)/shard_map/all_gather | solution.py:118
  10.3 247.9 %all-gather.5.cloned.1.call-start = ((), (), s32[]{:S(2)}) async-start(), calls=%async_computation.3 | async-start | bytes 1572864 | tf_op jit(solution)/shard_map/all_gather | solution.py:123
  10.4 98.6 %collective-permute-start.1 = (bf16[256,2304]{1,0:T(8,128)(2,1)}, bf16[256,2304]{1,0:T(8,128)(2,1)S(1)}, u32[]{:S(2)}, u32[]{:S(2)}) collective-permute-start(bf16[256,2304]{1,0:T(8,128)(2,1)} %param.14), channel_id=1, source_target_pairs={{0,16},{8,24},{16,0},{24,8},{1,17},{9,25},{17,1},{25,9},{2,18},{10... | collective-permute-start | bytes 3538952 | tf_op jit(solution)/shard_map/ppermute | solution.py:114
  14.5 94.5 %collective-permute-start = (bf16[256,2304]{1,0:T(8,128)(2,1)}, bf16[256,2304]{1,0:T(8,128)(2,1)S(1)}, u32[]{:S(2)}, u32[]{:S(2)}) collective-permute-start(bf16[256,2304]{1,0:T(8,128)(2,1)} %param.14), channel_id=1, source_target_pairs={{0,24},{8,0},{16,8},{24,16},{1,25},{9,1},{17,9},{25,17},{2,26},{10... | collective-permute-start | bytes 3538952 | tf_op jit(solution)/shard_map/ppermute | solution.py:114
  15.8 93.2 %collective-permute-start.2 = (bf16[256,2304]{1,0:T(8,128)(2,1)}, bf16[256,2304]{1,0:T(8,128)(2,1)}, u32[]{:S(2)}, u32[]{:S(2)}) collective-permute-start(bf16[256,2304]{1,0:T(8,128)(2,1)} %param.14), channel_id=1, source_target_pairs={{0,8},{8,16},{16,24},{24,0},{1,9},{9,17},{17,25},{25,1},{2,10},{10... | collective-permute-start | bytes 3538952 | tf_op jit(solution)/shard_map/ppermute | solution.py:114
  109.0 114.0 %copy-start.7 = (bf16[256,2304]{1,0:T(8,128)(2,1)}, bf16[256,2304]{1,0:T(8,128)(2,1)S(1)}, u32[]{:S(2)}) copy-start(bf16[256,2304]{1,0:T(8,128)(2,1)S(1)} %collective-permute-done.1) | copy-start | bytes 3538948
  109.0 114.0 %copy-start.8 = (bf16[256,2304]{1,0:T(8,128)(2,1)}, bf16[256,2304]{1,0:T(8,128)(2,1)S(1)}, u32[]{:S(2)}) copy-start(bf16[256,2304]{1,0:T(8,128)(2,1)S(1)} %collective-permute-done) | copy-start | bytes 3538948
  222.9 6.1 %copy-start.2 = (bf16[128,2048]{1,0:T(8,128)(2,1)S(1)}, bf16[128,2048]{1,0:T(8,128)(2,1)}, u32[]{:S(2)}) copy-start(bf16[128,2048]{1,0:T(8,128)(2,1)} %get-tuple-element.30) | copy-start | bytes 1572868 | tf_op jit(solution)/shard_map/cond
  229.4 11.8 %copy-start = (bf16[2048,1024]{0,1:T(8,128)(2,1)S(1)}, bf16[2048,1024]{0,1:T(8,128)(2,1)}, u32[]{:S(2)}) copy-start(bf16[2048,1024]{0,1:T(8,128)(2,1)} %get-tuple-element.34) | copy-start | bytes 12582916 | tf_op jit(solution)/shard_map/cond
  249.8 29.3 %copy-start.6 = (bf16[256,2304]{1,0:T(8,128)(2,1)S(1)}, bf16[256,2304]{1,0:T(8,128)(2,1)}, u32[]{:S(2)}) copy-start(bf16[256,2304]{1,0:T(8,128)(2,1)} %param.14) | copy-start | bytes 3538948
  260.6 18.0 %all-to-all-start = ((bf16[4,128,4,256]{1,3,2,0:T(8,128)(2,1)}), bf16[4,128,4,256]{1,3,2,0:T(8,128)(2,1)S(1)}, u32[]{:S(2)}, u32[]{:S(2)}) async-start(bf16[4,128,4,256]{1,3,2,0:T(8,128)(2,1)} %copy.41), calls=%async_computation | async-start | bytes 2097152 | tf_op jit(solution)/shard_map/all_to_all | solution.py:126
  264.5 79.0 %reduce-scatter.2.cloned.1.call-start = ((), (), s32[]{:S(2)}) async-start(), calls=%async_computation.4 | async-start | bytes 5898240 | tf_op jit(solution)/shard_map/reduce_scatter | solution.py:131
  286.1 61.3 %copy-start.1 = (bf16[128,2304]{1,0:T(8,128)(2,1)S(1)}, bf16[128,2304]{1,0:T(8,128)(2,1)}, u32[]{:S(2)}) copy-start(bf16[128,2304]{1,0:T(8,128)(2,1)} %param.13) | copy-start | bytes 1769476
  286.1 61.3 %copy-start.3 = (f32[2304]{0:T(1024)S(1)}, f32[2304]{0:T(1024)}, u32[]{:S(2)}) copy-start(f32[2304]{0:T(1024)} %param.16) | copy-start | bytes 27652
  286.1 61.3 %copy-start.4 = (f32[2304]{0:T(1024)S(1)}, f32[2304]{0:T(1024)}, u32[]{:S(2)}) copy-start(f32[2304]{0:T(1024)} %param.15) | copy-start | bytes 27652
  286.1 80.1 %copy-start.5 = (s32[16]{0:T(128)S(1)}, s32[16]{0:T(128)}, u32[]{:S(2)}) copy-start(s32[16]{0:T(128)} %param.17) | copy-start | bytes 196
  349.9 3.6 collective-permute-start.3
  353.5 4.4 %collective-permute-start.4 = (f32[16]{0:T(128)S(1)}, f32[16]{0:T(128)S(1)}, u32[]{:S(2)}, u32[]{:S(2)}) collective-permute-start(f32[16]{0:T(128)S(1)} %add.147), channel_id=1, source_target_pairs={{0,16},{8,24},{16,0},{24,8},{1,17},{9,25},{17,1},{25,9},{2,18},{10... | collective-permute-start | bytes 200 | tf_op jit(solution)/shard_map/ppermute | solution.py:34
  358.0 3.5 collective-permute-start.5
  361.5 3.5 collective-permute-start.6
  365.1 1.1 collective-permute-start.7
Sparse Core Ops, SparseCore 0:
  11.3 211.6 all-gather.2
  250.9 7.2 all-gather.4
  286.2 57.2 reduce-scatter.1

commit v4 on v3

--- a/solution.py
+++ b/solution.py
@@ -11,7 +11,8 @@
 
 
 soft_cap = 50.0
-CTX = ("ca", "cb")
+CTX = ("c0", "c1", "c2")
+INNER = ("c1", "c2")
 
 
 def storage_positions(rows, tok_dev, n_ctx):
@@ -24,6 +25,35 @@
 
 def document_of(positions, doc_ends):
     return jnp.sum((positions[:, None] >= doc_ends[None, :]).astype(jnp.int32), axis=1)
+
+
+def line_gather(x, axis):
+    n = lax.axis_size(axis)
+    i = lax.axis_index(axis)
+    if n == 2:
+        other = lax.ppermute(x, axis, [(0, 1), (1, 0)])
+        return lax.dynamic_slice_in_dim(jnp.stack([x, other, x]), i, 2, axis=0)
+    ahead, behind = x, x
+    from_left, from_right = [], []
+    for _ in range(n - 1):
+        ahead = lax.ppermute(ahead, axis, [(k, k + 1) for k in range(n - 1)])
+        behind = lax.ppermute(behind, axis, [(k + 1, k) for k in range(n - 1)])
+        from_left.append(ahead)
+        from_right.append(behind)
+    stacked = jnp.stack(from_left[::-1] + [x] + from_right)
+    return lax.dynamic_slice_in_dim(stacked, (n - 1) - i, n, axis=0)
+
+
+def gather_tokens(x):
+    width = x.shape[1]
+    first = (width // 4) // 128 * 128
+    second = first + (width - first) // 2 // 128 * 128
+    part_a, part_b, part_c = x[:, :first], x[:, first:second], x[:, second:]
+    got_a = line_gather(line_gather(line_gather(part_a, "c2"), "c1"), "c0")
+    got_b = line_gather(line_gather(line_gather(part_b, "c0"), "c2"), "c1").transpose(2, 0, 1, 3, 4)
+    got_c = line_gather(line_gather(line_gather(part_c, "c0"), "c1"), "c2").transpose(2, 1, 0, 3, 4)
+    rows = lax.axis_size(CTX) * x.shape[0]
+    return jnp.concatenate([g.reshape(rows, -1) for g in (got_a, got_b, got_c)], axis=1)
 
 
 def butterfly_sum(x, axes):
@@ -106,29 +136,24 @@
         jnp.zeros((kv_local, group_repeat, tok_dev, HEAD_WIDTH), jnp.float32),
         jnp.zeros((kv_local, group_repeat, tok_dev), jnp.float32),
     )
-    outer = lax.axis_size("ca")
-    inner = lax.axis_size("cb")
+    outer = lax.axis_size("c0")
+    inner = lax.axis_size(INNER)
     rows_each = out_weight.shape[0]
-    place = lax.axis_index("ca")
-    pieces = [out_weight] + [
-        lax.ppermute(out_weight, "ca", [(i, (i - shift) % outer) for i in range(outer)])
-        for shift in range(1, outer)
-    ]
     kv_width = keys.shape[1]
-    both = lax.all_gather(jnp.concatenate([keys, values], axis=1), CTX, axis=0, tiled=True)
-    both, pieces = lax.optimization_barrier((both, pieces))
+    both = gather_tokens(jnp.concatenate([keys, values], axis=1))
+    both, out_weight = lax.optimization_barrier((both, out_weight))
+    weight_rows = line_gather(out_weight, "c0")
     numerator, denominator = attend(initial, both[:, :kv_width], both[:, kv_width:], jnp.int32(0))
     attended = (numerator / denominator[..., None]).astype(jnp.bfloat16)
     attended = attended.transpose(2, 0, 1, 3).reshape(tok_dev, kv_local * group_repeat * HEAD_WIDTH)
     all_heads = lax.all_gather(attended, "head", axis=1, tiled=True)
-    weight_rows = jnp.stack(pieces).reshape(outer * rows_each, out_weight.shape[1])
+    weight_rows = weight_rows.reshape(outer * rows_each, out_weight.shape[1])
     blocks = all_heads.reshape(tok_dev, outer, inner, rows_each).transpose(2, 0, 1, 3)
-    regrouped = lax.all_to_all(blocks, "cb", 0, 0, tiled=True)
-    regrouped = jnp.roll(regrouped.reshape(inner * tok_dev, outer, rows_each), -place, axis=1)
+    regrouped = lax.all_to_all(blocks, INNER, 0, 0, tiled=True)
     partial = jnp.dot(
         regrouped.reshape(inner * tok_dev, outer * rows_each), weight_rows, preferred_element_type=jnp.float32
     )
-    mixed = lax.psum_scatter(partial, "cb", scatter_dimension=0, tiled=True)
+    mixed = lax.psum_scatter(partial, INNER, scatter_dimension=0, tiled=True)
     squares = lax.psum(jnp.sum(mixed * mixed, axis=1), "head")
     normed = mixed / jnp.sqrt(squares / D + 1e-06)[:, None]
     out32 = hidden_in.astype(jnp.float32) + normed * out_gain[None, :]
@@ -142,10 +167,7 @@
 
 def solution(mesh):
     n_ctx, n_head = mesh.devices.shape
-    inner = 1
-    while inner * inner * 4 <= n_ctx:
-        inner *= 2
-    split = Mesh(mesh.devices.reshape(n_ctx // inner, inner, n_head), ("ca", "cb", "head"))
+    split = Mesh(mesh.devices.reshape(n_ctx // 4, 2, 2, n_head), CTX + ("head",))
     rows = P(CTX, "head")
     in_specs = (rows, rows, rows, rows, rows, P("head"), P("head"), P())
     out_specs = (rows, P())

time: 374 us -> 367 us (0.981)
  waiting for transfers between devices: 291 us -> 142 us
  starting transfers between devices: 16.8 us -> 83.9 us
  local copies, waits for them, and re-layouts: 12.3 us -> 44.4 us
  other arithmetic: 8.5 us -> 34.9 us
  blocking collectives: 2.46 us -> 20 us
    all_gather x1 -> x0, waiting for transfers between devices: 114 us -> none  [shards(): lax.all_gather(jnp.concatenate([keys, values], axis=1), CTX, axis=0, tile...]
    ppermute x3 -> x30, starting transfers between devices: 6.13 us -> 77.1 us  [the longest x12 55.1 us: line_gather(): ahead = lax.ppermute(ahead, axis, [(k, k + 1) for k in range(n - 1)])]
    all_to_all x0 -> x1, blocking collectives: none -> 17.6 us  [shards(): regrouped = lax.all_to_all(blocks, INNER, 0, 0, tiled=True)]
    reshape x0 -> x4, local copies, waits for them, and re-layouts: none -> 15.1 us  [the longest x3 13.4 us: gather_tokens(): g.reshape(rows, -1)]
    all_to_all x1 -> x0, waiting for transfers between devices: 14.1 us -> none  [shards(): regrouped = lax.all_to_all(blocks, 'cb', 0, 0, tiled=True)]
    ppermute x3 -> x30, waiting for transfers between devices: 88.8 us -> 76.1 us  [the longest x12 44.7 us: line_gather(): behind = lax.ppermute(behind, axis, [(k + 1, k) for k in range(n - 1)])]
    transpose x1 -> x2, local copies, waits for them, and re-layouts: 2.35 us -> 14.7 us  [the longest x1 8.78 us: gather_tokens(): line_gather(line_gather(line_gather(part_c, 'c0'), 'c1'), 'c2')]
    transpose x0 -> x2, other arithmetic: none -> 9.94 us  [the longest x1 5.85 us: gather_tokens(): line_gather(line_gather(line_gather(part_c, 'c0'), 'c1'), 'c2')]
  transfers between devices with their start and end apart: 12 -> 37, of which waited for: 10 -> 13; matrix products, arithmetic and copies ran while one was open for 1% -> 18% of each run, Pallas kernels for 0% -> 0%
where the time goes in v4:
time: 367 us; the launch traced here: 365 us
  waiting for transfers between devices  142 us (39%)
  starting transfers between devices  83.9 us (23%)
  local copies, waits for them, and re-layouts  44.4 us (12%)
  other arithmetic  34.9 us (10%)
  matrix products  24.8 us (7%)
  blocking collectives  20 us (5%)
  between operations  15.4 us (4%)
    reduce_scatter x1, waiting for transfers between devices, shards(): mixed = lax.psum_scatter(partial, INNER, scatter_dimension=0, tiled=True)  56.1 us
    ppermute x12, starting transfers between devices, line_gather(): ahead = lax.ppermute(ahead, axis, [(k, k + 1) for k in range(n - 1)])  55.1 us
    ppermute x12, waiting for transfers between devices, line_gather(): behind = lax.ppermute(behind, axis, [(k + 1, k) for k in range(n - 1)])  44.7 us
    ppermute x12, waiting for transfers between devices, line_gather(): ahead = lax.ppermute(ahead, axis, [(k, k + 1) for k in range(n - 1)])  20.5 us
    all_to_all x1, blocking collectives, shards(): regrouped = lax.all_to_all(blocks, INNER, 0, 0, tiled=True)  17.6 us
    ppermute x12, starting transfers between devices, line_gather(): behind = lax.ppermute(behind, axis, [(k + 1, k) for k in range(n - 1)])  15.6 us
    reshape x3, local copies, waits for them, and re-layouts, gather_tokens(): g.reshape(rows, -1)  13.4 us
    dot_general x1, matrix products, compute(): jnp.einsum('qgrd,kgd->grqk', q_groups, key_piece.reshape(count, kv_local,...  11.9 us
  transfers between devices with their start and end apart: 37, of which 13 were waited for; matrix products, arithmetic and copies ran while one was open for 18% of the time, Pallas kernels for 0%

profile of v4, /device:TPU:0, one launch (start us, length us, event | category | flops | bytes accessed | tf_op | source)
XLA Modules:
  0.0 365.3 jit_solution(3798998583010074685)
XLA Ops:
  8.3 4.9 %collective-permute-start.8 = (bf16[128,768]{1,0:T(8,128)(2,1)S(1)}, bf16[128,768]{1,0:T(8,128)(2,1)S(1)}, u32[]{:S(2)}, u32[]{:S(2)}) collective-permute-start(bf16[128,768]{1,0:T(8,128)(2,1)S(1)} %get-tuple-element.36), channel_id=1, source_target_pairs={{0,8},{8,16},{16,24},{1,9},{9,17},{17,25},{2,10},{10,18},{18,26},{... | collective-permute-start | bytes 589832 | tf_op jit(solution)/shard_map/ppermute | solution.py:39
  17.0 4.6 %collective-permute-start.16 = (bf16[128,768]{1,0:T(8,128)(2,1)S(1)}, bf16[128,768]{1,0:T(8,128)(2,1)S(1)}, u32[]{:S(2)}, u32[]{:S(2)}) collective-permute-start(bf16[128,768]{1,0:T(8,128)(2,1)S(1)} %get-tuple-element.37), channel_id=1, source_target_pairs={{0,8},{8,16},{16,24},{1,9},{9,17},{17,25},{2,10},{10,18},{18,26},{... | collective-permute-start | bytes 589832 | tf_op jit(solution)/shard_map/ppermute | solution.py:39
  52.3 6.1 %collective-permute-done.13 = bf16[128,768]{1,0:T(8,128)(2,1)S(1)} collective-permute-done((bf16[128,768]{1,0:T(8,128)(2,1)S(1)}, bf16[128,768]{1,0:T(8,128)(2,1)S(1)}, u32[]{:S(2)}, u32[]{:S(2)}) %collective-permute-start.13) | collective-permute-done | bytes 196640 | tf_op jit(solution)/shard_map/ppermute | solution.py:40
  61.4 5.0 %collective-permute-start.3 = (bf16[2,2,128,512]{3,2,1,0:T(8,128)(2,1)S(1)}, bf16[2,2,128,512]{3,2,1,0:T(8,128)(2,1)S(1)}, u32[]{:S(2)}, u32[]{:S(2)}) collective-permute-start(bf16[2,2,128,512]{3,2,1,0:T(8,128)(2,1)S(1)} %collective-permute-done.2), channel_id=1, source_target_pairs={{0,8},{8,16},{16,24},{1,9},{9,17},{17,25},{2,10},{10,18},{18,26},{... | collective-permute-start | bytes 1572872 | tf_op jit(solution)/shard_map/ppermute | solution.py:39
  66.6 7.4 %collective-permute-done.5 = bf16[2,2,128,512]{3,2,1,0:T(8,128)(2,1)S(1)} collective-permute-done((bf16[2,2,128,512]{3,2,1,0:T(8,128)(2,1)S(1)}, bf16[2,2,128,512]{3,2,1,0:T(8,128)(2,1)S(1)}, u32[]{:S(2)}, u32[]{:S(2)}) %collective-permute-start.5) | collective-permute-done | bytes 524320 | tf_op jit(solution)/shard_map/ppermute | solution.py:40
  75.3 4.6 %collective-permute-start.4 = (bf16[2,2,128,512]{3,2,1,0:T(8,128)(2,1)S(1)}, bf16[2,2,128,512]{3,2,1,0:T(8,128)(2,1)S(1)}, u32[]{:S(2)}, u32[]{:S(2)}) collective-permute-start(bf16[2,2,128,512]{3,2,1,0:T(8,128)(2,1)S(1)} %collective-permute-done.3), channel_id=1, source_target_pairs={{0,8},{8,16},{16,24},{1,9},{9,17},{17,25},{2,10},{10,18},{18,26},{... | collective-permute-start | bytes 1572872 | tf_op jit(solution)/shard_map/ppermute | solution.py:39
  92.0 9.2 %collective-permute-done.7 = bf16[2,2,128,512]{3,2,1,0:T(8,128)(2,1)S(1)} collective-permute-done((bf16[2,2,128,512]{3,2,1,0:T(8,128)(2,1)S(1)}, bf16[2,2,128,512]{3,2,1,0:T(8,128)(2,1)S(1)}, u32[]{:S(2)}, u32[]{:S(2)}) %collective-permute-start.7) | collective-permute-done | bytes 524320 | tf_op jit(solution)/shard_map/ppermute | solution.py:40
  104.0 10.8 %collective-permute-done.15 = bf16[2,4,128,768]{3,2,1,0:T(8,128)(2,1)} collective-permute-done((bf16[2,4,128,768]{3,2,1,0:T(8,128)(2,1)}, bf16[2,4,128,768]{3,2,1,0:T(8,128)(2,1)}, u32[]{:S(2)}, u32[]{:S(2)}) %collective-permute-start.15) | collective-permute-done | bytes 1572896 | tf_op jit(solution)/shard_map/ppermute | solution.py:34
  118.9 5.9 %copy.32 = bf16[4,2,2,128,768]{3,2,1,0,4:T(2,128)(2,1)} copy(bf16[4,2,2,128,768]{4,3,0,2,1:T(8,128)(2,1)S(1)} %fusion.15) | data formatting | bytes 6291456 | tf_op jit(solution)/shard_map/transpose | solution.py:53
  124.8 4.8 %reshape.188 = bf16[2048,768]{0,1:T(8,128)(2,1)S(1)} reshape(bf16[4,2,2,128,768]{3,2,1,0,4:T(2,128)(2,1)} %copy.32) | data formatting | bytes 6291456 | tf_op jit(solution)/shard_map/reshape | solution.py:56
  129.6 5.8 %fusion.12 = bf16[4,2,2,128,768]{4,3,0,1,2:T(8,128)(2,1)} fusion(s32[]{:T(128)S(6)} %select_n.121, bf16[1,2,4,128,768]{4,3,2,1,0:T(8,128)(2,1)} %fusion.49, bf16[1,2,4,128,768]{4,3,2,1,0:T(8,128)(2,1)} %bitcast.40), kind=kLoop, calls=%fused_computation.19 | loop fusion | flops 3145728 | bytes 6291460 | tf_op jit(solution)/shard_map/transpose | solution.py:54
  135.4 8.8 %copy.33 = bf16[4,2,2,128,768]{3,2,1,0,4:T(2,128)(2,1)} copy(bf16[4,2,2,128,768]{4,3,0,1,2:T(8,128)(2,1)} %fusion.12) | data formatting | bytes 6291456 | tf_op jit(solution)/shard_map/transpose | solution.py:54
  144.2 6.1 %reshape.189 = bf16[2048,768]{0,1:T(8,128)(2,1)} reshape(bf16[4,2,2,128,768]{3,2,1,0,4:T(2,128)(2,1)} %copy.33) | data formatting | bytes 6291456 | tf_op jit(solution)/shard_map/reshape | solution.py:56
  150.4 6.5 %pad_maximum_fusion = bf16[2048,2048]{0,1:T(8,128)(2,1)} fusion(bf16[2048,768]{0,1:T(8,128)(2,1)} %reshape.189, bf16[2048,768]{0,1:T(8,128)(2,1)S(1)} %reshape.188, bf16[2048,512]{0,1:T(8,128)(2,1)} %copy.43), kind=kLoop, calls=%fused_computation.10 | loop fusion | flops 25165824 | bytes 16777216 | tf_op jit(solution)/shard_map/concatenate | solution.py:56
  162.0 20.3 %collective-permute-done.24 = bf16[256,2304]{1,0:T(8,128)(2,1)S(1)} collective-permute-done((bf16[256,2304]{1,0:T(8,128)(2,1)}, bf16[256,2304]{1,0:T(8,128)(2,1)S(1)}, u32[]{:S(2)}, u32[]{:S(2)}) %collective-permute-start.24) | collective-permute-done | bytes 1179680 | tf_op jit(solution)/shard_map/ppermute | solution.py:39
  182.3 5.3 %collective-permute-start.25 = (bf16[256,2304]{1,0:T(8,128)(2,1)S(1)}, bf16[256,2304]{1,0:T(8,128)(2,1)}, u32[]{:S(2)}, u32[]{:S(2)}) collective-permute-start(bf16[256,2304]{1,0:T(8,128)(2,1)S(1)} %collective-permute-done.24), channel_id=1, source_target_pairs={{0,8},{8,16},{16,24},{1,9},{9,17},{17,25},{2,10},{10,18},{18,26},{... | collective-permute-start | bytes 3538952 | tf_op jit(solution)/shard_map/ppermute | solution.py:39
  191.0 27.3 %conditional.1 = (f32[8,2,128]{2,1,0:T(2,128)S(1)}, f32[8,2,128,128]{2,3,1,0:T(8,128)S(1)}) conditional(s32[]{:T(128)} %convert_element_type.28, () %tuple.17, (pred[128,2048]{0,1:T(8,128)(4,1)}, bf16[2048,2048]{0,1:T(8,128)(2,1)}, bf16[128,2048]{1,0:T(8,128)(2,1)}) %tuple.19), branch_computations={%region_4.5_spmd, %region_5.7_spmd} | conditional | flops 2181036032 | bytes 81797216 | solution.py:114
  191.3 6.1 %fusion.39 = (bf16[2048,1024]{0,1:T(8,128)(2,1)}, bf16[2048,1024]{0,1:T(8,128)(2,1)}) fusion(bf16[2048,2048]{0,1:T(8,128)(2,1)} %get-tuple-element.11), kind=kLoop, calls=%fused_computation.121 | loop fusion | bytes 16777216 | tf_op jit(solution)/shard_map/slice | solution.py:146
  197.8 11.9 %fusion = (f32[8,2,128]{2,1,0:T(2,128)S(1)}, f32[8,2048,128,2]{2,1,3,0:T(8,128)}) fusion(pred[128,2048]{0,1:T(8,128)(4,1)} %get-tuple-element.10, bf16[2048,8,128,1]{0,2,3,1:T(8,128)(2,1)} %bitcast.119, bf16[128,8,2,128]{3,2,1,0:T(2,128)(2,1)S(1)} %reshape.174), kind=kOutput, calls=%fused_computation.1 | convolution fusion | flops 1090516992 | bytes 21766144 | tf_op jit(solution)/shard_map/cond/branch_1_fun/qgrd,kgd->grqk/dot_general | solution.py:95
  209.7 8.6 %fusion.2 = f32[8,2,128,128]{2,3,1,0:T(8,128)S(1)} fusion(bf16[2048,8,128,1]{0,2,3,1:T(8,128)(2,1)S(1)} %bitcast.118, f32[8,2048,128,2]{2,1,3,0:T(8,128)} %get-tuple-element.31, pred[128,2048]{0,1:T(8,128)(4,1)S(1)} %copy-done.4), kind=kOutput, calls=%fused_computation.3 | convolution fusion | flops 1090519040 | bytes 22282240 | tf_op jit(solution)/shard_map/cond | solution.py:114
  220.6 5.6 %collective-permute-start.26 = (bf16[256,2304]{1,0:T(8,128)(2,1)}, bf16[256,2304]{1,0:T(8,128)(2,1)}, u32[]{:S(2)}, u32[]{:S(2)}) collective-permute-start(bf16[256,2304]{1,0:T(8,128)(2,1)} %collective-permute-done.25), channel_id=1, source_target_pairs={{0,8},{8,16},{16,24},{1,9},{9,17},{17,25},{2,10},{10,18},{18,26},{... | collective-permute-start | bytes 3538952 | tf_op jit(solution)/shard_map/ppermute | solution.py:39
  227.9 17.6 %all_to_all.5 = bf16[4,128,4,256]{3,2,1,0:T(4,128)(2,1)S(1)} all-to-all(bf16[4,128,4,256]{3,2,1,0:T(4,128)(2,1)S(1)} %bitcast.116), channel_id=1, replica_groups=mesh['c0'=4,'c1'=2,'c2'=2,'head'=2] {'c1','c2'}, dimensions={0} | all-to-all | bytes 2097152 | tf_op jit(solution)/shard_map/all_to_all | solution.py:152
  252.5 21.9 %collective-permute-done.29 = bf16[256,2304]{1,0:T(8,128)(2,1)S(1)} collective-permute-done((bf16[256,2304]{1,0:T(8,128)(2,1)}, bf16[256,2304]{1,0:T(8,128)(2,1)S(1)}, u32[]{:S(2)}, u32[]{:S(2)}) %collective-permute-start.29) | collective-permute-done | bytes 1179680 | tf_op jit(solution)/shard_map/ppermute | solution.py:40
  279.1 56.1 %reduce-scatter.2.cloned.1.call-done = f32[128,2304]{1,0:T(8,128)} async-done(((f32[512,2304]{1,0:T(8,128)}), f32[128,2304]{1,0:T(8,128)}) %reduce-scatter.2.cloned.1.call-update) | async-done | bytes 1179664 | tf_op jit(solution)/shard_map/reduce_scatter | solution.py:156
  (147 shorter events, 105.7 us)
Async XLA Ops:
  7.2 219.0 %all-gather.2.cloned.1.call-start = ((), (), s32[]{:S(2)}) async-start(), calls=%async_computation.2 | async-start | bytes 1572864 | tf_op jit(solution)/shard_map/all_gather | solution.py:149
  8.3 14.6 %collective-permute-start.8 = (bf16[128,768]{1,0:T(8,128)(2,1)S(1)}, bf16[128,768]{1,0:T(8,128)(2,1)S(1)}, u32[]{:S(2)}, u32[]{:S(2)}) collective-permute-start(bf16[128,768]{1,0:T(8,128)(2,1)S(1)} %get-tuple-element.36), channel_id=1, source_target_pairs={{0,8},{8,16},{16,24},{1,9},{9,17},{17,25},{2,10},{10,18},{18,26},{... | collective-permute-start | bytes 589832 | tf_op jit(solution)/shard_map/ppermute | solution.py:39
  21.6 13.5 %collective-permute-start.11 = (bf16[128,768]{1,0:T(8,128)(2,1)S(1)}, bf16[128,768]{1,0:T(8,128)(2,1)S(1)}, u32[]{:S(2)}, u32[]{:S(2)}) collective-permute-start(bf16[128,768]{1,0:T(8,128)(2,1)S(1)} %get-tuple-element.36), channel_id=1, source_target_pairs={{8,0},{16,8},{24,16},{9,1},{17,9},{25,17},{10,2},{18,10},{26,18},{... | collective-permute-start | bytes 589832 | tf_op jit(solution)/shard_map/ppermute | solution.py:40
  29.2 15.7 %collective-permute-start.20 = (bf16[128,768]{1,0:T(8,128)(2,1)S(1)}, bf16[128,768]{1,0:T(8,128)(2,1)S(1)}, u32[]{:S(2)}, u32[]{:S(2)}) collective-permute-start(bf16[128,768]{1,0:T(8,128)(2,1)S(1)} %collective-permute-done.19), channel_id=1, source_target_pairs={{8,0},{16,8},{24,16},{9,1},{17,9},{25,17},{10,2},{18,10},{26,18},{... | collective-permute-start | bytes 589832 | tf_op jit(solution)/shard_map/ppermute | solution.py:40
  30.5 15.7 %collective-permute-start.17 = (bf16[128,768]{1,0:T(8,128)(2,1)S(1)}, bf16[128,768]{1,0:T(8,128)(2,1)S(1)}, u32[]{:S(2)}, u32[]{:S(2)}) collective-permute-start(bf16[128,768]{1,0:T(8,128)(2,1)S(1)} %collective-permute-done.16), channel_id=1, source_target_pairs={{0,8},{8,16},{16,24},{1,9},{9,17},{17,25},{2,10},{10,18},{18,26},{... | collective-permute-start | bytes 589832 | tf_op jit(solution)/shard_map/ppermute | solution.py:39
  35.1 15.7 %collective-permute-start.12 = (bf16[128,768]{1,0:T(8,128)(2,1)S(1)}, bf16[128,768]{1,0:T(8,128)(2,1)S(1)}, u32[]{:S(2)}, u32[]{:S(2)}) collective-permute-start(bf16[128,768]{1,0:T(8,128)(2,1)S(1)} %collective-permute-done.11), channel_id=1, source_target_pairs={{8,0},{16,8},{24,16},{9,1},{17,9},{25,17},{10,2},{18,10},{26,18},{... | collective-permute-start | bytes 589832 | tf_op jit(solution)/shard_map/ppermute | solution.py:40
  36.4 15.7 %collective-permute-start.10 = (bf16[128,768]{1,0:T(8,128)(2,1)S(1)}, bf16[128,768]{1,0:T(8,128)(2,1)S(1)}, u32[]{:S(2)}, u32[]{:S(2)}) collective-permute-start(bf16[128,768]{1,0:T(8,128)(2,1)S(1)} %collective-permute-done.9), channel_id=1, source_target_pairs={{0,8},{8,16},{16,24},{1,9},{9,17},{17,25},{2,10},{10,18},{18,26},{... | collective-permute-start | bytes 589832 | tf_op jit(solution)/shard_map/ppermute | solution.py:39
  41.4 20.0 %collective-permute-start.2 = (bf16[2,2,128,512]{3,2,1,0:T(8,128)(2,1)S(1)}, bf16[2,2,128,512]{3,2,1,0:T(8,128)(2,1)S(1)}, u32[]{:S(2)}, u32[]{:S(2)}) collective-permute-start(bf16[2,2,128,512]{3,2,1,0:T(8,128)(2,1)S(1)} %fusion.21), channel_id=1, source_target_pairs={{0,8},{8,16},{16,24},{1,9},{9,17},{17,25},{2,10},{10,18},{18,26},{... | collective-permute-start | bytes 1572872 | tf_op jit(solution)/shard_map/ppermute | solution.py:39
  44.9 14.5 %collective-permute-start.21 = (bf16[128,768]{1,0:T(8,128)(2,1)S(1)}, bf16[128,768]{1,0:T(8,128)(2,1)S(1)}, u32[]{:S(2)}, u32[]{:S(2)}) collective-permute-start(bf16[128,768]{1,0:T(8,128)(2,1)S(1)} %collective-permute-done.20), channel_id=1, source_target_pairs={{8,0},{16,8},{24,16},{9,1},{17,9},{25,17},{10,2},{18,10},{26,18},{... | collective-permute-start | bytes 589832 | tf_op jit(solution)/shard_map/ppermute | solution.py:40
  58.5 21.4 %collective-permute-start.14 = (bf16[4,128,768]{2,1,0:T(8,128)(2,1)S(1)}, bf16[4,128,768]{2,1,0:T(8,128)(2,1)S(1)}, u32[]{:S(2)}, u32[]{:S(2)}) collective-permute-start(bf16[4,128,768]{2,1,0:T(8,128)(2,1)S(1)} %constant_dynamic-slice_fusion.2), channel_id=1, source_target_pairs={{0,2},{2,0},{1,3},{3,1},{4,6},{6,4},{5,7},{7,5},{8,10},{10,8},{9,1... | collective-permute-start | bytes 2359304 | tf_op jit(solution)/shard_map/ppermute | solution.py:34
  59.5 23.9 %collective-permute-start.22 = (bf16[4,128,768]{2,1,0:T(8,128)(2,1)S(1)}, bf16[4,128,768]{2,1,0:T(8,128)(2,1)S(1)}, u32[]{:S(2)}, u32[]{:S(2)}) collective-permute-start(bf16[4,128,768]{2,1,0:T(8,128)(2,1)S(1)} %constant_dynamic-slice_fusion.1), channel_id=1, source_target_pairs={{0,4},{4,0},{1,5},{5,1},{2,6},{6,2},{3,7},{7,3},{8,12},{12,8},{9,1... | collective-permute-start | bytes 2359304 | tf_op jit(solution)/shard_map/ppermute | solution.py:34
  60.1 13.9 %collective-permute-start.5 = (bf16[2,2,128,512]{3,2,1,0:T(8,128)(2,1)S(1)}, bf16[2,2,128,512]{3,2,1,0:T(8,128)(2,1)S(1)}, u32[]{:S(2)}, u32[]{:S(2)}) collective-permute-start(bf16[2,2,128,512]{3,2,1,0:T(8,128)(2,1)S(1)} %fusion.21), channel_id=1, source_target_pairs={{8,0},{16,8},{24,16},{9,1},{17,9},{25,17},{10,2},{18,10},{26,18},{... | collective-permute-start | bytes 1572872 | tf_op jit(solution)/shard_map/ppermute | solution.py:40
  61.4 13.9 %collective-permute-start.3 = (bf16[2,2,128,512]{3,2,1,0:T(8,128)(2,1)S(1)}, bf16[2,2,128,512]{3,2,1,0:T(8,128)(2,1)S(1)}, u32[]{:S(2)}, u32[]{:S(2)}) collective-permute-start(bf16[2,2,128,512]{3,2,1,0:T(8,128)(2,1)S(1)} %collective-permute-done.2), channel_id=1, source_target_pairs={{0,8},{8,16},{16,24},{1,9},{9,17},{17,25},{2,10},{10,18},{18,26},{... | collective-permute-start | bytes 1572872 | tf_op jit(solution)/shard_map/ppermute | solution.py:39
  74.0 16.0 %collective-permute-start.6 = (bf16[2,2,128,512]{3,2,1,0:T(8,128)(2,1)S(1)}, bf16[2,2,128,512]{3,2,1,0:T(8,128)(2,1)S(1)}, u32[]{:S(2)}, u32[]{:S(2)}) collective-permute-start(bf16[2,2,128,512]{3,2,1,0:T(8,128)(2,1)S(1)} %collective-permute-done.5), channel_id=1, source_target_pairs={{8,0},{16,8},{24,16},{9,1},{17,9},{25,17},{10,2},{18,10},{26,18},{... | collective-permute-start | bytes 1572872 | tf_op jit(solution)/shard_map/ppermute | solution.py:40
  75.3 16.2 %collective-permute-start.4 = (bf16[2,2,128,512]{3,2,1,0:T(8,128)(2,1)S(1)}, bf16[2,2,128,512]{3,2,1,0:T(8,128)(2,1)S(1)}, u32[]{:S(2)}, u32[]{:S(2)}) collective-permute-start(bf16[2,2,128,512]{3,2,1,0:T(8,128)(2,1)S(1)} %collective-permute-done.3), channel_id=1, source_target_pairs={{0,8},{8,16},{16,24},{1,9},{9,17},{17,25},{2,10},{10,18},{18,26},{... | collective-permute-start | bytes 1572872 | tf_op jit(solution)/shard_map/ppermute | solution.py:39
  81.9 32.9 %collective-permute-start.15 = (bf16[2,4,128,768]{3,2,1,0:T(8,128)(2,1)}, bf16[2,4,128,768]{3,2,1,0:T(8,128)(2,1)}, u32[]{:S(2)}, u32[]{:S(2)}) collective-permute-start(bf16[2,4,128,768]{3,2,1,0:T(8,128)(2,1)} %fusion.19), channel_id=1, source_target_pairs={{0,4},{4,0},{1,5},{5,1},{2,6},{6,2},{3,7},{7,3},{8,12},{12,8},{9,1... | collective-permute-start | bytes 4718600 | tf_op jit(solution)/shard_map/ppermute | solution.py:34
  85.5 44.1 %collective-permute-start.23 = (bf16[2,4,128,768]{3,2,1,0:T(8,128)(2,1)}, bf16[2,4,128,768]{3,2,1,0:T(8,128)(2,1)}, u32[]{:S(2)}, u32[]{:S(2)}) collective-permute-start(bf16[2,4,128,768]{3,2,1,0:T(8,128)(2,1)} %fusion.17), channel_id=1, source_target_pairs={{0,2},{2,0},{1,3},{3,1},{4,6},{6,4},{5,7},{7,5},{8,10},{10,8},{9,1... | collective-permute-start | bytes 4718600 | tf_op jit(solution)/shard_map/ppermute | solution.py:34
  156.9 25.4 %collective-permute-start.24 = (bf16[256,2304]{1,0:T(8,128)(2,1)}, bf16[256,2304]{1,0:T(8,128)(2,1)S(1)}, u32[]{:S(2)}, u32[]{:S(2)}) collective-permute-start(bf16[256,2304]{1,0:T(8,128)(2,1)} %param.14), channel_id=1, source_target_pairs={{0,8},{8,16},{16,24},{1,9},{9,17},{17,25},{2,10},{10,18},{18,26},{... | collective-permute-start | bytes 3538952 | tf_op jit(solution)/shard_map/ppermute | solution.py:39
  160.7 58.6 %collective-permute-start.27 = (bf16[256,2304]{1,0:T(8,128)(2,1)}, bf16[256,2304]{1,0:T(8,128)(2,1)S(1)}, u32[]{:S(2)}, u32[]{:S(2)}) collective-permute-start(bf16[256,2304]{1,0:T(8,128)(2,1)} %param.14), channel_id=1, source_target_pairs={{8,0},{16,8},{24,16},{9,1},{17,9},{25,17},{10,2},{18,10},{26,18},{... | collective-permute-start | bytes 3538952 | tf_op jit(solution)/shard_map/ppermute | solution.py:40
  182.3 38.3 %collective-permute-start.25 = (bf16[256,2304]{1,0:T(8,128)(2,1)S(1)}, bf16[256,2304]{1,0:T(8,128)(2,1)}, u32[]{:S(2)}, u32[]{:S(2)}) collective-permute-start(bf16[256,2304]{1,0:T(8,128)(2,1)S(1)} %collective-permute-done.24), channel_id=1, source_target_pairs={{0,8},{8,16},{16,24},{1,9},{9,17},{17,25},{2,10},{10,18},{18,26},{... | collective-permute-start | bytes 3538952 | tf_op jit(solution)/shard_map/ppermute | solution.py:39
  219.2 116.0 %reduce-scatter.2.cloned.1.call-start = ((), (), s32[]{:S(2)}) async-start(), calls=%async_computation.3 | async-start | bytes 5898240 | tf_op jit(solution)/shard_map/reduce_scatter | solution.py:156
  219.3 26.3 %collective-permute-start.28 = (bf16[256,2304]{1,0:T(8,128)(2,1)S(1)}, bf16[256,2304]{1,0:T(8,128)(2,1)}, u32[]{:S(2)}, u32[]{:S(2)}) collective-permute-start(bf16[256,2304]{1,0:T(8,128)(2,1)S(1)} %collective-permute-done.27), channel_id=1, source_target_pairs={{8,0},{16,8},{24,16},{9,1},{17,9},{25,17},{10,2},{18,10},{26,18},{... | collective-permute-start | bytes 3538952 | tf_op jit(solution)/shard_map/ppermute | solution.py:40
  220.6 26.3 %collective-permute-start.26 = (bf16[256,2304]{1,0:T(8,128)(2,1)}, bf16[256,2304]{1,0:T(8,128)(2,1)}, u32[]{:S(2)}, u32[]{:S(2)}) collective-permute-start(bf16[256,2304]{1,0:T(8,128)(2,1)} %collective-permute-done.25), channel_id=1, source_target_pairs={{0,8},{8,16},{16,24},{1,9},{9,17},{17,25},{2,10},{10,18},{18,26},{... | collective-permute-start | bytes 3538952 | tf_op jit(solution)/shard_map/ppermute | solution.py:39
  245.7 28.8 %collective-permute-start.29 = (bf16[256,2304]{1,0:T(8,128)(2,1)}, bf16[256,2304]{1,0:T(8,128)(2,1)S(1)}, u32[]{:S(2)}, u32[]{:S(2)}) collective-permute-start(bf16[256,2304]{1,0:T(8,128)(2,1)} %collective-permute-done.28), channel_id=1, source_target_pairs={{8,0},{16,8},{24,16},{9,1},{17,9},{25,17},{10,2},{18,10},{26,18},{... | collective-permute-start | bytes 3538952 | tf_op jit(solution)/shard_map/ppermute | solution.py:40
  (21 other events, 353.5 us)
Sparse Core Ops, SparseCore 0:
  219.4 6.0 all-gather.1
  279.3 55.9 reduce-scatter.1

commit v5 on v4

--- a/solution.py
+++ b/solution.py
@@ -27,33 +27,23 @@
     return jnp.sum((positions[:, None] >= doc_ends[None, :]).astype(jnp.int32), axis=1)
 
 
-def line_gather(x, axis):
+def ring_gather(x, axis):
     n = lax.axis_size(axis)
-    i = lax.axis_index(axis)
-    if n == 2:
-        other = lax.ppermute(x, axis, [(0, 1), (1, 0)])
-        return lax.dynamic_slice_in_dim(jnp.stack([x, other, x]), i, 2, axis=0)
-    ahead, behind = x, x
-    from_left, from_right = [], []
+    pieces = [x]
     for _ in range(n - 1):
-        ahead = lax.ppermute(ahead, axis, [(k, k + 1) for k in range(n - 1)])
-        behind = lax.ppermute(behind, axis, [(k + 1, k) for k in range(n - 1)])
-        from_left.append(ahead)
-        from_right.append(behind)
-    stacked = jnp.stack(from_left[::-1] + [x] + from_right)
-    return lax.dynamic_slice_in_dim(stacked, (n - 1) - i, n, axis=0)
+        pieces.append(lax.ppermute(pieces[-1], axis, [(k, (k + 1) % n) for k in range(n)]))
+    return jnp.stack(pieces)
 
 
-def gather_tokens(x):
-    width = x.shape[1]
-    first = (width // 4) // 128 * 128
-    second = first + (width - first) // 2 // 128 * 128
-    part_a, part_b, part_c = x[:, :first], x[:, first:second], x[:, second:]
-    got_a = line_gather(line_gather(line_gather(part_a, "c2"), "c1"), "c0")
-    got_b = line_gather(line_gather(line_gather(part_b, "c0"), "c2"), "c1").transpose(2, 0, 1, 3, 4)
-    got_c = line_gather(line_gather(line_gather(part_c, "c0"), "c1"), "c2").transpose(2, 1, 0, 3, 4)
-    rows = lax.axis_size(CTX) * x.shape[0]
-    return jnp.concatenate([g.reshape(rows, -1) for g in (got_a, got_b, got_c)], axis=1)
+def gather_order(x, order):
+    stride = {"c2": 1, "c1": lax.axis_size("c2"), "c0": lax.axis_size("c1") * lax.axis_size("c2")}
+    source = jnp.zeros((), jnp.int32)
+    for axis in order:
+        x = ring_gather(x, axis)
+        n = lax.axis_size(axis)
+        came = (lax.axis_index(axis) - jnp.arange(n, dtype=jnp.int32)) % n
+        source = came.reshape((n,) + (1,) * source.ndim) * stride[axis] + source[None]
+    return x, source.reshape(-1)
 
 
 def butterfly_sum(x, axes):
@@ -80,9 +70,9 @@
     q_groups = queries.reshape(tok_dev, kv_local, group_repeat, HEAD_WIDTH)
     span = tok_dev * max(1, 2048 // tok_dev)
 
-    def attend_block(state, key_piece, value_piece, start):
+    def attend_block(state, q_part, key_piece, value_piece, key_rows):
         count = key_piece.shape[0]
-        key_rows = start + jnp.arange(count, dtype=jnp.int32)
+        heads = q_part.shape[1]
         key_pos = storage_positions(key_rows, tok_dev, n_ctx)
         key_doc = document_of(key_pos, doc_ends)
         visible = (query_doc[:, None] == key_doc[None, :]) & (
@@ -94,8 +84,8 @@
             scores = (
                 jnp.einsum(
                     "qgrd,kgd->grqk",
-                    q_groups,
-                    key_piece.reshape(count, kv_local, HEAD_WIDTH),
+                    q_part,
+                    key_piece.reshape(count, heads, HEAD_WIDTH),
                     preferred_element_type=jnp.float32,
                 )
                 * scale
@@ -105,7 +95,7 @@
             numerator = numerator + jnp.einsum(
                 "grqk,kgd->grqd",
                 weights.astype(jnp.bfloat16),
-                value_piece.reshape(count, kv_local, HEAD_WIDTH),
+                value_piece.reshape(count, heads, HEAD_WIDTH),
                 preferred_element_type=jnp.float32,
             )
             denominator = denominator + jnp.sum(weights, axis=-1)
@@ -113,37 +103,54 @@
 
         return lax.cond(jnp.any(visible), compute, lambda carry: carry, state)
 
-    def attend(state, key_piece, value_piece, start):
+    def attend(q_part, key_piece, value_piece, key_rows):
+        heads = q_part.shape[1]
+        state = (
+            jnp.zeros((heads, group_repeat, tok_dev, HEAD_WIDTH), jnp.float32),
+            jnp.zeros((heads, group_repeat, tok_dev), jnp.float32),
+        )
         count = key_piece.shape[0]
         if count <= span:
-            return attend_block(state, key_piece, value_piece, start)
+            return attend_block(state, q_part, key_piece, value_piece, key_rows)
         blocks = count // span
         whole = blocks * span
         width = key_piece.shape[1]
         key_blocks = key_piece[:whole].reshape(blocks, span, width)
         value_blocks = value_piece[:whole].reshape(blocks, span, width)
-        starts = start + span * jnp.arange(blocks, dtype=jnp.int32)
+        row_blocks = key_rows[:whole].reshape(blocks, span)
 
         def step_fn(carry, item):
-            return (attend_block(carry, item[0], item[1], item[2]), None)
+            return (attend_block(carry, q_part, item[0], item[1], item[2]), None)
 
-        state, _ = lax.scan(step_fn, state, (key_blocks, value_blocks, starts))
+        state, _ = lax.scan(step_fn, state, (key_blocks, value_blocks, row_blocks))
         if whole < count:
-            state = attend_block(state, key_piece[whole:], value_piece[whole:], start + whole)
+            state = attend_block(state, q_part, key_piece[whole:], value_piece[whole:], key_rows[whole:])
         return state
 
-    initial = (
-        jnp.zeros((kv_local, group_repeat, tok_dev, HEAD_WIDTH), jnp.float32),
-        jnp.zeros((kv_local, group_repeat, tok_dev), jnp.float32),
-    )
     outer = lax.axis_size("c0")
     inner = lax.axis_size(INNER)
     rows_each = out_weight.shape[0]
-    kv_width = keys.shape[1]
-    both = gather_tokens(jnp.concatenate([keys, values], axis=1))
-    both, out_weight = lax.optimization_barrier((both, out_weight))
-    weight_rows = line_gather(out_weight, "c0")
-    numerator, denominator = attend(initial, both[:, :kv_width], both[:, kv_width:], jnp.int32(0))
+    weight_rows = lax.all_gather(out_weight, "c0", axis=0, tiled=True)
+    half = kv_local // 2
+    splits = [(0, half, ("c0", "c2", "c1")), (half, kv_local, ("c0", "c1", "c2"))]
+    gathered, bounds = [], []
+    for first, last, order in splits:
+        if last == first:
+            continue
+        cols = slice(first * HEAD_WIDTH, last * HEAD_WIDTH)
+        got, source = gather_order(jnp.concatenate([keys[:, cols], values[:, cols]], axis=1), order)
+        key_rows = (source[:, None] * tok_dev + jnp.arange(tok_dev, dtype=jnp.int32)[None, :]).reshape(-1)
+        gathered.append((got.reshape(n_ctx * tok_dev, -1), key_rows))
+        bounds.append((first, last))
+    gathered, weight_rows = lax.optimization_barrier((gathered, weight_rows))
+    numerators, denominators = [], []
+    for (first, last), (got, key_rows) in zip(bounds, gathered):
+        width = (last - first) * HEAD_WIDTH
+        numerator, denominator = attend(q_groups[:, first:last], got[:, :width], got[:, width:], key_rows)
+        numerators.append(numerator)
+        denominators.append(denominator)
+    numerator = jnp.concatenate(numerators, axis=0)
+    denominator = jnp.concatenate(denominators, axis=0)
     attended = (numerator / denominator[..., None]).astype(jnp.bfloat16)
     attended = attended.transpose(2, 0, 1, 3).reshape(tok_dev, kv_local * group_repeat * HEAD_WIDTH)
     all_heads = lax.all_gather(attended, "head", axis=1, tiled=True)

time: 367 us -> 330 us (0.90)
  waiting for transfers between devices: 142 us -> 195 us
  starting transfers between devices: 83.9 us -> 36.8 us
  local copies, waits for them, and re-layouts: 44.4 us -> 22.8 us
  other arithmetic: 34.9 us -> 20.7 us
  matrix products: 24.8 us -> 17.1 us
    ppermute x30 -> x10, starting transfers between devices: 77.1 us -> 30.1 us  [ring_gather(): lax.ppermute(pieces[-1], axis, [(k, (k + 1) % n) for k in range(n)])]
    all_gather x1, waiting for transfers between devices: 0.01 us -> 28.5 us  [shards(): all_heads = lax.all_gather(attended, 'head', axis=1, tiled=True)]
    ppermute x30 -> x10, waiting for transfers between devices: 76.1 us -> 99.9 us  [ring_gather(): lax.ppermute(pieces[-1], axis, [(k, (k + 1) % n) for k in range(n)])]
    transpose x2 -> x0, local copies, waits for them, and re-layouts: 14.7 us -> none  [the longest x1 8.78 us: gather_tokens(): line_gather(line_gather(line_gather(part_c, 'c0'), 'c1'), 'c2')]
    transpose x2 -> x0, other arithmetic: 9.94 us -> none  [the longest x1 5.85 us: gather_tokens(): line_gather(line_gather(line_gather(part_c, 'c0'), 'c1'), 'c2')]
    concatenate x2 -> x1, other arithmetic: 7.57 us -> 0.01 us  [shards(): denominator = jnp.concatenate(denominators, axis=0)]
    dot_general x1 -> x2, matrix products: 11.9 us -> 5.34 us  [compute(): jnp.einsum('qgrd,kgd->grqk', q_part, key_piece.reshape(count, heads, HEAD...]
    unnamed x34 -> x14, local copies, waits for them, and re-layouts: 6.15 us -> 0.51 us
  transfers between devices with their start and end apart: 37 -> 18, of which waited for: 13 -> 16; matrix products, arithmetic and copies ran while one was open for 18% -> 8% of each run, Pallas kernels for 0% -> 0%
where the time goes in v5:
time: 330 us; the launch traced here: 329 us
  waiting for transfers between devices  195 us (59%)
  starting transfers between devices  36.8 us (11%)
  local copies, waits for them, and re-layouts  22.8 us (7%)
  blocking collectives  20.8 us (6%)
  other arithmetic  20.7 us (6%)
  matrix products  17.1 us (5%)
  between operations  15.2 us (5%)
    ppermute x10, waiting for transfers between devices, ring_gather(): lax.ppermute(pieces[-1], axis, [(k, (k + 1) % n) for k in range(n)])  99.9 us
    reduce_scatter x1, waiting for transfers between devices, shards(): mixed = lax.psum_scatter(partial, INNER, scatter_dimension=0, tiled=True)  56.7 us
    ppermute x10, starting transfers between devices, ring_gather(): lax.ppermute(pieces[-1], axis, [(k, (k + 1) % n) for k in range(n)])  30.1 us
    all_gather x1, waiting for transfers between devices, shards(): all_heads = lax.all_gather(attended, 'head', axis=1, tiled=True)  28.5 us
    all_to_all x1, blocking collectives, shards(): regrouped = lax.all_to_all(blocks, INNER, 0, 0, tiled=True)  18.3 us
    reshape x2, local copies, waits for them, and re-layouts, shards(): gathered.append((got.reshape(n_ctx * tok_dev, -1), key_rows))  13.2 us
    another operation x8, other arithmetic, ring_gather(): return jnp.stack(pieces)  12.3 us
    ppermute x5, waiting for transfers between devices, butterfly_sum(): x = x + lax.ppermute(x, axis, [(i, i ^ bit) for i in range(size)])  9.57 us
  transfers between devices with their start and end apart: 18, of which 16 were waited for; matrix products, arithmetic and copies ran while one was open for 8% of the time, Pallas kernels for 0%

profile of v5, /device:TPU:0, one launch (start us, length us, event | category | flops | bytes accessed | tf_op | source)
XLA Modules:
  0.0 329.1 jit_solution(1226481624394833671)
XLA Ops:
  9.1 3.1 collective-permute-start.5
  13.9 7.5 %collective-permute-done.5 = bf16[128,1024]{1,0:T(8,128)(2,1)S(1)} collective-permute-done((bf16[128,1024]{1,0:T(8,128)(2,1)S(1)}, bf16[128,1024]{1,0:T(8,128)(2,1)S(1)}, u32[]{:S(2)}, u32[]{:S(2)}) %collective-permute-start.5) | collective-permute-done | bytes 262176 | tf_op jit(solution)/shard_map/ppermute | solution.py:34
  21.4 7.3 %collective-permute-done = bf16[128,1024]{1,0:T(8,128)(2,1)S(1)} collective-permute-done((bf16[128,1024]{1,0:T(8,128)(2,1)S(1)}, bf16[128,1024]{1,0:T(8,128)(2,1)S(1)}, u32[]{:S(2)}, u32[]{:S(2)}) %collective-permute-start) | collective-permute-done | bytes 262176 | tf_op jit(solution)/shard_map/ppermute | solution.py:34
  28.7 3.3 %collective-permute-start.1 = (bf16[128,1024]{1,0:T(8,128)(2,1)S(1)}, bf16[128,1024]{1,0:T(8,128)(2,1)S(1)}, u32[]{:S(2)}, u32[]{:S(2)}) collective-permute-start(bf16[128,1024]{1,0:T(8,128)(2,1)S(1)} %collective-permute-done), channel_id=1, source_target_pairs={{0,8},{8,16},{16,24},{24,0},{1,9},{9,17},{17,25},{25,1},{2,10},{10... | collective-permute-start | bytes 786440 | tf_op jit(solution)/shard_map/ppermute | solution.py:34
  32.0 7.9 %collective-permute-done.6 = bf16[128,1024]{1,0:T(8,128)(2,1)S(1)} collective-permute-done((bf16[128,1024]{1,0:T(8,128)(2,1)S(1)}, bf16[128,1024]{1,0:T(8,128)(2,1)S(1)}, u32[]{:S(2)}, u32[]{:S(2)}) %collective-permute-start.6) | collective-permute-done | bytes 262176 | tf_op jit(solution)/shard_map/ppermute | solution.py:34
  39.9 6.5 %collective-permute-start.7 = (bf16[128,1024]{1,0:T(8,128)(2,1)S(1)}, bf16[128,1024]{1,0:T(8,128)(2,1)S(1)}, u32[]{:S(2)}, u32[]{:S(2)}) collective-permute-start(bf16[128,1024]{1,0:T(8,128)(2,1)S(1)} %collective-permute-done.6), channel_id=1, source_target_pairs={{0,8},{8,16},{16,24},{24,0},{1,9},{9,17},{17,25},{25,1},{2,10},{10... | collective-permute-start | bytes 786440 | tf_op jit(solution)/shard_map/ppermute | solution.py:34
  46.4 4.7 %collective-permute-done.1 = bf16[128,1024]{1,0:T(8,128)(2,1)S(1)} collective-permute-done((bf16[128,1024]{1,0:T(8,128)(2,1)S(1)}, bf16[128,1024]{1,0:T(8,128)(2,1)S(1)}, u32[]{:S(2)}, u32[]{:S(2)}) %collective-permute-start.1) | collective-permute-done | bytes 262176 | tf_op jit(solution)/shard_map/ppermute | solution.py:34
  51.1 9.7 %collective-permute-start.2 = (bf16[128,1024]{1,0:T(8,128)(2,1)S(1)}, bf16[128,1024]{1,0:T(8,128)(2,1)S(1)}, u32[]{:S(2)}, u32[]{:S(2)}) collective-permute-start(bf16[128,1024]{1,0:T(8,128)(2,1)S(1)} %collective-permute-done.1), channel_id=1, source_target_pairs={{0,8},{8,16},{16,24},{24,0},{1,9},{9,17},{17,25},{25,1},{2,10},{10... | collective-permute-start | bytes 786440 | tf_op jit(solution)/shard_map/ppermute | solution.py:34
  60.8 3.1 collective-permute-done.7
  65.6 15.2 %collective-permute-done.2 = bf16[128,1024]{1,0:T(8,128)(2,1)S(1)} collective-permute-done((bf16[128,1024]{1,0:T(8,128)(2,1)S(1)}, bf16[128,1024]{1,0:T(8,128)(2,1)S(1)}, u32[]{:S(2)}, u32[]{:S(2)}) %collective-permute-start.2) | collective-permute-done | bytes 262176 | tf_op jit(solution)/shard_map/ppermute | solution.py:34
  86.1 21.1 %collective-permute-done.3 = bf16[4,128,1024]{2,1,0:T(8,128)(2,1)S(1)} collective-permute-done((bf16[4,128,1024]{2,1,0:T(8,128)(2,1)S(1)}, bf16[4,128,1024]{2,1,0:T(8,128)(2,1)S(1)}, u32[]{:S(2)}, u32[]{:S(2)}) %collective-permute-start.3) | collective-permute-done | bytes 1048608 | tf_op jit(solution)/shard_map/ppermute | solution.py:34
  112.1 32.4 %collective-permute-done.9 = bf16[2,4,128,1024]{3,2,1,0:T(8,128)(2,1)} collective-permute-done((bf16[2,4,128,1024]{3,2,1,0:T(8,128)(2,1)}, bf16[2,4,128,1024]{3,2,1,0:T(8,128)(2,1)}, u32[]{:S(2)}, u32[]{:S(2)}) %collective-permute-start.9) | collective-permute-done | bytes 2097184 | tf_op jit(solution)/shard_map/ppermute | solution.py:34
  144.5 4.0 %pad_maximum_fusion.1 = bf16[2,2,4,128,1024]{4,3,2,1,0:T(8,128)(2,1)} fusion(bf16[1,2,4,128,1024]{4,3,2,1,0:T(8,128)(2,1)} %bitcast.28, bf16[1,2,4,128,1024]{4,3,2,1,0:T(8,128)(2,1)S(1)} %get-tuple-element.74), kind=kLoop, calls=%fused_computation.21 | loop fusion | flops 2097152 | bytes 8388608 | tf_op jit(solution)/shard_map/stack | solution.py:35
  148.5 6.7 %copy.58 = bf16[2048,1024]{0,1:T(8,128)(2,1)} copy(bf16[2048,1024]{1,0:T(8,128)(2,1)} %bitcast.78) | data formatting | bytes 8388608 | tf_op jit(solution)/shard_map/reshape | solution.py:143
  155.3 4.0 %pad_maximum_fusion = bf16[2,2,4,128,1024]{4,3,2,1,0:T(8,128)(2,1)} fusion(bf16[1,2,4,128,1024]{4,3,2,1,0:T(8,128)(2,1)} %bitcast.18, bf16[1,2,4,128,1024]{4,3,2,1,0:T(8,128)(2,1)S(1)} %copy-done), kind=kLoop, calls=%fused_computation.20 | loop fusion | flops 2097152 | bytes 8388608 | tf_op jit(solution)/shard_map/stack | solution.py:35
  159.2 6.5 %copy.57 = bf16[2048,1024]{0,1:T(8,128)(2,1)} copy(bf16[2048,1024]{1,0:T(8,128)(2,1)} %bitcast.79) | data formatting | bytes 8388608 | tf_op jit(solution)/shard_map/reshape | solution.py:143
  169.4 8.3 %conditional.2 = (f32[4,2,128]{2,1,0:T(2,128)S(1)}, f32[4,2,128,128]{2,3,1,0:T(8,128)S(1)}) conditional(s32[]{:T(128)} %convert_element_type.37, () %tuple.26, (pred[128,2048]{0,1:T(8,128)(4,1)S(1)}, bf16[2048,1024]{0,1:T(8,128)(2,1)}, bf16[128,8,2,128]{0,3,2,1:T(8,128)(2,1)S(1)}) %tuple.71), branch_computations={%region_4.5_spmd, %region_5.7_spmd} | conditional | flops 1090518016 | bytes 31723536 | solution.py:104
  169.7 2.7 fusion.47
  177.7 8.4 %conditional.3 = (f32[4,2,128]{2,1,0:T(2,128)S(1)}, f32[4,2,128,128]{2,3,1,0:T(8,128)S(1)}) conditional(s32[]{:T(128)} %convert_element_type.39, () %tuple.28, (pred[128,2048]{0,1:T(8,128)(4,1)S(1)}, bf16[2048,1024]{0,1:T(8,128)(2,1)}, bf16[128,8,2,128]{0,3,2,1:T(8,128)(2,1)S(1)}) %tuple.72), branch_computations={%region_9.10_spmd, %region_10.12_spmd} | conditional | flops 1090518016 | bytes 31723536 | solution.py:104
  178.2 2.7 fusion.48
  187.2 28.5 %all-gather.5.cloned.1.call-done = bf16[128,4096]{0,1:T(8,128)(2,1)} async-done(((bf16[128,2048]{0,1:T(8,128)(2,1)}), bf16[128,4096]{0,1:T(8,128)(2,1)}) %all-gather.5.cloned.1.call-update) | async-done | bytes 1048592 | tf_op jit(solution)/shard_map/all_gather | solution.py:156
  217.4 18.3 %all_to_all.5 = bf16[4,128,4,256]{3,2,1,0:T(4,128)(2,1)S(1)} all-to-all(bf16[4,128,4,256]{3,2,1,0:T(4,128)(2,1)S(1)} %bitcast.82), channel_id=1, replica_groups=mesh['c0'=4,'c1'=2,'c2'=2,'head'=2] {'c1','c2'}, dimensions={0} | all-to-all | bytes 2097152 | tf_op jit(solution)/shard_map/all_to_all | solution.py:159
  235.9 6.7 %fusion.51 = f32[512,2304]{1,0:T(8,128)} fusion(bf16[512,1024]{1,0:T(8,128)(2,1)S(1)} %bitcast.90, bf16[1024,2304]{1,0:T(8,128)(2,1)} %all-gather.3.cloned.1.call-done), kind=kOutput, calls=%fused_computation.118 | convolution fusion | flops 2415919104 | bytes 10485760 | tf_op jit(solution)/shard_map/dot_general | solution.py:160
  242.6 56.7 %reduce-scatter.2.cloned.1.call-done = f32[128,2304]{1,0:T(8,128)} async-done(((f32[512,2304]{1,0:T(8,128)}), f32[128,2304]{1,0:T(8,128)}) %reduce-scatter.2.cloned.1.call-update) | async-done | bytes 1179664 | tf_op jit(solution)/shard_map/reduce_scatter | solution.py:163
  (83 shorter events, 55.1 us)
Async XLA Ops:
  7.2 158.6 %all-gather.3.cloned.1.call-start = ((), (), s32[]{:S(2)}) async-start(), calls=%async_computation.2 | async-start | bytes 5898240 | tf_op jit(solution)/shard_map/all_gather | solution.py:133
  7.9 207.8 %all-gather.5.cloned.1.call-start = ((), (), s32[]{:S(2)}) async-start(), calls=%async_computation.3 | async-start | bytes 1572864 | tf_op jit(solution)/shard_map/all_gather | solution.py:156
  9.1 12.2 %collective-permute-start.5 = (bf16[128,1024]{1,0:T(8,128)(2,1)S(1)}, bf16[128,1024]{1,0:T(8,128)(2,1)S(1)}, u32[]{:S(2)}, u32[]{:S(2)}) collective-permute-start(bf16[128,1024]{1,0:T(8,128)(2,1)S(1)} %get-tuple-element.85), channel_id=1, source_target_pairs={{0,8},{8,16},{16,24},{24,0},{1,9},{9,17},{17,25},{25,1},{2,10},{10... | collective-permute-start | bytes 786440 | tf_op jit(solution)/shard_map/ppermute | solution.py:34
  12.2 16.5 %collective-permute-start = (bf16[128,1024]{1,0:T(8,128)(2,1)S(1)}, bf16[128,1024]{1,0:T(8,128)(2,1)S(1)}, u32[]{:S(2)}, u32[]{:S(2)}) collective-permute-start(bf16[128,1024]{1,0:T(8,128)(2,1)S(1)} %get-tuple-element.91), channel_id=1, source_target_pairs={{0,8},{8,16},{16,24},{24,0},{1,9},{9,17},{17,25},{25,1},{2,10},{10... | collective-permute-start | bytes 786440 | tf_op jit(solution)/shard_map/ppermute | solution.py:34
  21.4 18.5 %collective-permute-start.6 = (bf16[128,1024]{1,0:T(8,128)(2,1)S(1)}, bf16[128,1024]{1,0:T(8,128)(2,1)S(1)}, u32[]{:S(2)}, u32[]{:S(2)}) collective-permute-start(bf16[128,1024]{1,0:T(8,128)(2,1)S(1)} %collective-permute-done.5), channel_id=1, source_target_pairs={{0,8},{8,16},{16,24},{24,0},{1,9},{9,17},{17,25},{25,1},{2,10},{10... | collective-permute-start | bytes 786440 | tf_op jit(solution)/shard_map/ppermute | solution.py:34
  28.7 22.4 %collective-permute-start.1 = (bf16[128,1024]{1,0:T(8,128)(2,1)S(1)}, bf16[128,1024]{1,0:T(8,128)(2,1)S(1)}, u32[]{:S(2)}, u32[]{:S(2)}) collective-permute-start(bf16[128,1024]{1,0:T(8,128)(2,1)S(1)} %collective-permute-done), channel_id=1, source_target_pairs={{0,8},{8,16},{16,24},{24,0},{1,9},{9,17},{17,25},{25,1},{2,10},{10... | collective-permute-start | bytes 786440 | tf_op jit(solution)/shard_map/ppermute | solution.py:34
  39.9 24.0 %collective-permute-start.7 = (bf16[128,1024]{1,0:T(8,128)(2,1)S(1)}, bf16[128,1024]{1,0:T(8,128)(2,1)S(1)}, u32[]{:S(2)}, u32[]{:S(2)}) collective-permute-start(bf16[128,1024]{1,0:T(8,128)(2,1)S(1)} %collective-permute-done.6), channel_id=1, source_target_pairs={{0,8},{8,16},{16,24},{24,0},{1,9},{9,17},{17,25},{25,1},{2,10},{10... | collective-permute-start | bytes 786440 | tf_op jit(solution)/shard_map/ppermute | solution.py:34
  51.1 29.7 %collective-permute-start.2 = (bf16[128,1024]{1,0:T(8,128)(2,1)S(1)}, bf16[128,1024]{1,0:T(8,128)(2,1)S(1)}, u32[]{:S(2)}, u32[]{:S(2)}) collective-permute-start(bf16[128,1024]{1,0:T(8,128)(2,1)S(1)} %collective-permute-done.1), channel_id=1, source_target_pairs={{0,8},{8,16},{16,24},{24,0},{1,9},{9,17},{17,25},{25,1},{2,10},{10... | collective-permute-start | bytes 786440 | tf_op jit(solution)/shard_map/ppermute | solution.py:34
  64.0 19.2 %collective-permute-start.8 = (bf16[4,128,1024]{2,1,0:T(8,128)(2,1)S(1)}, bf16[4,128,1024]{2,1,0:T(8,128)(2,1)S(1)}, u32[]{:S(2)}, u32[]{:S(2)}) collective-permute-start(bf16[4,128,1024]{2,1,0:T(8,128)(2,1)S(1)} %get-tuple-element.81), channel_id=1, source_target_pairs={{0,4},{4,0},{1,5},{5,1},{2,6},{6,2},{3,7},{7,3},{8,12},{12,8},{9,1... | collective-permute-start | bytes 3145736 | tf_op jit(solution)/shard_map/ppermute | solution.py:34
  81.0 26.2 %collective-permute-start.3 = (bf16[4,128,1024]{2,1,0:T(8,128)(2,1)S(1)}, bf16[4,128,1024]{2,1,0:T(8,128)(2,1)S(1)}, u32[]{:S(2)}, u32[]{:S(2)}) collective-permute-start(bf16[4,128,1024]{2,1,0:T(8,128)(2,1)S(1)} %get-tuple-element.83), channel_id=1, source_target_pairs={{0,2},{2,0},{1,3},{3,1},{4,6},{6,4},{5,7},{7,5},{8,10},{10,8},{9,1... | collective-permute-start | bytes 3145736 | tf_op jit(solution)/shard_map/ppermute | solution.py:34
  84.9 26.4 %copy-start.5 = (s32[16]{0:T(128)S(1)}, s32[16]{0:T(128)}, u32[]{:S(2)}) copy-start(s32[16]{0:T(128)} %param.19) | copy-start | bytes 196
  84.9 26.6 %copy-start.2 = (bf16[128,2048]{1,0:T(8,128)(2,1)S(1)}, bf16[128,2048]{1,0:T(8,128)(2,1)}, u32[]{:S(2)}) copy-start(bf16[128,2048]{1,0:T(8,128)(2,1)} %param.12) | copy-start | bytes 1572868
  84.9 59.6 %collective-permute-start.9 = (bf16[2,4,128,1024]{3,2,1,0:T(8,128)(2,1)}, bf16[2,4,128,1024]{3,2,1,0:T(8,128)(2,1)}, u32[]{:S(2)}, u32[]{:S(2)}) collective-permute-start(bf16[2,4,128,1024]{3,2,1,0:T(8,128)(2,1)} %get-tuple-element.75), channel_id=1, source_target_pairs={{0,2},{2,0},{1,3},{3,1},{4,6},{6,4},{5,7},{7,5},{8,10},{10,8},{9,1... | collective-permute-start | bytes 6291464 | tf_op jit(solution)/shard_map/ppermute | solution.py:34
  109.4 45.8 %collective-permute-start.4 = (bf16[2,4,128,1024]{3,2,1,0:T(8,128)(2,1)}, bf16[2,4,128,1024]{3,2,1,0:T(8,128)(2,1)}, u32[]{:S(2)}, u32[]{:S(2)}) collective-permute-start(bf16[2,4,128,1024]{3,2,1,0:T(8,128)(2,1)} %get-tuple-element.77), channel_id=1, source_target_pairs={{0,4},{4,0},{1,5},{5,1},{2,6},{6,2},{3,7},{7,3},{8,12},{12,8},{9,1... | collective-permute-start | bytes 6291464 | tf_op jit(solution)/shard_map/ppermute | solution.py:34
  148.5 6.7 %copy-start = (bf16[1,2,4,128,1024]{4,3,2,1,0:T(8,128)(2,1)S(1)}, bf16[1,2,4,128,1024]{4,3,2,1,0:T(8,128)(2,1)}, u32[]{:S(2)}) copy-start(bf16[1,2,4,128,1024]{4,3,2,1,0:T(8,128)(2,1)} %get-tuple-element.76) | copy-start | bytes 6291460
  187.1 112.2 %reduce-scatter.2.cloned.1.call-start = ((), (), s32[]{:S(2)}) async-start(), calls=%async_computation.4 | async-start | bytes 5898240 | tf_op jit(solution)/shard_map/reduce_scatter | solution.py:163
  242.6 60.6 %copy-start.1 = (bf16[128,2304]{1,0:T(8,128)(2,1)S(1)}, bf16[128,2304]{1,0:T(8,128)(2,1)}, u32[]{:S(2)}) copy-start(bf16[128,2304]{1,0:T(8,128)(2,1)} %param.15) | copy-start | bytes 1769476
  242.6 60.6 %copy-start.3 = (f32[2304]{0:T(1024)S(1)}, f32[2304]{0:T(1024)}, u32[]{:S(2)}) copy-start(f32[2304]{0:T(1024)} %param.18) | copy-start | bytes 27652
  242.6 60.6 %copy-start.4 = (f32[2304]{0:T(1024)S(1)}, f32[2304]{0:T(1024)}, u32[]{:S(2)}) copy-start(f32[2304]{0:T(1024)} %param.17) | copy-start | bytes 27652
  305.8 3.6 %collective-permute-start.10 = (f32[16]{0:T(128)S(1)}, f32[16]{0:T(128)S(1)}, u32[]{:S(2)}, u32[]{:S(2)}) collective-permute-start(f32[16]{0:T(128)S(1)} %select_reduce_fusion), channel_id=1, source_target_pairs={{0,8},{8,0},{16,24},{24,16},{1,9},{9,1},{17,25},{25,17},{2,10},{10... | collective-permute-start | bytes 200 | tf_op jit(solution)/shard_map/ppermute | solution.py:54
  309.4 4.4 %collective-permute-start.11 = (f32[16]{0:T(128)S(1)}, f32[16]{0:T(128)S(1)}, u32[]{:S(2)}, u32[]{:S(2)}) collective-permute-start(f32[16]{0:T(128)S(1)} %add.284), channel_id=1, source_target_pairs={{0,16},{8,24},{16,0},{24,8},{1,17},{9,25},{17,1},{25,9},{2,18},{10... | collective-permute-start | bytes 200 | tf_op jit(solution)/shard_map/ppermute | solution.py:54
  313.8 3.5 %collective-permute-start.12 = (f32[16]{0:T(128)S(1)}, f32[16]{0:T(128)S(1)}, u32[]{:S(2)}, u32[]{:S(2)}) collective-permute-start(f32[16]{0:T(128)S(1)} %add.285), channel_id=1, source_target_pairs={{0,4},{4,0},{1,5},{5,1},{2,6},{6,2},{3,7},{7,3},{8,12},{12,8},{9,1... | collective-permute-start | bytes 200 | tf_op jit(solution)/shard_map/ppermute | solution.py:54
  317.4 3.5 %collective-permute-start.13 = (f32[16]{0:T(128)S(1)}, f32[16]{0:T(128)S(1)}, u32[]{:S(2)}, u32[]{:S(2)}) collective-permute-start(f32[16]{0:T(128)S(1)} %add.286), channel_id=1, source_target_pairs={{0,2},{2,0},{1,3},{3,1},{4,6},{6,4},{5,7},{7,5},{8,10},{10,8},{9,1... | collective-permute-start | bytes 200 | tf_op jit(solution)/shard_map/ppermute | solution.py:54
  320.9 1.1 collective-permute-start.14
Sparse Core Ops, SparseCore 0:
  9.6 115.5 all-gather.2
  187.3 28.4 all-gather.4
  242.8 56.5 reduce-scatter.1

commit v6 on v5

--- a/solution.py
+++ b/solution.py
@@ -44,6 +44,22 @@
         came = (lax.axis_index(axis) - jnp.arange(n, dtype=jnp.int32)) % n
         source = came.reshape((n,) + (1,) * source.ndim) * stride[axis] + source[None]
     return x, source.reshape(-1)
+
+
+def ring_all_gather(x, axis):
+    n = lax.axis_size(axis)
+    arrived = ring_gather(x, axis)[::-1]
+    return jnp.roll(arrived, lax.axis_index(axis) + 1, axis=0)
+
+
+def permute_all_to_all(x, axes):
+    n = lax.axis_size(axes)
+    own = lax.axis_index(axes)
+    pieces = [lax.dynamic_index_in_dim(x, own, axis=0, keepdims=False)]
+    for shift in range(1, n):
+        sent = lax.dynamic_index_in_dim(x, (own + shift) % n, axis=0, keepdims=False)
+        pieces.append(lax.ppermute(sent, axes, [(k, (k + shift) % n) for k in range(n)]))
+    return jnp.roll(jnp.stack(pieces[::-1]), own + 1, axis=0)
 
 
 def butterfly_sum(x, axes):
@@ -153,10 +169,10 @@
     denominator = jnp.concatenate(denominators, axis=0)
     attended = (numerator / denominator[..., None]).astype(jnp.bfloat16)
     attended = attended.transpose(2, 0, 1, 3).reshape(tok_dev, kv_local * group_repeat * HEAD_WIDTH)
-    all_heads = lax.all_gather(attended, "head", axis=1, tiled=True)
+    all_heads = ring_all_gather(attended, "head").transpose(1, 0, 2).reshape(tok_dev, -1)
     weight_rows = weight_rows.reshape(outer * rows_each, out_weight.shape[1])
     blocks = all_heads.reshape(tok_dev, outer, inner, rows_each).transpose(2, 0, 1, 3)
-    regrouped = lax.all_to_all(blocks, INNER, 0, 0, tiled=True)
+    regrouped = permute_all_to_all(blocks, INNER)
     partial = jnp.dot(
         regrouped.reshape(inner * tok_dev, outer * rows_each), weight_rows, preferred_element_type=jnp.float32
     )

time: 330 us -> 326 us (0.988)
  blocking collectives: 20.8 us -> 2.46 us
  waiting for transfers between devices: 195 us -> 199 us
  starting transfers between devices: 36.8 us -> 40.7 us
  local copies, waits for them, and re-layouts: 22.8 us -> 26.3 us
    all_gather x1 -> x0, waiting for transfers between devices: 28.5 us -> none  [shards(): all_heads = lax.all_gather(attended, 'head', axis=1, tiled=True)]
    all_to_all x1 -> x0, blocking collectives: 18.3 us -> none  [shards(): regrouped = lax.all_to_all(blocks, INNER, 0, 0, tiled=True)]
    reduce_scatter x1, waiting for transfers between devices: 56.7 us -> 74.6 us  [shards(): mixed = lax.psum_scatter(partial, INNER, scatter_dimension=0, tiled=True)]
    ppermute x0 -> x3, waiting for transfers between devices: none -> 12.2 us  [permute_all_to_all(): lax.ppermute(sent, axes, [(k, (k + shift) % n) for k in range(n)])]
    ppermute x0 -> x3, starting transfers between devices: none -> 3.81 us  [permute_all_to_all(): lax.ppermute(sent, axes, [(k, (k + shift) % n) for k in range(n)])]
    slice x2, local copies, waits for them, and re-layouts: 5.46 us -> 8.81 us  [shards(): got[:, width:]]
    ppermute x10 -> x11, waiting for transfers between devices: 99.9 us -> 102 us  [ring_gather(): lax.ppermute(pieces[-1], axis, [(k, (k + 1) % n) for k in range(n)])]
    ppermute x10 -> x11, starting transfers between devices: 30.1 us -> 30.1 us  [ring_gather(): lax.ppermute(pieces[-1], axis, [(k, (k + 1) % n) for k in range(n)])]
  transfers between devices with their start and end apart: 18 -> 21, of which waited for: 16 -> 18; matrix products, arithmetic and copies ran while one was open for 8% -> 9% of each run, Pallas kernels for 0% -> 0%
where the time goes in v6:
time: 326 us; the launch traced here: 325 us
  waiting for transfers between devices  199 us (61%)
  starting transfers between devices  40.7 us (12%)
  local copies, waits for them, and re-layouts  26.3 us (8%)
  other arithmetic  21.2 us (7%)
  matrix products  19.8 us (6%)
  between operations  15.7 us (5%)
    ppermute x11, waiting for transfers between devices, ring_gather(): lax.ppermute(pieces[-1], axis, [(k, (k + 1) % n) for k in range(n)])  102 us
    reduce_scatter x1, waiting for transfers between devices, shards(): mixed = lax.psum_scatter(partial, INNER, scatter_dimension=0, tiled=True)  74.6 us
    ppermute x11, starting transfers between devices, ring_gather(): lax.ppermute(pieces[-1], axis, [(k, (k + 1) % n) for k in range(n)])  30.1 us
    reshape x2, local copies, waits for them, and re-layouts, shards(): gathered.append((got.reshape(n_ctx * tok_dev, -1), key_rows))  13.2 us
    another operation x9, other arithmetic, ring_gather(): return jnp.stack(pieces)  12.3 us
    ppermute x3, waiting for transfers between devices, permute_all_to_all(): lax.ppermute(sent, axes, [(k, (k + shift) % n) for k in range(n)])  12.2 us
    ppermute x5, waiting for transfers between devices, butterfly_sum(): x = x + lax.ppermute(x, axis, [(i, i ^ bit) for i in range(size)])  9.56 us
    slice x2, local copies, waits for them, and re-layouts, shards(): got[:, width:]  8.81 us
  transfers between devices with their start and end apart: 21, of which 18 were waited for; matrix products, arithmetic and copies ran while one was open for 9% of the time, Pallas kernels for 0%

profile of v6, /device:TPU:0, one launch (start us, length us, event | category | flops | bytes accessed | tf_op | source)
XLA Modules:
  0.0 325.4 jit_solution(2168547829323027470)
XLA Ops:
  13.9 7.5 %collective-permute-done.5 = bf16[128,1024]{1,0:T(8,128)(2,1)S(1)} collective-permute-done((bf16[128,1024]{1,0:T(8,128)(2,1)S(1)}, bf16[128,1024]{1,0:T(8,128)(2,1)S(1)}, u32[]{:S(2)}, u32[]{:S(2)}) %collective-permute-start.5) | collective-permute-done | bytes 262176 | tf_op jit(solution)/shard_map/ppermute | solution.py:34
  21.4 7.3 %collective-permute-done = bf16[128,1024]{1,0:T(8,128)(2,1)S(1)} collective-permute-done((bf16[128,1024]{1,0:T(8,128)(2,1)S(1)}, bf16[128,1024]{1,0:T(8,128)(2,1)S(1)}, u32[]{:S(2)}, u32[]{:S(2)}) %collective-permute-start) | collective-permute-done | bytes 262176 | tf_op jit(solution)/shard_map/ppermute | solution.py:34
  28.7 3.3 %collective-permute-start.1 = (bf16[128,1024]{1,0:T(8,128)(2,1)S(1)}, bf16[128,1024]{1,0:T(8,128)(2,1)S(1)}, u32[]{:S(2)}, u32[]{:S(2)}) collective-permute-start(bf16[128,1024]{1,0:T(8,128)(2,1)S(1)} %collective-permute-done), channel_id=1, source_target_pairs={{0,8},{8,16},{16,24},{24,0},{1,9},{9,17},{17,25},{25,1},{2,10},{10... | collective-permute-start | bytes 786440 | tf_op jit(solution)/shard_map/ppermute | solution.py:34
  32.0 7.9 %collective-permute-done.6 = bf16[128,1024]{1,0:T(8,128)(2,1)S(1)} collective-permute-done((bf16[128,1024]{1,0:T(8,128)(2,1)S(1)}, bf16[128,1024]{1,0:T(8,128)(2,1)S(1)}, u32[]{:S(2)}, u32[]{:S(2)}) %collective-permute-start.6) | collective-permute-done | bytes 262176 | tf_op jit(solution)/shard_map/ppermute | solution.py:34
  39.9 6.5 %collective-permute-start.7 = (bf16[128,1024]{1,0:T(8,128)(2,1)S(1)}, bf16[128,1024]{1,0:T(8,128)(2,1)S(1)}, u32[]{:S(2)}, u32[]{:S(2)}) collective-permute-start(bf16[128,1024]{1,0:T(8,128)(2,1)S(1)} %collective-permute-done.6), channel_id=1, source_target_pairs={{0,8},{8,16},{16,24},{24,0},{1,9},{9,17},{17,25},{25,1},{2,10},{10... | collective-permute-start | bytes 786440 | tf_op jit(solution)/shard_map/ppermute | solution.py:34
  46.4 4.7 %collective-permute-done.1 = bf16[128,1024]{1,0:T(8,128)(2,1)S(1)} collective-permute-done((bf16[128,1024]{1,0:T(8,128)(2,1)S(1)}, bf16[128,1024]{1,0:T(8,128)(2,1)S(1)}, u32[]{:S(2)}, u32[]{:S(2)}) %collective-permute-start.1) | collective-permute-done | bytes 262176 | tf_op jit(solution)/shard_map/ppermute | solution.py:34
  51.1 9.7 %collective-permute-start.2 = (bf16[128,1024]{1,0:T(8,128)(2,1)S(1)}, bf16[128,1024]{1,0:T(8,128)(2,1)S(1)}, u32[]{:S(2)}, u32[]{:S(2)}) collective-permute-start(bf16[128,1024]{1,0:T(8,128)(2,1)S(1)} %collective-permute-done.1), channel_id=1, source_target_pairs={{0,8},{8,16},{16,24},{24,0},{1,9},{9,17},{17,25},{25,1},{2,10},{10... | collective-permute-start | bytes 786440 | tf_op jit(solution)/shard_map/ppermute | solution.py:34
  65.6 15.2 %collective-permute-done.2 = bf16[128,1024]{1,0:T(8,128)(2,1)S(1)} collective-permute-done((bf16[128,1024]{1,0:T(8,128)(2,1)S(1)}, bf16[128,1024]{1,0:T(8,128)(2,1)S(1)}, u32[]{:S(2)}, u32[]{:S(2)}) %collective-permute-start.2) | collective-permute-done | bytes 262176 | tf_op jit(solution)/shard_map/ppermute | solution.py:34
  86.1 21.1 %collective-permute-done.3 = bf16[4,128,1024]{2,1,0:T(8,128)(2,1)S(1)} collective-permute-done((bf16[4,128,1024]{2,1,0:T(8,128)(2,1)S(1)}, bf16[4,128,1024]{2,1,0:T(8,128)(2,1)S(1)}, u32[]{:S(2)}, u32[]{:S(2)}) %collective-permute-start.3) | collective-permute-done | bytes 1048608 | tf_op jit(solution)/shard_map/ppermute | solution.py:34
  112.1 32.4 %collective-permute-done.9 = bf16[2,4,128,1024]{3,2,1,0:T(8,128)(2,1)} collective-permute-done((bf16[2,4,128,1024]{3,2,1,0:T(8,128)(2,1)}, bf16[2,4,128,1024]{3,2,1,0:T(8,128)(2,1)}, u32[]{:S(2)}, u32[]{:S(2)}) %collective-permute-start.9) | collective-permute-done | bytes 2097184 | tf_op jit(solution)/shard_map/ppermute | solution.py:34
  144.5 4.0 %pad_maximum_fusion.1 = bf16[2,2,4,128,1024]{4,3,2,1,0:T(8,128)(2,1)} fusion(bf16[1,2,4,128,1024]{4,3,2,1,0:T(8,128)(2,1)} %bitcast.28, bf16[1,2,4,128,1024]{4,3,2,1,0:T(8,128)(2,1)S(1)} %get-tuple-element.80), kind=kLoop, calls=%fused_computation.21 | loop fusion | flops 2097152 | bytes 8388608 | tf_op jit(solution)/shard_map/stack | solution.py:35
  148.6 6.7 %copy.84 = bf16[2048,1024]{0,1:T(8,128)(2,1)} copy(bf16[2048,1024]{1,0:T(8,128)(2,1)} %bitcast.97) | data formatting | bytes 8388608 | tf_op jit(solution)/shard_map/reshape | solution.py:159
  155.3 3.9 %pad_maximum_fusion = bf16[2,2,4,128,1024]{4,3,2,1,0:T(8,128)(2,1)} fusion(bf16[1,2,4,128,1024]{4,3,2,1,0:T(8,128)(2,1)} %bitcast.18, bf16[1,2,4,128,1024]{4,3,2,1,0:T(8,128)(2,1)S(1)} %copy-done), kind=kLoop, calls=%fused_computation.20 | loop fusion | flops 2097152 | bytes 8388608 | tf_op jit(solution)/shard_map/stack | solution.py:35
  159.2 6.5 %copy.83 = bf16[2048,1024]{0,1:T(8,128)(2,1)} copy(bf16[2048,1024]{1,0:T(8,128)(2,1)} %bitcast.98) | data formatting | bytes 8388608 | tf_op jit(solution)/shard_map/reshape | solution.py:159
  170.3 10.7 %conditional.2 = (f32[4,2,128]{2,1,0:T(2,128)S(1)}, f32[4,2,128,128]{2,3,1,0:T(8,128)S(1)}) conditional(s32[]{:T(128)} %convert_element_type.37, () %tuple.26, (pred[128,2048]{0,1:T(8,128)(4,1)}, bf16[2048,1024]{0,1:T(8,128)(2,1)}, bf16[128,8,2,128]{0,3,2,1:T(8,128)(2,1)S(1)}) %tuple.74), branch_computations={%region_4.5_spmd, %region_5.7_spmd} | conditional | flops 1090518016 | bytes 41160776 | solution.py:120
  170.3 4.0 %fusion.48 = (bf16[2048,512]{0,1:T(8,128)(2,1)}, bf16[2048,512]{0,1:T(8,128)(2,1)S(1)}) fusion(bf16[2048,1024]{0,1:T(8,128)(2,1)} %get-tuple-element.21), kind=kLoop, calls=%fused_computation.131 | loop fusion | bytes 8388608 | tf_op jit(solution)/shard_map/slice | solution.py:165
  174.6 3.8 %fusion = (f32[4,2,128]{2,1,0:T(2,128)S(1)}, f32[4,2048,128,2]{2,1,3,0:T(8,128)S(1)}) fusion(pred[128,2048]{0,1:T(8,128)(4,1)} %get-tuple-element.20, bf16[2048,4,128,1]{0,2,3,1:T(8,128)(2,1)S(1)} %bitcast.107, bf16[128,8,2,128]{3,0,2,1:T(8,128)(2,1)S(1)} %copy.60), kind=kOutput, calls=%fused_computation.1 | convolution fusion | flops 545258496 | bytes 11014144 | tf_op jit(solution)/shard_map/cond/branch_1_fun/qgrd,kgd->grqk/dot_general | solution.py:101
  180.9 12.2 %conditional.3 = (f32[4,2,128]{2,1,0:T(2,128)S(1)}, f32[4,2,128,128]{2,3,1,0:T(8,128)S(1)}) conditional(s32[]{:T(128)} %convert_element_type.39, () %tuple.28, (pred[128,2048]{0,1:T(8,128)(4,1)S(1)}, bf16[2048,1024]{0,1:T(8,128)(2,1)}, bf16[128,8,2,128]{0,3,2,1:T(8,128)(2,1)S(1)}) %tuple.75), branch_computations={%region_9.10_spmd, %region_10.12_spmd} | conditional | flops 1090518016 | bytes 40112172 | solution.py:120
  181.2 4.8 %fusion.49 = (bf16[2048,512]{0,1:T(8,128)(2,1)}, bf16[2048,512]{0,1:T(8,128)(2,1)}) fusion(bf16[2048,1024]{0,1:T(8,128)(2,1)} %get-tuple-element.24), kind=kLoop, calls=%fused_computation.132 | loop fusion | bytes 8388608 | tf_op jit(solution)/shard_map/slice | solution.py:165
  186.3 4.3 %fusion.10 = (f32[4,2,128]{2,1,0:T(2,128)S(1)}, f32[4,2048,128,2]{2,1,3,0:T(8,128)S(1)}) fusion(pred[128,2048]{0,1:T(8,128)(4,1)S(1)} %get-tuple-element.23, bf16[2048,4,128,1]{0,2,3,1:T(8,128)(2,1)} %bitcast.108, bf16[128,8,2,128]{3,0,2,1:T(8,128)(2,1)S(1)} %copy.61), kind=kOutput, calls=%fused_computation.11 | convolution fusion | flops 545258496 | bytes 11014144 | tf_op jit(solution)/shard_map/cond/branch_1_fun/qgrd,kgd->grqk/dot_general | solution.py:101
  200.4 5.1 %collective-permute-done.11 = bf16[128,4,256]{2,0,1:T(8,128)(2,1)S(1)} collective-permute-done((bf16[128,4,256]{2,0,1:T(8,128)(2,1)S(1)}, bf16[128,4,256]{2,0,1:T(8,128)(2,1)S(1)}, u32[]{:S(2)}, u32[]{:S(2)}) %collective-permute-start.11) | collective-permute-done | bytes 262176 | tf_op jit(solution)/shard_map/ppermute | solution.py:61
  205.5 7.2 %collective-permute-done.12 = bf16[128,4,256]{2,0,1:T(8,128)(2,1)S(1)} collective-permute-done((bf16[128,4,256]{2,0,1:T(8,128)(2,1)S(1)}, bf16[128,4,256]{2,0,1:T(8,128)(2,1)S(1)}, u32[]{:S(2)}, u32[]{:S(2)}) %collective-permute-start.12) | collective-permute-done | bytes 262176 | tf_op jit(solution)/shard_map/ppermute | solution.py:61
  214.0 6.7 %fusion.52 = f32[512,2304]{1,0:T(8,128)} fusion(bf16[512,1024]{1,0:T(8,128)(2,1)S(1)} %bitcast.109, bf16[1024,2304]{1,0:T(8,128)(2,1)} %all-gather.2.cloned.1.call-done), kind=kOutput, calls=%fused_computation.135 | convolution fusion | flops 2415919104 | bytes 10485760 | tf_op jit(solution)/shard_map/dot_general | solution.py:176
  220.7 74.6 %reduce-scatter.2.cloned.1.call-done = f32[128,2304]{1,0:T(8,128)} async-done(((f32[512,2304]{1,0:T(8,128)}), f32[128,2304]{1,0:T(8,128)}) %reduce-scatter.2.cloned.1.call-update) | async-done | bytes 1179664 | tf_op jit(solution)/shard_map/reduce_scatter | solution.py:179
  (110 shorter events, 62.3 us)
Async XLA Ops:
  7.2 158.6 %all-gather.2.cloned.1.call-start = ((), (), s32[]{:S(2)}) async-start(), calls=%async_computation.1 | async-start | bytes 5898240 | tf_op jit(solution)/shard_map/all_gather | solution.py:149
  7.9 287.4 %reduce-scatter.2.cloned.1.call-start = ((), (), s32[]{:S(2)}) async-start(), calls=%async_computation.2 | async-start | bytes 5898240 | tf_op jit(solution)/shard_map/reduce_scatter | solution.py:179
  9.1 12.2 %collective-permute-start.5 = (bf16[128,1024]{1,0:T(8,128)(2,1)S(1)}, bf16[128,1024]{1,0:T(8,128)(2,1)S(1)}, u32[]{:S(2)}, u32[]{:S(2)}) collective-permute-start(bf16[128,1024]{1,0:T(8,128)(2,1)S(1)} %get-tuple-element.95), channel_id=1, source_target_pairs={{0,8},{8,16},{16,24},{24,0},{1,9},{9,17},{17,25},{25,1},{2,10},{10... | collective-permute-start | bytes 786440 | tf_op jit(solution)/shard_map/ppermute | solution.py:34
  12.2 16.5 %collective-permute-start = (bf16[128,1024]{1,0:T(8,128)(2,1)S(1)}, bf16[128,1024]{1,0:T(8,128)(2,1)S(1)}, u32[]{:S(2)}, u32[]{:S(2)}) collective-permute-start(bf16[128,1024]{1,0:T(8,128)(2,1)S(1)} %get-tuple-element.101), channel_id=1, source_target_pairs={{0,8},{8,16},{16,24},{24,0},{1,9},{9,17},{17,25},{25,1},{2,10},{10... | collective-permute-start | bytes 786440 | tf_op jit(solution)/shard_map/ppermute | solution.py:34
  21.4 18.5 %collective-permute-start.6 = (bf16[128,1024]{1,0:T(8,128)(2,1)S(1)}, bf16[128,1024]{1,0:T(8,128)(2,1)S(1)}, u32[]{:S(2)}, u32[]{:S(2)}) collective-permute-start(bf16[128,1024]{1,0:T(8,128)(2,1)S(1)} %collective-permute-done.5), channel_id=1, source_target_pairs={{0,8},{8,16},{16,24},{24,0},{1,9},{9,17},{17,25},{25,1},{2,10},{10... | collective-permute-start | bytes 786440 | tf_op jit(solution)/shard_map/ppermute | solution.py:34
  28.7 22.4 %collective-permute-start.1 = (bf16[128,1024]{1,0:T(8,128)(2,1)S(1)}, bf16[128,1024]{1,0:T(8,128)(2,1)S(1)}, u32[]{:S(2)}, u32[]{:S(2)}) collective-permute-start(bf16[128,1024]{1,0:T(8,128)(2,1)S(1)} %collective-permute-done), channel_id=1, source_target_pairs={{0,8},{8,16},{16,24},{24,0},{1,9},{9,17},{17,25},{25,1},{2,10},{10... | collective-permute-start | bytes 786440 | tf_op jit(solution)/shard_map/ppermute | solution.py:34
  39.9 24.0 %collective-permute-start.7 = (bf16[128,1024]{1,0:T(8,128)(2,1)S(1)}, bf16[128,1024]{1,0:T(8,128)(2,1)S(1)}, u32[]{:S(2)}, u32[]{:S(2)}) collective-permute-start(bf16[128,1024]{1,0:T(8,128)(2,1)S(1)} %collective-permute-done.6), channel_id=1, source_target_pairs={{0,8},{8,16},{16,24},{24,0},{1,9},{9,17},{17,25},{25,1},{2,10},{10... | collective-permute-start | bytes 786440 | tf_op jit(solution)/shard_map/ppermute | solution.py:34
  51.1 29.7 %collective-permute-start.2 = (bf16[128,1024]{1,0:T(8,128)(2,1)S(1)}, bf16[128,1024]{1,0:T(8,128)(2,1)S(1)}, u32[]{:S(2)}, u32[]{:S(2)}) collective-permute-start(bf16[128,1024]{1,0:T(8,128)(2,1)S(1)} %collective-permute-done.1), channel_id=1, source_target_pairs={{0,8},{8,16},{16,24},{24,0},{1,9},{9,17},{17,25},{25,1},{2,10},{10... | collective-permute-start | bytes 786440 | tf_op jit(solution)/shard_map/ppermute | solution.py:34
  64.0 19.2 %collective-permute-start.8 = (bf16[4,128,1024]{2,1,0:T(8,128)(2,1)S(1)}, bf16[4,128,1024]{2,1,0:T(8,128)(2,1)S(1)}, u32[]{:S(2)}, u32[]{:S(2)}) collective-permute-start(bf16[4,128,1024]{2,1,0:T(8,128)(2,1)S(1)} %get-tuple-element.91), channel_id=1, source_target_pairs={{0,4},{4,0},{1,5},{5,1},{2,6},{6,2},{3,7},{7,3},{8,12},{12,8},{9,1... | collective-permute-start | bytes 3145736 | tf_op jit(solution)/shard_map/ppermute | solution.py:34
  81.0 26.2 %collective-permute-start.3 = (bf16[4,128,1024]{2,1,0:T(8,128)(2,1)S(1)}, bf16[4,128,1024]{2,1,0:T(8,128)(2,1)S(1)}, u32[]{:S(2)}, u32[]{:S(2)}) collective-permute-start(bf16[4,128,1024]{2,1,0:T(8,128)(2,1)S(1)} %get-tuple-element.93), channel_id=1, source_target_pairs={{0,2},{2,0},{1,3},{3,1},{4,6},{6,4},{5,7},{7,5},{8,10},{10,8},{9,1... | collective-permute-start | bytes 3145736 | tf_op jit(solution)/shard_map/ppermute | solution.py:34
  84.9 59.6 %collective-permute-start.9 = (bf16[2,4,128,1024]{3,2,1,0:T(8,128)(2,1)}, bf16[2,4,128,1024]{3,2,1,0:T(8,128)(2,1)}, u32[]{:S(2)}, u32[]{:S(2)}) collective-permute-start(bf16[2,4,128,1024]{3,2,1,0:T(8,128)(2,1)} %get-tuple-element.81), channel_id=1, source_target_pairs={{0,2},{2,0},{1,3},{3,1},{4,6},{6,4},{5,7},{7,5},{8,10},{10,8},{9,1... | collective-permute-start | bytes 6291464 | tf_op jit(solution)/shard_map/ppermute | solution.py:34
  109.4 45.9 %collective-permute-start.4 = (bf16[2,4,128,1024]{3,2,1,0:T(8,128)(2,1)}, bf16[2,4,128,1024]{3,2,1,0:T(8,128)(2,1)}, u32[]{:S(2)}, u32[]{:S(2)}) collective-permute-start(bf16[2,4,128,1024]{3,2,1,0:T(8,128)(2,1)} %get-tuple-element.83), channel_id=1, source_target_pairs={{0,4},{4,0},{1,5},{5,1},{2,6},{6,2},{3,7},{7,3},{8,12},{12,8},{9,1... | collective-permute-start | bytes 6291464 | tf_op jit(solution)/shard_map/ppermute | solution.py:34
  193.3 2.0 collective-permute-start.10
  196.1 9.3 %collective-permute-start.11 = (bf16[128,4,256]{2,0,1:T(8,128)(2,1)S(1)}, bf16[128,4,256]{2,0,1:T(8,128)(2,1)S(1)}, u32[]{:S(2)}, u32[]{:S(2)}) collective-permute-start(bf16[128,4,256]{2,0,1:T(8,128)(2,1)S(1)} %bitcast.119), channel_id=1, source_target_pairs={{0,6},{2,0},{4,2},{6,4},{1,7},{3,1},{5,3},{7,5},{8,14},{10,8},{12,... | collective-permute-start | bytes 786440 | tf_op jit(solution)/shard_map/ppermute | solution.py:61
  198.9 13.8 %collective-permute-start.12 = (bf16[128,4,256]{2,0,1:T(8,128)(2,1)S(1)}, bf16[128,4,256]{2,0,1:T(8,128)(2,1)S(1)}, u32[]{:S(2)}, u32[]{:S(2)}) collective-permute-start(bf16[128,4,256]{2,0,1:T(8,128)(2,1)S(1)} %bitcast.120), channel_id=1, source_target_pairs={{0,4},{2,6},{4,0},{6,2},{1,5},{3,7},{5,1},{7,3},{8,12},{10,14},{12... | collective-permute-start | bytes 786440 | tf_op jit(solution)/shard_map/ppermute | solution.py:61
  199.6 13.1 %collective-permute-start.13 = (bf16[128,4,256]{2,0,1:T(8,128)(2,1)S(1)}, bf16[128,4,256]{2,0,1:T(8,128)(2,1)S(1)}, u32[]{:S(2)}, u32[]{:S(2)}) collective-permute-start(bf16[128,4,256]{2,0,1:T(8,128)(2,1)S(1)} %bitcast.121), channel_id=1, source_target_pairs={{0,2},{2,4},{4,6},{6,0},{1,3},{3,5},{5,7},{7,1},{8,10},{10,12},{12... | collective-permute-start | bytes 786440 | tf_op jit(solution)/shard_map/ppermute | solution.py:61
  220.6 78.6 %copy-start.3 = (bf16[128,2304]{1,0:T(8,128)(2,1)S(1)}, bf16[128,2304]{1,0:T(8,128)(2,1)}, u32[]{:S(2)}) copy-start(bf16[128,2304]{1,0:T(8,128)(2,1)} %param.15) | copy-start | bytes 1769476
  220.6 78.6 %copy-start.6 = (f32[2304]{0:T(1024)S(1)}, f32[2304]{0:T(1024)}, u32[]{:S(2)}) copy-start(f32[2304]{0:T(1024)} %param.18) | copy-start | bytes 27652
  220.6 78.6 %copy-start.7 = (f32[2304]{0:T(1024)S(1)}, f32[2304]{0:T(1024)}, u32[]{:S(2)}) copy-start(f32[2304]{0:T(1024)} %param.17) | copy-start | bytes 27652
  301.8 3.6 %collective-permute-start.14 = (f32[16]{0:T(128)S(1)}, f32[16]{0:T(128)S(1)}, u32[]{:S(2)}, u32[]{:S(2)}) collective-permute-start(f32[16]{0:T(128)S(1)} %select_reduce_fusion), channel_id=1, source_target_pairs={{0,8},{8,0},{16,24},{24,16},{1,9},{9,1},{17,25},{25,17},{2,10},{10... | collective-permute-start | bytes 200 | tf_op jit(solution)/shard_map/ppermute | solution.py:70
  305.4 4.4 %collective-permute-start.15 = (f32[16]{0:T(128)S(1)}, f32[16]{0:T(128)S(1)}, u32[]{:S(2)}, u32[]{:S(2)}) collective-permute-start(f32[16]{0:T(128)S(1)} %add.352), channel_id=1, source_target_pairs={{0,16},{8,24},{16,0},{24,8},{1,17},{9,25},{17,1},{25,9},{2,18},{10... | collective-permute-start | bytes 200 | tf_op jit(solution)/shard_map/ppermute | solution.py:70
  309.8 3.5 %collective-permute-start.16 = (f32[16]{0:T(128)S(1)}, f32[16]{0:T(128)S(1)}, u32[]{:S(2)}, u32[]{:S(2)}) collective-permute-start(f32[16]{0:T(128)S(1)} %add.353), channel_id=1, source_target_pairs={{0,4},{4,0},{1,5},{5,1},{2,6},{6,2},{3,7},{7,3},{8,12},{12,8},{9,1... | collective-permute-start | bytes 200 | tf_op jit(solution)/shard_map/ppermute | solution.py:70
  313.4 3.5 %collective-permute-start.17 = (f32[16]{0:T(128)S(1)}, f32[16]{0:T(128)S(1)}, u32[]{:S(2)}, u32[]{:S(2)}) collective-permute-start(f32[16]{0:T(128)S(1)} %add.354), channel_id=1, source_target_pairs={{0,2},{2,0},{1,3},{3,1},{4,6},{6,4},{5,7},{7,5},{8,10},{10,8},{9,1... | collective-permute-start | bytes 200 | tf_op jit(solution)/shard_map/ppermute | solution.py:70
  316.9 1.1 collective-permute-start.18
  (6 other events, 27.3 us)
Sparse Core Ops, SparseCore 0:
  9.6 115.5 all-gather.1
  220.8 74.4 reduce-scatter.1

commit v7 on v6

--- a/solution.py
+++ b/solution.py
@@ -176,7 +176,8 @@
     partial = jnp.dot(
         regrouped.reshape(inner * tok_dev, outer * rows_each), weight_rows, preferred_element_type=jnp.float32
     )
-    mixed = lax.psum_scatter(partial, INNER, scatter_dimension=0, tiled=True)
+    mixed = lax.psum_scatter(partial.astype(jnp.bfloat16), INNER, scatter_dimension=0, tiled=True)
+    mixed = mixed.astype(jnp.float32)
     squares = lax.psum(jnp.sum(mixed * mixed, axis=1), "head")
     normed = mixed / jnp.sqrt(squares / D + 1e-06)[:, None]
     out32 = hidden_in.astype(jnp.float32) + normed * out_gain[None, :]

time: 326 us -> 306 us (0.939)
  waiting for transfers between devices: 199 us -> 179 us
    reduce_scatter x1, waiting for transfers between devices: 74.6 us -> 54.9 us  [shards(): lax.psum_scatter(partial.astype(jnp.bfloat16), INNER, scatter_dimension=0...]
where the time goes in v7:
time: 306 us; the launch traced here: 305 us
  waiting for transfers between devices  179 us (58%)
  starting transfers between devices  40.8 us (13%)
  local copies, waits for them, and re-layouts  26.3 us (9%)
  other arithmetic  20.9 us (7%)
  matrix products  19.4 us (6%)
  between operations  15.7 us (5%)
    ppermute x11, waiting for transfers between devices, ring_gather(): lax.ppermute(pieces[-1], axis, [(k, (k + 1) % n) for k in range(n)])  102 us
    reduce_scatter x1, waiting for transfers between devices, shards(): lax.psum_scatter(partial.astype(jnp.bfloat16), INNER, scatter_dimension=0...  54.9 us
    ppermute x11, starting transfers between devices, ring_gather(): lax.ppermute(pieces[-1], axis, [(k, (k + 1) % n) for k in range(n)])  30.1 us
    reshape x2, local copies, waits for them, and re-layouts, shards(): gathered.append((got.reshape(n_ctx * tok_dev, -1), key_rows))  13.2 us
    another operation x9, other arithmetic, ring_gather(): return jnp.stack(pieces)  12.3 us
    ppermute x3, waiting for transfers between devices, permute_all_to_all(): lax.ppermute(sent, axes, [(k, (k + shift) % n) for k in range(n)])  12.2 us
    ppermute x5, waiting for transfers between devices, butterfly_sum(): x = x + lax.ppermute(x, axis, [(i, i ^ bit) for i in range(size)])  9.47 us
    slice x2, local copies, waits for them, and re-layouts, shards(): got[:, width:]  8.81 us
  transfers between devices with their start and end apart: 21, of which 18 were waited for; matrix products, arithmetic and copies ran while one was open for 9% of the time, Pallas kernels for 0%

profile of v7, /device:TPU:0, one launch (start us, length us, event | category | flops | bytes accessed | tf_op | source)
XLA Modules:
  0.0 304.9 jit_solution(7743352501496223823)
XLA Ops:
  13.9 7.5 %collective-permute-done.5 = bf16[128,1024]{1,0:T(8,128)(2,1)S(1)} collective-permute-done((bf16[128,1024]{1,0:T(8,128)(2,1)S(1)}, bf16[128,1024]{1,0:T(8,128)(2,1)S(1)}, u32[]{:S(2)}, u32[]{:S(2)}) %collective-permute-start.5) | collective-permute-done | bytes 262176 | tf_op jit(solution)/shard_map/ppermute | solution.py:34
  21.4 7.3 %collective-permute-done = bf16[128,1024]{1,0:T(8,128)(2,1)S(1)} collective-permute-done((bf16[128,1024]{1,0:T(8,128)(2,1)S(1)}, bf16[128,1024]{1,0:T(8,128)(2,1)S(1)}, u32[]{:S(2)}, u32[]{:S(2)}) %collective-permute-start) | collective-permute-done | bytes 262176 | tf_op jit(solution)/shard_map/ppermute | solution.py:34
  28.7 3.3 %collective-permute-start.1 = (bf16[128,1024]{1,0:T(8,128)(2,1)S(1)}, bf16[128,1024]{1,0:T(8,128)(2,1)S(1)}, u32[]{:S(2)}, u32[]{:S(2)}) collective-permute-start(bf16[128,1024]{1,0:T(8,128)(2,1)S(1)} %collective-permute-done), channel_id=1, source_target_pairs={{0,8},{8,16},{16,24},{24,0},{1,9},{9,17},{17,25},{25,1},{2,10},{10... | collective-permute-start | bytes 786440 | tf_op jit(solution)/shard_map/ppermute | solution.py:34
  32.0 7.9 %collective-permute-done.6 = bf16[128,1024]{1,0:T(8,128)(2,1)S(1)} collective-permute-done((bf16[128,1024]{1,0:T(8,128)(2,1)S(1)}, bf16[128,1024]{1,0:T(8,128)(2,1)S(1)}, u32[]{:S(2)}, u32[]{:S(2)}) %collective-permute-start.6) | collective-permute-done | bytes 262176 | tf_op jit(solution)/shard_map/ppermute | solution.py:34
  39.9 6.5 %collective-permute-start.7 = (bf16[128,1024]{1,0:T(8,128)(2,1)S(1)}, bf16[128,1024]{1,0:T(8,128)(2,1)S(1)}, u32[]{:S(2)}, u32[]{:S(2)}) collective-permute-start(bf16[128,1024]{1,0:T(8,128)(2,1)S(1)} %collective-permute-done.6), channel_id=1, source_target_pairs={{0,8},{8,16},{16,24},{24,0},{1,9},{9,17},{17,25},{25,1},{2,10},{10... | collective-permute-start | bytes 786440 | tf_op jit(solution)/shard_map/ppermute | solution.py:34
  46.4 4.7 %collective-permute-done.1 = bf16[128,1024]{1,0:T(8,128)(2,1)S(1)} collective-permute-done((bf16[128,1024]{1,0:T(8,128)(2,1)S(1)}, bf16[128,1024]{1,0:T(8,128)(2,1)S(1)}, u32[]{:S(2)}, u32[]{:S(2)}) %collective-permute-start.1) | collective-permute-done | bytes 262176 | tf_op jit(solution)/shard_map/ppermute | solution.py:34
  51.1 9.7 %collective-permute-start.2 = (bf16[128,1024]{1,0:T(8,128)(2,1)S(1)}, bf16[128,1024]{1,0:T(8,128)(2,1)S(1)}, u32[]{:S(2)}, u32[]{:S(2)}) collective-permute-start(bf16[128,1024]{1,0:T(8,128)(2,1)S(1)} %collective-permute-done.1), channel_id=1, source_target_pairs={{0,8},{8,16},{16,24},{24,0},{1,9},{9,17},{17,25},{25,1},{2,10},{10... | collective-permute-start | bytes 786440 | tf_op jit(solution)/shard_map/ppermute | solution.py:34
  65.6 15.2 %collective-permute-done.2 = bf16[128,1024]{1,0:T(8,128)(2,1)S(1)} collective-permute-done((bf16[128,1024]{1,0:T(8,128)(2,1)S(1)}, bf16[128,1024]{1,0:T(8,128)(2,1)S(1)}, u32[]{:S(2)}, u32[]{:S(2)}) %collective-permute-start.2) | collective-permute-done | bytes 262176 | tf_op jit(solution)/shard_map/ppermute | solution.py:34
  86.1 21.1 %collective-permute-done.3 = bf16[4,128,1024]{2,1,0:T(8,128)(2,1)S(1)} collective-permute-done((bf16[4,128,1024]{2,1,0:T(8,128)(2,1)S(1)}, bf16[4,128,1024]{2,1,0:T(8,128)(2,1)S(1)}, u32[]{:S(2)}, u32[]{:S(2)}) %collective-permute-start.3) | collective-permute-done | bytes 1048608 | tf_op jit(solution)/shard_map/ppermute | solution.py:34
  112.1 32.4 %collective-permute-done.9 = bf16[2,4,128,1024]{3,2,1,0:T(8,128)(2,1)} collective-permute-done((bf16[2,4,128,1024]{3,2,1,0:T(8,128)(2,1)}, bf16[2,4,128,1024]{3,2,1,0:T(8,128)(2,1)}, u32[]{:S(2)}, u32[]{:S(2)}) %collective-permute-start.9) | collective-permute-done | bytes 2097184 | tf_op jit(solution)/shard_map/ppermute | solution.py:34
  144.5 4.0 %pad_maximum_fusion.1 = bf16[2,2,4,128,1024]{4,3,2,1,0:T(8,128)(2,1)} fusion(bf16[1,2,4,128,1024]{4,3,2,1,0:T(8,128)(2,1)} %bitcast.28, bf16[1,2,4,128,1024]{4,3,2,1,0:T(8,128)(2,1)S(1)} %get-tuple-element.80), kind=kLoop, calls=%fused_computation.22 | loop fusion | flops 2097152 | bytes 8388608 | tf_op jit(solution)/shard_map/stack | solution.py:35
  148.6 6.7 %copy.84 = bf16[2048,1024]{0,1:T(8,128)(2,1)} copy(bf16[2048,1024]{1,0:T(8,128)(2,1)} %bitcast.97) | data formatting | bytes 8388608 | tf_op jit(solution)/shard_map/reshape | solution.py:159
  155.3 3.9 %pad_maximum_fusion = bf16[2,2,4,128,1024]{4,3,2,1,0:T(8,128)(2,1)} fusion(bf16[1,2,4,128,1024]{4,3,2,1,0:T(8,128)(2,1)} %bitcast.18, bf16[1,2,4,128,1024]{4,3,2,1,0:T(8,128)(2,1)S(1)} %copy-done), kind=kLoop, calls=%fused_computation.21 | loop fusion | flops 2097152 | bytes 8388608 | tf_op jit(solution)/shard_map/stack | solution.py:35
  159.2 6.5 %copy.83 = bf16[2048,1024]{0,1:T(8,128)(2,1)} copy(bf16[2048,1024]{1,0:T(8,128)(2,1)} %bitcast.98) | data formatting | bytes 8388608 | tf_op jit(solution)/shard_map/reshape | solution.py:159
  170.3 10.7 %conditional.2 = (f32[4,2,128]{2,1,0:T(2,128)S(1)}, f32[4,2,128,128]{2,3,1,0:T(8,128)S(1)}) conditional(s32[]{:T(128)} %convert_element_type.43, () %tuple.26, (pred[128,2048]{0,1:T(8,128)(4,1)}, bf16[2048,1024]{0,1:T(8,128)(2,1)}, bf16[128,8,2,128]{0,3,2,1:T(8,128)(2,1)S(1)}) %tuple.74), branch_computations={%region_4.5_spmd, %region_5.7_spmd} | conditional | flops 1090518016 | bytes 41160776 | solution.py:120
  170.3 4.0 %fusion.51 = (bf16[2048,512]{0,1:T(8,128)(2,1)}, bf16[2048,512]{0,1:T(8,128)(2,1)S(1)}) fusion(bf16[2048,1024]{0,1:T(8,128)(2,1)} %get-tuple-element.21), kind=kLoop, calls=%fused_computation.135 | loop fusion | bytes 8388608 | tf_op jit(solution)/shard_map/slice | solution.py:165
  174.6 3.8 %fusion = (f32[4,2,128]{2,1,0:T(2,128)S(1)}, f32[4,2048,128,2]{2,1,3,0:T(8,128)S(1)}) fusion(pred[128,2048]{0,1:T(8,128)(4,1)} %get-tuple-element.20, bf16[2048,4,128,1]{0,2,3,1:T(8,128)(2,1)S(1)} %bitcast.107, bf16[128,8,2,128]{3,0,2,1:T(8,128)(2,1)S(1)} %copy.60), kind=kOutput, calls=%fused_computation.1 | convolution fusion | flops 545258496 | bytes 11014144 | tf_op jit(solution)/shard_map/cond/branch_1_fun/qgrd,kgd->grqk/dot_general | solution.py:101
  180.9 12.2 %conditional.3 = (f32[4,2,128]{2,1,0:T(2,128)S(1)}, f32[4,2,128,128]{2,3,1,0:T(8,128)S(1)}) conditional(s32[]{:T(128)} %convert_element_type.45, () %tuple.28, (pred[128,2048]{0,1:T(8,128)(4,1)S(1)}, bf16[2048,1024]{0,1:T(8,128)(2,1)}, bf16[128,8,2,128]{0,3,2,1:T(8,128)(2,1)S(1)}) %tuple.75), branch_computations={%region_9.10_spmd, %region_10.12_spmd} | conditional | flops 1090518016 | bytes 40112172 | solution.py:120
  181.2 4.8 %fusion.52 = (bf16[2048,512]{0,1:T(8,128)(2,1)}, bf16[2048,512]{0,1:T(8,128)(2,1)}) fusion(bf16[2048,1024]{0,1:T(8,128)(2,1)} %get-tuple-element.24), kind=kLoop, calls=%fused_computation.136 | loop fusion | bytes 8388608 | tf_op jit(solution)/shard_map/slice | solution.py:165
  186.3 4.3 %fusion.10 = (f32[4,2,128]{2,1,0:T(2,128)S(1)}, f32[4,2048,128,2]{2,1,3,0:T(8,128)S(1)}) fusion(pred[128,2048]{0,1:T(8,128)(4,1)S(1)} %get-tuple-element.23, bf16[2048,4,128,1]{0,2,3,1:T(8,128)(2,1)} %bitcast.108, bf16[128,8,2,128]{3,0,2,1:T(8,128)(2,1)S(1)} %copy.61), kind=kOutput, calls=%fused_computation.11 | convolution fusion | flops 545258496 | bytes 11014144 | tf_op jit(solution)/shard_map/cond/branch_1_fun/qgrd,kgd->grqk/dot_general | solution.py:101
  200.4 5.1 %collective-permute-done.11 = bf16[128,4,256]{2,0,1:T(8,128)(2,1)S(1)} collective-permute-done((bf16[128,4,256]{2,0,1:T(8,128)(2,1)S(1)}, bf16[128,4,256]{2,0,1:T(8,128)(2,1)S(1)}, u32[]{:S(2)}, u32[]{:S(2)}) %collective-permute-start.11) | collective-permute-done | bytes 262176 | tf_op jit(solution)/shard_map/ppermute | solution.py:61
  205.5 7.2 %collective-permute-done.12 = bf16[128,4,256]{2,0,1:T(8,128)(2,1)S(1)} collective-permute-done((bf16[128,4,256]{2,0,1:T(8,128)(2,1)S(1)}, bf16[128,4,256]{2,0,1:T(8,128)(2,1)S(1)}, u32[]{:S(2)}, u32[]{:S(2)}) %collective-permute-start.12) | collective-permute-done | bytes 262176 | tf_op jit(solution)/shard_map/ppermute | solution.py:61
  214.0 6.2 %convolution_convert_fusion = bf16[512,2304]{1,0:T(8,128)(2,1)} fusion(bf16[512,1024]{1,0:T(8,128)(2,1)S(1)} %bitcast.109, bf16[1024,2304]{1,0:T(8,128)(2,1)} %all-gather.2.cloned.1.call-done), kind=kOutput, calls=%fused_computation.20 | convolution fusion | flops 2417098752 | bytes 8126464 | tf_op jit(solution)/shard_map/dot_general | solution.py:176
  220.2 54.9 %reduce-scatter.2.cloned.1.call-done = bf16[128,2304]{1,0:T(8,128)(2,1)} async-done(((bf16[512,2304]{1,0:T(8,128)(2,1)}), bf16[128,2304]{1,0:T(8,128)(2,1)}) %reduce-scatter.2.cloned.1.call-update) | async-done | bytes 589840 | tf_op jit(solution)/shard_map/reduce_scatter | solution.py:179
  (110 shorter events, 61.9 us)
Async XLA Ops:
  7.2 158.6 %all-gather.2.cloned.1.call-start = ((), (), s32[]{:S(2)}) async-start(), calls=%async_computation.1 | async-start | bytes 5898240 | tf_op jit(solution)/shard_map/all_gather | solution.py:149
  7.9 267.2 %reduce-scatter.2.cloned.1.call-start = ((), (), s32[]{:S(2)}) async-start(), calls=%async_computation.2 | async-start | bytes 2949120 | tf_op jit(solution)/shard_map/reduce_scatter | solution.py:179
  9.1 12.2 %collective-permute-start.5 = (bf16[128,1024]{1,0:T(8,128)(2,1)S(1)}, bf16[128,1024]{1,0:T(8,128)(2,1)S(1)}, u32[]{:S(2)}, u32[]{:S(2)}) collective-permute-start(bf16[128,1024]{1,0:T(8,128)(2,1)S(1)} %get-tuple-element.95), channel_id=1, source_target_pairs={{0,8},{8,16},{16,24},{24,0},{1,9},{9,17},{17,25},{25,1},{2,10},{10... | collective-permute-start | bytes 786440 | tf_op jit(solution)/shard_map/ppermute | solution.py:34
  12.2 16.5 %collective-permute-start = (bf16[128,1024]{1,0:T(8,128)(2,1)S(1)}, bf16[128,1024]{1,0:T(8,128)(2,1)S(1)}, u32[]{:S(2)}, u32[]{:S(2)}) collective-permute-start(bf16[128,1024]{1,0:T(8,128)(2,1)S(1)} %get-tuple-element.101), channel_id=1, source_target_pairs={{0,8},{8,16},{16,24},{24,0},{1,9},{9,17},{17,25},{25,1},{2,10},{10... | collective-permute-start | bytes 786440 | tf_op jit(solution)/shard_map/ppermute | solution.py:34
  21.4 18.5 %collective-permute-start.6 = (bf16[128,1024]{1,0:T(8,128)(2,1)S(1)}, bf16[128,1024]{1,0:T(8,128)(2,1)S(1)}, u32[]{:S(2)}, u32[]{:S(2)}) collective-permute-start(bf16[128,1024]{1,0:T(8,128)(2,1)S(1)} %collective-permute-done.5), channel_id=1, source_target_pairs={{0,8},{8,16},{16,24},{24,0},{1,9},{9,17},{17,25},{25,1},{2,10},{10... | collective-permute-start | bytes 786440 | tf_op jit(solution)/shard_map/ppermute | solution.py:34
  28.7 22.4 %collective-permute-start.1 = (bf16[128,1024]{1,0:T(8,128)(2,1)S(1)}, bf16[128,1024]{1,0:T(8,128)(2,1)S(1)}, u32[]{:S(2)}, u32[]{:S(2)}) collective-permute-start(bf16[128,1024]{1,0:T(8,128)(2,1)S(1)} %collective-permute-done), channel_id=1, source_target_pairs={{0,8},{8,16},{16,24},{24,0},{1,9},{9,17},{17,25},{25,1},{2,10},{10... | collective-permute-start | bytes 786440 | tf_op jit(solution)/shard_map/ppermute | solution.py:34
  39.9 24.0 %collective-permute-start.7 = (bf16[128,1024]{1,0:T(8,128)(2,1)S(1)}, bf16[128,1024]{1,0:T(8,128)(2,1)S(1)}, u32[]{:S(2)}, u32[]{:S(2)}) collective-permute-start(bf16[128,1024]{1,0:T(8,128)(2,1)S(1)} %collective-permute-done.6), channel_id=1, source_target_pairs={{0,8},{8,16},{16,24},{24,0},{1,9},{9,17},{17,25},{25,1},{2,10},{10... | collective-permute-start | bytes 786440 | tf_op jit(solution)/shard_map/ppermute | solution.py:34
  51.1 29.7 %collective-permute-start.2 = (bf16[128,1024]{1,0:T(8,128)(2,1)S(1)}, bf16[128,1024]{1,0:T(8,128)(2,1)S(1)}, u32[]{:S(2)}, u32[]{:S(2)}) collective-permute-start(bf16[128,1024]{1,0:T(8,128)(2,1)S(1)} %collective-permute-done.1), channel_id=1, source_target_pairs={{0,8},{8,16},{16,24},{24,0},{1,9},{9,17},{17,25},{25,1},{2,10},{10... | collective-permute-start | bytes 786440 | tf_op jit(solution)/shard_map/ppermute | solution.py:34
  64.0 19.2 %collective-permute-start.8 = (bf16[4,128,1024]{2,1,0:T(8,128)(2,1)S(1)}, bf16[4,128,1024]{2,1,0:T(8,128)(2,1)S(1)}, u32[]{:S(2)}, u32[]{:S(2)}) collective-permute-start(bf16[4,128,1024]{2,1,0:T(8,128)(2,1)S(1)} %get-tuple-element.91), channel_id=1, source_target_pairs={{0,4},{4,0},{1,5},{5,1},{2,6},{6,2},{3,7},{7,3},{8,12},{12,8},{9,1... | collective-permute-start | bytes 3145736 | tf_op jit(solution)/shard_map/ppermute | solution.py:34
  81.0 26.2 %collective-permute-start.3 = (bf16[4,128,1024]{2,1,0:T(8,128)(2,1)S(1)}, bf16[4,128,1024]{2,1,0:T(8,128)(2,1)S(1)}, u32[]{:S(2)}, u32[]{:S(2)}) collective-permute-start(bf16[4,128,1024]{2,1,0:T(8,128)(2,1)S(1)} %get-tuple-element.93), channel_id=1, source_target_pairs={{0,2},{2,0},{1,3},{3,1},{4,6},{6,4},{5,7},{7,5},{8,10},{10,8},{9,1... | collective-permute-start | bytes 3145736 | tf_op jit(solution)/shard_map/ppermute | solution.py:34
  84.9 59.6 %collective-permute-start.9 = (bf16[2,4,128,1024]{3,2,1,0:T(8,128)(2,1)}, bf16[2,4,128,1024]{3,2,1,0:T(8,128)(2,1)}, u32[]{:S(2)}, u32[]{:S(2)}) collective-permute-start(bf16[2,4,128,1024]{3,2,1,0:T(8,128)(2,1)} %get-tuple-element.81), channel_id=1, source_target_pairs={{0,2},{2,0},{1,3},{3,1},{4,6},{6,4},{5,7},{7,5},{8,10},{10,8},{9,1... | collective-permute-start | bytes 6291464 | tf_op jit(solution)/shard_map/ppermute | solution.py:34
  109.4 45.9 %collective-permute-start.4 = (bf16[2,4,128,1024]{3,2,1,0:T(8,128)(2,1)}, bf16[2,4,128,1024]{3,2,1,0:T(8,128)(2,1)}, u32[]{:S(2)}, u32[]{:S(2)}) collective-permute-start(bf16[2,4,128,1024]{3,2,1,0:T(8,128)(2,1)} %get-tuple-element.83), channel_id=1, source_target_pairs={{0,4},{4,0},{1,5},{5,1},{2,6},{6,2},{3,7},{7,3},{8,12},{12,8},{9,1... | collective-permute-start | bytes 6291464 | tf_op jit(solution)/shard_map/ppermute | solution.py:34
  193.3 2.0 collective-permute-start.10
  196.1 9.3 %collective-permute-start.11 = (bf16[128,4,256]{2,0,1:T(8,128)(2,1)S(1)}, bf16[128,4,256]{2,0,1:T(8,128)(2,1)S(1)}, u32[]{:S(2)}, u32[]{:S(2)}) collective-permute-start(bf16[128,4,256]{2,0,1:T(8,128)(2,1)S(1)} %bitcast.119), channel_id=1, source_target_pairs={{0,6},{2,0},{4,2},{6,4},{1,7},{3,1},{5,3},{7,5},{8,14},{10,8},{12,... | collective-permute-start | bytes 786440 | tf_op jit(solution)/shard_map/ppermute | solution.py:61
  198.9 13.8 %collective-permute-start.12 = (bf16[128,4,256]{2,0,1:T(8,128)(2,1)S(1)}, bf16[128,4,256]{2,0,1:T(8,128)(2,1)S(1)}, u32[]{:S(2)}, u32[]{:S(2)}) collective-permute-start(bf16[128,4,256]{2,0,1:T(8,128)(2,1)S(1)} %bitcast.120), channel_id=1, source_target_pairs={{0,4},{2,6},{4,0},{6,2},{1,5},{3,7},{5,1},{7,3},{8,12},{10,14},{12... | collective-permute-start | bytes 786440 | tf_op jit(solution)/shard_map/ppermute | solution.py:61
  199.6 13.1 %collective-permute-start.13 = (bf16[128,4,256]{2,0,1:T(8,128)(2,1)S(1)}, bf16[128,4,256]{2,0,1:T(8,128)(2,1)S(1)}, u32[]{:S(2)}, u32[]{:S(2)}) collective-permute-start(bf16[128,4,256]{2,0,1:T(8,128)(2,1)S(1)} %bitcast.121), channel_id=1, source_target_pairs={{0,2},{2,4},{4,6},{6,0},{1,3},{3,5},{5,7},{7,1},{8,10},{10,12},{12... | collective-permute-start | bytes 786440 | tf_op jit(solution)/shard_map/ppermute | solution.py:61
  220.2 58.7 %copy-start.3 = (bf16[128,2304]{1,0:T(8,128)(2,1)S(1)}, bf16[128,2304]{1,0:T(8,128)(2,1)}, u32[]{:S(2)}) copy-start(bf16[128,2304]{1,0:T(8,128)(2,1)} %param.15) | copy-start | bytes 1769476
  220.2 58.7 %copy-start.6 = (f32[2304]{0:T(1024)S(1)}, f32[2304]{0:T(1024)}, u32[]{:S(2)}) copy-start(f32[2304]{0:T(1024)} %param.18) | copy-start | bytes 27652
  220.2 58.7 %copy-start.7 = (f32[2304]{0:T(1024)S(1)}, f32[2304]{0:T(1024)}, u32[]{:S(2)}) copy-start(f32[2304]{0:T(1024)} %param.17) | copy-start | bytes 27652
  281.3 3.6 %collective-permute-start.14 = (f32[16]{0:T(128)S(1)}, f32[16]{0:T(128)S(1)}, u32[]{:S(2)}, u32[]{:S(2)}) collective-permute-start(f32[16]{0:T(128)S(1)} %select_reduce_fusion), channel_id=1, source_target_pairs={{0,8},{8,0},{16,24},{24,16},{1,9},{9,1},{17,25},{25,17},{2,10},{10... | collective-permute-start | bytes 200 | tf_op jit(solution)/shard_map/ppermute | solution.py:70
  284.9 4.4 %collective-permute-start.15 = (f32[16]{0:T(128)S(1)}, f32[16]{0:T(128)S(1)}, u32[]{:S(2)}, u32[]{:S(2)}) collective-permute-start(f32[16]{0:T(128)S(1)} %add.352), channel_id=1, source_target_pairs={{0,16},{8,24},{16,0},{24,8},{1,17},{9,25},{17,1},{25,9},{2,18},{10... | collective-permute-start | bytes 200 | tf_op jit(solution)/shard_map/ppermute | solution.py:70
  289.3 3.5 %collective-permute-start.16 = (f32[16]{0:T(128)S(1)}, f32[16]{0:T(128)S(1)}, u32[]{:S(2)}, u32[]{:S(2)}) collective-permute-start(f32[16]{0:T(128)S(1)} %add.353), channel_id=1, source_target_pairs={{0,4},{4,0},{1,5},{5,1},{2,6},{6,2},{3,7},{7,3},{8,12},{12,8},{9,1... | collective-permute-start | bytes 200 | tf_op jit(solution)/shard_map/ppermute | solution.py:70
  292.9 3.5 %collective-permute-start.17 = (f32[16]{0:T(128)S(1)}, f32[16]{0:T(128)S(1)}, u32[]{:S(2)}, u32[]{:S(2)}) collective-permute-start(f32[16]{0:T(128)S(1)} %add.354), channel_id=1, source_target_pairs={{0,2},{2,0},{1,3},{3,1},{4,6},{6,4},{5,7},{7,5},{8,10},{10,8},{9,1... | collective-permute-start | bytes 200 | tf_op jit(solution)/shard_map/ppermute | solution.py:70
  296.4 1.1 collective-permute-start.18
  (6 other events, 27.3 us)
Sparse Core Ops, SparseCore 0:
  9.6 115.5 all-gather.1
  220.3 54.7 reduce-scatter.1

commit v8 on v6

--- a/solution.py
+++ b/solution.py
@@ -12,7 +12,7 @@
 
 soft_cap = 50.0
 CTX = ("c0", "c1", "c2")
-INNER = ("c1", "c2")
+OUTER = ("c0", "c2")
 
 
 def storage_positions(rows, tok_dev, n_ctx):
@@ -143,10 +143,8 @@
             state = attend_block(state, q_part, key_piece[whole:], value_piece[whole:], key_rows[whole:])
         return state
 
-    outer = lax.axis_size("c0")
-    inner = lax.axis_size(INNER)
     rows_each = out_weight.shape[0]
-    weight_rows = lax.all_gather(out_weight, "c0", axis=0, tiled=True)
+    weight_rows = lax.all_gather(out_weight, OUTER, axis=0, tiled=True)
     half = kv_local // 2
     splits = [(0, half, ("c0", "c2", "c1")), (half, kv_local, ("c0", "c1", "c2"))]
     gathered, bounds = [], []
@@ -170,13 +168,16 @@
     attended = (numerator / denominator[..., None]).astype(jnp.bfloat16)
     attended = attended.transpose(2, 0, 1, 3).reshape(tok_dev, kv_local * group_repeat * HEAD_WIDTH)
     all_heads = ring_all_gather(attended, "head").transpose(1, 0, 2).reshape(tok_dev, -1)
-    weight_rows = weight_rows.reshape(outer * rows_each, out_weight.shape[1])
-    blocks = all_heads.reshape(tok_dev, outer, inner, rows_each).transpose(2, 0, 1, 3)
-    regrouped = permute_all_to_all(blocks, INNER)
+    n0 = lax.axis_size("c0")
+    n1 = lax.axis_size("c1")
+    n2 = lax.axis_size("c2")
+    weight_rows = weight_rows.reshape(n0 * n2 * rows_each, out_weight.shape[1])
+    blocks = all_heads.reshape(tok_dev, n0, n1, n2, rows_each).transpose(2, 0, 1, 3, 4)
+    regrouped = permute_all_to_all(blocks, "c1")
     partial = jnp.dot(
-        regrouped.reshape(inner * tok_dev, outer * rows_each), weight_rows, preferred_element_type=jnp.float32
+        regrouped.reshape(n1 * tok_dev, n0 * n2 * rows_each), weight_rows, preferred_element_type=jnp.float32
     )
-    mixed = lax.psum_scatter(partial, INNER, scatter_dimension=0, tiled=True)
+    mixed = lax.psum_scatter(partial, "c1", scatter_dimension=0, tiled=True)
     squares = lax.psum(jnp.sum(mixed * mixed, axis=1), "head")
     normed = mixed / jnp.sqrt(squares / D + 1e-06)[:, None]
     out32 = hidden_in.astype(jnp.float32) + normed * out_gain[None, :]

time: 326 us -> 347 us (1.064)
  waiting for transfers between devices: 199 us -> 225 us
  starting transfers between devices: 40.7 us -> 33.6 us
    ppermute x11, waiting for transfers between devices: 102 us -> 153 us  [ring_gather(): lax.ppermute(pieces[-1], axis, [(k, (k + 1) % n) for k in range(n)])]
    reduce_scatter x1, waiting for transfers between devices: 74.6 us -> 38 us  [shards(): mixed = lax.psum_scatter(partial, 'c1', scatter_dimension=0, tiled=True)]
    all_gather x1, waiting for transfers between devices: 0.01 us -> 10.8 us  [shards(): weight_rows = lax.all_gather(out_weight, OUTER, axis=0, tiled=True)]
    ppermute x11, starting transfers between devices: 30.1 us -> 26.3 us  [ring_gather(): lax.ppermute(pieces[-1], axis, [(k, (k + 1) % n) for k in range(n)])]
    ppermute x3 -> x1, waiting for transfers between devices: 12.2 us -> 12.3 us  [permute_all_to_all(): lax.ppermute(sent, axes, [(k, (k + shift) % n) for k in range(n)])]
  transfers between devices with their start and end apart: 21 -> 19, of which waited for: 18 -> 18; matrix products, arithmetic and copies ran while one was open for 9% -> 8% of each run, Pallas kernels for 0% -> 0%
where the time goes in v8:
time: 347 us
  waiting for transfers between devices  225 us (65%)
  starting transfers between devices  33.6 us (10%)
  local copies, waits for them, and re-layouts  26.6 us (8%)
  other arithmetic  22 us (6%)
  matrix products  20.8 us (6%)
  between operations  15.6 us (4%)
    ppermute x11, waiting for transfers between devices, ring_gather(): lax.ppermute(pieces[-1], axis, [(k, (k + 1) % n) for k in range(n)])  153 us
    reduce_scatter x1, waiting for transfers between devices, shards(): mixed = lax.psum_scatter(partial, 'c1', scatter_dimension=0, tiled=True)  38 us
    ppermute x11, starting transfers between devices, ring_gather(): lax.ppermute(pieces[-1], axis, [(k, (k + 1) % n) for k in range(n)])  26.3 us
    reshape x2, local copies, waits for them, and re-layouts, shards(): gathered.append((got.reshape(n_ctx * tok_dev, -1), key_rows))  13.1 us
    another operation x9, other arithmetic, ring_gather(): return jnp.stack(pieces)  12.3 us
    ppermute x1, waiting for transfers between devices, permute_all_to_all(): lax.ppermute(sent, axes, [(k, (k + shift) % n) for k in range(n)])  12.3 us
    all_gather x1, waiting for transfers between devices, shards(): weight_rows = lax.all_gather(out_weight, OUTER, axis=0, tiled=True)  10.8 us
    ppermute x5, waiting for transfers between devices, butterfly_sum(): x = x + lax.ppermute(x, axis, [(i, i ^ bit) for i in range(size)])  10.6 us
  transfers between devices with their start and end apart: 19, of which 18 were waited for; matrix products, arithmetic and copies ran while one was open for 8% of the time, Pallas kernels for 0%

profile of v8, /device:TPU:0, one launch (start us, length us, event | category | flops | bytes accessed | tf_op | source)
XLA Modules:
  0.0 346.5 jit_solution(9241056519685333760)
XLA Ops:
  13.9 7.5 %collective-permute-done.5 = bf16[128,1024]{1,0:T(8,128)(2,1)S(1)} collective-permute-done((bf16[128,1024]{1,0:T(8,128)(2,1)S(1)}, bf16[128,1024]{1,0:T(8,128)(2,1)S(1)}, u32[]{:S(2)}, u32[]{:S(2)}) %collective-permute-start.5) | collective-permute-done | bytes 262176 | tf_op jit(solution)/shard_map/ppermute | solution.py:34
  21.4 6.0 %collective-permute-done = bf16[128,1024]{1,0:T(8,128)(2,1)S(1)} collective-permute-done((bf16[128,1024]{1,0:T(8,128)(2,1)S(1)}, bf16[128,1024]{1,0:T(8,128)(2,1)S(1)}, u32[]{:S(2)}, u32[]{:S(2)}) %collective-permute-start) | collective-permute-done | bytes 262176 | tf_op jit(solution)/shard_map/ppermute | solution.py:34
  29.3 9.3 %collective-permute-done.6 = bf16[128,1024]{1,0:T(8,128)(2,1)S(1)} collective-permute-done((bf16[128,1024]{1,0:T(8,128)(2,1)S(1)}, bf16[128,1024]{1,0:T(8,128)(2,1)S(1)}, u32[]{:S(2)}, u32[]{:S(2)}) %collective-permute-start.6) | collective-permute-done | bytes 262176 | tf_op jit(solution)/shard_map/ppermute | solution.py:34
  38.7 4.6 %collective-permute-start.7 = (bf16[128,1024]{1,0:T(8,128)(2,1)S(1)}, bf16[128,1024]{1,0:T(8,128)(2,1)S(1)}, u32[]{:S(2)}, u32[]{:S(2)}) collective-permute-start(bf16[128,1024]{1,0:T(8,128)(2,1)S(1)} %collective-permute-done.6), channel_id=1, source_target_pairs={{0,8},{8,16},{16,24},{24,0},{1,9},{9,17},{17,25},{25,1},{2,10},{10... | collective-permute-start | bytes 786440 | tf_op jit(solution)/shard_map/ppermute | solution.py:34
  43.3 6.6 %collective-permute-done.1 = bf16[128,1024]{1,0:T(8,128)(2,1)S(1)} collective-permute-done((bf16[128,1024]{1,0:T(8,128)(2,1)S(1)}, bf16[128,1024]{1,0:T(8,128)(2,1)S(1)}, u32[]{:S(2)}, u32[]{:S(2)}) %collective-permute-start.1) | collective-permute-done | bytes 262176 | tf_op jit(solution)/shard_map/ppermute | solution.py:34
  49.9 9.3 %collective-permute-start.2 = (bf16[128,1024]{1,0:T(8,128)(2,1)S(1)}, bf16[128,1024]{1,0:T(8,128)(2,1)S(1)}, u32[]{:S(2)}, u32[]{:S(2)}) collective-permute-start(bf16[128,1024]{1,0:T(8,128)(2,1)S(1)} %collective-permute-done.1), channel_id=1, source_target_pairs={{0,8},{8,16},{16,24},{24,0},{1,9},{9,17},{17,25},{25,1},{2,10},{10... | collective-permute-start | bytes 786440 | tf_op jit(solution)/shard_map/ppermute | solution.py:34
  63.5 14.6 %collective-permute-done.2 = bf16[128,1024]{1,0:T(8,128)(2,1)S(1)} collective-permute-done((bf16[128,1024]{1,0:T(8,128)(2,1)S(1)}, bf16[128,1024]{1,0:T(8,128)(2,1)S(1)}, u32[]{:S(2)}, u32[]{:S(2)}) %collective-permute-start.2) | collective-permute-done | bytes 262176 | tf_op jit(solution)/shard_map/ppermute | solution.py:34
  85.4 30.8 %collective-permute-done.3 = bf16[4,128,1024]{2,1,0:T(8,128)(2,1)S(1)} collective-permute-done((bf16[4,128,1024]{2,1,0:T(8,128)(2,1)S(1)}, bf16[4,128,1024]{2,1,0:T(8,128)(2,1)S(1)}, u32[]{:S(2)}, u32[]{:S(2)}) %collective-permute-start.3) | collective-permute-done | bytes 1048608 | tf_op jit(solution)/shard_map/ppermute | solution.py:34
  121.1 70.8 %collective-permute-done.9 = bf16[2,4,128,1024]{3,2,1,0:T(8,128)(2,1)} collective-permute-done((bf16[2,4,128,1024]{3,2,1,0:T(8,128)(2,1)}, bf16[2,4,128,1024]{3,2,1,0:T(8,128)(2,1)}, u32[]{:S(2)}, u32[]{:S(2)}) %collective-permute-start.9) | collective-permute-done | bytes 2097184 | tf_op jit(solution)/shard_map/ppermute | solution.py:34
  191.9 3.9 %pad_maximum_fusion.1 = bf16[2,2,4,128,1024]{4,3,2,1,0:T(8,128)(2,1)} fusion(bf16[1,2,4,128,1024]{4,3,2,1,0:T(8,128)(2,1)} %bitcast.28, bf16[1,2,4,128,1024]{4,3,2,1,0:T(8,128)(2,1)S(1)} %get-tuple-element.86), kind=kLoop, calls=%fused_computation.21 | loop fusion | flops 2097152 | bytes 8388608 | tf_op jit(solution)/shard_map/stack | solution.py:35
  195.8 6.6 %copy.90 = bf16[2048,1024]{0,1:T(8,128)(2,1)} copy(bf16[2048,1024]{1,0:T(8,128)(2,1)} %bitcast.82) | data formatting | bytes 8388608 | tf_op jit(solution)/shard_map/reshape | solution.py:157
  202.5 4.0 %pad_maximum_fusion = bf16[2,2,4,128,1024]{4,3,2,1,0:T(8,128)(2,1)} fusion(bf16[1,2,4,128,1024]{4,3,2,1,0:T(8,128)(2,1)} %bitcast.18, bf16[1,2,4,128,1024]{4,3,2,1,0:T(8,128)(2,1)S(1)} %copy-done), kind=kLoop, calls=%fused_computation.20 | loop fusion | flops 2097152 | bytes 8388608 | tf_op jit(solution)/shard_map/stack | solution.py:35
  206.4 6.5 %copy.89 = bf16[2048,1024]{0,1:T(8,128)(2,1)} copy(bf16[2048,1024]{1,0:T(8,128)(2,1)} %bitcast.83) | data formatting | bytes 8388608 | tf_op jit(solution)/shard_map/reshape | solution.py:157
  212.9 10.8 %all-gather.2.cloned.1.call-done = bf16[2048,2304]{1,0:T(8,128)(2,1)} async-done(((bf16[256,2304]{1,0:T(8,128)(2,1)}), bf16[2048,2304]{1,0:T(8,128)(2,1)}) %all-gather.2.cloned.1.call-update) | async-done | bytes 9437200 | tf_op jit(solution)/shard_map/all_gather | solution.py:147
  228.3 10.7 %conditional.2 = (f32[4,2,128]{2,1,0:T(2,128)S(1)}, f32[4,2,128,128]{2,3,1,0:T(8,128)S(1)}) conditional(s32[]{:T(128)} %convert_element_type.37, () %tuple.26, (pred[128,2048]{0,1:T(8,128)(4,1)}, bf16[2048,1024]{0,1:T(8,128)(2,1)}, bf16[128,8,2,128]{0,3,2,1:T(8,128)(2,1)S(1)}) %tuple.74), branch_computations={%region_4.5_spmd, %region_5.7_spmd} | conditional | flops 1090518016 | bytes 41160776 | solution.py:120
  228.3 4.0 %fusion.51 = (bf16[2048,512]{0,1:T(8,128)(2,1)}, bf16[2048,512]{0,1:T(8,128)(2,1)S(1)}) fusion(bf16[2048,1024]{0,1:T(8,128)(2,1)} %get-tuple-element.21), kind=kLoop, calls=%fused_computation.127 | loop fusion | bytes 8388608 | tf_op jit(solution)/shard_map/slice | solution.py:163
  232.6 3.8 %fusion = (f32[4,2,128]{2,1,0:T(2,128)S(1)}, f32[4,2048,128,2]{2,1,3,0:T(8,128)S(1)}) fusion(pred[128,2048]{0,1:T(8,128)(4,1)} %get-tuple-element.20, bf16[2048,4,128,1]{0,2,3,1:T(8,128)(2,1)S(1)} %bitcast.92, bf16[128,8,2,128]{3,0,2,1:T(8,128)(2,1)S(1)} %copy.68), kind=kOutput, calls=%fused_computation.1 | convolution fusion | flops 545258496 | bytes 11014144 | tf_op jit(solution)/shard_map/cond/branch_1_fun/qgrd,kgd->grqk/dot_general | solution.py:101
  239.0 12.1 %conditional.3 = (f32[4,2,128]{2,1,0:T(2,128)S(1)}, f32[4,2,128,128]{2,3,1,0:T(8,128)S(1)}) conditional(s32[]{:T(128)} %convert_element_type.39, () %tuple.28, (pred[128,2048]{0,1:T(8,128)(4,1)S(1)}, bf16[2048,1024]{0,1:T(8,128)(2,1)}, bf16[128,8,2,128]{0,3,2,1:T(8,128)(2,1)S(1)}) %tuple.75), branch_computations={%region_9.10_spmd, %region_10.12_spmd} | conditional | flops 1090518016 | bytes 40112172 | solution.py:120
  239.2 4.8 %fusion.52 = (bf16[2048,512]{0,1:T(8,128)(2,1)}, bf16[2048,512]{0,1:T(8,128)(2,1)}) fusion(bf16[2048,1024]{0,1:T(8,128)(2,1)} %get-tuple-element.24), kind=kLoop, calls=%fused_computation.128 | loop fusion | bytes 8388608 | tf_op jit(solution)/shard_map/slice | solution.py:163
  244.2 4.3 %fusion.10 = (f32[4,2,128]{2,1,0:T(2,128)S(1)}, f32[4,2048,128,2]{2,1,3,0:T(8,128)S(1)}) fusion(pred[128,2048]{0,1:T(8,128)(4,1)S(1)} %get-tuple-element.23, bf16[2048,4,128,1]{0,2,3,1:T(8,128)(2,1)} %bitcast.93, bf16[128,8,2,128]{3,0,2,1:T(8,128)(2,1)S(1)} %copy.69), kind=kOutput, calls=%fused_computation.11 | convolution fusion | flops 545258496 | bytes 11014144 | tf_op jit(solution)/shard_map/cond/branch_1_fun/qgrd,kgd->grqk/dot_general | solution.py:101
  255.9 12.3 %collective-permute-done.11 = bf16[128,4,2,256]{3,0,2,1:T(8,128)(2,1)S(1)} collective-permute-done((bf16[128,4,2,256]{3,0,2,1:T(8,128)(2,1)S(1)}, bf16[128,4,2,256]{3,0,2,1:T(8,128)(2,1)S(1)}, u32[]{:S(2)}, u32[]{:S(2)}) %collective-permute-start.11) | collective-permute-done | bytes 524320 | tf_op jit(solution)/shard_map/ppermute | solution.py:61
  270.8 7.7 %fusion.55 = f32[256,2304]{1,0:T(8,128)} fusion(bf16[256,2048]{1,0:T(8,128)(2,1)S(1)} %reshape.304, bf16[2048,2304]{1,0:T(8,128)(2,1)} %all-gather.2.cloned.1.call-done), kind=kOutput, calls=%fused_computation.131 | convolution fusion | flops 2415919104 | bytes 12845056 | tf_op jit(solution)/shard_map/dot_general | solution.py:177
  278.5 38.0 %reduce-scatter.2.cloned.1.call-done = f32[128,2304]{1,0:T(8,128)} async-done(((f32[256,2304]{1,0:T(8,128)}), f32[128,2304]{1,0:T(8,128)}) %reduce-scatter.2.cloned.1.call-update) | async-done | bytes 1179664 | tf_op jit(solution)/shard_map/reduce_scatter | solution.py:180
  331.3 3.2 collective-permute-done.14
  (96 shorter events, 61.3 us)
Async XLA Ops:
  7.2 216.5 %all-gather.2.cloned.1.call-start = ((), (), s32[]{:S(2)}) async-start(), calls=%async_computation.1 | async-start | bytes 10616832 | tf_op jit(solution)/shard_map/all_gather | solution.py:147
  7.9 308.6 %reduce-scatter.2.cloned.1.call-start = ((), (), s32[]{:S(2)}) async-start(), calls=%async_computation.2 | async-start | bytes 3538944 | tf_op jit(solution)/shard_map/reduce_scatter | solution.py:180
  9.1 12.2 %collective-permute-start.5 = (bf16[128,1024]{1,0:T(8,128)(2,1)S(1)}, bf16[128,1024]{1,0:T(8,128)(2,1)S(1)}, u32[]{:S(2)}, u32[]{:S(2)}) collective-permute-start(bf16[128,1024]{1,0:T(8,128)(2,1)S(1)} %get-tuple-element.99), channel_id=1, source_target_pairs={{0,8},{8,16},{16,24},{24,0},{1,9},{9,17},{17,25},{25,1},{2,10},{10... | collective-permute-start | bytes 786440 | tf_op jit(solution)/shard_map/ppermute | solution.py:34
  12.2 15.2 %collective-permute-start = (bf16[128,1024]{1,0:T(8,128)(2,1)S(1)}, bf16[128,1024]{1,0:T(8,128)(2,1)S(1)}, u32[]{:S(2)}, u32[]{:S(2)}) collective-permute-start(bf16[128,1024]{1,0:T(8,128)(2,1)S(1)} %get-tuple-element.105), channel_id=1, source_target_pairs={{0,8},{8,16},{16,24},{24,0},{1,9},{9,17},{17,25},{25,1},{2,10},{10... | collective-permute-start | bytes 786440 | tf_op jit(solution)/shard_map/ppermute | solution.py:34
  21.4 17.3 %collective-permute-start.6 = (bf16[128,1024]{1,0:T(8,128)(2,1)S(1)}, bf16[128,1024]{1,0:T(8,128)(2,1)S(1)}, u32[]{:S(2)}, u32[]{:S(2)}) collective-permute-start(bf16[128,1024]{1,0:T(8,128)(2,1)S(1)} %collective-permute-done.5), channel_id=1, source_target_pairs={{0,8},{8,16},{16,24},{24,0},{1,9},{9,17},{17,25},{25,1},{2,10},{10... | collective-permute-start | bytes 786440 | tf_op jit(solution)/shard_map/ppermute | solution.py:34
  27.4 22.5 %collective-permute-start.1 = (bf16[128,1024]{1,0:T(8,128)(2,1)S(1)}, bf16[128,1024]{1,0:T(8,128)(2,1)S(1)}, u32[]{:S(2)}, u32[]{:S(2)}) collective-permute-start(bf16[128,1024]{1,0:T(8,128)(2,1)S(1)} %collective-permute-done), channel_id=1, source_target_pairs={{0,8},{8,16},{16,24},{24,0},{1,9},{9,17},{17,25},{25,1},{2,10},{10... | collective-permute-start | bytes 786440 | tf_op jit(solution)/shard_map/ppermute | solution.py:34
  38.7 23.2 %collective-permute-start.7 = (bf16[128,1024]{1,0:T(8,128)(2,1)S(1)}, bf16[128,1024]{1,0:T(8,128)(2,1)S(1)}, u32[]{:S(2)}, u32[]{:S(2)}) collective-permute-start(bf16[128,1024]{1,0:T(8,128)(2,1)S(1)} %collective-permute-done.6), channel_id=1, source_target_pairs={{0,8},{8,16},{16,24},{24,0},{1,9},{9,17},{17,25},{25,1},{2,10},{10... | collective-permute-start | bytes 786440 | tf_op jit(solution)/shard_map/ppermute | solution.py:34
  49.9 28.2 %collective-permute-start.2 = (bf16[128,1024]{1,0:T(8,128)(2,1)S(1)}, bf16[128,1024]{1,0:T(8,128)(2,1)S(1)}, u32[]{:S(2)}, u32[]{:S(2)}) collective-permute-start(bf16[128,1024]{1,0:T(8,128)(2,1)S(1)} %collective-permute-done.1), channel_id=1, source_target_pairs={{0,8},{8,16},{16,24},{24,0},{1,9},{9,17},{17,25},{25,1},{2,10},{10... | collective-permute-start | bytes 786440 | tf_op jit(solution)/shard_map/ppermute | solution.py:34
  62.0 20.4 %collective-permute-start.8 = (bf16[4,128,1024]{2,1,0:T(8,128)(2,1)S(1)}, bf16[4,128,1024]{2,1,0:T(8,128)(2,1)S(1)}, u32[]{:S(2)}, u32[]{:S(2)}) collective-permute-start(bf16[4,128,1024]{2,1,0:T(8,128)(2,1)S(1)} %get-tuple-element.95), channel_id=1, source_target_pairs={{0,4},{4,0},{1,5},{5,1},{2,6},{6,2},{3,7},{7,3},{8,12},{12,8},{9,1... | collective-permute-start | bytes 3145736 | tf_op jit(solution)/shard_map/ppermute | solution.py:34
  78.3 37.9 %collective-permute-start.3 = (bf16[4,128,1024]{2,1,0:T(8,128)(2,1)S(1)}, bf16[4,128,1024]{2,1,0:T(8,128)(2,1)S(1)}, u32[]{:S(2)}, u32[]{:S(2)}) collective-permute-start(bf16[4,128,1024]{2,1,0:T(8,128)(2,1)S(1)} %get-tuple-element.97), channel_id=1, source_target_pairs={{0,2},{2,0},{1,3},{3,1},{4,6},{6,4},{5,7},{7,5},{8,10},{10,8},{9,1... | collective-permute-start | bytes 3145736 | tf_op jit(solution)/shard_map/ppermute | solution.py:34
  84.1 107.8 %collective-permute-start.9 = (bf16[2,4,128,1024]{3,2,1,0:T(8,128)(2,1)}, bf16[2,4,128,1024]{3,2,1,0:T(8,128)(2,1)}, u32[]{:S(2)}, u32[]{:S(2)}) collective-permute-start(bf16[2,4,128,1024]{3,2,1,0:T(8,128)(2,1)} %get-tuple-element.87), channel_id=1, source_target_pairs={{0,2},{2,0},{1,3},{3,1},{4,6},{6,4},{5,7},{7,5},{8,10},{10,8},{9,1... | collective-permute-start | bytes 6291464 | tf_op jit(solution)/shard_map/ppermute | solution.py:34
  116.2 4.4 %copy-start.4 = (bf16[128,2048]{1,0:T(8,128)(2,1)S(1)}, bf16[128,2048]{1,0:T(8,128)(2,1)}, u32[]{:S(2)}) copy-start(bf16[128,2048]{1,0:T(8,128)(2,1)} %param.12) | copy-start | bytes 1572868
  118.4 84.1 %collective-permute-start.4 = (bf16[2,4,128,1024]{3,2,1,0:T(8,128)(2,1)}, bf16[2,4,128,1024]{3,2,1,0:T(8,128)(2,1)}, u32[]{:S(2)}, u32[]{:S(2)}) collective-permute-start(bf16[2,4,128,1024]{3,2,1,0:T(8,128)(2,1)} %get-tuple-element.89), channel_id=1, source_target_pairs={{0,4},{4,0},{1,5},{5,1},{2,6},{6,2},{3,7},{7,3},{8,12},{12,8},{9,1... | collective-permute-start | bytes 6291464 | tf_op jit(solution)/shard_map/ppermute | solution.py:34
  195.8 6.6 %copy-start = (bf16[1,2,4,128,1024]{4,3,2,1,0:T(8,128)(2,1)S(1)}, bf16[1,2,4,128,1024]{4,3,2,1,0:T(8,128)(2,1)}, u32[]{:S(2)}) copy-start(bf16[1,2,4,128,1024]{4,3,2,1,0:T(8,128)(2,1)} %get-tuple-element.88) | copy-start | bytes 6291460
  251.2 2.0 collective-permute-start.10
  254.1 14.0 %collective-permute-start.11 = (bf16[128,4,2,256]{3,0,2,1:T(8,128)(2,1)S(1)}, bf16[128,4,2,256]{3,0,2,1:T(8,128)(2,1)S(1)}, u32[]{:S(2)}, u32[]{:S(2)}) collective-permute-start(bf16[128,4,2,256]{3,0,2,1:T(8,128)(2,1)S(1)} %bitcast.97), channel_id=1, source_target_pairs={{0,4},{4,0},{1,5},{5,1},{2,6},{6,2},{3,7},{7,3},{8,12},{12,8},{9,1... | collective-permute-start | bytes 1572872 | tf_op jit(solution)/shard_map/ppermute | solution.py:61
  278.4 41.9 %copy-start.3 = (bf16[128,2304]{1,0:T(8,128)(2,1)S(1)}, bf16[128,2304]{1,0:T(8,128)(2,1)}, u32[]{:S(2)}) copy-start(bf16[128,2304]{1,0:T(8,128)(2,1)} %param.15) | copy-start | bytes 1769476
  278.4 41.9 %copy-start.6 = (f32[2304]{0:T(1024)S(1)}, f32[2304]{0:T(1024)}, u32[]{:S(2)}) copy-start(f32[2304]{0:T(1024)} %param.18) | copy-start | bytes 27652
  278.4 41.9 %copy-start.7 = (f32[2304]{0:T(1024)S(1)}, f32[2304]{0:T(1024)}, u32[]{:S(2)}) copy-start(f32[2304]{0:T(1024)} %param.17) | copy-start | bytes 27652
  322.9 3.6 %collective-permute-start.12 = (f32[16]{0:T(128)S(1)}, f32[16]{0:T(128)S(1)}, u32[]{:S(2)}, u32[]{:S(2)}) collective-permute-start(f32[16]{0:T(128)S(1)} %select_reduce_fusion), channel_id=1, source_target_pairs={{0,8},{8,0},{16,24},{24,16},{1,9},{9,1},{17,25},{25,17},{2,10},{10... | collective-permute-start | bytes 200 | tf_op jit(solution)/shard_map/ppermute | solution.py:70
  326.5 4.4 %collective-permute-start.13 = (f32[16]{0:T(128)S(1)}, f32[16]{0:T(128)S(1)}, u32[]{:S(2)}, u32[]{:S(2)}) collective-permute-start(f32[16]{0:T(128)S(1)} %add.327), channel_id=1, source_target_pairs={{0,16},{8,24},{16,0},{24,8},{1,17},{9,25},{17,1},{25,9},{2,18},{10... | collective-permute-start | bytes 200 | tf_op jit(solution)/shard_map/ppermute | solution.py:70
  331.0 3.5 %collective-permute-start.14 = (f32[16]{0:T(128)S(1)}, f32[16]{0:T(128)S(1)}, u32[]{:S(2)}, u32[]{:S(2)}) collective-permute-start(f32[16]{0:T(128)S(1)} %add.328), channel_id=1, source_target_pairs={{0,4},{4,0},{1,5},{5,1},{2,6},{6,2},{3,7},{7,3},{8,12},{12,8},{9,1... | collective-permute-start | bytes 200 | tf_op jit(solution)/shard_map/ppermute | solution.py:70
  334.5 3.5 %collective-permute-start.15 = (f32[16]{0:T(128)S(1)}, f32[16]{0:T(128)S(1)}, u32[]{:S(2)}, u32[]{:S(2)}) collective-permute-start(f32[16]{0:T(128)S(1)} %add.329), channel_id=1, source_target_pairs={{0,2},{2,0},{1,3},{3,1},{4,6},{6,4},{5,7},{7,5},{8,10},{10,8},{9,1... | collective-permute-start | bytes 200 | tf_op jit(solution)/shard_map/ppermute | solution.py:70
  338.1 1.1 collective-permute-start.16
  (4 other events, 16.1 us)
Sparse Core Ops, SparseCore 0:
  10.2 213.4 all-gather.1
  278.6 37.8 reduce-scatter.1

commit v9 on v6

--- a/solution.py
+++ b/solution.py
@@ -60,6 +60,16 @@
         sent = lax.dynamic_index_in_dim(x, (own + shift) % n, axis=0, keepdims=False)
         pieces.append(lax.ppermute(sent, axes, [(k, (k + shift) % n) for k in range(n)]))
     return jnp.roll(jnp.stack(pieces[::-1]), own + 1, axis=0)
+
+
+def permute_reduce_scatter(x, axes):
+    n = lax.axis_size(axes)
+    own = lax.axis_index(axes)
+    total = lax.dynamic_index_in_dim(x, own, axis=0, keepdims=False)
+    for shift in range(1, n):
+        sent = lax.dynamic_index_in_dim(x, (own + shift) % n, axis=0, keepdims=False)
+        total = total + lax.ppermute(sent, axes, [(k, (k + shift) % n) for k in range(n)])
+    return total
 
 
 def butterfly_sum(x, axes):
@@ -176,7 +186,7 @@
     partial = jnp.dot(
         regrouped.reshape(inner * tok_dev, outer * rows_each), weight_rows, preferred_element_type=jnp.float32
     )
-    mixed = lax.psum_scatter(partial, INNER, scatter_dimension=0, tiled=True)
+    mixed = permute_reduce_scatter(partial.reshape(inner, tok_dev, -1), INNER)
     squares = lax.psum(jnp.sum(mixed * mixed, axis=1), "head")
     normed = mixed / jnp.sqrt(squares / D + 1e-06)[:, None]
     out32 = hidden_in.astype(jnp.float32) + normed * out_gain[None, :]

time: 326 us -> 316 us (0.969)
  waiting for transfers between devices: 199 us -> 172 us
  starting transfers between devices: 40.7 us -> 62.5 us
    reduce_scatter x1 -> x0, waiting for transfers between devices: 74.6 us -> none  [shards(): mixed = lax.psum_scatter(partial, INNER, scatter_dimension=0, tiled=True)]
    ppermute x0 -> x3, waiting for transfers between devices: none -> 48.9 us  [permute_reduce_scatter(): lax.ppermute(sent, axes, [(k, (k + shift) % n) for k in range(n)])]
    ppermute x5, starting transfers between devices: 6.68 us -> 25.1 us  [butterfly_sum(): x = x + lax.ppermute(x, axis, [(i, i ^ bit) for i in range(size)])]
    ppermute x0 -> x3, starting transfers between devices: none -> 3.44 us  [permute_reduce_scatter(): lax.ppermute(sent, axes, [(k, (k + shift) % n) for k in range(n)])]
  transfers between devices with their start and end apart: 21 -> 23, of which waited for: 18 -> 19; matrix products, arithmetic and copies ran while one was open for 9% -> 9% of each run, Pallas kernels for 0% -> 0%
where the time goes in v9:
time: 316 us
  waiting for transfers between devices  172 us (54%)
  starting transfers between devices  62.5 us (20%)
  local copies, waits for them, and re-layouts  25.7 us (8%)
  other arithmetic  18.9 us (6%)
  matrix products  18.1 us (6%)
  between operations  15.7 us (5%)
    ppermute x11, waiting for transfers between devices, ring_gather(): lax.ppermute(pieces[-1], axis, [(k, (k + 1) % n) for k in range(n)])  102 us
    ppermute x3, waiting for transfers between devices, permute_reduce_scatter(): lax.ppermute(sent, axes, [(k, (k + shift) % n) for k in range(n)])  48.9 us
    ppermute x11, starting transfers between devices, ring_gather(): lax.ppermute(pieces[-1], axis, [(k, (k + 1) % n) for k in range(n)])  30.1 us
    ppermute x5, starting transfers between devices, butterfly_sum(): x = x + lax.ppermute(x, axis, [(i, i ^ bit) for i in range(size)])  25.1 us
    reshape x2, local copies, waits for them, and re-layouts, shards(): gathered.append((got.reshape(n_ctx * tok_dev, -1), key_rows))  13.2 us
    another operation x9, other arithmetic, ring_gather(): return jnp.stack(pieces)  12.3 us
    ppermute x3, waiting for transfers between devices, permute_all_to_all(): lax.ppermute(sent, axes, [(k, (k + shift) % n) for k in range(n)])  12.2 us
    slice x2, local copies, waits for them, and re-layouts, shards(): got[:, width:]  8.85 us
  transfers between devices with their start and end apart: 23, of which 19 were waited for; matrix products, arithmetic and copies ran while one was open for 9% of the time, Pallas kernels for 0%

profile of v9, /device:TPU:0, one launch (start us, length us, event | category | flops | bytes accessed | tf_op | source)
XLA Modules:
  0.0 315.6 jit_solution(10044658774386454223)
XLA Ops:
  13.8 7.5 %collective-permute-done.5 = bf16[128,1024]{1,0:T(8,128)(2,1)S(1)} collective-permute-done((bf16[128,1024]{1,0:T(8,128)(2,1)S(1)}, bf16[128,1024]{1,0:T(8,128)(2,1)S(1)}, u32[]{:S(2)}, u32[]{:S(2)}) %collective-permute-start.5) | collective-permute-done | bytes 262176 | tf_op jit(solution)/shard_map/ppermute | solution.py:34
  21.3 7.3 %collective-permute-done = bf16[128,1024]{1,0:T(8,128)(2,1)S(1)} collective-permute-done((bf16[128,1024]{1,0:T(8,128)(2,1)S(1)}, bf16[128,1024]{1,0:T(8,128)(2,1)S(1)}, u32[]{:S(2)}, u32[]{:S(2)}) %collective-permute-start) | collective-permute-done | bytes 262176 | tf_op jit(solution)/shard_map/ppermute | solution.py:34
  31.9 7.9 %collective-permute-done.6 = bf16[128,1024]{1,0:T(8,128)(2,1)S(1)} collective-permute-done((bf16[128,1024]{1,0:T(8,128)(2,1)S(1)}, bf16[128,1024]{1,0:T(8,128)(2,1)S(1)}, u32[]{:S(2)}, u32[]{:S(2)}) %collective-permute-start.6) | collective-permute-done | bytes 262176 | tf_op jit(solution)/shard_map/ppermute | solution.py:34
  39.8 6.5 %collective-permute-start.7 = (bf16[128,1024]{1,0:T(8,128)(2,1)S(1)}, bf16[128,1024]{1,0:T(8,128)(2,1)S(1)}, u32[]{:S(2)}, u32[]{:S(2)}) collective-permute-start(bf16[128,1024]{1,0:T(8,128)(2,1)S(1)} %collective-permute-done.6), channel_id=1, source_target_pairs={{0,8},{8,16},{16,24},{24,0},{1,9},{9,17},{17,25},{25,1},{2,10},{10... | collective-permute-start | bytes 786440 | tf_op jit(solution)/shard_map/ppermute | solution.py:34
  46.3 4.7 %collective-permute-done.1 = bf16[128,1024]{1,0:T(8,128)(2,1)S(1)} collective-permute-done((bf16[128,1024]{1,0:T(8,128)(2,1)S(1)}, bf16[128,1024]{1,0:T(8,128)(2,1)S(1)}, u32[]{:S(2)}, u32[]{:S(2)}) %collective-permute-start.1) | collective-permute-done | bytes 262176 | tf_op jit(solution)/shard_map/ppermute | solution.py:34
  51.0 9.7 %collective-permute-start.2 = (bf16[128,1024]{1,0:T(8,128)(2,1)S(1)}, bf16[128,1024]{1,0:T(8,128)(2,1)S(1)}, u32[]{:S(2)}, u32[]{:S(2)}) collective-permute-start(bf16[128,1024]{1,0:T(8,128)(2,1)S(1)} %collective-permute-done.1), channel_id=1, source_target_pairs={{0,8},{8,16},{16,24},{24,0},{1,9},{9,17},{17,25},{25,1},{2,10},{10... | collective-permute-start | bytes 786440 | tf_op jit(solution)/shard_map/ppermute | solution.py:34
  65.5 15.2 %collective-permute-done.2 = bf16[128,1024]{1,0:T(8,128)(2,1)S(1)} collective-permute-done((bf16[128,1024]{1,0:T(8,128)(2,1)S(1)}, bf16[128,1024]{1,0:T(8,128)(2,1)S(1)}, u32[]{:S(2)}, u32[]{:S(2)}) %collective-permute-start.2) | collective-permute-done | bytes 262176 | tf_op jit(solution)/shard_map/ppermute | solution.py:34
  86.0 21.0 %collective-permute-done.3 = bf16[4,128,1024]{2,1,0:T(8,128)(2,1)S(1)} collective-permute-done((bf16[4,128,1024]{2,1,0:T(8,128)(2,1)S(1)}, bf16[4,128,1024]{2,1,0:T(8,128)(2,1)S(1)}, u32[]{:S(2)}, u32[]{:S(2)}) %collective-permute-start.3) | collective-permute-done | bytes 1048608 | tf_op jit(solution)/shard_map/ppermute | solution.py:34
  112.0 32.5 %collective-permute-done.9 = bf16[2,4,128,1024]{3,2,1,0:T(8,128)(2,1)} collective-permute-done((bf16[2,4,128,1024]{3,2,1,0:T(8,128)(2,1)}, bf16[2,4,128,1024]{3,2,1,0:T(8,128)(2,1)}, u32[]{:S(2)}, u32[]{:S(2)}) %collective-permute-start.9) | collective-permute-done | bytes 2097184 | tf_op jit(solution)/shard_map/ppermute | solution.py:34
  144.5 4.0 %pad_maximum_fusion.1 = bf16[2,2,4,128,1024]{4,3,2,1,0:T(8,128)(2,1)} fusion(bf16[1,2,4,128,1024]{4,3,2,1,0:T(8,128)(2,1)} %bitcast.28, bf16[1,2,4,128,1024]{4,3,2,1,0:T(8,128)(2,1)S(1)} %get-tuple-element.85), kind=kLoop, calls=%fused_computation.23 | loop fusion | flops 2097152 | bytes 8388608 | tf_op jit(solution)/shard_map/stack | solution.py:35
  148.5 6.7 %copy.80 = bf16[2048,1024]{0,1:T(8,128)(2,1)} copy(bf16[2048,1024]{1,0:T(8,128)(2,1)} %bitcast.112) | data formatting | bytes 8388608 | tf_op jit(solution)/shard_map/reshape | solution.py:169
  159.1 6.5 %copy.79 = bf16[2048,1024]{0,1:T(8,128)(2,1)} copy(bf16[2048,1024]{1,0:T(8,128)(2,1)} %bitcast.113) | data formatting | bytes 8388608 | tf_op jit(solution)/shard_map/reshape | solution.py:169
  170.2 10.7 %conditional.2 = (f32[4,2,128]{2,1,0:T(2,128)S(1)}, f32[4,2,128,128]{2,3,1,0:T(8,128)S(1)}) conditional(s32[]{:T(128)} %convert_element_type.37, () %tuple.26, (pred[128,2048]{0,1:T(8,128)(4,1)}, bf16[2048,1024]{0,1:T(8,128)(2,1)}, bf16[128,8,2,128]{0,3,2,1:T(8,128)(2,1)S(1)}) %tuple.75), branch_computations={%region_4.5_spmd, %region_5.7_spmd} | conditional | flops 1090518016 | bytes 41160776 | solution.py:130
  170.2 4.0 %fusion.53 = (bf16[2048,512]{0,1:T(8,128)(2,1)}, bf16[2048,512]{0,1:T(8,128)(2,1)S(1)}) fusion(bf16[2048,1024]{0,1:T(8,128)(2,1)} %get-tuple-element.21), kind=kLoop, calls=%fused_computation.139 | loop fusion | bytes 8388608 | tf_op jit(solution)/shard_map/slice | solution.py:175
  180.9 12.2 %conditional.3 = (f32[4,2,128]{2,1,0:T(2,128)S(1)}, f32[4,2,128,128]{2,3,1,0:T(8,128)S(1)}) conditional(s32[]{:T(128)} %convert_element_type.39, () %tuple.28, (pred[128,2048]{0,1:T(8,128)(4,1)S(1)}, bf16[2048,1024]{0,1:T(8,128)(2,1)}, bf16[128,8,2,128]{0,3,2,1:T(8,128)(2,1)S(1)}) %tuple.76), branch_computations={%region_9.10_spmd, %region_10.12_spmd} | conditional | flops 1090518016 | bytes 40112172 | solution.py:130
  181.1 4.9 %fusion.54 = (bf16[2048,512]{0,1:T(8,128)(2,1)}, bf16[2048,512]{0,1:T(8,128)(2,1)}) fusion(bf16[2048,1024]{0,1:T(8,128)(2,1)} %get-tuple-element.24), kind=kLoop, calls=%fused_computation.140 | loop fusion | bytes 8388608 | tf_op jit(solution)/shard_map/slice | solution.py:175
  186.2 4.3 %fusion.10 = (f32[4,2,128]{2,1,0:T(2,128)S(1)}, f32[4,2048,128,2]{2,1,3,0:T(8,128)S(1)}) fusion(pred[128,2048]{0,1:T(8,128)(4,1)S(1)} %get-tuple-element.23, bf16[2048,4,128,1]{0,2,3,1:T(8,128)(2,1)} %bitcast.122, bf16[128,8,2,128]{3,0,2,1:T(8,128)(2,1)S(1)} %copy.57), kind=kOutput, calls=%fused_computation.11 | convolution fusion | flops 545258496 | bytes 11014144 | tf_op jit(solution)/shard_map/cond/branch_1_fun/qgrd,kgd->grqk/dot_general | solution.py:111
  200.3 5.1 %collective-permute-done.11 = bf16[128,4,256]{2,0,1:T(8,128)(2,1)S(1)} collective-permute-done((bf16[128,4,256]{2,0,1:T(8,128)(2,1)S(1)}, bf16[128,4,256]{2,0,1:T(8,128)(2,1)S(1)}, u32[]{:S(2)}, u32[]{:S(2)}) %collective-permute-start.11) | collective-permute-done | bytes 262176 | tf_op jit(solution)/shard_map/ppermute | solution.py:61
  205.4 7.2 %collective-permute-done.12 = bf16[128,4,256]{2,0,1:T(8,128)(2,1)S(1)} collective-permute-done((bf16[128,4,256]{2,0,1:T(8,128)(2,1)S(1)}, bf16[128,4,256]{2,0,1:T(8,128)(2,1)S(1)}, u32[]{:S(2)}, u32[]{:S(2)}) %collective-permute-start.12) | collective-permute-done | bytes 262176 | tf_op jit(solution)/shard_map/ppermute | solution.py:61
  213.0 5.0 %fusion.20 = f32[4,128,2304]{2,1,0:T(8,128)S(1)} fusion(bf16[4,128,1024]{2,1,0:T(8,128)(2,1)S(1)} %bitcast.123, bf16[1024,2304]{1,0:T(8,128)(2,1)} %all-gather.2.cloned.1.call-done), kind=kOutput, calls=%fused_computation.20 | convolution fusion | flops 2415919104 | bytes 10485760 | tf_op jit(solution)/shard_map/dot_general | solution.py:186
  221.7 26.4 %collective-permute-done.14 = f32[128,2304]{1,0:T(8,128)S(1)} collective-permute-done((f32[128,2304]{1,0:T(8,128)S(1)}, f32[128,2304]{1,0:T(8,128)S(1)}, u32[]{:S(2)}, u32[]{:S(2)}) %collective-permute-start.14) | collective-permute-done | bytes 1179680 | tf_op jit(solution)/shard_map/ppermute | solution.py:71
  248.1 22.4 %collective-permute-done.15 = f32[128,2304]{1,0:T(8,128)S(1)} collective-permute-done((f32[128,2304]{1,0:T(8,128)S(1)}, f32[128,2304]{1,0:T(8,128)S(1)}, u32[]{:S(2)}, u32[]{:S(2)}) %collective-permute-start.15) | collective-permute-done | bytes 1179680 | tf_op jit(solution)/shard_map/ppermute | solution.py:71
  274.7 17.1 %collective-permute-start.17 = (f32[16]{0:T(128)S(1)}, f32[16]{0:T(128)S(1)}, u32[]{:S(2)}, u32[]{:S(2)}) collective-permute-start(f32[16]{0:T(128)S(1)} %select_reduce_fusion), channel_id=1, source_target_pairs={{0,8},{8,0},{16,24},{24,16},{1,9},{9,1},{17,25},{25,17},{2,10},{10... | collective-permute-start | bytes 200 | tf_op jit(solution)/shard_map/ppermute | solution.py:80
  293.3 5.1 %collective-permute-start.18 = (f32[16]{0:T(128)S(1)}, f32[16]{0:T(128)S(1)}, u32[]{:S(2)}, u32[]{:S(2)}) collective-permute-start(f32[16]{0:T(128)S(1)} %add.374), channel_id=1, source_target_pairs={{0,16},{8,24},{16,0},{24,8},{1,17},{9,25},{17,1},{25,9},{2,18},{10... | collective-permute-start | bytes 200 | tf_op jit(solution)/shard_map/ppermute | solution.py:80
  (113 shorter events, 68.7 us)
Async XLA Ops:
  7.2 158.4 %all-gather.2.cloned.1.call-start = ((), (), s32[]{:S(2)}) async-start(), calls=%async_computation | async-start | bytes 5898240 | tf_op jit(solution)/shard_map/all_gather | solution.py:159
  9.1 12.2 %collective-permute-start.5 = (bf16[128,1024]{1,0:T(8,128)(2,1)S(1)}, bf16[128,1024]{1,0:T(8,128)(2,1)S(1)}, u32[]{:S(2)}, u32[]{:S(2)}) collective-permute-start(bf16[128,1024]{1,0:T(8,128)(2,1)S(1)} %get-tuple-element.100), channel_id=1, source_target_pairs={{0,8},{8,16},{16,24},{24,0},{1,9},{9,17},{17,25},{25,1},{2,10},{10... | collective-permute-start | bytes 786440 | tf_op jit(solution)/shard_map/ppermute | solution.py:34
  12.2 16.4 %collective-permute-start = (bf16[128,1024]{1,0:T(8,128)(2,1)S(1)}, bf16[128,1024]{1,0:T(8,128)(2,1)S(1)}, u32[]{:S(2)}, u32[]{:S(2)}) collective-permute-start(bf16[128,1024]{1,0:T(8,128)(2,1)S(1)} %get-tuple-element.106), channel_id=1, source_target_pairs={{0,8},{8,16},{16,24},{24,0},{1,9},{9,17},{17,25},{25,1},{2,10},{10... | collective-permute-start | bytes 786440 | tf_op jit(solution)/shard_map/ppermute | solution.py:34
  21.3 18.5 %collective-permute-start.6 = (bf16[128,1024]{1,0:T(8,128)(2,1)S(1)}, bf16[128,1024]{1,0:T(8,128)(2,1)S(1)}, u32[]{:S(2)}, u32[]{:S(2)}) collective-permute-start(bf16[128,1024]{1,0:T(8,128)(2,1)S(1)} %collective-permute-done.5), channel_id=1, source_target_pairs={{0,8},{8,16},{16,24},{24,0},{1,9},{9,17},{17,25},{25,1},{2,10},{10... | collective-permute-start | bytes 786440 | tf_op jit(solution)/shard_map/ppermute | solution.py:34
  28.6 22.4 %collective-permute-start.1 = (bf16[128,1024]{1,0:T(8,128)(2,1)S(1)}, bf16[128,1024]{1,0:T(8,128)(2,1)S(1)}, u32[]{:S(2)}, u32[]{:S(2)}) collective-permute-start(bf16[128,1024]{1,0:T(8,128)(2,1)S(1)} %collective-permute-done), channel_id=1, source_target_pairs={{0,8},{8,16},{16,24},{24,0},{1,9},{9,17},{17,25},{25,1},{2,10},{10... | collective-permute-start | bytes 786440 | tf_op jit(solution)/shard_map/ppermute | solution.py:34
  39.8 24.0 %collective-permute-start.7 = (bf16[128,1024]{1,0:T(8,128)(2,1)S(1)}, bf16[128,1024]{1,0:T(8,128)(2,1)S(1)}, u32[]{:S(2)}, u32[]{:S(2)}) collective-permute-start(bf16[128,1024]{1,0:T(8,128)(2,1)S(1)} %collective-permute-done.6), channel_id=1, source_target_pairs={{0,8},{8,16},{16,24},{24,0},{1,9},{9,17},{17,25},{25,1},{2,10},{10... | collective-permute-start | bytes 786440 | tf_op jit(solution)/shard_map/ppermute | solution.py:34
  51.0 29.7 %collective-permute-start.2 = (bf16[128,1024]{1,0:T(8,128)(2,1)S(1)}, bf16[128,1024]{1,0:T(8,128)(2,1)S(1)}, u32[]{:S(2)}, u32[]{:S(2)}) collective-permute-start(bf16[128,1024]{1,0:T(8,128)(2,1)S(1)} %collective-permute-done.1), channel_id=1, source_target_pairs={{0,8},{8,16},{16,24},{24,0},{1,9},{9,17},{17,25},{25,1},{2,10},{10... | collective-permute-start | bytes 786440 | tf_op jit(solution)/shard_map/ppermute | solution.py:34
  63.9 19.3 %collective-permute-start.8 = (bf16[4,128,1024]{2,1,0:T(8,128)(2,1)S(1)}, bf16[4,128,1024]{2,1,0:T(8,128)(2,1)S(1)}, u32[]{:S(2)}, u32[]{:S(2)}) collective-permute-start(bf16[4,128,1024]{2,1,0:T(8,128)(2,1)S(1)} %get-tuple-element.96), channel_id=1, source_target_pairs={{0,4},{4,0},{1,5},{5,1},{2,6},{6,2},{3,7},{7,3},{8,12},{12,8},{9,1... | collective-permute-start | bytes 3145736 | tf_op jit(solution)/shard_map/ppermute | solution.py:34
  80.9 26.2 %collective-permute-start.3 = (bf16[4,128,1024]{2,1,0:T(8,128)(2,1)S(1)}, bf16[4,128,1024]{2,1,0:T(8,128)(2,1)S(1)}, u32[]{:S(2)}, u32[]{:S(2)}) collective-permute-start(bf16[4,128,1024]{2,1,0:T(8,128)(2,1)S(1)} %get-tuple-element.98), channel_id=1, source_target_pairs={{0,2},{2,0},{1,3},{3,1},{4,6},{6,4},{5,7},{7,5},{8,10},{10,8},{9,1... | collective-permute-start | bytes 3145736 | tf_op jit(solution)/shard_map/ppermute | solution.py:34
  84.9 59.6 %collective-permute-start.9 = (bf16[2,4,128,1024]{3,2,1,0:T(8,128)(2,1)}, bf16[2,4,128,1024]{3,2,1,0:T(8,128)(2,1)}, u32[]{:S(2)}, u32[]{:S(2)}) collective-permute-start(bf16[2,4,128,1024]{3,2,1,0:T(8,128)(2,1)} %get-tuple-element.86), channel_id=1, source_target_pairs={{0,2},{2,0},{1,3},{3,1},{4,6},{6,4},{5,7},{7,5},{8,10},{10,8},{9,1... | collective-permute-start | bytes 6291464 | tf_op jit(solution)/shard_map/ppermute | solution.py:34
  109.2 46.0 %collective-permute-start.4 = (bf16[2,4,128,1024]{3,2,1,0:T(8,128)(2,1)}, bf16[2,4,128,1024]{3,2,1,0:T(8,128)(2,1)}, u32[]{:S(2)}, u32[]{:S(2)}) collective-permute-start(bf16[2,4,128,1024]{3,2,1,0:T(8,128)(2,1)} %get-tuple-element.88), channel_id=1, source_target_pairs={{0,4},{4,0},{1,5},{5,1},{2,6},{6,2},{3,7},{7,3},{8,12},{12,8},{9,1... | collective-permute-start | bytes 6291464 | tf_op jit(solution)/shard_map/ppermute | solution.py:34
  193.2 2.0 collective-permute-start.10
  196.0 9.3 %collective-permute-start.11 = (bf16[128,4,256]{2,0,1:T(8,128)(2,1)S(1)}, bf16[128,4,256]{2,0,1:T(8,128)(2,1)S(1)}, u32[]{:S(2)}, u32[]{:S(2)}) collective-permute-start(bf16[128,4,256]{2,0,1:T(8,128)(2,1)S(1)} %bitcast.133), channel_id=1, source_target_pairs={{0,6},{2,0},{4,2},{6,4},{1,7},{3,1},{5,3},{7,5},{8,14},{10,8},{12,... | collective-permute-start | bytes 786440 | tf_op jit(solution)/shard_map/ppermute | solution.py:61
  198.8 13.8 %collective-permute-start.12 = (bf16[128,4,256]{2,0,1:T(8,128)(2,1)S(1)}, bf16[128,4,256]{2,0,1:T(8,128)(2,1)S(1)}, u32[]{:S(2)}, u32[]{:S(2)}) collective-permute-start(bf16[128,4,256]{2,0,1:T(8,128)(2,1)S(1)} %bitcast.134), channel_id=1, source_target_pairs={{0,4},{2,6},{4,0},{6,2},{1,5},{3,7},{5,1},{7,3},{8,12},{10,14},{12... | collective-permute-start | bytes 786440 | tf_op jit(solution)/shard_map/ppermute | solution.py:61
  199.5 13.1 %collective-permute-start.13 = (bf16[128,4,256]{2,0,1:T(8,128)(2,1)S(1)}, bf16[128,4,256]{2,0,1:T(8,128)(2,1)S(1)}, u32[]{:S(2)}, u32[]{:S(2)}) collective-permute-start(bf16[128,4,256]{2,0,1:T(8,128)(2,1)S(1)} %bitcast.135), channel_id=1, source_target_pairs={{0,2},{2,4},{4,6},{6,0},{1,3},{3,5},{5,7},{7,1},{8,10},{10,12},{12... | collective-permute-start | bytes 786440 | tf_op jit(solution)/shard_map/ppermute | solution.py:61
  218.3 29.9 %collective-permute-start.14 = (f32[128,2304]{1,0:T(8,128)S(1)}, f32[128,2304]{1,0:T(8,128)S(1)}, u32[]{:S(2)}, u32[]{:S(2)}) collective-permute-start(f32[128,2304]{1,0:T(8,128)S(1)} %get-tuple-element.82), channel_id=1, source_target_pairs={{0,2},{2,4},{4,6},{6,0},{1,3},{3,5},{5,7},{7,1},{8,10},{10,12},{12... | collective-permute-start | bytes 3538952 | tf_op jit(solution)/shard_map/ppermute | solution.py:71
  218.4 52.2 %collective-permute-start.15 = (f32[128,2304]{1,0:T(8,128)S(1)}, f32[128,2304]{1,0:T(8,128)S(1)}, u32[]{:S(2)}, u32[]{:S(2)}) collective-permute-start(f32[128,2304]{1,0:T(8,128)S(1)} %get-tuple-element.84), channel_id=1, source_target_pairs={{0,4},{2,6},{4,0},{6,2},{1,5},{3,7},{5,1},{7,3},{8,12},{10,14},{12... | collective-permute-start | bytes 3538952 | tf_op jit(solution)/shard_map/ppermute | solution.py:71
  219.4 54.1 %copy-start.7 = (f32[2304]{0:T(1024)S(1)}, f32[2304]{0:T(1024)}, u32[]{:S(2)}) copy-start(f32[2304]{0:T(1024)} %param.17) | copy-start | bytes 27652
  219.4 51.2 %collective-permute-start.16 = (f32[128,2304]{1,0:T(8,128)S(1)}, f32[128,2304]{1,0:T(8,128)S(1)}, u32[]{:S(2)}, u32[]{:S(2)}) collective-permute-start(f32[128,2304]{1,0:T(8,128)S(1)} %get-tuple-element.83), channel_id=1, source_target_pairs={{0,6},{2,0},{4,2},{6,4},{1,7},{3,1},{5,3},{7,5},{8,14},{10,8},{12,... | collective-permute-start | bytes 3538952 | tf_op jit(solution)/shard_map/ppermute | solution.py:71
  274.7 18.6 %collective-permute-start.17 = (f32[16]{0:T(128)S(1)}, f32[16]{0:T(128)S(1)}, u32[]{:S(2)}, u32[]{:S(2)}) collective-permute-start(f32[16]{0:T(128)S(1)} %select_reduce_fusion), channel_id=1, source_target_pairs={{0,8},{8,0},{16,24},{24,16},{1,9},{9,1},{17,25},{25,17},{2,10},{10... | collective-permute-start | bytes 200 | tf_op jit(solution)/shard_map/ppermute | solution.py:80
  293.3 6.7 %collective-permute-start.18 = (f32[16]{0:T(128)S(1)}, f32[16]{0:T(128)S(1)}, u32[]{:S(2)}, u32[]{:S(2)}) collective-permute-start(f32[16]{0:T(128)S(1)} %add.374), channel_id=1, source_target_pairs={{0,16},{8,24},{16,0},{24,8},{1,17},{9,25},{17,1},{25,9},{2,18},{10... | collective-permute-start | bytes 200 | tf_op jit(solution)/shard_map/ppermute | solution.py:80
  300.0 3.5 %collective-permute-start.19 = (f32[16]{0:T(128)S(1)}, f32[16]{0:T(128)S(1)}, u32[]{:S(2)}, u32[]{:S(2)}) collective-permute-start(f32[16]{0:T(128)S(1)} %add.375), channel_id=1, source_target_pairs={{0,4},{4,0},{1,5},{5,1},{2,6},{6,2},{3,7},{7,3},{8,12},{12,8},{9,1... | collective-permute-start | bytes 200 | tf_op jit(solution)/shard_map/ppermute | solution.py:80
  303.5 3.5 %collective-permute-start.20 = (f32[16]{0:T(128)S(1)}, f32[16]{0:T(128)S(1)}, u32[]{:S(2)}, u32[]{:S(2)}) collective-permute-start(f32[16]{0:T(128)S(1)} %add.376), channel_id=1, source_target_pairs={{0,2},{2,0},{1,3},{3,1},{4,6},{6,4},{5,7},{7,5},{8,10},{10,8},{9,1... | collective-permute-start | bytes 200 | tf_op jit(solution)/shard_map/ppermute | solution.py:80
  307.1 1.1 collective-permute-start.21
  (8 other events, 135.4 us)
Sparse Core Ops, SparseCore 0:
  9.6 115.4 all-gather.1

commit v10 on v9

--- a/solution.py
+++ b/solution.py
@@ -156,7 +156,7 @@
     outer = lax.axis_size("c0")
     inner = lax.axis_size(INNER)
     rows_each = out_weight.shape[0]
-    weight_rows = lax.all_gather(out_weight, "c0", axis=0, tiled=True)
+    weight_rows = ring_all_gather(out_weight, "c0")
     half = kv_local // 2
     splits = [(0, half, ("c0", "c2", "c1")), (half, kv_local, ("c0", "c1", "c2"))]
     gathered, bounds = [], []

time: 316 us -> 288 us (0.911)
  starting transfers between devices: 62.5 us -> 26.8 us
  other arithmetic: 18.9 us -> 34 us
  between operations: 15.7 us -> 2.33 us
  local copies, waits for them, and re-layouts: 25.7 us -> 30.3 us
    ppermute x5, starting transfers between devices: 25.1 us -> 5 us  [butterfly_sum(): x = x + lax.ppermute(x, axis, [(i, i ^ bit) for i in range(size)])]
    ppermute x11 -> x14, starting transfers between devices: 30.1 us -> 14.6 us  [ring_gather(): lax.ppermute(pieces[-1], axis, [(k, (k + 1) % n) for k in range(n)])]
    another operation x9 -> x10, other arithmetic: 12.3 us -> 21.2 us  [ring_gather(): return jnp.stack(pieces)]
    concatenate x1 -> x2, other arithmetic: 0.39 us -> 6.54 us  [ring_all_gather(): return jnp.roll(arrived, lax.axis_index(axis) + 1, axis=0)]
    rev x1 -> x2, local copies, waits for them, and re-layouts: 0.07 us -> 4.9 us  [ring_all_gather(): arrived = ring_gather(x, axis)[::-1]]
    ppermute x11 -> x14, waiting for transfers between devices: 102 us -> 101 us  [ring_gather(): lax.ppermute(pieces[-1], axis, [(k, (k + 1) % n) for k in range(n)])]
  transfers between devices with their start and end apart: 23 -> 25, of which waited for: 19 -> 19; matrix products, arithmetic and copies ran while one was open for 9% -> 13% of each run, Pallas kernels for 0% -> 0%
where the time goes in v10:
time: 288 us
  waiting for transfers between devices  173 us (60%)
  other arithmetic  34 us (12%)
  local copies, waits for them, and re-layouts  30.3 us (11%)
  starting transfers between devices  26.8 us (9%)
  matrix products  18 us (6%)
    ppermute x14, waiting for transfers between devices, ring_gather(): lax.ppermute(pieces[-1], axis, [(k, (k + 1) % n) for k in range(n)])  101 us
    ppermute x3, waiting for transfers between devices, permute_reduce_scatter(): lax.ppermute(sent, axes, [(k, (k + shift) % n) for k in range(n)])  49.1 us
    another operation x10, other arithmetic, ring_gather(): return jnp.stack(pieces)  21.2 us
    ppermute x14, starting transfers between devices, ring_gather(): lax.ppermute(pieces[-1], axis, [(k, (k + 1) % n) for k in range(n)])  14.6 us
    reshape x2, local copies, waits for them, and re-layouts, shards(): gathered.append((got.reshape(n_ctx * tok_dev, -1), key_rows))  13.2 us
    ppermute x3, waiting for transfers between devices, permute_all_to_all(): lax.ppermute(sent, axes, [(k, (k + shift) % n) for k in range(n)])  12 us
    ppermute x5, waiting for transfers between devices, butterfly_sum(): x = x + lax.ppermute(x, axis, [(i, i ^ bit) for i in range(size)])  11.2 us
    slice x2, local copies, waits for them, and re-layouts, shards(): got[:, width:]  8.85 us
  transfers between devices with their start and end apart: 25, of which 19 were waited for; matrix products, arithmetic and copies ran while one was open for 13% of the time, Pallas kernels for 0%

profile of v10, /device:TPU:0, one launch (start us, length us, event | category | flops | bytes accessed | tf_op | source)
XLA Modules:
  0.0 287.6 jit_solution(16146614101725753128)
XLA Ops:
  8.2 30.2 %collective-permute-done.5 = bf16[128,1024]{1,0:T(8,128)(2,1)S(1)} collective-permute-done((bf16[128,1024]{1,0:T(8,128)(2,1)S(1)}, bf16[128,1024]{1,0:T(8,128)(2,1)S(1)}, u32[]{:S(2)}, u32[]{:S(2)}) %collective-permute-start.5) | collective-permute-done | bytes 262176 | tf_op jit(solution)/shard_map/ppermute | solution.py:34
  38.4 5.6 %collective-permute-done = bf16[128,1024]{1,0:T(8,128)(2,1)S(1)} collective-permute-done((bf16[128,1024]{1,0:T(8,128)(2,1)S(1)}, bf16[128,1024]{1,0:T(8,128)(2,1)S(1)}, u32[]{:S(2)}, u32[]{:S(2)}) %collective-permute-start) | collective-permute-done | bytes 262176 | tf_op jit(solution)/shard_map/ppermute | solution.py:34
  44.0 5.6 %collective-permute-done.6 = bf16[128,1024]{1,0:T(8,128)(2,1)S(1)} collective-permute-done((bf16[128,1024]{1,0:T(8,128)(2,1)S(1)}, bf16[128,1024]{1,0:T(8,128)(2,1)S(1)}, u32[]{:S(2)}, u32[]{:S(2)}) %collective-permute-start.6) | collective-permute-done | bytes 262176 | tf_op jit(solution)/shard_map/ppermute | solution.py:34
  49.6 5.6 %collective-permute-done.1 = bf16[128,1024]{1,0:T(8,128)(2,1)S(1)} collective-permute-done((bf16[128,1024]{1,0:T(8,128)(2,1)S(1)}, bf16[128,1024]{1,0:T(8,128)(2,1)S(1)}, u32[]{:S(2)}, u32[]{:S(2)}) %collective-permute-start.1) | collective-permute-done | bytes 262176 | tf_op jit(solution)/shard_map/ppermute | solution.py:34
  56.8 4.0 %collective-permute-done.7 = bf16[128,1024]{1,0:T(8,128)(2,1)S(1)} collective-permute-done((bf16[128,1024]{1,0:T(8,128)(2,1)S(1)}, bf16[128,1024]{1,0:T(8,128)(2,1)S(1)}, u32[]{:S(2)}, u32[]{:S(2)}) %collective-permute-start.7) | collective-permute-done | bytes 262176 | tf_op jit(solution)/shard_map/ppermute | solution.py:34
  70.0 21.0 %collective-permute-done.11 = bf16[256,2304]{1,0:T(8,128)(2,1)} collective-permute-done((bf16[256,2304]{1,0:T(8,128)(2,1)S(1)}, bf16[256,2304]{1,0:T(8,128)(2,1)}, u32[]{:S(2)}, u32[]{:S(2)}) %collective-permute-start.11) | collective-permute-done | bytes 1179680 | tf_op jit(solution)/shard_map/ppermute | solution.py:34
  101.4 18.8 %collective-permute-done.12 = bf16[256,2304]{1,0:T(8,128)(2,1)} collective-permute-done((bf16[256,2304]{1,0:T(8,128)(2,1)}, bf16[256,2304]{1,0:T(8,128)(2,1)}, u32[]{:S(2)}, u32[]{:S(2)}) %collective-permute-start.12) | collective-permute-done | bytes 1179680 | tf_op jit(solution)/shard_map/ppermute | solution.py:34
  120.3 4.0 %pad_maximum_fusion = bf16[4,256,2304]{2,1,0:T(8,128)(2,1)} fusion(bf16[1,256,2304]{2,1,0:T(8,128)(2,1)} %bitcast.34, bf16[1,256,2304]{2,1,0:T(8,128)(2,1)} %bitcast.33, bf16[1,256,2304]{2,1,0:T(8,128)(2,1)} %bitcast.127, bf16[1,256,2304]{2,1,0:T(8,128)(2,1)} %bitcast.126), kind=kLoop, calls=%fused_computation.24 | loop fusion | flops 7077888 | bytes 9437184 | tf_op jit(solution)/shard_map/stack | solution.py:35
  124.3 4.8 %rev.6 = bf16[4,256,2304]{2,1,0:T(8,128)(2,1)} reverse(bf16[4,256,2304]{2,1,0:T(8,128)(2,1)} %pad_maximum_fusion), dimensions={0} | reverse | bytes 9437184 | tf_op jit(solution)/shard_map/rev | solution.py:51
  129.1 6.2 %fusion.20 = bf16[4,256,2304]{2,1,0:T(8,128)(2,1)} fusion(s32[]{:T(128)S(6)} %select_n.192, bf16[4,256,2304]{2,1,0:T(8,128)(2,1)} %rev.6), kind=kLoop, calls=%fused_computation.23 | loop fusion | flops 2359296 | bytes 9437188 | tf_op jit(solution)/shard_map/jit(_roll_dynamic)/concatenate | solution.py:52
  135.3 5.8 %collective-permute-done.9 = bf16[2,4,128,1024]{3,2,1,0:T(8,128)(2,1)} collective-permute-done((bf16[2,4,128,1024]{3,2,1,0:T(8,128)(2,1)}, bf16[2,4,128,1024]{3,2,1,0:T(8,128)(2,1)}, u32[]{:S(2)}, u32[]{:S(2)}) %collective-permute-start.9) | collective-permute-done | bytes 2097184 | tf_op jit(solution)/shard_map/ppermute | solution.py:34
  141.0 4.0 %pad_maximum_fusion.2 = bf16[2,2,4,128,1024]{4,3,2,1,0:T(8,128)(2,1)} fusion(bf16[1,2,4,128,1024]{4,3,2,1,0:T(8,128)(2,1)} %bitcast.28, bf16[1,2,4,128,1024]{4,3,2,1,0:T(8,128)(2,1)S(1)} %get-tuple-element.79), kind=kLoop, calls=%fused_computation.27 | loop fusion | flops 2097152 | bytes 8388608 | tf_op jit(solution)/shard_map/stack | solution.py:35
  145.1 6.7 %copy.65 = bf16[2048,1024]{0,1:T(8,128)(2,1)} copy(bf16[2048,1024]{1,0:T(8,128)(2,1)} %bitcast.115) | data formatting | bytes 8388608 | tf_op jit(solution)/shard_map/reshape | solution.py:169
  155.7 6.5 %copy.64 = bf16[2048,1024]{0,1:T(8,128)(2,1)} copy(bf16[2048,1024]{1,0:T(8,128)(2,1)} %bitcast.116) | data formatting | bytes 8388608 | tf_op jit(solution)/shard_map/reshape | solution.py:169
  166.8 10.9 %conditional.2 = (f32[4,2,128]{2,1,0:T(2,128)S(1)}, f32[4,2,128,128]{2,3,1,0:T(8,128)S(1)}) conditional(s32[]{:T(128)} %convert_element_type.37, () %tuple.26, (pred[128,2048]{0,1:T(8,128)(4,1)}, bf16[2048,1024]{0,1:T(8,128)(2,1)}, bf16[128,8,2,128]{0,3,2,1:T(8,128)(2,1)S(1)}) %tuple.71), branch_computations={%region_4.5_spmd, %region_5.7_spmd} | conditional | flops 1090518016 | bytes 41160776 | solution.py:130
  167.0 4.0 %fusion.55 = (bf16[2048,512]{0,1:T(8,128)(2,1)}, bf16[2048,512]{0,1:T(8,128)(2,1)S(1)}) fusion(bf16[2048,1024]{0,1:T(8,128)(2,1)} %get-tuple-element.21), kind=kLoop, calls=%fused_computation.144 | loop fusion | bytes 8388608 | tf_op jit(solution)/shard_map/slice | solution.py:175
  177.7 12.0 %conditional.3 = (f32[4,2,128]{2,1,0:T(2,128)S(1)}, f32[4,2,128,128]{2,3,1,0:T(8,128)S(1)}) conditional(s32[]{:T(128)} %convert_element_type.39, () %tuple.28, (pred[128,2048]{0,1:T(8,128)(4,1)S(1)}, bf16[2048,1024]{0,1:T(8,128)(2,1)}, bf16[128,8,2,128]{0,3,2,1:T(8,128)(2,1)S(1)}) %tuple.72), branch_computations={%region_9.10_spmd, %region_10.12_spmd} | conditional | flops 1090518016 | bytes 40112172 | solution.py:130
  177.7 4.9 %fusion.56 = (bf16[2048,512]{0,1:T(8,128)(2,1)}, bf16[2048,512]{0,1:T(8,128)(2,1)}) fusion(bf16[2048,1024]{0,1:T(8,128)(2,1)} %get-tuple-element.24), kind=kLoop, calls=%fused_computation.145 | loop fusion | bytes 8388608 | tf_op jit(solution)/shard_map/slice | solution.py:175
  182.9 4.3 %fusion.10 = (f32[4,2,128]{2,1,0:T(2,128)S(1)}, f32[4,2048,128,2]{2,1,3,0:T(8,128)S(1)}) fusion(pred[128,2048]{0,1:T(8,128)(4,1)S(1)} %get-tuple-element.23, bf16[2048,4,128,1]{0,2,3,1:T(8,128)(2,1)} %bitcast.125, bf16[128,8,2,128]{3,0,2,1:T(8,128)(2,1)S(1)} %copy.42), kind=kOutput, calls=%fused_computation.11 | convolution fusion | flops 545258496 | bytes 11014144 | tf_op jit(solution)/shard_map/cond/branch_1_fun/qgrd,kgd->grqk/dot_general | solution.py:111
  196.8 5.1 %collective-permute-done.14 = bf16[128,4,256]{2,0,1:T(8,128)(2,1)S(1)} collective-permute-done((bf16[128,4,256]{2,0,1:T(8,128)(2,1)S(1)}, bf16[128,4,256]{2,0,1:T(8,128)(2,1)S(1)}, u32[]{:S(2)}, u32[]{:S(2)}) %collective-permute-start.14) | collective-permute-done | bytes 262176 | tf_op jit(solution)/shard_map/ppermute | solution.py:61
  201.9 6.9 %collective-permute-done.15 = bf16[128,4,256]{2,0,1:T(8,128)(2,1)S(1)} collective-permute-done((bf16[128,4,256]{2,0,1:T(8,128)(2,1)S(1)}, bf16[128,4,256]{2,0,1:T(8,128)(2,1)S(1)}, u32[]{:S(2)}, u32[]{:S(2)}) %collective-permute-start.15) | collective-permute-done | bytes 262176 | tf_op jit(solution)/shard_map/ppermute | solution.py:61
  209.0 4.8 %convolution_bitcast_fusion = f32[4,128,2304]{2,1,0:T(8,128)S(1)} fusion(bf16[4,256,2304]{2,1,0:T(8,128)(2,1)} %fusion.20, bf16[8,128,4,256]{3,1,2,0:T(8,128)(2,1)S(1)} %bitcast_dynamic-update-slice_fusion.1, s32[]{:T(128)S(6)} %select_n.210), kind=kOutput, calls=%fused_computation.22 | convolution fusion | flops 2415919104 | bytes 10485764 | tf_op jit(solution)/shard_map/dot_general | solution.py:186
  217.6 26.4 %collective-permute-done.17 = f32[128,2304]{1,0:T(8,128)S(1)} collective-permute-done((f32[128,2304]{1,0:T(8,128)S(1)}, f32[128,2304]{1,0:T(8,128)S(1)}, u32[]{:S(2)}, u32[]{:S(2)}) %collective-permute-start.17) | collective-permute-done | bytes 1179680 | tf_op jit(solution)/shard_map/ppermute | solution.py:71
  244.0 22.7 %collective-permute-done.18 = f32[128,2304]{1,0:T(8,128)S(1)} collective-permute-done((f32[128,2304]{1,0:T(8,128)S(1)}, f32[128,2304]{1,0:T(8,128)S(1)}, u32[]{:S(2)}, u32[]{:S(2)}) %collective-permute-start.18) | collective-permute-done | bytes 1179680 | tf_op jit(solution)/shard_map/ppermute | solution.py:71
  (121 shorter events, 77.2 us)
Async XLA Ops:
  0.6 54.6 %collective-permute-start.10 = (bf16[256,2304]{1,0:T(8,128)(2,1)}, bf16[256,2304]{1,0:T(8,128)(2,1)S(1)}, u32[]{:S(2)}, u32[]{:S(2)}) collective-permute-start(bf16[256,2304]{1,0:T(8,128)(2,1)} %param.16), channel_id=1, source_target_pairs={{0,8},{8,16},{16,24},{24,0},{1,9},{9,17},{17,25},{25,1},{2,10},{10... | collective-permute-start | bytes 3538952 | tf_op jit(solution)/shard_map/ppermute | solution.py:34
  4.9 33.5 %collective-permute-start.5 = (bf16[128,1024]{1,0:T(8,128)(2,1)S(1)}, bf16[128,1024]{1,0:T(8,128)(2,1)S(1)}, u32[]{:S(2)}, u32[]{:S(2)}) collective-permute-start(bf16[128,1024]{1,0:T(8,128)(2,1)S(1)} %get-tuple-element.94), channel_id=1, source_target_pairs={{0,8},{8,16},{16,24},{24,0},{1,9},{9,17},{17,25},{25,1},{2,10},{10... | collective-permute-start | bytes 786440 | tf_op jit(solution)/shard_map/ppermute | solution.py:34
  6.5 37.4 %collective-permute-start = (bf16[128,1024]{1,0:T(8,128)(2,1)S(1)}, bf16[128,1024]{1,0:T(8,128)(2,1)S(1)}, u32[]{:S(2)}, u32[]{:S(2)}) collective-permute-start(bf16[128,1024]{1,0:T(8,128)(2,1)S(1)} %get-tuple-element.100), channel_id=1, source_target_pairs={{0,8},{8,16},{16,24},{24,0},{1,9},{9,17},{17,25},{25,1},{2,10},{10... | collective-permute-start | bytes 786440 | tf_op jit(solution)/shard_map/ppermute | solution.py:34
  38.4 11.2 %collective-permute-start.6 = (bf16[128,1024]{1,0:T(8,128)(2,1)S(1)}, bf16[128,1024]{1,0:T(8,128)(2,1)S(1)}, u32[]{:S(2)}, u32[]{:S(2)}) collective-permute-start(bf16[128,1024]{1,0:T(8,128)(2,1)S(1)} %collective-permute-done.5), channel_id=1, source_target_pairs={{0,8},{8,16},{16,24},{24,0},{1,9},{9,17},{17,25},{25,1},{2,10},{10... | collective-permute-start | bytes 786440 | tf_op jit(solution)/shard_map/ppermute | solution.py:34
  44.0 11.2 %collective-permute-start.1 = (bf16[128,1024]{1,0:T(8,128)(2,1)S(1)}, bf16[128,1024]{1,0:T(8,128)(2,1)S(1)}, u32[]{:S(2)}, u32[]{:S(2)}) collective-permute-start(bf16[128,1024]{1,0:T(8,128)(2,1)S(1)} %collective-permute-done), channel_id=1, source_target_pairs={{0,8},{8,16},{16,24},{24,0},{1,9},{9,17},{17,25},{25,1},{2,10},{10... | collective-permute-start | bytes 786440 | tf_op jit(solution)/shard_map/ppermute | solution.py:34
  49.6 11.2 %collective-permute-start.7 = (bf16[128,1024]{1,0:T(8,128)(2,1)S(1)}, bf16[128,1024]{1,0:T(8,128)(2,1)S(1)}, u32[]{:S(2)}, u32[]{:S(2)}) collective-permute-start(bf16[128,1024]{1,0:T(8,128)(2,1)S(1)} %collective-permute-done.6), channel_id=1, source_target_pairs={{0,8},{8,16},{16,24},{24,0},{1,9},{9,17},{17,25},{25,1},{2,10},{10... | collective-permute-start | bytes 786440 | tf_op jit(solution)/shard_map/ppermute | solution.py:34
  55.2 11.2 %collective-permute-start.2 = (bf16[128,1024]{1,0:T(8,128)(2,1)S(1)}, bf16[128,1024]{1,0:T(8,128)(2,1)S(1)}, u32[]{:S(2)}, u32[]{:S(2)}) collective-permute-start(bf16[128,1024]{1,0:T(8,128)(2,1)S(1)} %collective-permute-done.1), channel_id=1, source_target_pairs={{0,8},{8,16},{16,24},{24,0},{1,9},{9,17},{17,25},{25,1},{2,10},{10... | collective-permute-start | bytes 786440 | tf_op jit(solution)/shard_map/ppermute | solution.py:34
  55.2 35.8 %collective-permute-start.11 = (bf16[256,2304]{1,0:T(8,128)(2,1)S(1)}, bf16[256,2304]{1,0:T(8,128)(2,1)}, u32[]{:S(2)}, u32[]{:S(2)}) collective-permute-start(bf16[256,2304]{1,0:T(8,128)(2,1)S(1)} %collective-permute-done.10), channel_id=1, source_target_pairs={{0,8},{8,16},{16,24},{24,0},{1,9},{9,17},{17,25},{25,1},{2,10},{10... | collective-permute-start | bytes 3538952 | tf_op jit(solution)/shard_map/ppermute | solution.py:34
  62.0 29.1 %collective-permute-start.8 = (bf16[4,128,1024]{2,1,0:T(8,128)(2,1)}, bf16[4,128,1024]{2,1,0:T(8,128)(2,1)}, u32[]{:S(2)}, u32[]{:S(2)}) collective-permute-start(bf16[4,128,1024]{2,1,0:T(8,128)(2,1)} %get-tuple-element.90), channel_id=1, source_target_pairs={{0,4},{4,0},{1,5},{5,1},{2,6},{6,2},{3,7},{7,3},{8,12},{12,8},{9,1... | collective-permute-start | bytes 3145736 | tf_op jit(solution)/shard_map/ppermute | solution.py:34
  68.0 27.4 %collective-permute-start.3 = (bf16[4,128,1024]{2,1,0:T(8,128)(2,1)}, bf16[4,128,1024]{2,1,0:T(8,128)(2,1)}, u32[]{:S(2)}, u32[]{:S(2)}) collective-permute-start(bf16[4,128,1024]{2,1,0:T(8,128)(2,1)} %get-tuple-element.92), channel_id=1, source_target_pairs={{0,2},{2,0},{1,3},{3,1},{4,6},{6,4},{5,7},{7,5},{8,10},{10,8},{9,1... | collective-permute-start | bytes 3145736 | tf_op jit(solution)/shard_map/ppermute | solution.py:34
  91.0 29.3 %collective-permute-start.12 = (bf16[256,2304]{1,0:T(8,128)(2,1)}, bf16[256,2304]{1,0:T(8,128)(2,1)}, u32[]{:S(2)}, u32[]{:S(2)}) collective-permute-start(bf16[256,2304]{1,0:T(8,128)(2,1)} %collective-permute-done.11), channel_id=1, source_target_pairs={{0,8},{8,16},{16,24},{24,0},{1,9},{9,17},{17,25},{25,1},{2,10},{10... | collective-permute-start | bytes 3538952 | tf_op jit(solution)/shard_map/ppermute | solution.py:34
  93.9 47.1 %collective-permute-start.9 = (bf16[2,4,128,1024]{3,2,1,0:T(8,128)(2,1)}, bf16[2,4,128,1024]{3,2,1,0:T(8,128)(2,1)}, u32[]{:S(2)}, u32[]{:S(2)}) collective-permute-start(bf16[2,4,128,1024]{3,2,1,0:T(8,128)(2,1)} %get-tuple-element.80), channel_id=1, source_target_pairs={{0,2},{2,0},{1,3},{3,1},{4,6},{6,4},{5,7},{7,5},{8,10},{10,8},{9,1... | collective-permute-start | bytes 6291464 | tf_op jit(solution)/shard_map/ppermute | solution.py:34
  98.9 52.8 %collective-permute-start.4 = (bf16[2,4,128,1024]{3,2,1,0:T(8,128)(2,1)}, bf16[2,4,128,1024]{3,2,1,0:T(8,128)(2,1)}, u32[]{:S(2)}, u32[]{:S(2)}) collective-permute-start(bf16[2,4,128,1024]{3,2,1,0:T(8,128)(2,1)} %get-tuple-element.82), channel_id=1, source_target_pairs={{0,4},{4,0},{1,5},{5,1},{2,6},{6,2},{3,7},{7,3},{8,12},{12,8},{9,1... | collective-permute-start | bytes 6291464 | tf_op jit(solution)/shard_map/ppermute | solution.py:34
  189.9 2.0 collective-permute-start.13
  192.7 9.2 %collective-permute-start.14 = (bf16[128,4,256]{2,0,1:T(8,128)(2,1)S(1)}, bf16[128,4,256]{2,0,1:T(8,128)(2,1)S(1)}, u32[]{:S(2)}, u32[]{:S(2)}) collective-permute-start(bf16[128,4,256]{2,0,1:T(8,128)(2,1)S(1)} %bitcast.135), channel_id=1, source_target_pairs={{0,6},{2,0},{4,2},{6,4},{1,7},{3,1},{5,3},{7,5},{8,14},{10,8},{12,... | collective-permute-start | bytes 786440 | tf_op jit(solution)/shard_map/ppermute | solution.py:61
  195.1 13.8 %collective-permute-start.15 = (bf16[128,4,256]{2,0,1:T(8,128)(2,1)S(1)}, bf16[128,4,256]{2,0,1:T(8,128)(2,1)S(1)}, u32[]{:S(2)}, u32[]{:S(2)}) collective-permute-start(bf16[128,4,256]{2,0,1:T(8,128)(2,1)S(1)} %bitcast.136), channel_id=1, source_target_pairs={{0,4},{2,6},{4,0},{6,2},{1,5},{3,7},{5,1},{7,3},{8,12},{10,14},{12... | collective-permute-start | bytes 786440 | tf_op jit(solution)/shard_map/ppermute | solution.py:61
  195.8 13.1 %collective-permute-start.16 = (bf16[128,4,256]{2,0,1:T(8,128)(2,1)S(1)}, bf16[128,4,256]{2,0,1:T(8,128)(2,1)S(1)}, u32[]{:S(2)}, u32[]{:S(2)}) collective-permute-start(bf16[128,4,256]{2,0,1:T(8,128)(2,1)S(1)} %bitcast.137), channel_id=1, source_target_pairs={{0,2},{2,4},{4,6},{6,0},{1,3},{3,5},{5,7},{7,1},{8,10},{10,12},{12... | collective-permute-start | bytes 786440 | tf_op jit(solution)/shard_map/ppermute | solution.py:61
  214.1 29.9 %collective-permute-start.17 = (f32[128,2304]{1,0:T(8,128)S(1)}, f32[128,2304]{1,0:T(8,128)S(1)}, u32[]{:S(2)}, u32[]{:S(2)}) collective-permute-start(f32[128,2304]{1,0:T(8,128)S(1)} %get-tuple-element.76), channel_id=1, source_target_pairs={{0,2},{2,4},{4,6},{6,0},{1,3},{3,5},{5,7},{7,1},{8,10},{10,12},{12... | collective-permute-start | bytes 3538952 | tf_op jit(solution)/shard_map/ppermute | solution.py:71
  214.2 52.4 %collective-permute-start.18 = (f32[128,2304]{1,0:T(8,128)S(1)}, f32[128,2304]{1,0:T(8,128)S(1)}, u32[]{:S(2)}, u32[]{:S(2)}) collective-permute-start(f32[128,2304]{1,0:T(8,128)S(1)} %get-tuple-element.78), channel_id=1, source_target_pairs={{0,4},{2,6},{4,0},{6,2},{1,5},{3,7},{5,1},{7,3},{8,12},{10,14},{12... | collective-permute-start | bytes 3538952 | tf_op jit(solution)/shard_map/ppermute | solution.py:71
  215.3 51.4 %collective-permute-start.19 = (f32[128,2304]{1,0:T(8,128)S(1)}, f32[128,2304]{1,0:T(8,128)S(1)}, u32[]{:S(2)}, u32[]{:S(2)}) collective-permute-start(f32[128,2304]{1,0:T(8,128)S(1)} %get-tuple-element.77), channel_id=1, source_target_pairs={{0,6},{2,0},{4,2},{6,4},{1,7},{3,1},{5,3},{7,5},{8,14},{10,8},{12,... | collective-permute-start | bytes 3538952 | tf_op jit(solution)/shard_map/ppermute | solution.py:71
  270.8 3.6 %collective-permute-start.20 = (f32[16]{0:T(128)S(1)}, f32[16]{0:T(128)S(1)}, u32[]{:S(2)}, u32[]{:S(2)}) collective-permute-start(f32[16]{0:T(128)S(1)} %select_reduce_fusion), channel_id=1, source_target_pairs={{0,8},{8,0},{16,24},{24,16},{1,9},{9,1},{17,25},{25,17},{2,10},{10... | collective-permute-start | bytes 200 | tf_op jit(solution)/shard_map/ppermute | solution.py:80
  274.4 4.4 %collective-permute-start.21 = (f32[16]{0:T(128)S(1)}, f32[16]{0:T(128)S(1)}, u32[]{:S(2)}, u32[]{:S(2)}) collective-permute-start(f32[16]{0:T(128)S(1)} %add.389), channel_id=1, source_target_pairs={{0,16},{8,24},{16,0},{24,8},{1,17},{9,25},{17,1},{25,9},{2,18},{10... | collective-permute-start | bytes 200 | tf_op jit(solution)/shard_map/ppermute | solution.py:80
  278.9 3.5 %collective-permute-start.22 = (f32[16]{0:T(128)S(1)}, f32[16]{0:T(128)S(1)}, u32[]{:S(2)}, u32[]{:S(2)}) collective-permute-start(f32[16]{0:T(128)S(1)} %add.390), channel_id=1, source_target_pairs={{0,4},{4,0},{1,5},{5,1},{2,6},{6,2},{3,7},{7,3},{8,12},{12,8},{9,1... | collective-permute-start | bytes 200 | tf_op jit(solution)/shard_map/ppermute | solution.py:80
  282.4 3.5 %collective-permute-start.23 = (f32[16]{0:T(128)S(1)}, f32[16]{0:T(128)S(1)}, u32[]{:S(2)}, u32[]{:S(2)}) collective-permute-start(f32[16]{0:T(128)S(1)} %add.391), channel_id=1, source_target_pairs={{0,2},{2,0},{1,3},{3,1},{4,6},{6,4},{5,7},{7,5},{8,10},{10,8},{9,1... | collective-permute-start | bytes 200 | tf_op jit(solution)/shard_map/ppermute | solution.py:80
  (12 other events, 210.5 us)

commit v11 on v10

--- a/solution.py
+++ b/solution.py
@@ -127,6 +127,8 @@
             denominator = denominator + jnp.sum(weights, axis=-1)
             return (numerator, denominator)
 
+        if count == n_ctx * tok_dev:
+            return compute(state)
         return lax.cond(jnp.any(visible), compute, lambda carry: carry, state)
 
     def attend(q_part, key_piece, value_piece, key_rows):
@@ -156,7 +158,8 @@
     outer = lax.axis_size("c0")
     inner = lax.axis_size(INNER)
     rows_each = out_weight.shape[0]
-    weight_rows = ring_all_gather(out_weight, "c0")
+    weight_rows = ring_gather(out_weight, "c0")
+    arrival = (lax.axis_index("c0") - jnp.arange(outer, dtype=jnp.int32)) % outer
     half = kv_local // 2
     splits = [(0, half, ("c0", "c2", "c1")), (half, kv_local, ("c0", "c1", "c2"))]
     gathered, bounds = [], []
@@ -183,6 +186,7 @@
     weight_rows = weight_rows.reshape(outer * rows_each, out_weight.shape[1])
     blocks = all_heads.reshape(tok_dev, outer, inner, rows_each).transpose(2, 0, 1, 3)
     regrouped = permute_all_to_all(blocks, INNER)
+    regrouped = jnp.take(regrouped.reshape(inner * tok_dev, outer, rows_each), arrival, axis=1)
     partial = jnp.dot(
         regrouped.reshape(inner * tok_dev, outer * rows_each), weight_rows, preferred_element_type=jnp.float32
     )

time: 288 us -> 277 us (0.962)
  waiting for transfers between devices: 173 us -> 186 us
  other arithmetic: 34 us -> 25.7 us
  local copies, waits for them, and re-layouts: 30.3 us -> 24.1 us
  starting transfers between devices: 26.8 us -> 21.3 us
    ppermute x14, waiting for transfers between devices: 101 us -> 110 us  [ring_gather(): lax.ppermute(pieces[-1], axis, [(k, (k + 1) % n) for k in range(n)])]
    concatenate x2 -> x1, other arithmetic: 6.54 us -> 0.39 us  [ring_all_gather(): return jnp.roll(arrived, lax.axis_index(axis) + 1, axis=0)]
    slice x2, local copies, waits for them, and re-layouts: 8.85 us -> 3.45 us  [shards(): got[:, :width]]
    cond x2 -> x0, matrix products: 5.1 us -> none  [attend_block(): return lax.cond(jnp.any(visible), compute, lambda carry: carry, state)]
    dot_general x0 -> x2, matrix products: none -> 5.1 us  [compute(): jnp.einsum('grqk,kgd->grqd', weights.astype(jnp.bfloat16), value_piece.re...]
    rev x2 -> x1, local copies, waits for them, and re-layouts: 4.9 us -> 0.07 us  [ring_all_gather(): arrived = ring_gather(x, axis)[::-1]]
    reduce_or x1 -> x0, other arithmetic: 3.12 us -> none  [attend_block(): return lax.cond(jnp.any(visible), compute, lambda carry: carry, state)]
  transfers between devices with their start and end apart: 25 -> 25, of which waited for: 19 -> 20; matrix products, arithmetic and copies ran while one was open for 13% -> 9% of each run, Pallas kernels for 0% -> 0%
where the time goes in v11:
time: 277 us; the launch traced here: 276 us
  waiting for transfers between devices  186 us (67%)
  other arithmetic  25.7 us (9%)
  local copies, waits for them, and re-layouts  24.1 us (9%)
  starting transfers between devices  21.3 us (8%)
  matrix products  15.3 us (6%)
    ppermute x14, waiting for transfers between devices, ring_gather(): lax.ppermute(pieces[-1], axis, [(k, (k + 1) % n) for k in range(n)])  110 us
    ppermute x3, waiting for transfers between devices, permute_reduce_scatter(): lax.ppermute(sent, axes, [(k, (k + shift) % n) for k in range(n)])  50.5 us
    another operation x10, other arithmetic, ring_gather(): return jnp.stack(pieces)  20.2 us
    ppermute x5, waiting for transfers between devices, butterfly_sum(): x = x + lax.ppermute(x, axis, [(i, i ^ bit) for i in range(size)])  13.7 us
    reshape x2, local copies, waits for them, and re-layouts, shards(): gathered.append((got.reshape(n_ctx * tok_dev, -1), key_rows))  13.2 us
    ppermute x14, starting transfers between devices, ring_gather(): lax.ppermute(pieces[-1], axis, [(k, (k + 1) % n) for k in range(n)])  12.6 us
    ppermute x3, waiting for transfers between devices, permute_all_to_all(): lax.ppermute(sent, axes, [(k, (k + shift) % n) for k in range(n)])  12 us
  transfers between devices with their start and end apart: 25, of which 20 were waited for; matrix products, arithmetic and copies ran while one was open for 9% of the time, Pallas kernels for 0%

profile of v11, /device:TPU:0, one launch (start us, length us, event | category | flops | bytes accessed | tf_op | source)
XLA Modules:
  0.0 276.4 jit_solution(3751591678385956098)
XLA Ops:
  1.8 3.1 %collective-permute-start = (bf16[128,1024]{1,0:T(8,128)(2,1)S(1)}, bf16[128,1024]{1,0:T(8,128)(2,1)S(1)}, u32[]{:S(2)}, u32[]{:S(2)}) collective-permute-start(bf16[128,1024]{1,0:T(8,128)(2,1)S(1)} %get-tuple-element.44), channel_id=1, source_target_pairs={{0,8},{8,16},{16,24},{24,0},{1,9},{9,17},{17,25},{25,1},{2,10},{10... | collective-permute-start | bytes 786440 | tf_op jit(solution)/shard_map/ppermute | solution.py:34
  8.1 5.9 %collective-permute-done = bf16[128,1024]{1,0:T(8,128)(2,1)S(1)} collective-permute-done((bf16[128,1024]{1,0:T(8,128)(2,1)S(1)}, bf16[128,1024]{1,0:T(8,128)(2,1)S(1)}, u32[]{:S(2)}, u32[]{:S(2)}) %collective-permute-start) | collective-permute-done | bytes 262176 | tf_op jit(solution)/shard_map/ppermute | solution.py:34
  14.1 30.9 %collective-permute-done.5 = bf16[128,1024]{1,0:T(8,128)(2,1)S(1)} collective-permute-done((bf16[128,1024]{1,0:T(8,128)(2,1)S(1)}, bf16[128,1024]{1,0:T(8,128)(2,1)S(1)}, u32[]{:S(2)}, u32[]{:S(2)}) %collective-permute-start.5) | collective-permute-done | bytes 262176 | tf_op jit(solution)/shard_map/ppermute | solution.py:34
  45.0 5.6 %collective-permute-done.1 = bf16[128,1024]{1,0:T(8,128)(2,1)S(1)} collective-permute-done((bf16[128,1024]{1,0:T(8,128)(2,1)S(1)}, bf16[128,1024]{1,0:T(8,128)(2,1)S(1)}, u32[]{:S(2)}, u32[]{:S(2)}) %collective-permute-start.1) | collective-permute-done | bytes 262176 | tf_op jit(solution)/shard_map/ppermute | solution.py:34
  50.6 5.6 %collective-permute-done.6 = bf16[128,1024]{1,0:T(8,128)(2,1)S(1)} collective-permute-done((bf16[128,1024]{1,0:T(8,128)(2,1)S(1)}, bf16[128,1024]{1,0:T(8,128)(2,1)S(1)}, u32[]{:S(2)}, u32[]{:S(2)}) %collective-permute-start.6) | collective-permute-done | bytes 262176 | tf_op jit(solution)/shard_map/ppermute | solution.py:34
  56.2 5.6 %collective-permute-done.2 = bf16[128,1024]{1,0:T(8,128)(2,1)S(1)} collective-permute-done((bf16[128,1024]{1,0:T(8,128)(2,1)S(1)}, bf16[128,1024]{1,0:T(8,128)(2,1)S(1)}, u32[]{:S(2)}, u32[]{:S(2)}) %collective-permute-start.2) | collective-permute-done | bytes 262176 | tf_op jit(solution)/shard_map/ppermute | solution.py:34
  69.6 16.0 %collective-permute-done.3 = bf16[4,128,1024]{2,1,0:T(8,128)(2,1)} collective-permute-done((bf16[4,128,1024]{2,1,0:T(8,128)(2,1)S(1)}, bf16[4,128,1024]{2,1,0:T(8,128)(2,1)}, u32[]{:S(2)}, u32[]{:S(2)}) %collective-permute-start.3) | collective-permute-done | bytes 1048608 | tf_op jit(solution)/shard_map/ppermute | solution.py:34
  85.7 2.9 %fusion.46 = (bf16[1,2,4,128,1024]{4,3,2,1,0:T(8,128)(2,1)S(1)}, bf16[2,4,128,1024]{3,2,1,0:T(8,128)(2,1)}) fusion(bf16[1,4,128,1024]{3,2,1,0:T(8,128)(2,1)} %bitcast.6, bf16[1,4,128,1024]{3,2,1,0:T(8,128)(2,1)S(1)} %get-tuple-element.35), kind=kLoop, calls=%fused_computation.144 | loop fusion | flops 1048576 | bytes 6291456 | tf_op jit(solution)/shard_map/stack | solution.py:35
  89.9 4.6 %collective-permute-done.8 = bf16[4,128,1024]{2,1,0:T(8,128)(2,1)} collective-permute-done((bf16[4,128,1024]{2,1,0:T(8,128)(2,1)}, bf16[4,128,1024]{2,1,0:T(8,128)(2,1)}, u32[]{:S(2)}, u32[]{:S(2)}) %collective-permute-start.8) | collective-permute-done | bytes 1048608 | tf_op jit(solution)/shard_map/ppermute | solution.py:34
  94.5 3.5 %fusion.45 = (bf16[1,2,4,128,1024]{4,3,2,1,0:T(8,128)(2,1)}, bf16[2,4,128,1024]{3,2,1,0:T(8,128)(2,1)}) fusion(bf16[1,4,128,1024]{3,2,1,0:T(8,128)(2,1)} %bitcast.16, bf16[1,4,128,1024]{3,2,1,0:T(8,128)(2,1)S(1)} %copy-done.2), kind=kLoop, calls=%fused_computation.143 | loop fusion | flops 1048576 | bytes 6291456 | tf_op jit(solution)/shard_map/stack | solution.py:35
  102.5 23.7 %collective-permute-done.12 = bf16[256,2304]{1,0:T(8,128)(2,1)} collective-permute-done((bf16[256,2304]{1,0:T(8,128)(2,1)}, bf16[256,2304]{1,0:T(8,128)(2,1)}, u32[]{:S(2)}, u32[]{:S(2)}) %collective-permute-start.12) | collective-permute-done | bytes 1179680 | tf_op jit(solution)/shard_map/ppermute | solution.py:34
  126.2 3.8 %pad_maximum_fusion = bf16[4,256,2304]{2,1,0:T(8,128)(2,1)} fusion(bf16[1,256,2304]{2,1,0:T(8,128)(2,1)} %bitcast.24, bf16[1,256,2304]{2,1,0:T(8,128)(2,1)} %bitcast.23, bf16[1,256,2304]{2,1,0:T(8,128)(2,1)} %bitcast.22, bf16[1,256,2304]{2,1,0:T(8,128)(2,1)S(1)} %bitcast.130), kind=kLoop, calls=%fused_computation.7 | loop fusion | flops 7077888 | bytes 9437184 | tf_op jit(solution)/shard_map/stack | solution.py:35
  130.0 7.7 %collective-permute-done.4 = bf16[2,4,128,1024]{3,2,1,0:T(8,128)(2,1)} collective-permute-done((bf16[2,4,128,1024]{3,2,1,0:T(8,128)(2,1)}, bf16[2,4,128,1024]{3,2,1,0:T(8,128)(2,1)}, u32[]{:S(2)}, u32[]{:S(2)}) %collective-permute-start.4) | collective-permute-done | bytes 2097184 | tf_op jit(solution)/shard_map/ppermute | solution.py:34
  137.7 4.0 %pad_maximum_fusion.1 = bf16[2,2,4,128,1024]{4,3,2,1,0:T(8,128)(2,1)} fusion(bf16[1,2,4,128,1024]{4,3,2,1,0:T(8,128)(2,1)} %bitcast.8, bf16[1,2,4,128,1024]{4,3,2,1,0:T(8,128)(2,1)S(1)} %get-tuple-element.25), kind=kLoop, calls=%fused_computation.8 | loop fusion | flops 2097152 | bytes 8388608 | tf_op jit(solution)/shard_map/stack | solution.py:35
  141.7 6.7 %copy.65 = bf16[2048,1024]{0,1:T(8,128)(2,1)} copy(bf16[2048,1024]{1,0:T(8,128)(2,1)} %bitcast.119) | data formatting | bytes 8388608 | tf_op jit(solution)/shard_map/reshape | solution.py:172
  148.4 4.0 %pad_maximum_fusion.2 = bf16[2,2,4,128,1024]{4,3,2,1,0:T(8,128)(2,1)} fusion(bf16[1,2,4,128,1024]{4,3,2,1,0:T(8,128)(2,1)} %bitcast.18, bf16[1,2,4,128,1024]{4,3,2,1,0:T(8,128)(2,1)S(1)} %copy-done.1), kind=kLoop, calls=%fused_computation.9 | loop fusion | flops 2097152 | bytes 8388608 | tf_op jit(solution)/shard_map/stack | solution.py:35
  152.4 6.5 %copy.66 = bf16[2048,1024]{0,1:T(8,128)(2,1)} copy(bf16[2048,1024]{1,0:T(8,128)(2,1)} %bitcast.120) | data formatting | bytes 8388608 | tf_op jit(solution)/shard_map/reshape | solution.py:172
  182.5 5.0 %collective-permute-done.14 = bf16[128,4,256]{2,0,1:T(8,128)(2,1)S(1)} collective-permute-done((bf16[128,4,256]{2,0,1:T(8,128)(2,1)S(1)}, bf16[128,4,256]{2,0,1:T(8,128)(2,1)S(1)}, u32[]{:S(2)}, u32[]{:S(2)}) %collective-permute-start.14) | collective-permute-done | bytes 262176 | tf_op jit(solution)/shard_map/ppermute | solution.py:61
  187.5 7.0 %collective-permute-done.15 = bf16[128,4,256]{2,0,1:T(8,128)(2,1)S(1)} collective-permute-done((bf16[128,4,256]{2,0,1:T(8,128)(2,1)S(1)}, bf16[128,4,256]{2,0,1:T(8,128)(2,1)S(1)}, u32[]{:S(2)}, u32[]{:S(2)}) %collective-permute-start.15) | collective-permute-done | bytes 262176 | tf_op jit(solution)/shard_map/ppermute | solution.py:61
  197.2 4.9 %fusion.54 = f32[4,128,2304]{2,1,0:T(8,128)S(1)} fusion(bf16[4,128,1024]{2,1,0:T(8,128)(2,1)S(1)} %select_n.249, bf16[1024,2304,1]{1,0,2:T(8,128)(2,1)} %bitcast.121), kind=kOutput, calls=%fused_computation.151 | convolution fusion | flops 2415919104 | bytes 10485760 | tf_op jit(solution)/shard_map/dot_general | solution.py:190
  205.0 26.4 %collective-permute-done.19 = f32[128,2304]{1,0:T(8,128)S(1)} collective-permute-done((f32[128,2304]{1,0:T(8,128)S(1)}, f32[128,2304]{1,0:T(8,128)S(1)}, u32[]{:S(2)}, u32[]{:S(2)}) %collective-permute-start.19) | collective-permute-done | bytes 1179680 | tf_op jit(solution)/shard_map/ppermute | solution.py:71
  231.4 24.1 %collective-permute-done.18 = f32[128,2304]{1,0:T(8,128)S(1)} collective-permute-done((f32[128,2304]{1,0:T(8,128)S(1)}, f32[128,2304]{1,0:T(8,128)S(1)}, u32[]{:S(2)}, u32[]{:S(2)}) %collective-permute-start.18) | collective-permute-done | bytes 1179680 | tf_op jit(solution)/shard_map/ppermute | solution.py:71
  259.7 3.5 %collective-permute-done.20 = f32[16]{0:T(128)S(1)} collective-permute-done((f32[16]{0:T(128)S(1)}, f32[16]{0:T(128)S(1)}, u32[]{:S(2)}, u32[]{:S(2)}) %collective-permute-start.20) | collective-permute-done | bytes 96 | tf_op jit(solution)/shard_map/ppermute | solution.py:80
  263.9 3.8 %collective-permute-done.21 = f32[16]{0:T(128)S(1)} collective-permute-done((f32[16]{0:T(128)S(1)}, f32[16]{0:T(128)S(1)}, u32[]{:S(2)}, u32[]{:S(2)}) %collective-permute-start.21) | collective-permute-done | bytes 96 | tf_op jit(solution)/shard_map/ppermute | solution.py:80
  (119 shorter events, 60.5 us)
Async XLA Ops:
  1.8 12.2 %collective-permute-start = (bf16[128,1024]{1,0:T(8,128)(2,1)S(1)}, bf16[128,1024]{1,0:T(8,128)(2,1)S(1)}, u32[]{:S(2)}, u32[]{:S(2)}) collective-permute-start(bf16[128,1024]{1,0:T(8,128)(2,1)S(1)} %get-tuple-element.44), channel_id=1, source_target_pairs={{0,8},{8,16},{16,24},{24,0},{1,9},{9,17},{17,25},{25,1},{2,10},{10... | collective-permute-start | bytes 786440 | tf_op jit(solution)/shard_map/ppermute | solution.py:34
  4.9 64.7 %collective-permute-start.10 = (bf16[256,2304]{1,0:T(8,128)(2,1)}, bf16[256,2304]{1,0:T(8,128)(2,1)}, u32[]{:S(2)}, u32[]{:S(2)}) collective-permute-start(bf16[256,2304]{1,0:T(8,128)(2,1)} %param.12), channel_id=1, source_target_pairs={{0,8},{8,16},{16,24},{24,0},{1,9},{9,17},{17,25},{25,1},{2,10},{10... | collective-permute-start | bytes 3538952 | tf_op jit(solution)/shard_map/ppermute | solution.py:34
  6.5 38.4 %collective-permute-start.5 = (bf16[128,1024]{1,0:T(8,128)(2,1)S(1)}, bf16[128,1024]{1,0:T(8,128)(2,1)S(1)}, u32[]{:S(2)}, u32[]{:S(2)}) collective-permute-start(bf16[128,1024]{1,0:T(8,128)(2,1)S(1)} %get-tuple-element.38), channel_id=1, source_target_pairs={{0,8},{8,16},{16,24},{24,0},{1,9},{9,17},{17,25},{25,1},{2,10},{10... | collective-permute-start | bytes 786440 | tf_op jit(solution)/shard_map/ppermute | solution.py:34
  14.0 36.5 %collective-permute-start.1 = (bf16[128,1024]{1,0:T(8,128)(2,1)S(1)}, bf16[128,1024]{1,0:T(8,128)(2,1)S(1)}, u32[]{:S(2)}, u32[]{:S(2)}) collective-permute-start(bf16[128,1024]{1,0:T(8,128)(2,1)S(1)} %collective-permute-done), channel_id=1, source_target_pairs={{0,8},{8,16},{16,24},{24,0},{1,9},{9,17},{17,25},{25,1},{2,10},{10... | collective-permute-start | bytes 786440 | tf_op jit(solution)/shard_map/ppermute | solution.py:34
  44.9 11.2 %collective-permute-start.6 = (bf16[128,1024]{1,0:T(8,128)(2,1)S(1)}, bf16[128,1024]{1,0:T(8,128)(2,1)S(1)}, u32[]{:S(2)}, u32[]{:S(2)}) collective-permute-start(bf16[128,1024]{1,0:T(8,128)(2,1)S(1)} %collective-permute-done.5), channel_id=1, source_target_pairs={{0,8},{8,16},{16,24},{24,0},{1,9},{9,17},{17,25},{25,1},{2,10},{10... | collective-permute-start | bytes 786440 | tf_op jit(solution)/shard_map/ppermute | solution.py:34
  50.6 11.2 %collective-permute-start.2 = (bf16[128,1024]{1,0:T(8,128)(2,1)S(1)}, bf16[128,1024]{1,0:T(8,128)(2,1)S(1)}, u32[]{:S(2)}, u32[]{:S(2)}) collective-permute-start(bf16[128,1024]{1,0:T(8,128)(2,1)S(1)} %collective-permute-done.1), channel_id=1, source_target_pairs={{0,8},{8,16},{16,24},{24,0},{1,9},{9,17},{17,25},{25,1},{2,10},{10... | collective-permute-start | bytes 786440 | tf_op jit(solution)/shard_map/ppermute | solution.py:34
  56.2 10.4 %collective-permute-start.7 = (bf16[128,1024]{1,0:T(8,128)(2,1)S(1)}, bf16[128,1024]{1,0:T(8,128)(2,1)S(1)}, u32[]{:S(2)}, u32[]{:S(2)}) collective-permute-start(bf16[128,1024]{1,0:T(8,128)(2,1)S(1)} %collective-permute-done.6), channel_id=1, source_target_pairs={{0,8},{8,16},{16,24},{24,0},{1,9},{9,17},{17,25},{25,1},{2,10},{10... | collective-permute-start | bytes 786440 | tf_op jit(solution)/shard_map/ppermute | solution.py:34
  62.0 23.7 %collective-permute-start.3 = (bf16[4,128,1024]{2,1,0:T(8,128)(2,1)S(1)}, bf16[4,128,1024]{2,1,0:T(8,128)(2,1)}, u32[]{:S(2)}, u32[]{:S(2)}) collective-permute-start(bf16[4,128,1024]{2,1,0:T(8,128)(2,1)S(1)} %get-tuple-element.36), channel_id=1, source_target_pairs={{0,2},{2,0},{1,3},{3,1},{4,6},{6,4},{5,7},{7,5},{8,10},{10,8},{9,1... | collective-permute-start | bytes 3145736 | tf_op jit(solution)/shard_map/ppermute | solution.py:34
  68.1 26.4 %collective-permute-start.8 = (bf16[4,128,1024]{2,1,0:T(8,128)(2,1)}, bf16[4,128,1024]{2,1,0:T(8,128)(2,1)}, u32[]{:S(2)}, u32[]{:S(2)}) collective-permute-start(bf16[4,128,1024]{2,1,0:T(8,128)(2,1)} %get-tuple-element.34), channel_id=1, source_target_pairs={{0,4},{4,0},{1,5},{5,1},{2,6},{6,2},{3,7},{7,3},{8,12},{12,8},{9,1... | collective-permute-start | bytes 3145736 | tf_op jit(solution)/shard_map/ppermute | solution.py:34
  69.6 29.9 %collective-permute-start.11 = (bf16[256,2304]{1,0:T(8,128)(2,1)}, bf16[256,2304]{1,0:T(8,128)(2,1)}, u32[]{:S(2)}, u32[]{:S(2)}) collective-permute-start(bf16[256,2304]{1,0:T(8,128)(2,1)} %collective-permute-done.10), channel_id=1, source_target_pairs={{0,8},{8,16},{16,24},{24,0},{1,9},{9,17},{17,25},{25,1},{2,10},{10... | collective-permute-start | bytes 3538952 | tf_op jit(solution)/shard_map/ppermute | solution.py:34
  88.6 49.1 %collective-permute-start.4 = (bf16[2,4,128,1024]{3,2,1,0:T(8,128)(2,1)}, bf16[2,4,128,1024]{3,2,1,0:T(8,128)(2,1)}, u32[]{:S(2)}, u32[]{:S(2)}) collective-permute-start(bf16[2,4,128,1024]{3,2,1,0:T(8,128)(2,1)} %get-tuple-element.26), channel_id=1, source_target_pairs={{0,4},{4,0},{1,5},{5,1},{2,6},{6,2},{3,7},{7,3},{8,12},{12,8},{9,1... | collective-permute-start | bytes 6291464 | tf_op jit(solution)/shard_map/ppermute | solution.py:34
  98.0 50.4 %collective-permute-start.9 = (bf16[2,4,128,1024]{3,2,1,0:T(8,128)(2,1)}, bf16[2,4,128,1024]{3,2,1,0:T(8,128)(2,1)}, u32[]{:S(2)}, u32[]{:S(2)}) collective-permute-start(bf16[2,4,128,1024]{3,2,1,0:T(8,128)(2,1)} %get-tuple-element.24), channel_id=1, source_target_pairs={{0,2},{2,0},{1,3},{3,1},{4,6},{6,4},{5,7},{7,5},{8,10},{10,8},{9,1... | collective-permute-start | bytes 6291464 | tf_op jit(solution)/shard_map/ppermute | solution.py:34
  99.5 26.6 %collective-permute-start.12 = (bf16[256,2304]{1,0:T(8,128)(2,1)}, bf16[256,2304]{1,0:T(8,128)(2,1)}, u32[]{:S(2)}, u32[]{:S(2)}) collective-permute-start(bf16[256,2304]{1,0:T(8,128)(2,1)} %collective-permute-done.11), channel_id=1, source_target_pairs={{0,8},{8,16},{16,24},{24,0},{1,9},{9,17},{17,25},{25,1},{2,10},{10... | collective-permute-start | bytes 3538952 | tf_op jit(solution)/shard_map/ppermute | solution.py:34
  175.5 2.0 collective-permute-start.13
  178.3 9.2 %collective-permute-start.14 = (bf16[128,4,256]{2,0,1:T(8,128)(2,1)S(1)}, bf16[128,4,256]{2,0,1:T(8,128)(2,1)S(1)}, u32[]{:S(2)}, u32[]{:S(2)}) collective-permute-start(bf16[128,4,256]{2,0,1:T(8,128)(2,1)S(1)} %bitcast.140), channel_id=1, source_target_pairs={{0,6},{2,0},{4,2},{6,4},{1,7},{3,1},{5,3},{7,5},{8,14},{10,8},{12,... | collective-permute-start | bytes 786440 | tf_op jit(solution)/shard_map/ppermute | solution.py:61
  180.7 13.8 %collective-permute-start.15 = (bf16[128,4,256]{2,0,1:T(8,128)(2,1)S(1)}, bf16[128,4,256]{2,0,1:T(8,128)(2,1)S(1)}, u32[]{:S(2)}, u32[]{:S(2)}) collective-permute-start(bf16[128,4,256]{2,0,1:T(8,128)(2,1)S(1)} %bitcast.141), channel_id=1, source_target_pairs={{0,4},{2,6},{4,0},{6,2},{1,5},{3,7},{5,1},{7,3},{8,12},{10,14},{12... | collective-permute-start | bytes 786440 | tf_op jit(solution)/shard_map/ppermute | solution.py:61
  181.5 13.0 %collective-permute-start.16 = (bf16[128,4,256]{2,0,1:T(8,128)(2,1)S(1)}, bf16[128,4,256]{2,0,1:T(8,128)(2,1)S(1)}, u32[]{:S(2)}, u32[]{:S(2)}) collective-permute-start(bf16[128,4,256]{2,0,1:T(8,128)(2,1)S(1)} %bitcast.142), channel_id=1, source_target_pairs={{0,2},{2,4},{4,6},{6,0},{1,3},{3,5},{5,7},{7,1},{8,10},{10,12},{12... | collective-permute-start | bytes 786440 | tf_op jit(solution)/shard_map/ppermute | solution.py:61
  202.4 29.0 %collective-permute-start.19 = (f32[128,2304]{1,0:T(8,128)S(1)}, f32[128,2304]{1,0:T(8,128)S(1)}, u32[]{:S(2)}, u32[]{:S(2)}) collective-permute-start(f32[128,2304]{1,0:T(8,128)S(1)} %get-tuple-element.17), channel_id=1, source_target_pairs={{0,6},{2,0},{4,2},{6,4},{1,7},{3,1},{5,3},{7,5},{8,14},{10,8},{12,... | collective-permute-start | bytes 3538952 | tf_op jit(solution)/shard_map/ppermute | solution.py:71
  203.0 52.5 %collective-permute-start.18 = (f32[128,2304]{1,0:T(8,128)S(1)}, f32[128,2304]{1,0:T(8,128)S(1)}, u32[]{:S(2)}, u32[]{:S(2)}) collective-permute-start(f32[128,2304]{1,0:T(8,128)S(1)} %get-tuple-element.18), channel_id=1, source_target_pairs={{0,4},{2,6},{4,0},{6,2},{1,5},{3,7},{5,1},{7,3},{8,12},{10,14},{12... | collective-permute-start | bytes 3538952 | tf_op jit(solution)/shard_map/ppermute | solution.py:71
  204.0 51.5 %collective-permute-start.17 = (f32[128,2304]{1,0:T(8,128)S(1)}, f32[128,2304]{1,0:T(8,128)S(1)}, u32[]{:S(2)}, u32[]{:S(2)}) collective-permute-start(f32[128,2304]{1,0:T(8,128)S(1)} %get-tuple-element.16), channel_id=1, source_target_pairs={{0,2},{2,4},{4,6},{6,0},{1,3},{3,5},{5,7},{7,1},{8,10},{10,12},{12... | collective-permute-start | bytes 3538952 | tf_op jit(solution)/shard_map/ppermute | solution.py:71
  259.6 3.6 %collective-permute-start.20 = (f32[16]{0:T(128)S(1)}, f32[16]{0:T(128)S(1)}, u32[]{:S(2)}, u32[]{:S(2)}) collective-permute-start(f32[16]{0:T(128)S(1)} %select_reduce_fusion), channel_id=1, source_target_pairs={{0,8},{8,0},{16,24},{24,16},{1,9},{9,1},{17,25},{25,17},{2,10},{10... | collective-permute-start | bytes 200 | tf_op jit(solution)/shard_map/ppermute | solution.py:80
  263.2 4.4 %collective-permute-start.21 = (f32[16]{0:T(128)S(1)}, f32[16]{0:T(128)S(1)}, u32[]{:S(2)}, u32[]{:S(2)}) collective-permute-start(f32[16]{0:T(128)S(1)} %add.405), channel_id=1, source_target_pairs={{0,16},{8,24},{16,0},{24,8},{1,17},{9,25},{17,1},{25,9},{2,18},{10... | collective-permute-start | bytes 200 | tf_op jit(solution)/shard_map/ppermute | solution.py:80
  267.7 3.5 %collective-permute-start.22 = (f32[16]{0:T(128)S(1)}, f32[16]{0:T(128)S(1)}, u32[]{:S(2)}, u32[]{:S(2)}) collective-permute-start(f32[16]{0:T(128)S(1)} %add.406), channel_id=1, source_target_pairs={{0,4},{4,0},{1,5},{5,1},{2,6},{6,2},{3,7},{7,3},{8,12},{12,8},{9,1... | collective-permute-start | bytes 200 | tf_op jit(solution)/shard_map/ppermute | solution.py:80
  271.2 3.5 %collective-permute-start.23 = (f32[16]{0:T(128)S(1)}, f32[16]{0:T(128)S(1)}, u32[]{:S(2)}, u32[]{:S(2)}) collective-permute-start(f32[16]{0:T(128)S(1)} %add.407), channel_id=1, source_target_pairs={{0,2},{2,0},{1,3},{3,1},{4,6},{6,4},{5,7},{7,5},{8,10},{10,8},{9,1... | collective-permute-start | bytes 200 | tf_op jit(solution)/shard_map/ppermute | solution.py:80
  (10 other events, 222.8 us)

commit v12 on v11

--- a/solution.py
+++ b/solution.py
@@ -27,23 +27,33 @@
     return jnp.sum((positions[:, None] >= doc_ends[None, :]).astype(jnp.int32), axis=1)
 
 
-def ring_gather(x, axis):
+def ring_pieces(x, axis):
     n = lax.axis_size(axis)
     pieces = [x]
     for _ in range(n - 1):
         pieces.append(lax.ppermute(pieces[-1], axis, [(k, (k + 1) % n) for k in range(n)]))
-    return jnp.stack(pieces)
+    return pieces
+
+
+def ring_gather(x, axis):
+    return jnp.stack(ring_pieces(x, axis))
 
 
 def gather_order(x, order):
     stride = {"c2": 1, "c1": lax.axis_size("c2"), "c0": lax.axis_size("c1") * lax.axis_size("c2")}
     source = jnp.zeros((), jnp.int32)
-    for axis in order:
+    for axis in order[:-1]:
         x = ring_gather(x, axis)
         n = lax.axis_size(axis)
         came = (lax.axis_index(axis) - jnp.arange(n, dtype=jnp.int32)) % n
         source = came.reshape((n,) + (1,) * source.ndim) * stride[axis] + source[None]
-    return x, source.reshape(-1)
+    last = order[-1]
+    n = lax.axis_size(last)
+    own = lax.axis_index(last)
+    return [
+        (piece, (((own - t) % n) * stride[last] + source).reshape(-1))
+        for t, piece in enumerate(ring_pieces(x, last))
+    ]
 
 
 def ring_all_gather(x, axis):
@@ -127,16 +137,11 @@
             denominator = denominator + jnp.sum(weights, axis=-1)
             return (numerator, denominator)
 
-        if count == n_ctx * tok_dev:
+        if count <= span:
             return compute(state)
         return lax.cond(jnp.any(visible), compute, lambda carry: carry, state)
 
-    def attend(q_part, key_piece, value_piece, key_rows):
-        heads = q_part.shape[1]
-        state = (
-            jnp.zeros((heads, group_repeat, tok_dev, HEAD_WIDTH), jnp.float32),
-            jnp.zeros((heads, group_repeat, tok_dev), jnp.float32),
-        )
+    def attend(state, q_part, key_piece, value_piece, key_rows):
         count = key_piece.shape[0]
         if count <= span:
             return attend_block(state, q_part, key_piece, value_piece, key_rows)
@@ -167,17 +172,24 @@
         if last == first:
             continue
         cols = slice(first * HEAD_WIDTH, last * HEAD_WIDTH)
-        got, source = gather_order(jnp.concatenate([keys[:, cols], values[:, cols]], axis=1), order)
-        key_rows = (source[:, None] * tok_dev + jnp.arange(tok_dev, dtype=jnp.int32)[None, :]).reshape(-1)
-        gathered.append((got.reshape(n_ctx * tok_dev, -1), key_rows))
-        bounds.append((first, last))
+        for got, source in gather_order(jnp.concatenate([keys[:, cols], values[:, cols]], axis=1), order):
+            key_rows = (source[:, None] * tok_dev + jnp.arange(tok_dev, dtype=jnp.int32)[None, :]).reshape(-1)
+            gathered.append((got.reshape(key_rows.shape[0], -1), key_rows))
+            bounds.append((first, last))
     gathered, weight_rows = lax.optimization_barrier((gathered, weight_rows))
     numerators, denominators = [], []
+    states = {}
     for (first, last), (got, key_rows) in zip(bounds, gathered):
         width = (last - first) * HEAD_WIDTH
-        numerator, denominator = attend(q_groups[:, first:last], got[:, :width], got[:, width:], key_rows)
-        numerators.append(numerator)
-        denominators.append(denominator)
+        q_part = q_groups[:, first:last]
+        state = states.get((first, last), (
+            jnp.zeros((last - first, group_repeat, tok_dev, HEAD_WIDTH), jnp.float32),
+            jnp.zeros((last - first, group_repeat, tok_dev), jnp.float32),
+        ))
+        states[(first, last)] = attend(state, q_part, got[:, :width], got[:, width:], key_rows)
+    for key in sorted(states):
+        numerators.append(states[key][0])
+        denominators.append(states[key][1])
     numerator = jnp.concatenate(numerators, axis=0)
     denominator = jnp.concatenate(denominators, axis=0)
     attended = (numerator / denominator[..., None]).astype(jnp.bfloat16)

time: 277 us -> 265 us (0.957)
  other arithmetic: 25.7 us -> 15.2 us
    another operation x12 -> x10, other arithmetic: 20.4 us -> 10 us  [the longest x8 9.88 us: ring_gather(): return jnp.stack(ring_pieces(x, axis))]
    dot_general x2 -> x4, matrix products: 5.31 us -> 5.76 us  [compute(): jnp.einsum('qgrd,kgd->grqk', q_part, key_piece.reshape(count, heads, HEAD...]
    reshape x2 -> x4, local copies, waits for them, and re-layouts: 13.2 us -> 13.3 us  [shards(): gathered.append((got.reshape(key_rows.shape[0], -1), key_rows))]
  transfers between devices with their start and end apart: 25 -> 25, of which waited for: 20 -> 21; matrix products, arithmetic and copies ran while one was open for 9% -> 8% of each run, Pallas kernels for 0% -> 0%
where the time goes in v12:
time: 265 us; the launch traced here: 264 us
  waiting for transfers between devices  184 us (69%)
  local copies, waits for them, and re-layouts  23.7 us (9%)
  starting transfers between devices  21.4 us (8%)
  matrix products  16.2 us (6%)
  other arithmetic  15.2 us (6%)
    ppermute x14, waiting for transfers between devices, ring_pieces(): lax.ppermute(pieces[-1], axis, [(k, (k + 1) % n) for k in range(n)])  108 us
    ppermute x3, waiting for transfers between devices, permute_reduce_scatter(): lax.ppermute(sent, axes, [(k, (k + shift) % n) for k in range(n)])  50.5 us
    ppermute x5, waiting for transfers between devices, butterfly_sum(): x = x + lax.ppermute(x, axis, [(i, i ^ bit) for i in range(size)])  13.4 us
    reshape x4, local copies, waits for them, and re-layouts, shards(): gathered.append((got.reshape(key_rows.shape[0], -1), key_rows))  13.3 us
    ppermute x14, starting transfers between devices, ring_pieces(): lax.ppermute(pieces[-1], axis, [(k, (k + 1) % n) for k in range(n)])  12.7 us
    ppermute x3, waiting for transfers between devices, permute_all_to_all(): lax.ppermute(sent, axes, [(k, (k + shift) % n) for k in range(n)])  12.2 us
    another operation x8, other arithmetic, ring_gather(): return jnp.stack(ring_pieces(x, axis))  9.88 us
    dot_general x4, matrix products, compute(): jnp.einsum('qgrd,kgd->grqk', q_part, key_piece.reshape(count, heads, HEAD...  5.76 us
  transfers between devices with their start and end apart: 25, of which 21 were waited for; matrix products, arithmetic and copies ran while one was open for 8% of the time, Pallas kernels for 0%

profile of v12, /device:TPU:0, one launch (start us, length us, event | category | flops | bytes accessed | tf_op | source)
XLA Modules:
  0.0 264.0 jit_solution(13893518603766595592)
XLA Ops:
  2.7 3.1 %collective-permute-start = (bf16[128,1024]{1,0:T(8,128)(2,1)S(1)}, bf16[128,1024]{1,0:T(8,128)(2,1)S(1)}, u32[]{:S(2)}, u32[]{:S(2)}) collective-permute-start(bf16[128,1024]{1,0:T(8,128)(2,1)S(1)} %get-tuple-element.54), channel_id=1, source_target_pairs={{0,8},{8,16},{16,24},{24,0},{1,9},{9,17},{17,25},{25,1},{2,10},{10... | collective-permute-start | bytes 786440 | tf_op jit(solution)/shard_map/ppermute | solution.py:34
  9.0 5.9 %collective-permute-done = bf16[128,1024]{1,0:T(8,128)(2,1)S(1)} collective-permute-done((bf16[128,1024]{1,0:T(8,128)(2,1)S(1)}, bf16[128,1024]{1,0:T(8,128)(2,1)S(1)}, u32[]{:S(2)}, u32[]{:S(2)}) %collective-permute-start) | collective-permute-done | bytes 262176 | tf_op jit(solution)/shard_map/ppermute | solution.py:34
  14.9 5.6 %collective-permute-done.5 = bf16[128,1024]{1,0:T(8,128)(2,1)S(1)} collective-permute-done((bf16[128,1024]{1,0:T(8,128)(2,1)S(1)}, bf16[128,1024]{1,0:T(8,128)(2,1)S(1)}, u32[]{:S(2)}, u32[]{:S(2)}) %collective-permute-start.5) | collective-permute-done | bytes 262176 | tf_op jit(solution)/shard_map/ppermute | solution.py:34
  20.5 30.9 %collective-permute-done.1 = bf16[128,1024]{1,0:T(8,128)(2,1)S(1)} collective-permute-done((bf16[128,1024]{1,0:T(8,128)(2,1)S(1)}, bf16[128,1024]{1,0:T(8,128)(2,1)S(1)}, u32[]{:S(2)}, u32[]{:S(2)}) %collective-permute-start.1) | collective-permute-done | bytes 262176 | tf_op jit(solution)/shard_map/ppermute | solution.py:34
  51.4 5.6 %collective-permute-done.6 = bf16[128,1024]{1,0:T(8,128)(2,1)S(1)} collective-permute-done((bf16[128,1024]{1,0:T(8,128)(2,1)S(1)}, bf16[128,1024]{1,0:T(8,128)(2,1)S(1)}, u32[]{:S(2)}, u32[]{:S(2)}) %collective-permute-start.6) | collective-permute-done | bytes 262176 | tf_op jit(solution)/shard_map/ppermute | solution.py:34
  57.1 5.6 %collective-permute-done.2 = bf16[128,1024]{1,0:T(8,128)(2,1)S(1)} collective-permute-done((bf16[128,1024]{1,0:T(8,128)(2,1)S(1)}, bf16[128,1024]{1,0:T(8,128)(2,1)S(1)}, u32[]{:S(2)}, u32[]{:S(2)}) %collective-permute-start.2) | collective-permute-done | bytes 262176 | tf_op jit(solution)/shard_map/ppermute | solution.py:34
  64.6 2.8 %collective-permute-done.7 = bf16[128,1024]{1,0:T(8,128)(2,1)S(1)} collective-permute-done((bf16[128,1024]{1,0:T(8,128)(2,1)S(1)}, bf16[128,1024]{1,0:T(8,128)(2,1)S(1)}, u32[]{:S(2)}, u32[]{:S(2)}) %collective-permute-start.7) | collective-permute-done | bytes 262176 | tf_op jit(solution)/shard_map/ppermute | solution.py:34
  70.5 16.1 %collective-permute-done.3 = bf16[4,128,1024]{2,1,0:T(8,128)(2,1)} collective-permute-done((bf16[4,128,1024]{2,1,0:T(8,128)(2,1)S(1)}, bf16[4,128,1024]{2,1,0:T(8,128)(2,1)}, u32[]{:S(2)}, u32[]{:S(2)}) %collective-permute-start.3) | collective-permute-done | bytes 1048608 | tf_op jit(solution)/shard_map/ppermute | solution.py:34
  89.3 6.0 %collective-permute-done.8 = bf16[4,128,1024]{2,1,0:T(8,128)(2,1)} collective-permute-done((bf16[4,128,1024]{2,1,0:T(8,128)(2,1)}, bf16[4,128,1024]{2,1,0:T(8,128)(2,1)}, u32[]{:S(2)}, u32[]{:S(2)}) %collective-permute-start.8) | collective-permute-done | bytes 1048608 | tf_op jit(solution)/shard_map/ppermute | solution.py:34
  95.3 2.8 %pad_maximum_fusion.2 = bf16[2,4,128,1024]{3,2,1,0:T(8,128)(2,1)} fusion(bf16[1,4,128,1024]{3,2,1,0:T(8,128)(2,1)} %bitcast.16, bf16[1,4,128,1024]{3,2,1,0:T(8,128)(2,1)S(1)} %copy-done.1), kind=kLoop, calls=%fused_computation.15 | loop fusion | flops 1048576 | bytes 4194304 | tf_op jit(solution)/shard_map/stack | solution.py:39
  104.3 3.9 %copy.95 = bf16[1024,1024]{0,1:T(8,128)(2,1)} copy(bf16[1024,1024]{1,0:T(8,128)(2,1)} %bitcast.17) | data formatting | bytes 4194304 | tf_op jit(solution)/shard_map/reshape | solution.py:177
  108.3 18.7 %collective-permute-done.12 = bf16[256,2304]{1,0:T(8,128)(2,1)} collective-permute-done((bf16[256,2304]{1,0:T(8,128)(2,1)}, bf16[256,2304]{1,0:T(8,128)(2,1)}, u32[]{:S(2)}, u32[]{:S(2)}) %collective-permute-start.12) | collective-permute-done | bytes 1179680 | tf_op jit(solution)/shard_map/ppermute | solution.py:34
  127.0 3.9 %pad_maximum_fusion = bf16[4,256,2304]{2,1,0:T(8,128)(2,1)} fusion(bf16[1,256,2304]{2,1,0:T(8,128)(2,1)} %bitcast.24, bf16[1,256,2304]{2,1,0:T(8,128)(2,1)} %bitcast.23, bf16[1,256,2304]{2,1,0:T(8,128)(2,1)} %bitcast.22, bf16[1,256,2304]{2,1,0:T(8,128)(2,1)S(1)} %bitcast.167), kind=kLoop, calls=%fused_computation.1 | loop fusion | flops 7077888 | bytes 9437184 | tf_op jit(solution)/shard_map/stack | solution.py:39
  130.9 7.7 %collective-permute-done.4 = bf16[2,4,128,1024]{3,2,1,0:T(8,128)(2,1)} collective-permute-done((bf16[2,4,128,1024]{3,2,1,0:T(8,128)(2,1)S(1)}, bf16[2,4,128,1024]{3,2,1,0:T(8,128)(2,1)}, u32[]{:S(2)}, u32[]{:S(2)}) %collective-permute-start.4) | collective-permute-done | bytes 2097184 | tf_op jit(solution)/shard_map/ppermute | solution.py:34
  138.5 2.9 %copy.94 = bf16[1024,1024]{0,1:T(8,128)(2,1)S(1)} copy(bf16[1024,1024]{1,0:T(8,128)(2,1)} %bitcast.9) | data formatting | bytes 4194304 | tf_op jit(solution)/shard_map/reshape | solution.py:177
  142.6 4.0 %copy.96 = bf16[1024,1024]{0,1:T(8,128)(2,1)} copy(bf16[1024,1024]{1,0:T(8,128)(2,1)} %bitcast.19) | data formatting | bytes 4194304 | tf_op jit(solution)/shard_map/reshape | solution.py:177
  146.5 2.7 %fusion.90 = (bf16[1024,512]{0,1:T(8,128)(2,1)S(1)}, bf16[1024,512]{0,1:T(8,128)(2,1)S(1)}, bf16[1024,512]{0,1:T(8,128)(2,1)S(1)}, bf16[1024,512]{0,1:T(8,128)(2,1)S(1)}) fusion(bf16[1024,1024]{0,1:T(8,128)(2,1)} %copy.95, bf16[1024,1024]{0,1:T(8,128)(2,1)} %copy.96), kind=kLoop, calls=%fused_computation.207 | loop fusion | bytes 8388608 | tf_op jit(solution)/shard_map/slice | solution.py:189
  169.8 5.5 %collective-permute-done.14 = bf16[128,4,256]{2,0,1:T(8,128)(2,1)S(1)} collective-permute-done((bf16[128,4,256]{2,0,1:T(8,128)(2,1)S(1)}, bf16[128,4,256]{2,0,1:T(8,128)(2,1)S(1)}, u32[]{:S(2)}, u32[]{:S(2)}) %collective-permute-start.14) | collective-permute-done | bytes 262176 | tf_op jit(solution)/shard_map/ppermute | solution.py:71
  175.3 6.7 %collective-permute-done.15 = bf16[128,4,256]{2,0,1:T(8,128)(2,1)S(1)} collective-permute-done((bf16[128,4,256]{2,0,1:T(8,128)(2,1)S(1)}, bf16[128,4,256]{2,0,1:T(8,128)(2,1)S(1)}, u32[]{:S(2)}, u32[]{:S(2)}) %collective-permute-start.15) | collective-permute-done | bytes 262176 | tf_op jit(solution)/shard_map/ppermute | solution.py:71
  184.7 4.9 %fusion.94 = f32[4,128,2304]{2,1,0:T(8,128)S(1)} fusion(bf16[4,128,1024]{2,1,0:T(8,128)(2,1)S(1)} %select_n.301, bf16[1024,2304,1]{1,0,2:T(8,128)(2,1)} %bitcast.162), kind=kOutput, calls=%fused_computation.211 | convolution fusion | flops 2415919104 | bytes 10485760 | tf_op jit(solution)/shard_map/dot_general | solution.py:202
  192.6 26.4 %collective-permute-done.19 = f32[128,2304]{1,0:T(8,128)S(1)} collective-permute-done((f32[128,2304]{1,0:T(8,128)S(1)}, f32[128,2304]{1,0:T(8,128)S(1)}, u32[]{:S(2)}, u32[]{:S(2)}) %collective-permute-start.19) | collective-permute-done | bytes 1179680 | tf_op jit(solution)/shard_map/ppermute | solution.py:81
  219.0 24.1 %collective-permute-done.18 = f32[128,2304]{1,0:T(8,128)S(1)} collective-permute-done((f32[128,2304]{1,0:T(8,128)S(1)}, f32[128,2304]{1,0:T(8,128)S(1)}, u32[]{:S(2)}, u32[]{:S(2)}) %collective-permute-start.18) | collective-permute-done | bytes 1179680 | tf_op jit(solution)/shard_map/ppermute | solution.py:81
  247.3 3.5 %collective-permute-done.20 = f32[16]{0:T(128)S(1)} collective-permute-done((f32[16]{0:T(128)S(1)}, f32[16]{0:T(128)S(1)}, u32[]{:S(2)}, u32[]{:S(2)}) %collective-permute-start.20) | collective-permute-done | bytes 96 | tf_op jit(solution)/shard_map/ppermute | solution.py:90
  251.4 3.8 %collective-permute-done.21 = f32[16]{0:T(128)S(1)} collective-permute-done((f32[16]{0:T(128)S(1)}, f32[16]{0:T(128)S(1)}, u32[]{:S(2)}, u32[]{:S(2)}) %collective-permute-start.21) | collective-permute-done | bytes 96 | tf_op jit(solution)/shard_map/ppermute | solution.py:90
  (129 shorter events, 59.9 us)
Async XLA Ops:
  2.7 12.2 %collective-permute-start = (bf16[128,1024]{1,0:T(8,128)(2,1)S(1)}, bf16[128,1024]{1,0:T(8,128)(2,1)S(1)}, u32[]{:S(2)}, u32[]{:S(2)}) collective-permute-start(bf16[128,1024]{1,0:T(8,128)(2,1)S(1)} %get-tuple-element.54), channel_id=1, source_target_pairs={{0,8},{8,16},{16,24},{24,0},{1,9},{9,17},{17,25},{25,1},{2,10},{10... | collective-permute-start | bytes 786440 | tf_op jit(solution)/shard_map/ppermute | solution.py:34
  5.8 14.7 %collective-permute-start.5 = (bf16[128,1024]{1,0:T(8,128)(2,1)S(1)}, bf16[128,1024]{1,0:T(8,128)(2,1)S(1)}, u32[]{:S(2)}, u32[]{:S(2)}) collective-permute-start(bf16[128,1024]{1,0:T(8,128)(2,1)S(1)} %get-tuple-element.48), channel_id=1, source_target_pairs={{0,8},{8,16},{16,24},{24,0},{1,9},{9,17},{17,25},{25,1},{2,10},{10... | collective-permute-start | bytes 786440 | tf_op jit(solution)/shard_map/ppermute | solution.py:34
  7.4 63.0 %collective-permute-start.10 = (bf16[256,2304]{1,0:T(8,128)(2,1)}, bf16[256,2304]{1,0:T(8,128)(2,1)}, u32[]{:S(2)}, u32[]{:S(2)}) collective-permute-start(bf16[256,2304]{1,0:T(8,128)(2,1)} %param.12), channel_id=1, source_target_pairs={{0,8},{8,16},{16,24},{24,0},{1,9},{9,17},{17,25},{25,1},{2,10},{10... | collective-permute-start | bytes 3538952 | tf_op jit(solution)/shard_map/ppermute | solution.py:34
  14.9 36.5 %collective-permute-start.1 = (bf16[128,1024]{1,0:T(8,128)(2,1)S(1)}, bf16[128,1024]{1,0:T(8,128)(2,1)S(1)}, u32[]{:S(2)}, u32[]{:S(2)}) collective-permute-start(bf16[128,1024]{1,0:T(8,128)(2,1)S(1)} %collective-permute-done), channel_id=1, source_target_pairs={{0,8},{8,16},{16,24},{24,0},{1,9},{9,17},{17,25},{25,1},{2,10},{10... | collective-permute-start | bytes 786440 | tf_op jit(solution)/shard_map/ppermute | solution.py:34
  20.5 36.5 %collective-permute-start.6 = (bf16[128,1024]{1,0:T(8,128)(2,1)S(1)}, bf16[128,1024]{1,0:T(8,128)(2,1)S(1)}, u32[]{:S(2)}, u32[]{:S(2)}) collective-permute-start(bf16[128,1024]{1,0:T(8,128)(2,1)S(1)} %collective-permute-done.5), channel_id=1, source_target_pairs={{0,8},{8,16},{16,24},{24,0},{1,9},{9,17},{17,25},{25,1},{2,10},{10... | collective-permute-start | bytes 786440 | tf_op jit(solution)/shard_map/ppermute | solution.py:34
  51.4 11.2 %collective-permute-start.2 = (bf16[128,1024]{1,0:T(8,128)(2,1)S(1)}, bf16[128,1024]{1,0:T(8,128)(2,1)S(1)}, u32[]{:S(2)}, u32[]{:S(2)}) collective-permute-start(bf16[128,1024]{1,0:T(8,128)(2,1)S(1)} %collective-permute-done.1), channel_id=1, source_target_pairs={{0,8},{8,16},{16,24},{24,0},{1,9},{9,17},{17,25},{25,1},{2,10},{10... | collective-permute-start | bytes 786440 | tf_op jit(solution)/shard_map/ppermute | solution.py:34
  57.0 10.4 %collective-permute-start.7 = (bf16[128,1024]{1,0:T(8,128)(2,1)S(1)}, bf16[128,1024]{1,0:T(8,128)(2,1)S(1)}, u32[]{:S(2)}, u32[]{:S(2)}) collective-permute-start(bf16[128,1024]{1,0:T(8,128)(2,1)S(1)} %collective-permute-done.6), channel_id=1, source_target_pairs={{0,8},{8,16},{16,24},{24,0},{1,9},{9,17},{17,25},{25,1},{2,10},{10... | collective-permute-start | bytes 786440 | tf_op jit(solution)/shard_map/ppermute | solution.py:34
  62.8 23.7 %collective-permute-start.3 = (bf16[4,128,1024]{2,1,0:T(8,128)(2,1)S(1)}, bf16[4,128,1024]{2,1,0:T(8,128)(2,1)}, u32[]{:S(2)}, u32[]{:S(2)}) collective-permute-start(bf16[4,128,1024]{2,1,0:T(8,128)(2,1)S(1)} %get-tuple-element.46), channel_id=1, source_target_pairs={{0,2},{2,0},{1,3},{3,1},{4,6},{6,4},{5,7},{7,5},{8,10},{10,8},{9,1... | collective-permute-start | bytes 3145736 | tf_op jit(solution)/shard_map/ppermute | solution.py:34
  68.9 26.4 %collective-permute-start.8 = (bf16[4,128,1024]{2,1,0:T(8,128)(2,1)}, bf16[4,128,1024]{2,1,0:T(8,128)(2,1)}, u32[]{:S(2)}, u32[]{:S(2)}) collective-permute-start(bf16[4,128,1024]{2,1,0:T(8,128)(2,1)} %get-tuple-element.44), channel_id=1, source_target_pairs={{0,4},{4,0},{1,5},{5,1},{2,6},{6,2},{3,7},{7,3},{8,12},{12,8},{9,1... | collective-permute-start | bytes 3145736 | tf_op jit(solution)/shard_map/ppermute | solution.py:34
  70.4 29.2 %collective-permute-start.11 = (bf16[256,2304]{1,0:T(8,128)(2,1)}, bf16[256,2304]{1,0:T(8,128)(2,1)}, u32[]{:S(2)}, u32[]{:S(2)}) collective-permute-start(bf16[256,2304]{1,0:T(8,128)(2,1)} %collective-permute-done.10), channel_id=1, source_target_pairs={{0,8},{8,16},{16,24},{24,0},{1,9},{9,17},{17,25},{25,1},{2,10},{10... | collective-permute-start | bytes 3538952 | tf_op jit(solution)/shard_map/ppermute | solution.py:34
  88.0 50.6 %collective-permute-start.4 = (bf16[2,4,128,1024]{3,2,1,0:T(8,128)(2,1)S(1)}, bf16[2,4,128,1024]{3,2,1,0:T(8,128)(2,1)}, u32[]{:S(2)}, u32[]{:S(2)}) collective-permute-start(bf16[2,4,128,1024]{3,2,1,0:T(8,128)(2,1)S(1)} %pad_maximum_fusion.1), channel_id=1, source_target_pairs={{0,4},{4,0},{1,5},{5,1},{2,6},{6,2},{3,7},{7,3},{8,12},{12,8},{9,1... | collective-permute-start | bytes 6291464 | tf_op jit(solution)/shard_map/ppermute | solution.py:34
  98.1 44.5 %collective-permute-start.9 = (bf16[2,4,128,1024]{3,2,1,0:T(8,128)(2,1)}, bf16[2,4,128,1024]{3,2,1,0:T(8,128)(2,1)}, u32[]{:S(2)}, u32[]{:S(2)}) collective-permute-start(bf16[2,4,128,1024]{3,2,1,0:T(8,128)(2,1)} %pad_maximum_fusion.2), channel_id=1, source_target_pairs={{0,2},{2,0},{1,3},{3,1},{4,6},{6,4},{5,7},{7,5},{8,10},{10,8},{9,1... | collective-permute-start | bytes 6291464 | tf_op jit(solution)/shard_map/ppermute | solution.py:34
  99.6 27.4 %collective-permute-start.12 = (bf16[256,2304]{1,0:T(8,128)(2,1)}, bf16[256,2304]{1,0:T(8,128)(2,1)}, u32[]{:S(2)}, u32[]{:S(2)}) collective-permute-start(bf16[256,2304]{1,0:T(8,128)(2,1)} %collective-permute-done.11), channel_id=1, source_target_pairs={{0,8},{8,16},{16,24},{24,0},{1,9},{9,17},{17,25},{25,1},{2,10},{10... | collective-permute-start | bytes 3538952 | tf_op jit(solution)/shard_map/ppermute | solution.py:34
  163.1 2.0 collective-permute-start.13
  166.1 9.2 %collective-permute-start.14 = (bf16[128,4,256]{2,0,1:T(8,128)(2,1)S(1)}, bf16[128,4,256]{2,0,1:T(8,128)(2,1)S(1)}, u32[]{:S(2)}, u32[]{:S(2)}) collective-permute-start(bf16[128,4,256]{2,0,1:T(8,128)(2,1)S(1)} %bitcast.187), channel_id=1, source_target_pairs={{0,6},{2,0},{4,2},{6,4},{1,7},{3,1},{5,3},{7,5},{8,14},{10,8},{12,... | collective-permute-start | bytes 786440 | tf_op jit(solution)/shard_map/ppermute | solution.py:71
  168.3 13.8 %collective-permute-start.15 = (bf16[128,4,256]{2,0,1:T(8,128)(2,1)S(1)}, bf16[128,4,256]{2,0,1:T(8,128)(2,1)S(1)}, u32[]{:S(2)}, u32[]{:S(2)}) collective-permute-start(bf16[128,4,256]{2,0,1:T(8,128)(2,1)S(1)} %bitcast.188), channel_id=1, source_target_pairs={{0,4},{2,6},{4,0},{6,2},{1,5},{3,7},{5,1},{7,3},{8,12},{10,14},{12... | collective-permute-start | bytes 786440 | tf_op jit(solution)/shard_map/ppermute | solution.py:71
  169.0 13.0 %collective-permute-start.16 = (bf16[128,4,256]{2,0,1:T(8,128)(2,1)S(1)}, bf16[128,4,256]{2,0,1:T(8,128)(2,1)S(1)}, u32[]{:S(2)}, u32[]{:S(2)}) collective-permute-start(bf16[128,4,256]{2,0,1:T(8,128)(2,1)S(1)} %bitcast.189), channel_id=1, source_target_pairs={{0,2},{2,4},{4,6},{6,0},{1,3},{3,5},{5,7},{7,1},{8,10},{10,12},{12... | collective-permute-start | bytes 786440 | tf_op jit(solution)/shard_map/ppermute | solution.py:71
  190.0 29.0 %collective-permute-start.19 = (f32[128,2304]{1,0:T(8,128)S(1)}, f32[128,2304]{1,0:T(8,128)S(1)}, u32[]{:S(2)}, u32[]{:S(2)}) collective-permute-start(f32[128,2304]{1,0:T(8,128)S(1)} %get-tuple-element.27), channel_id=1, source_target_pairs={{0,6},{2,0},{4,2},{6,4},{1,7},{3,1},{5,3},{7,5},{8,14},{10,8},{12,... | collective-permute-start | bytes 3538952 | tf_op jit(solution)/shard_map/ppermute | solution.py:81
  190.6 52.5 %collective-permute-start.18 = (f32[128,2304]{1,0:T(8,128)S(1)}, f32[128,2304]{1,0:T(8,128)S(1)}, u32[]{:S(2)}, u32[]{:S(2)}) collective-permute-start(f32[128,2304]{1,0:T(8,128)S(1)} %get-tuple-element.28), channel_id=1, source_target_pairs={{0,4},{2,6},{4,0},{6,2},{1,5},{3,7},{5,1},{7,3},{8,12},{10,14},{12... | collective-permute-start | bytes 3538952 | tf_op jit(solution)/shard_map/ppermute | solution.py:81
  191.6 51.5 %collective-permute-start.17 = (f32[128,2304]{1,0:T(8,128)S(1)}, f32[128,2304]{1,0:T(8,128)S(1)}, u32[]{:S(2)}, u32[]{:S(2)}) collective-permute-start(f32[128,2304]{1,0:T(8,128)S(1)} %get-tuple-element.26), channel_id=1, source_target_pairs={{0,2},{2,4},{4,6},{6,0},{1,3},{3,5},{5,7},{7,1},{8,10},{10,12},{12... | collective-permute-start | bytes 3538952 | tf_op jit(solution)/shard_map/ppermute | solution.py:81
  247.2 3.6 %collective-permute-start.20 = (f32[16]{0:T(128)S(1)}, f32[16]{0:T(128)S(1)}, u32[]{:S(2)}, u32[]{:S(2)}) collective-permute-start(f32[16]{0:T(128)S(1)} %select_reduce_fusion), channel_id=1, source_target_pairs={{0,8},{8,0},{16,24},{24,16},{1,9},{9,1},{17,25},{25,17},{2,10},{10... | collective-permute-start | bytes 200 | tf_op jit(solution)/shard_map/ppermute | solution.py:90
  250.8 4.4 %collective-permute-start.21 = (f32[16]{0:T(128)S(1)}, f32[16]{0:T(128)S(1)}, u32[]{:S(2)}, u32[]{:S(2)}) collective-permute-start(f32[16]{0:T(128)S(1)} %add.523), channel_id=1, source_target_pairs={{0,16},{8,24},{16,0},{24,8},{1,17},{9,25},{17,1},{25,9},{2,18},{10... | collective-permute-start | bytes 200 | tf_op jit(solution)/shard_map/ppermute | solution.py:90
  255.3 3.5 %collective-permute-start.22 = (f32[16]{0:T(128)S(1)}, f32[16]{0:T(128)S(1)}, u32[]{:S(2)}, u32[]{:S(2)}) collective-permute-start(f32[16]{0:T(128)S(1)} %add.524), channel_id=1, source_target_pairs={{0,4},{4,0},{1,5},{5,1},{2,6},{6,2},{3,7},{7,3},{8,12},{12,8},{9,1... | collective-permute-start | bytes 200 | tf_op jit(solution)/shard_map/ppermute | solution.py:90
  258.8 3.5 %collective-permute-start.23 = (f32[16]{0:T(128)S(1)}, f32[16]{0:T(128)S(1)}, u32[]{:S(2)}, u32[]{:S(2)}) collective-permute-start(f32[16]{0:T(128)S(1)} %add.525), channel_id=1, source_target_pairs={{0,2},{2,0},{1,3},{3,1},{4,6},{6,4},{5,7},{7,5},{8,10},{10,8},{9,1... | collective-permute-start | bytes 200 | tf_op jit(solution)/shard_map/ppermute | solution.py:90
  (10 other events, 251.2 us)

commit v13 on v12

--- a/solution.py
+++ b/solution.py
@@ -203,13 +203,22 @@
         regrouped.reshape(inner * tok_dev, outer * rows_each), weight_rows, preferred_element_type=jnp.float32
     )
     mixed = permute_reduce_scatter(partial.reshape(inner, tok_dev, -1), INNER)
-    squares = lax.psum(jnp.sum(mixed * mixed, axis=1), "head")
-    normed = mixed / jnp.sqrt(squares / D + 1e-06)[:, None]
-    out32 = hidden_in.astype(jnp.float32) + normed * out_gain[None, :]
-    tok_reward = jnp.sum(out32 * reward_weight[None, :], axis=1)
+    hidden = hidden_in.astype(jnp.float32)
+    sums = lax.psum(
+        jnp.stack([
+            jnp.sum(mixed * mixed, axis=1),
+            jnp.sum(hidden * reward_weight[None, :], axis=1),
+            jnp.sum(mixed * (out_gain * reward_weight)[None, :], axis=1),
+        ]),
+        "head",
+    )
+    rms = jnp.sqrt(sums[0] / D + 1e-06)
+    normed = mixed / rms[:, None]
+    out32 = hidden + normed * out_gain[None, :]
+    tok_reward = sums[1] + sums[2] / rms
     onehot = (query_doc[:, None] == jnp.arange(NDOC, dtype=jnp.int32)[None, :]).astype(jnp.float32)
     partial_sums = jnp.sum(onehot * tok_reward[:, None], axis=0)
-    totals = butterfly_sum(partial_sums, CTX + ("head",))
+    totals = butterfly_sum(partial_sums, CTX)
     rewards = totals / jnp.sqrt(doc_lengths.astype(jnp.float32))
     return (out32.astype(jnp.bfloat16), rewards)
 

time: 265 us -> 262 us (0.989)
    ppermute x5 -> x4, waiting for transfers between devices: 13.4 us -> 11.2 us  [butterfly_sum(): x = x + lax.ppermute(x, axis, [(i, i ^ bit) for i in range(size)])]
  transfers between devices with their start and end apart: 25 -> 24, of which waited for: 21 -> 20; matrix products, arithmetic and copies ran while one was open for 8% -> 9% of each run, Pallas kernels for 0% -> 0%
where the time goes in v13:
time: 262 us
  waiting for transfers between devices  182 us (69%)
  local copies, waits for them, and re-layouts  23.7 us (9%)
  starting transfers between devices  21.3 us (8%)
  matrix products  16.2 us (6%)
  other arithmetic  15.5 us (6%)
    ppermute x14, waiting for transfers between devices, ring_pieces(): lax.ppermute(pieces[-1], axis, [(k, (k + 1) % n) for k in range(n)])  108 us
    ppermute x3, waiting for transfers between devices, permute_reduce_scatter(): lax.ppermute(sent, axes, [(k, (k + shift) % n) for k in range(n)])  50.3 us
    reshape x4, local copies, waits for them, and re-layouts, shards(): gathered.append((got.reshape(key_rows.shape[0], -1), key_rows))  13.3 us
    ppermute x14, starting transfers between devices, ring_pieces(): lax.ppermute(pieces[-1], axis, [(k, (k + 1) % n) for k in range(n)])  12.7 us
    ppermute x3, waiting for transfers between devices, permute_all_to_all(): lax.ppermute(sent, axes, [(k, (k + shift) % n) for k in range(n)])  12.2 us
    ppermute x4, waiting for transfers between devices, butterfly_sum(): x = x + lax.ppermute(x, axis, [(i, i ^ bit) for i in range(size)])  11.2 us
    another operation x8, other arithmetic, ring_gather(): return jnp.stack(ring_pieces(x, axis))  9.94 us
    dot_general x4, matrix products, compute(): jnp.einsum('qgrd,kgd->grqk', q_part, key_piece.reshape(count, heads, HEAD...  5.76 us
  transfers between devices with their start and end apart: 24, of which 20 were waited for; matrix products, arithmetic and copies ran while one was open for 9% of the time, Pallas kernels for 0%

profile of v13, /device:TPU:0, one launch (start us, length us, event | category | flops | bytes accessed | tf_op | source)
XLA Modules:
  0.0 261.9 jit_solution(16325915447663655393)
XLA Ops:
  2.7 3.1 %collective-permute-start = (bf16[128,1024]{1,0:T(8,128)(2,1)S(1)}, bf16[128,1024]{1,0:T(8,128)(2,1)S(1)}, u32[]{:S(2)}, u32[]{:S(2)}) collective-permute-start(bf16[128,1024]{1,0:T(8,128)(2,1)S(1)} %get-tuple-element.53), channel_id=1, source_target_pairs={{0,8},{8,16},{16,24},{24,0},{1,9},{9,17},{17,25},{25,1},{2,10},{10... | collective-permute-start | bytes 786440 | tf_op jit(solution)/shard_map/ppermute | solution.py:34
  9.0 5.9 %collective-permute-done = bf16[128,1024]{1,0:T(8,128)(2,1)S(1)} collective-permute-done((bf16[128,1024]{1,0:T(8,128)(2,1)S(1)}, bf16[128,1024]{1,0:T(8,128)(2,1)S(1)}, u32[]{:S(2)}, u32[]{:S(2)}) %collective-permute-start) | collective-permute-done | bytes 262176 | tf_op jit(solution)/shard_map/ppermute | solution.py:34
  14.9 5.6 %collective-permute-done.5 = bf16[128,1024]{1,0:T(8,128)(2,1)S(1)} collective-permute-done((bf16[128,1024]{1,0:T(8,128)(2,1)S(1)}, bf16[128,1024]{1,0:T(8,128)(2,1)S(1)}, u32[]{:S(2)}, u32[]{:S(2)}) %collective-permute-start.5) | collective-permute-done | bytes 262176 | tf_op jit(solution)/shard_map/ppermute | solution.py:34
  20.5 30.9 %collective-permute-done.1 = bf16[128,1024]{1,0:T(8,128)(2,1)S(1)} collective-permute-done((bf16[128,1024]{1,0:T(8,128)(2,1)S(1)}, bf16[128,1024]{1,0:T(8,128)(2,1)S(1)}, u32[]{:S(2)}, u32[]{:S(2)}) %collective-permute-start.1) | collective-permute-done | bytes 262176 | tf_op jit(solution)/shard_map/ppermute | solution.py:34
  51.4 5.6 %collective-permute-done.6 = bf16[128,1024]{1,0:T(8,128)(2,1)S(1)} collective-permute-done((bf16[128,1024]{1,0:T(8,128)(2,1)S(1)}, bf16[128,1024]{1,0:T(8,128)(2,1)S(1)}, u32[]{:S(2)}, u32[]{:S(2)}) %collective-permute-start.6) | collective-permute-done | bytes 262176 | tf_op jit(solution)/shard_map/ppermute | solution.py:34
  57.1 5.6 %collective-permute-done.2 = bf16[128,1024]{1,0:T(8,128)(2,1)S(1)} collective-permute-done((bf16[128,1024]{1,0:T(8,128)(2,1)S(1)}, bf16[128,1024]{1,0:T(8,128)(2,1)S(1)}, u32[]{:S(2)}, u32[]{:S(2)}) %collective-permute-start.2) | collective-permute-done | bytes 262176 | tf_op jit(solution)/shard_map/ppermute | solution.py:34
  64.6 2.8 %collective-permute-done.7 = bf16[128,1024]{1,0:T(8,128)(2,1)S(1)} collective-permute-done((bf16[128,1024]{1,0:T(8,128)(2,1)S(1)}, bf16[128,1024]{1,0:T(8,128)(2,1)S(1)}, u32[]{:S(2)}, u32[]{:S(2)}) %collective-permute-start.7) | collective-permute-done | bytes 262176 | tf_op jit(solution)/shard_map/ppermute | solution.py:34
  70.5 16.0 %collective-permute-done.3 = bf16[4,128,1024]{2,1,0:T(8,128)(2,1)} collective-permute-done((bf16[4,128,1024]{2,1,0:T(8,128)(2,1)S(1)}, bf16[4,128,1024]{2,1,0:T(8,128)(2,1)}, u32[]{:S(2)}, u32[]{:S(2)}) %collective-permute-start.3) | collective-permute-done | bytes 1048608 | tf_op jit(solution)/shard_map/ppermute | solution.py:34
  89.3 6.1 %collective-permute-done.8 = bf16[4,128,1024]{2,1,0:T(8,128)(2,1)} collective-permute-done((bf16[4,128,1024]{2,1,0:T(8,128)(2,1)}, bf16[4,128,1024]{2,1,0:T(8,128)(2,1)}, u32[]{:S(2)}, u32[]{:S(2)}) %collective-permute-start.8) | collective-permute-done | bytes 1048608 | tf_op jit(solution)/shard_map/ppermute | solution.py:34
  95.4 2.8 %pad_maximum_fusion.2 = bf16[2,4,128,1024]{3,2,1,0:T(8,128)(2,1)} fusion(bf16[1,4,128,1024]{3,2,1,0:T(8,128)(2,1)} %bitcast.16, bf16[1,4,128,1024]{3,2,1,0:T(8,128)(2,1)S(1)} %copy-done.1), kind=kLoop, calls=%fused_computation.15 | loop fusion | flops 1048576 | bytes 4194304 | tf_op jit(solution)/shard_map/stack | solution.py:39
  104.4 4.0 %copy.95 = bf16[1024,1024]{0,1:T(8,128)(2,1)} copy(bf16[1024,1024]{1,0:T(8,128)(2,1)} %bitcast.17) | data formatting | bytes 4194304 | tf_op jit(solution)/shard_map/reshape | solution.py:177
  108.4 18.7 %collective-permute-done.12 = bf16[256,2304]{1,0:T(8,128)(2,1)} collective-permute-done((bf16[256,2304]{1,0:T(8,128)(2,1)}, bf16[256,2304]{1,0:T(8,128)(2,1)}, u32[]{:S(2)}, u32[]{:S(2)}) %collective-permute-start.12) | collective-permute-done | bytes 1179680 | tf_op jit(solution)/shard_map/ppermute | solution.py:34
  127.0 3.8 %pad_maximum_fusion = bf16[4,256,2304]{2,1,0:T(8,128)(2,1)} fusion(bf16[1,256,2304]{2,1,0:T(8,128)(2,1)} %bitcast.24, bf16[1,256,2304]{2,1,0:T(8,128)(2,1)} %bitcast.23, bf16[1,256,2304]{2,1,0:T(8,128)(2,1)} %bitcast.22, bf16[1,256,2304]{2,1,0:T(8,128)(2,1)S(1)} %bitcast.174), kind=kLoop, calls=%fused_computation.1 | loop fusion | flops 7077888 | bytes 9437184 | tf_op jit(solution)/shard_map/stack | solution.py:39
  130.9 7.7 %collective-permute-done.4 = bf16[2,4,128,1024]{3,2,1,0:T(8,128)(2,1)} collective-permute-done((bf16[2,4,128,1024]{3,2,1,0:T(8,128)(2,1)S(1)}, bf16[2,4,128,1024]{3,2,1,0:T(8,128)(2,1)}, u32[]{:S(2)}, u32[]{:S(2)}) %collective-permute-start.4) | collective-permute-done | bytes 2097184 | tf_op jit(solution)/shard_map/ppermute | solution.py:34
  138.6 2.9 %copy.94 = bf16[1024,1024]{0,1:T(8,128)(2,1)S(1)} copy(bf16[1024,1024]{1,0:T(8,128)(2,1)} %bitcast.9) | data formatting | bytes 4194304 | tf_op jit(solution)/shard_map/reshape | solution.py:177
  142.6 4.0 %copy.96 = bf16[1024,1024]{0,1:T(8,128)(2,1)} copy(bf16[1024,1024]{1,0:T(8,128)(2,1)} %bitcast.19) | data formatting | bytes 4194304 | tf_op jit(solution)/shard_map/reshape | solution.py:177
  146.6 2.7 %fusion.91 = (bf16[1024,512]{0,1:T(8,128)(2,1)S(1)}, bf16[1024,512]{0,1:T(8,128)(2,1)S(1)}, bf16[1024,512]{0,1:T(8,128)(2,1)S(1)}, bf16[1024,512]{0,1:T(8,128)(2,1)S(1)}) fusion(bf16[1024,1024]{0,1:T(8,128)(2,1)} %copy.95, bf16[1024,1024]{0,1:T(8,128)(2,1)} %copy.96), kind=kLoop, calls=%fused_computation.212 | loop fusion | bytes 8388608 | tf_op jit(solution)/shard_map/slice | solution.py:189
  169.9 5.5 %collective-permute-done.14 = bf16[128,4,256]{2,0,1:T(8,128)(2,1)S(1)} collective-permute-done((bf16[128,4,256]{2,0,1:T(8,128)(2,1)S(1)}, bf16[128,4,256]{2,0,1:T(8,128)(2,1)S(1)}, u32[]{:S(2)}, u32[]{:S(2)}) %collective-permute-start.14) | collective-permute-done | bytes 262176 | tf_op jit(solution)/shard_map/ppermute | solution.py:71
  175.4 6.7 %collective-permute-done.15 = bf16[128,4,256]{2,0,1:T(8,128)(2,1)S(1)} collective-permute-done((bf16[128,4,256]{2,0,1:T(8,128)(2,1)S(1)}, bf16[128,4,256]{2,0,1:T(8,128)(2,1)S(1)}, u32[]{:S(2)}, u32[]{:S(2)}) %collective-permute-start.15) | collective-permute-done | bytes 262176 | tf_op jit(solution)/shard_map/ppermute | solution.py:71
  184.8 4.9 %fusion.95 = f32[4,128,2304]{2,1,0:T(8,128)S(1)} fusion(bf16[4,128,1024]{2,1,0:T(8,128)(2,1)S(1)} %select_n.301, bf16[1024,2304,1]{1,0,2:T(8,128)(2,1)} %bitcast.169), kind=kOutput, calls=%fused_computation.216 | convolution fusion | flops 2415919104 | bytes 10485760 | tf_op jit(solution)/shard_map/dot_general | solution.py:202
  192.9 26.1 %collective-permute-done.19 = f32[128,2304]{1,0:T(8,128)S(1)} collective-permute-done((f32[128,2304]{1,0:T(8,128)S(1)}, f32[128,2304]{1,0:T(8,128)S(1)}, u32[]{:S(2)}, u32[]{:S(2)}) %collective-permute-start.19) | collective-permute-done | bytes 1179680 | tf_op jit(solution)/shard_map/ppermute | solution.py:81
  219.1 24.1 %collective-permute-done.18 = f32[128,2304]{1,0:T(8,128)S(1)} collective-permute-done((f32[128,2304]{1,0:T(8,128)S(1)}, f32[128,2304]{1,0:T(8,128)S(1)}, u32[]{:S(2)}, u32[]{:S(2)}) %collective-permute-start.18) | collective-permute-done | bytes 1179680 | tf_op jit(solution)/shard_map/ppermute | solution.py:81
  246.3 3.5 %collective-permute-done.20 = f32[16]{0:T(128)S(1)} collective-permute-done((f32[16]{0:T(128)S(1)}, f32[16]{0:T(128)S(1)}, u32[]{:S(2)}, u32[]{:S(2)}) %collective-permute-start.20) | collective-permute-done | bytes 96 | tf_op jit(solution)/shard_map/ppermute | solution.py:90
  250.4 3.9 %collective-permute-done.21 = f32[16]{0:T(128)S(1)} collective-permute-done((f32[16]{0:T(128)S(1)}, f32[16]{0:T(128)S(1)}, u32[]{:S(2)}, u32[]{:S(2)}) %collective-permute-start.21) | collective-permute-done | bytes 96 | tf_op jit(solution)/shard_map/ppermute | solution.py:90
  (129 shorter events, 58.0 us)
Async XLA Ops:
  2.7 12.2 %collective-permute-start = (bf16[128,1024]{1,0:T(8,128)(2,1)S(1)}, bf16[128,1024]{1,0:T(8,128)(2,1)S(1)}, u32[]{:S(2)}, u32[]{:S(2)}) collective-permute-start(bf16[128,1024]{1,0:T(8,128)(2,1)S(1)} %get-tuple-element.53), channel_id=1, source_target_pairs={{0,8},{8,16},{16,24},{24,0},{1,9},{9,17},{17,25},{25,1},{2,10},{10... | collective-permute-start | bytes 786440 | tf_op jit(solution)/shard_map/ppermute | solution.py:34
  5.8 14.7 %collective-permute-start.5 = (bf16[128,1024]{1,0:T(8,128)(2,1)S(1)}, bf16[128,1024]{1,0:T(8,128)(2,1)S(1)}, u32[]{:S(2)}, u32[]{:S(2)}) collective-permute-start(bf16[128,1024]{1,0:T(8,128)(2,1)S(1)} %get-tuple-element.47), channel_id=1, source_target_pairs={{0,8},{8,16},{16,24},{24,0},{1,9},{9,17},{17,25},{25,1},{2,10},{10... | collective-permute-start | bytes 786440 | tf_op jit(solution)/shard_map/ppermute | solution.py:34
  7.4 63.1 %collective-permute-start.10 = (bf16[256,2304]{1,0:T(8,128)(2,1)}, bf16[256,2304]{1,0:T(8,128)(2,1)}, u32[]{:S(2)}, u32[]{:S(2)}) collective-permute-start(bf16[256,2304]{1,0:T(8,128)(2,1)} %param.12), channel_id=1, source_target_pairs={{0,8},{8,16},{16,24},{24,0},{1,9},{9,17},{17,25},{25,1},{2,10},{10... | collective-permute-start | bytes 3538952 | tf_op jit(solution)/shard_map/ppermute | solution.py:34
  14.9 36.5 %collective-permute-start.1 = (bf16[128,1024]{1,0:T(8,128)(2,1)S(1)}, bf16[128,1024]{1,0:T(8,128)(2,1)S(1)}, u32[]{:S(2)}, u32[]{:S(2)}) collective-permute-start(bf16[128,1024]{1,0:T(8,128)(2,1)S(1)} %collective-permute-done), channel_id=1, source_target_pairs={{0,8},{8,16},{16,24},{24,0},{1,9},{9,17},{17,25},{25,1},{2,10},{10... | collective-permute-start | bytes 786440 | tf_op jit(solution)/shard_map/ppermute | solution.py:34
  20.5 36.5 %collective-permute-start.6 = (bf16[128,1024]{1,0:T(8,128)(2,1)S(1)}, bf16[128,1024]{1,0:T(8,128)(2,1)S(1)}, u32[]{:S(2)}, u32[]{:S(2)}) collective-permute-start(bf16[128,1024]{1,0:T(8,128)(2,1)S(1)} %collective-permute-done.5), channel_id=1, source_target_pairs={{0,8},{8,16},{16,24},{24,0},{1,9},{9,17},{17,25},{25,1},{2,10},{10... | collective-permute-start | bytes 786440 | tf_op jit(solution)/shard_map/ppermute | solution.py:34
  51.4 11.2 %collective-permute-start.2 = (bf16[128,1024]{1,0:T(8,128)(2,1)S(1)}, bf16[128,1024]{1,0:T(8,128)(2,1)S(1)}, u32[]{:S(2)}, u32[]{:S(2)}) collective-permute-start(bf16[128,1024]{1,0:T(8,128)(2,1)S(1)} %collective-permute-done.1), channel_id=1, source_target_pairs={{0,8},{8,16},{16,24},{24,0},{1,9},{9,17},{17,25},{25,1},{2,10},{10... | collective-permute-start | bytes 786440 | tf_op jit(solution)/shard_map/ppermute | solution.py:34
  57.0 10.4 %collective-permute-start.7 = (bf16[128,1024]{1,0:T(8,128)(2,1)S(1)}, bf16[128,1024]{1,0:T(8,128)(2,1)S(1)}, u32[]{:S(2)}, u32[]{:S(2)}) collective-permute-start(bf16[128,1024]{1,0:T(8,128)(2,1)S(1)} %collective-permute-done.6), channel_id=1, source_target_pairs={{0,8},{8,16},{16,24},{24,0},{1,9},{9,17},{17,25},{25,1},{2,10},{10... | collective-permute-start | bytes 786440 | tf_op jit(solution)/shard_map/ppermute | solution.py:34
  62.8 23.7 %collective-permute-start.3 = (bf16[4,128,1024]{2,1,0:T(8,128)(2,1)S(1)}, bf16[4,128,1024]{2,1,0:T(8,128)(2,1)}, u32[]{:S(2)}, u32[]{:S(2)}) collective-permute-start(bf16[4,128,1024]{2,1,0:T(8,128)(2,1)S(1)} %get-tuple-element.45), channel_id=1, source_target_pairs={{0,2},{2,0},{1,3},{3,1},{4,6},{6,4},{5,7},{7,5},{8,10},{10,8},{9,1... | collective-permute-start | bytes 3145736 | tf_op jit(solution)/shard_map/ppermute | solution.py:34
  69.0 26.4 %collective-permute-start.8 = (bf16[4,128,1024]{2,1,0:T(8,128)(2,1)}, bf16[4,128,1024]{2,1,0:T(8,128)(2,1)}, u32[]{:S(2)}, u32[]{:S(2)}) collective-permute-start(bf16[4,128,1024]{2,1,0:T(8,128)(2,1)} %get-tuple-element.43), channel_id=1, source_target_pairs={{0,4},{4,0},{1,5},{5,1},{2,6},{6,2},{3,7},{7,3},{8,12},{12,8},{9,1... | collective-permute-start | bytes 3145736 | tf_op jit(solution)/shard_map/ppermute | solution.py:34
  70.5 29.2 %collective-permute-start.11 = (bf16[256,2304]{1,0:T(8,128)(2,1)}, bf16[256,2304]{1,0:T(8,128)(2,1)}, u32[]{:S(2)}, u32[]{:S(2)}) collective-permute-start(bf16[256,2304]{1,0:T(8,128)(2,1)} %collective-permute-done.10), channel_id=1, source_target_pairs={{0,8},{8,16},{16,24},{24,0},{1,9},{9,17},{17,25},{25,1},{2,10},{10... | collective-permute-start | bytes 3538952 | tf_op jit(solution)/shard_map/ppermute | solution.py:34
  88.0 50.6 %collective-permute-start.4 = (bf16[2,4,128,1024]{3,2,1,0:T(8,128)(2,1)S(1)}, bf16[2,4,128,1024]{3,2,1,0:T(8,128)(2,1)}, u32[]{:S(2)}, u32[]{:S(2)}) collective-permute-start(bf16[2,4,128,1024]{3,2,1,0:T(8,128)(2,1)S(1)} %pad_maximum_fusion.1), channel_id=1, source_target_pairs={{0,4},{4,0},{1,5},{5,1},{2,6},{6,2},{3,7},{7,3},{8,12},{12,8},{9,1... | collective-permute-start | bytes 6291464 | tf_op jit(solution)/shard_map/ppermute | solution.py:34
  98.2 44.5 %collective-permute-start.9 = (bf16[2,4,128,1024]{3,2,1,0:T(8,128)(2,1)}, bf16[2,4,128,1024]{3,2,1,0:T(8,128)(2,1)}, u32[]{:S(2)}, u32[]{:S(2)}) collective-permute-start(bf16[2,4,128,1024]{3,2,1,0:T(8,128)(2,1)} %pad_maximum_fusion.2), channel_id=1, source_target_pairs={{0,2},{2,0},{1,3},{3,1},{4,6},{6,4},{5,7},{7,5},{8,10},{10,8},{9,1... | collective-permute-start | bytes 6291464 | tf_op jit(solution)/shard_map/ppermute | solution.py:34
  99.7 27.3 %collective-permute-start.12 = (bf16[256,2304]{1,0:T(8,128)(2,1)}, bf16[256,2304]{1,0:T(8,128)(2,1)}, u32[]{:S(2)}, u32[]{:S(2)}) collective-permute-start(bf16[256,2304]{1,0:T(8,128)(2,1)} %collective-permute-done.11), channel_id=1, source_target_pairs={{0,8},{8,16},{16,24},{24,0},{1,9},{9,17},{17,25},{25,1},{2,10},{10... | collective-permute-start | bytes 3538952 | tf_op jit(solution)/shard_map/ppermute | solution.py:34
  163.2 2.0 collective-permute-start.13
  166.2 9.2 %collective-permute-start.14 = (bf16[128,4,256]{2,0,1:T(8,128)(2,1)S(1)}, bf16[128,4,256]{2,0,1:T(8,128)(2,1)S(1)}, u32[]{:S(2)}, u32[]{:S(2)}) collective-permute-start(bf16[128,4,256]{2,0,1:T(8,128)(2,1)S(1)} %bitcast.194), channel_id=1, source_target_pairs={{0,6},{2,0},{4,2},{6,4},{1,7},{3,1},{5,3},{7,5},{8,14},{10,8},{12,... | collective-permute-start | bytes 786440 | tf_op jit(solution)/shard_map/ppermute | solution.py:71
  168.4 13.8 %collective-permute-start.15 = (bf16[128,4,256]{2,0,1:T(8,128)(2,1)S(1)}, bf16[128,4,256]{2,0,1:T(8,128)(2,1)S(1)}, u32[]{:S(2)}, u32[]{:S(2)}) collective-permute-start(bf16[128,4,256]{2,0,1:T(8,128)(2,1)S(1)} %bitcast.195), channel_id=1, source_target_pairs={{0,4},{2,6},{4,0},{6,2},{1,5},{3,7},{5,1},{7,3},{8,12},{10,14},{12... | collective-permute-start | bytes 786440 | tf_op jit(solution)/shard_map/ppermute | solution.py:71
  169.1 13.0 %collective-permute-start.16 = (bf16[128,4,256]{2,0,1:T(8,128)(2,1)S(1)}, bf16[128,4,256]{2,0,1:T(8,128)(2,1)S(1)}, u32[]{:S(2)}, u32[]{:S(2)}) collective-permute-start(bf16[128,4,256]{2,0,1:T(8,128)(2,1)S(1)} %bitcast.196), channel_id=1, source_target_pairs={{0,2},{2,4},{4,6},{6,0},{1,3},{3,5},{5,7},{7,1},{8,10},{10,12},{12... | collective-permute-start | bytes 786440 | tf_op jit(solution)/shard_map/ppermute | solution.py:71
  190.1 29.0 %collective-permute-start.19 = (f32[128,2304]{1,0:T(8,128)S(1)}, f32[128,2304]{1,0:T(8,128)S(1)}, u32[]{:S(2)}, u32[]{:S(2)}) collective-permute-start(f32[128,2304]{1,0:T(8,128)S(1)} %get-tuple-element.28), channel_id=1, source_target_pairs={{0,6},{2,0},{4,2},{6,4},{1,7},{3,1},{5,3},{7,5},{8,14},{10,8},{12,... | collective-permute-start | bytes 3538952 | tf_op jit(solution)/shard_map/ppermute | solution.py:81
  190.7 52.5 %collective-permute-start.18 = (f32[128,2304]{1,0:T(8,128)S(1)}, f32[128,2304]{1,0:T(8,128)S(1)}, u32[]{:S(2)}, u32[]{:S(2)}) collective-permute-start(f32[128,2304]{1,0:T(8,128)S(1)} %get-tuple-element.29), channel_id=1, source_target_pairs={{0,4},{2,6},{4,0},{6,2},{1,5},{3,7},{5,1},{7,3},{8,12},{10,14},{12... | collective-permute-start | bytes 3538952 | tf_op jit(solution)/shard_map/ppermute | solution.py:81
  191.7 51.5 %collective-permute-start.17 = (f32[128,2304]{1,0:T(8,128)S(1)}, f32[128,2304]{1,0:T(8,128)S(1)}, u32[]{:S(2)}, u32[]{:S(2)}) collective-permute-start(f32[128,2304]{1,0:T(8,128)S(1)} %get-tuple-element.27), channel_id=1, source_target_pairs={{0,2},{2,4},{4,6},{6,0},{1,3},{3,5},{5,7},{7,1},{8,10},{10,12},{12... | collective-permute-start | bytes 3538952 | tf_op jit(solution)/shard_map/ppermute | solution.py:81
  246.2 3.6 %collective-permute-start.20 = (f32[16]{0:T(128)S(1)}, f32[16]{0:T(128)S(1)}, u32[]{:S(2)}, u32[]{:S(2)}) collective-permute-start(f32[16]{0:T(128)S(1)} %select_reduce_fusion), channel_id=1, source_target_pairs={{0,8},{8,0},{16,24},{24,16},{1,9},{9,1},{17,25},{25,17},{2,10},{10... | collective-permute-start | bytes 200 | tf_op jit(solution)/shard_map/ppermute | solution.py:90
  249.8 4.4 %collective-permute-start.21 = (f32[16]{0:T(128)S(1)}, f32[16]{0:T(128)S(1)}, u32[]{:S(2)}, u32[]{:S(2)}) collective-permute-start(f32[16]{0:T(128)S(1)} %add.536), channel_id=1, source_target_pairs={{0,16},{8,24},{16,0},{24,8},{1,17},{9,25},{17,1},{25,9},{2,18},{10... | collective-permute-start | bytes 200 | tf_op jit(solution)/shard_map/ppermute | solution.py:90
  254.3 3.5 %collective-permute-start.22 = (f32[16]{0:T(128)S(1)}, f32[16]{0:T(128)S(1)}, u32[]{:S(2)}, u32[]{:S(2)}) collective-permute-start(f32[16]{0:T(128)S(1)} %add.537), channel_id=1, source_target_pairs={{0,4},{4,0},{1,5},{5,1},{2,6},{6,2},{3,7},{7,3},{8,12},{12,8},{9,1... | collective-permute-start | bytes 200 | tf_op jit(solution)/shard_map/ppermute | solution.py:90
  257.8 3.5 %collective-permute-start.23 = (f32[16]{0:T(128)S(1)}, f32[16]{0:T(128)S(1)}, u32[]{:S(2)}, u32[]{:S(2)}) collective-permute-start(f32[16]{0:T(128)S(1)} %add.538), channel_id=1, source_target_pairs={{0,2},{2,0},{1,3},{3,1},{4,6},{6,4},{5,7},{7,5},{8,10},{10,8},{9,1... | collective-permute-start | bytes 200 | tf_op jit(solution)/shard_map/ppermute | solution.py:90
  (9 other events, 91.1 us)

commit v14 on v13

--- a/solution.py
+++ b/solution.py
@@ -80,6 +80,17 @@
         sent = lax.dynamic_index_in_dim(x, (own + shift) % n, axis=0, keepdims=False)
         total = total + lax.ppermute(sent, axes, [(k, (k + shift) % n) for k in range(n)])
     return total
+
+
+def swap_reduce_scatter(x, first, second):
+    own_first = lax.axis_index(first)
+    own_second = lax.axis_index(second)
+    keep = lax.dynamic_index_in_dim(x, own_first, axis=1, keepdims=False)
+    sent = lax.dynamic_index_in_dim(x, 1 - own_first, axis=1, keepdims=False)
+    keep = keep + lax.ppermute(sent, first, [(0, 1), (1, 0)])
+    mine = lax.dynamic_index_in_dim(keep, own_second, axis=0, keepdims=False)
+    sent = lax.dynamic_index_in_dim(keep, 1 - own_second, axis=0, keepdims=False)
+    return mine + lax.ppermute(sent, second, [(0, 1), (1, 0)])
 
 
 def butterfly_sum(x, axes):
@@ -202,7 +213,12 @@
     partial = jnp.dot(
         regrouped.reshape(inner * tok_dev, outer * rows_each), weight_rows, preferred_element_type=jnp.float32
     )
-    mixed = permute_reduce_scatter(partial.reshape(inner, tok_dev, -1), INNER)
+    by_dest = partial.reshape(2, 2, tok_dev, -1)
+    cut = by_dest.shape[-1] // 2
+    mixed = jnp.concatenate([
+        swap_reduce_scatter(by_dest[..., :cut], "c2", "c1"),
+        swap_reduce_scatter(by_dest[..., cut:].transpose(1, 0, 2, 3), "c1", "c2"),
+    ], axis=-1)
     hidden = hidden_in.astype(jnp.float32)
     sums = lax.psum(
         jnp.stack([

time: 262 us -> 256 us (0.977)
  waiting for transfers between devices: 182 us -> 170 us
  other arithmetic: 15.5 us -> 19.2 us
  local copies, waits for them, and re-layouts: 23.7 us -> 26.6 us
    ppermute x3 -> x4, waiting for transfers between devices: 50.3 us -> 37.1 us  [the longest x2 24.1 us: swap_reduce_scatter(): keep = keep + lax.ppermute(sent, first, [(0, 1), (1, 0)])]
    add x0 -> x4, other arithmetic: none -> 3.28 us  [the longest x2 3.14 us: swap_reduce_scatter(): keep = keep + lax.ppermute(sent, first, [(0, 1), (1, 0)])]
  transfers between devices with their start and end apart: 24 -> 25, of which waited for: 20 -> 21; matrix products, arithmetic and copies ran while one was open for 9% -> 11% of each run, Pallas kernels for 0% -> 0%
where the time goes in v14:
time: 256 us
  waiting for transfers between devices  170 us (66%)
  local copies, waits for them, and re-layouts  26.6 us (10%)
  starting transfers between devices  19.6 us (8%)
  other arithmetic  19.2 us (8%)
  matrix products  16.2 us (6%)
    ppermute x14, waiting for transfers between devices, ring_pieces(): lax.ppermute(pieces[-1], axis, [(k, (k + 1) % n) for k in range(n)])  108 us
    ppermute x2, waiting for transfers between devices, swap_reduce_scatter(): keep = keep + lax.ppermute(sent, first, [(0, 1), (1, 0)])  24.1 us
    reshape x4, local copies, waits for them, and re-layouts, shards(): gathered.append((got.reshape(key_rows.shape[0], -1), key_rows))  13.4 us
    ppermute x4, waiting for transfers between devices, butterfly_sum(): x = x + lax.ppermute(x, axis, [(i, i ^ bit) for i in range(size)])  13.3 us
    ppermute x2, waiting for transfers between devices, swap_reduce_scatter(): return mine + lax.ppermute(sent, second, [(0, 1), (1, 0)])  13.1 us
    ppermute x14, starting transfers between devices, ring_pieces(): lax.ppermute(pieces[-1], axis, [(k, (k + 1) % n) for k in range(n)])  12.7 us
    ppermute x3, waiting for transfers between devices, permute_all_to_all(): lax.ppermute(sent, axes, [(k, (k + shift) % n) for k in range(n)])  12.2 us
    another operation x8, other arithmetic, ring_gather(): return jnp.stack(ring_pieces(x, axis))  9.85 us
  transfers between devices with their start and end apart: 25, of which 21 were waited for; matrix products, arithmetic and copies ran while one was open for 11% of the time, Pallas kernels for 0%

profile of v14, /device:TPU:0, one launch (start us, length us, event | category | flops | bytes accessed | tf_op | source)
XLA Modules:
  0.0 255.7 jit_solution(13450858270598081525)
XLA Ops:
  2.8 3.1 %collective-permute-start = (bf16[128,1024]{1,0:T(8,128)(2,1)S(1)}, bf16[128,1024]{1,0:T(8,128)(2,1)S(1)}, u32[]{:S(2)}, u32[]{:S(2)}) collective-permute-start(bf16[128,1024]{1,0:T(8,128)(2,1)S(1)} %get-tuple-element.51), channel_id=1, source_target_pairs={{0,8},{8,16},{16,24},{24,0},{1,9},{9,17},{17,25},{25,1},{2,10},{10... | collective-permute-start | bytes 786440 | tf_op jit(solution)/shard_map/ppermute | solution.py:34
  9.1 5.9 %collective-permute-done = bf16[128,1024]{1,0:T(8,128)(2,1)S(1)} collective-permute-done((bf16[128,1024]{1,0:T(8,128)(2,1)S(1)}, bf16[128,1024]{1,0:T(8,128)(2,1)S(1)}, u32[]{:S(2)}, u32[]{:S(2)}) %collective-permute-start) | collective-permute-done | bytes 262176 | tf_op jit(solution)/shard_map/ppermute | solution.py:34
  15.0 5.6 %collective-permute-done.5 = bf16[128,1024]{1,0:T(8,128)(2,1)S(1)} collective-permute-done((bf16[128,1024]{1,0:T(8,128)(2,1)S(1)}, bf16[128,1024]{1,0:T(8,128)(2,1)S(1)}, u32[]{:S(2)}, u32[]{:S(2)}) %collective-permute-start.5) | collective-permute-done | bytes 262176 | tf_op jit(solution)/shard_map/ppermute | solution.py:34
  20.7 30.9 %collective-permute-done.1 = bf16[128,1024]{1,0:T(8,128)(2,1)S(1)} collective-permute-done((bf16[128,1024]{1,0:T(8,128)(2,1)S(1)}, bf16[128,1024]{1,0:T(8,128)(2,1)S(1)}, u32[]{:S(2)}, u32[]{:S(2)}) %collective-permute-start.1) | collective-permute-done | bytes 262176 | tf_op jit(solution)/shard_map/ppermute | solution.py:34
  51.5 5.6 %collective-permute-done.6 = bf16[128,1024]{1,0:T(8,128)(2,1)S(1)} collective-permute-done((bf16[128,1024]{1,0:T(8,128)(2,1)S(1)}, bf16[128,1024]{1,0:T(8,128)(2,1)S(1)}, u32[]{:S(2)}, u32[]{:S(2)}) %collective-permute-start.6) | collective-permute-done | bytes 262176 | tf_op jit(solution)/shard_map/ppermute | solution.py:34
  57.2 5.6 %collective-permute-done.2 = bf16[128,1024]{1,0:T(8,128)(2,1)S(1)} collective-permute-done((bf16[128,1024]{1,0:T(8,128)(2,1)S(1)}, bf16[128,1024]{1,0:T(8,128)(2,1)S(1)}, u32[]{:S(2)}, u32[]{:S(2)}) %collective-permute-start.2) | collective-permute-done | bytes 262176 | tf_op jit(solution)/shard_map/ppermute | solution.py:34
  64.7 2.8 %collective-permute-done.7 = bf16[128,1024]{1,0:T(8,128)(2,1)S(1)} collective-permute-done((bf16[128,1024]{1,0:T(8,128)(2,1)S(1)}, bf16[128,1024]{1,0:T(8,128)(2,1)S(1)}, u32[]{:S(2)}, u32[]{:S(2)}) %collective-permute-start.7) | collective-permute-done | bytes 262176 | tf_op jit(solution)/shard_map/ppermute | solution.py:34
  70.6 16.1 %collective-permute-done.3 = bf16[4,128,1024]{2,1,0:T(8,128)(2,1)} collective-permute-done((bf16[4,128,1024]{2,1,0:T(8,128)(2,1)S(1)}, bf16[4,128,1024]{2,1,0:T(8,128)(2,1)}, u32[]{:S(2)}, u32[]{:S(2)}) %collective-permute-start.3) | collective-permute-done | bytes 1048608 | tf_op jit(solution)/shard_map/ppermute | solution.py:34
  89.4 6.0 %collective-permute-done.8 = bf16[4,128,1024]{2,1,0:T(8,128)(2,1)} collective-permute-done((bf16[4,128,1024]{2,1,0:T(8,128)(2,1)}, bf16[4,128,1024]{2,1,0:T(8,128)(2,1)}, u32[]{:S(2)}, u32[]{:S(2)}) %collective-permute-start.8) | collective-permute-done | bytes 1048608 | tf_op jit(solution)/shard_map/ppermute | solution.py:34
  104.4 4.0 %copy.96 = bf16[1024,1024]{0,1:T(8,128)(2,1)} copy(bf16[1024,1024]{1,0:T(8,128)(2,1)} %bitcast.17) | data formatting | bytes 4194304 | tf_op jit(solution)/shard_map/reshape | solution.py:188
  108.4 18.7 %collective-permute-done.12 = bf16[256,2304]{1,0:T(8,128)(2,1)} collective-permute-done((bf16[256,2304]{1,0:T(8,128)(2,1)}, bf16[256,2304]{1,0:T(8,128)(2,1)}, u32[]{:S(2)}, u32[]{:S(2)}) %collective-permute-start.12) | collective-permute-done | bytes 1179680 | tf_op jit(solution)/shard_map/ppermute | solution.py:34
  127.1 3.9 %pad_maximum_fusion = bf16[4,256,2304]{2,1,0:T(8,128)(2,1)} fusion(bf16[1,256,2304]{2,1,0:T(8,128)(2,1)} %bitcast.24, bf16[1,256,2304]{2,1,0:T(8,128)(2,1)} %bitcast.23, bf16[1,256,2304]{2,1,0:T(8,128)(2,1)} %bitcast.22, bf16[1,256,2304]{2,1,0:T(8,128)(2,1)S(1)} %bitcast.179), kind=kLoop, calls=%fused_computation.1 | loop fusion | flops 7077888 | bytes 9437184 | tf_op jit(solution)/shard_map/stack | solution.py:39
  131.0 7.7 %collective-permute-done.4 = bf16[2,4,128,1024]{3,2,1,0:T(8,128)(2,1)} collective-permute-done((bf16[2,4,128,1024]{3,2,1,0:T(8,128)(2,1)S(1)}, bf16[2,4,128,1024]{3,2,1,0:T(8,128)(2,1)}, u32[]{:S(2)}, u32[]{:S(2)}) %collective-permute-start.4) | collective-permute-done | bytes 2097184 | tf_op jit(solution)/shard_map/ppermute | solution.py:34
  138.6 2.9 %copy.95 = bf16[1024,1024]{0,1:T(8,128)(2,1)S(1)} copy(bf16[1024,1024]{1,0:T(8,128)(2,1)} %bitcast.9) | data formatting | bytes 4194304 | tf_op jit(solution)/shard_map/reshape | solution.py:188
  142.7 4.0 %copy.97 = bf16[1024,1024]{0,1:T(8,128)(2,1)} copy(bf16[1024,1024]{1,0:T(8,128)(2,1)} %bitcast.19) | data formatting | bytes 4194304 | tf_op jit(solution)/shard_map/reshape | solution.py:188
  169.9 5.5 %collective-permute-done.14 = bf16[128,4,256]{2,0,1:T(8,128)(2,1)S(1)} collective-permute-done((bf16[128,4,256]{2,0,1:T(8,128)(2,1)S(1)}, bf16[128,4,256]{2,0,1:T(8,128)(2,1)S(1)}, u32[]{:S(2)}, u32[]{:S(2)}) %collective-permute-start.14) | collective-permute-done | bytes 262176 | tf_op jit(solution)/shard_map/ppermute | solution.py:71
  175.4 6.7 %collective-permute-done.15 = bf16[128,4,256]{2,0,1:T(8,128)(2,1)S(1)} collective-permute-done((bf16[128,4,256]{2,0,1:T(8,128)(2,1)S(1)}, bf16[128,4,256]{2,0,1:T(8,128)(2,1)S(1)}, u32[]{:S(2)}, u32[]{:S(2)}) %collective-permute-start.15) | collective-permute-done | bytes 262176 | tf_op jit(solution)/shard_map/ppermute | solution.py:71
  184.8 4.9 %fusion.93 = f32[2,2,128,2304]{3,2,1,0:T(8,128)S(1)} fusion(bf16[2,2,128,1024]{3,2,1,0:T(8,128)(2,1)S(1)} %select_n.308, bf16[1024,2304,1,1]{1,0,3,2:T(8,128)(2,1)} %bitcast.174), kind=kOutput, calls=%fused_computation.220 | convolution fusion | flops 2415919104 | bytes 10485760 | tf_op jit(solution)/shard_map/dot_general | solution.py:213
  194.6 24.1 %collective-permute-done.19 = f32[2,128,1152]{2,1,0:T(8,128)} collective-permute-done((f32[2,128,1152]{2,1,0:T(8,128)S(1)}, f32[2,128,1152]{2,1,0:T(8,128)}, u32[]{:S(2)}, u32[]{:S(2)}) %collective-permute-start.19) | collective-permute-done | bytes 1179680 | tf_op jit(solution)/shard_map/ppermute | solution.py:90
  224.0 10.2 %collective-permute-done.20 = f32[128,1152]{1,0:T(8,128)S(1)} collective-permute-done((f32[128,1152]{1,0:T(8,128)S(1)}, f32[128,1152]{1,0:T(8,128)S(1)}, u32[]{:S(2)}, u32[]{:S(2)}) %collective-permute-start.20) | collective-permute-done | bytes 589856 | tf_op jit(solution)/shard_map/ppermute | solution.py:93
  234.2 2.9 %collective-permute-done.18 = f32[128,1152]{1,0:T(8,128)S(1)} collective-permute-done((f32[128,1152]{1,0:T(8,128)S(1)}, f32[128,1152]{1,0:T(8,128)S(1)}, u32[]{:S(2)}, u32[]{:S(2)}) %collective-permute-start.18) | collective-permute-done | bytes 589856 | tf_op jit(solution)/shard_map/ppermute | solution.py:93
  240.1 3.5 %collective-permute-done.21 = f32[16]{0:T(128)S(1)} collective-permute-done((f32[16]{0:T(128)S(1)}, f32[16]{0:T(128)S(1)}, u32[]{:S(2)}, u32[]{:S(2)}) %collective-permute-start.21) | collective-permute-done | bytes 96 | tf_op jit(solution)/shard_map/ppermute | solution.py:101
  243.7 4.4 %collective-permute-done.22 = f32[16]{0:T(128)S(1)} collective-permute-done((f32[16]{0:T(128)S(1)}, f32[16]{0:T(128)S(1)}, u32[]{:S(2)}, u32[]{:S(2)}) %collective-permute-start.22) | collective-permute-done | bytes 96 | tf_op jit(solution)/shard_map/ppermute | solution.py:101
  248.4 3.2 %collective-permute-done.23 = f32[16]{0:T(128)S(1)} collective-permute-done((f32[16]{0:T(128)S(1)}, f32[16]{0:T(128)S(1)}, u32[]{:S(2)}, u32[]{:S(2)}) %collective-permute-start.23) | collective-permute-done | bytes 96 | tf_op jit(solution)/shard_map/ppermute | solution.py:101
  (147 shorter events, 66.5 us)
Async XLA Ops:
  2.8 12.2 %collective-permute-start = (bf16[128,1024]{1,0:T(8,128)(2,1)S(1)}, bf16[128,1024]{1,0:T(8,128)(2,1)S(1)}, u32[]{:S(2)}, u32[]{:S(2)}) collective-permute-start(bf16[128,1024]{1,0:T(8,128)(2,1)S(1)} %get-tuple-element.51), channel_id=1, source_target_pairs={{0,8},{8,16},{16,24},{24,0},{1,9},{9,17},{17,25},{25,1},{2,10},{10... | collective-permute-start | bytes 786440 | tf_op jit(solution)/shard_map/ppermute | solution.py:34
  5.9 14.7 %collective-permute-start.5 = (bf16[128,1024]{1,0:T(8,128)(2,1)S(1)}, bf16[128,1024]{1,0:T(8,128)(2,1)S(1)}, u32[]{:S(2)}, u32[]{:S(2)}) collective-permute-start(bf16[128,1024]{1,0:T(8,128)(2,1)S(1)} %get-tuple-element.45), channel_id=1, source_target_pairs={{0,8},{8,16},{16,24},{24,0},{1,9},{9,17},{17,25},{25,1},{2,10},{10... | collective-permute-start | bytes 786440 | tf_op jit(solution)/shard_map/ppermute | solution.py:34
  7.5 63.0 %collective-permute-start.10 = (bf16[256,2304]{1,0:T(8,128)(2,1)S(1)}, bf16[256,2304]{1,0:T(8,128)(2,1)}, u32[]{:S(2)}, u32[]{:S(2)}) collective-permute-start(bf16[256,2304]{1,0:T(8,128)(2,1)S(1)} %copy-done.4), channel_id=1, source_target_pairs={{0,8},{8,16},{16,24},{24,0},{1,9},{9,17},{17,25},{25,1},{2,10},{10... | collective-permute-start | bytes 3538952 | tf_op jit(solution)/shard_map/ppermute | solution.py:34
  15.0 36.5 %collective-permute-start.1 = (bf16[128,1024]{1,0:T(8,128)(2,1)S(1)}, bf16[128,1024]{1,0:T(8,128)(2,1)S(1)}, u32[]{:S(2)}, u32[]{:S(2)}) collective-permute-start(bf16[128,1024]{1,0:T(8,128)(2,1)S(1)} %collective-permute-done), channel_id=1, source_target_pairs={{0,8},{8,16},{16,24},{24,0},{1,9},{9,17},{17,25},{25,1},{2,10},{10... | collective-permute-start | bytes 786440 | tf_op jit(solution)/shard_map/ppermute | solution.py:34
  20.6 36.5 %collective-permute-start.6 = (bf16[128,1024]{1,0:T(8,128)(2,1)S(1)}, bf16[128,1024]{1,0:T(8,128)(2,1)S(1)}, u32[]{:S(2)}, u32[]{:S(2)}) collective-permute-start(bf16[128,1024]{1,0:T(8,128)(2,1)S(1)} %collective-permute-done.5), channel_id=1, source_target_pairs={{0,8},{8,16},{16,24},{24,0},{1,9},{9,17},{17,25},{25,1},{2,10},{10... | collective-permute-start | bytes 786440 | tf_op jit(solution)/shard_map/ppermute | solution.py:34
  51.5 11.2 %collective-permute-start.2 = (bf16[128,1024]{1,0:T(8,128)(2,1)S(1)}, bf16[128,1024]{1,0:T(8,128)(2,1)S(1)}, u32[]{:S(2)}, u32[]{:S(2)}) collective-permute-start(bf16[128,1024]{1,0:T(8,128)(2,1)S(1)} %collective-permute-done.1), channel_id=1, source_target_pairs={{0,8},{8,16},{16,24},{24,0},{1,9},{9,17},{17,25},{25,1},{2,10},{10... | collective-permute-start | bytes 786440 | tf_op jit(solution)/shard_map/ppermute | solution.py:34
  57.1 10.4 %collective-permute-start.7 = (bf16[128,1024]{1,0:T(8,128)(2,1)S(1)}, bf16[128,1024]{1,0:T(8,128)(2,1)S(1)}, u32[]{:S(2)}, u32[]{:S(2)}) collective-permute-start(bf16[128,1024]{1,0:T(8,128)(2,1)S(1)} %collective-permute-done.6), channel_id=1, source_target_pairs={{0,8},{8,16},{16,24},{24,0},{1,9},{9,17},{17,25},{25,1},{2,10},{10... | collective-permute-start | bytes 786440 | tf_op jit(solution)/shard_map/ppermute | solution.py:34
  62.9 23.7 %collective-permute-start.3 = (bf16[4,128,1024]{2,1,0:T(8,128)(2,1)S(1)}, bf16[4,128,1024]{2,1,0:T(8,128)(2,1)}, u32[]{:S(2)}, u32[]{:S(2)}) collective-permute-start(bf16[4,128,1024]{2,1,0:T(8,128)(2,1)S(1)} %get-tuple-element.43), channel_id=1, source_target_pairs={{0,2},{2,0},{1,3},{3,1},{4,6},{6,4},{5,7},{7,5},{8,10},{10,8},{9,1... | collective-permute-start | bytes 3145736 | tf_op jit(solution)/shard_map/ppermute | solution.py:34
  69.0 26.4 %collective-permute-start.8 = (bf16[4,128,1024]{2,1,0:T(8,128)(2,1)}, bf16[4,128,1024]{2,1,0:T(8,128)(2,1)}, u32[]{:S(2)}, u32[]{:S(2)}) collective-permute-start(bf16[4,128,1024]{2,1,0:T(8,128)(2,1)} %get-tuple-element.41), channel_id=1, source_target_pairs={{0,4},{4,0},{1,5},{5,1},{2,6},{6,2},{3,7},{7,3},{8,12},{12,8},{9,1... | collective-permute-start | bytes 3145736 | tf_op jit(solution)/shard_map/ppermute | solution.py:34
  70.5 29.2 %collective-permute-start.11 = (bf16[256,2304]{1,0:T(8,128)(2,1)}, bf16[256,2304]{1,0:T(8,128)(2,1)}, u32[]{:S(2)}, u32[]{:S(2)}) collective-permute-start(bf16[256,2304]{1,0:T(8,128)(2,1)} %collective-permute-done.10), channel_id=1, source_target_pairs={{0,8},{8,16},{16,24},{24,0},{1,9},{9,17},{17,25},{25,1},{2,10},{10... | collective-permute-start | bytes 3538952 | tf_op jit(solution)/shard_map/ppermute | solution.py:34
  88.1 50.6 %collective-permute-start.4 = (bf16[2,4,128,1024]{3,2,1,0:T(8,128)(2,1)S(1)}, bf16[2,4,128,1024]{3,2,1,0:T(8,128)(2,1)}, u32[]{:S(2)}, u32[]{:S(2)}) collective-permute-start(bf16[2,4,128,1024]{3,2,1,0:T(8,128)(2,1)S(1)} %pad_maximum_fusion.1), channel_id=1, source_target_pairs={{0,4},{4,0},{1,5},{5,1},{2,6},{6,2},{3,7},{7,3},{8,12},{12,8},{9,1... | collective-permute-start | bytes 6291464 | tf_op jit(solution)/shard_map/ppermute | solution.py:34
  98.2 44.5 %collective-permute-start.9 = (bf16[2,4,128,1024]{3,2,1,0:T(8,128)(2,1)}, bf16[2,4,128,1024]{3,2,1,0:T(8,128)(2,1)}, u32[]{:S(2)}, u32[]{:S(2)}) collective-permute-start(bf16[2,4,128,1024]{3,2,1,0:T(8,128)(2,1)} %pad_maximum_fusion.2), channel_id=1, source_target_pairs={{0,2},{2,0},{1,3},{3,1},{4,6},{6,4},{5,7},{7,5},{8,10},{10,8},{9,1... | collective-permute-start | bytes 6291464 | tf_op jit(solution)/shard_map/ppermute | solution.py:34
  99.7 27.4 %collective-permute-start.12 = (bf16[256,2304]{1,0:T(8,128)(2,1)}, bf16[256,2304]{1,0:T(8,128)(2,1)}, u32[]{:S(2)}, u32[]{:S(2)}) collective-permute-start(bf16[256,2304]{1,0:T(8,128)(2,1)} %collective-permute-done.11), channel_id=1, source_target_pairs={{0,8},{8,16},{16,24},{24,0},{1,9},{9,17},{17,25},{25,1},{2,10},{10... | collective-permute-start | bytes 3538952 | tf_op jit(solution)/shard_map/ppermute | solution.py:34
  166.2 9.2 %collective-permute-start.14 = (bf16[128,4,256]{2,0,1:T(8,128)(2,1)S(1)}, bf16[128,4,256]{2,0,1:T(8,128)(2,1)S(1)}, u32[]{:S(2)}, u32[]{:S(2)}) collective-permute-start(bf16[128,4,256]{2,0,1:T(8,128)(2,1)S(1)} %bitcast.199), channel_id=1, source_target_pairs={{0,6},{2,0},{4,2},{6,4},{1,7},{3,1},{5,3},{7,5},{8,14},{10,8},{12,... | collective-permute-start | bytes 786440 | tf_op jit(solution)/shard_map/ppermute | solution.py:71
  168.4 13.8 %collective-permute-start.15 = (bf16[128,4,256]{2,0,1:T(8,128)(2,1)S(1)}, bf16[128,4,256]{2,0,1:T(8,128)(2,1)S(1)}, u32[]{:S(2)}, u32[]{:S(2)}) collective-permute-start(bf16[128,4,256]{2,0,1:T(8,128)(2,1)S(1)} %bitcast.200), channel_id=1, source_target_pairs={{0,4},{2,6},{4,0},{6,2},{1,5},{3,7},{5,1},{7,3},{8,12},{10,14},{12... | collective-permute-start | bytes 786440 | tf_op jit(solution)/shard_map/ppermute | solution.py:71
  169.2 13.0 %collective-permute-start.16 = (bf16[128,4,256]{2,0,1:T(8,128)(2,1)S(1)}, bf16[128,4,256]{2,0,1:T(8,128)(2,1)S(1)}, u32[]{:S(2)}, u32[]{:S(2)}) collective-permute-start(bf16[128,4,256]{2,0,1:T(8,128)(2,1)S(1)} %bitcast.201), channel_id=1, source_target_pairs={{0,2},{2,4},{4,6},{6,0},{1,3},{3,5},{5,7},{7,1},{8,10},{10,12},{12... | collective-permute-start | bytes 786440 | tf_op jit(solution)/shard_map/ppermute | solution.py:71
  191.6 27.0 %collective-permute-start.19 = (f32[2,128,1152]{2,1,0:T(8,128)S(1)}, f32[2,128,1152]{2,1,0:T(8,128)}, u32[]{:S(2)}, u32[]{:S(2)}) collective-permute-start(f32[2,128,1152]{2,1,0:T(8,128)S(1)} %dynamic-slice_bitcast_fusion), channel_id=1, source_target_pairs={{0,4},{4,0},{1,5},{5,1},{2,6},{6,2},{3,7},{7,3},{8,12},{12,8},{9,1... | collective-permute-start | bytes 3538952 | tf_op jit(solution)/shard_map/ppermute | solution.py:90
  193.3 28.2 %collective-permute-start.17 = (f32[2,128,1152]{2,1,0:T(8,128)}, f32[2,128,1152]{2,1,0:T(8,128)}, u32[]{:S(2)}, u32[]{:S(2)}) collective-permute-start(f32[2,128,1152]{2,1,0:T(8,128)} %dynamic-slice_bitcast_fusion.1), channel_id=1, source_target_pairs={{0,2},{2,0},{1,3},{3,1},{4,6},{6,4},{5,7},{7,5},{8,10},{10,8},{9,1... | collective-permute-start | bytes 3538952 | tf_op jit(solution)/shard_map/ppermute | solution.py:90
  220.5 13.7 %collective-permute-start.20 = (f32[128,1152]{1,0:T(8,128)S(1)}, f32[128,1152]{1,0:T(8,128)S(1)}, u32[]{:S(2)}, u32[]{:S(2)}) collective-permute-start(f32[128,1152]{1,0:T(8,128)S(1)} %dynamic-slice_bitcast_fusion.2), channel_id=1, source_target_pairs={{0,2},{2,0},{1,3},{3,1},{4,6},{6,4},{5,7},{7,5},{8,10},{10,8},{9,1... | collective-permute-start | bytes 1769480 | tf_op jit(solution)/shard_map/ppermute | solution.py:93
  223.0 14.1 %collective-permute-start.18 = (f32[128,1152]{1,0:T(8,128)S(1)}, f32[128,1152]{1,0:T(8,128)S(1)}, u32[]{:S(2)}, u32[]{:S(2)}) collective-permute-start(f32[128,1152]{1,0:T(8,128)S(1)} %dynamic-slice_bitcast_fusion.3), channel_id=1, source_target_pairs={{0,4},{4,0},{1,5},{5,1},{2,6},{6,2},{3,7},{7,3},{8,12},{12,8},{9,1... | collective-permute-start | bytes 1769480 | tf_op jit(solution)/shard_map/ppermute | solution.py:93
  240.1 3.6 %collective-permute-start.21 = (f32[16]{0:T(128)S(1)}, f32[16]{0:T(128)S(1)}, u32[]{:S(2)}, u32[]{:S(2)}) collective-permute-start(f32[16]{0:T(128)S(1)} %select_reduce_fusion), channel_id=1, source_target_pairs={{0,8},{8,0},{16,24},{24,16},{1,9},{9,1},{17,25},{25,17},{2,10},{10... | collective-permute-start | bytes 200 | tf_op jit(solution)/shard_map/ppermute | solution.py:101
  243.7 4.4 %collective-permute-start.22 = (f32[16]{0:T(128)S(1)}, f32[16]{0:T(128)S(1)}, u32[]{:S(2)}, u32[]{:S(2)}) collective-permute-start(f32[16]{0:T(128)S(1)} %add.552), channel_id=1, source_target_pairs={{0,16},{8,24},{16,0},{24,8},{1,17},{9,25},{17,1},{25,9},{2,18},{10... | collective-permute-start | bytes 200 | tf_op jit(solution)/shard_map/ppermute | solution.py:101
  248.1 3.5 %collective-permute-start.23 = (f32[16]{0:T(128)S(1)}, f32[16]{0:T(128)S(1)}, u32[]{:S(2)}, u32[]{:S(2)}) collective-permute-start(f32[16]{0:T(128)S(1)} %add.553), channel_id=1, source_target_pairs={{0,4},{4,0},{1,5},{5,1},{2,6},{6,2},{3,7},{7,3},{8,12},{12,8},{9,1... | collective-permute-start | bytes 200 | tf_op jit(solution)/shard_map/ppermute | solution.py:101
  251.6 3.5 %collective-permute-start.24 = (f32[16]{0:T(128)S(1)}, f32[16]{0:T(128)S(1)}, u32[]{:S(2)}, u32[]{:S(2)}) collective-permute-start(f32[16]{0:T(128)S(1)} %add.554), channel_id=1, source_target_pairs={{0,2},{2,0},{1,3},{3,1},{4,6},{6,4},{5,7},{7,5},{8,10},{10,8},{9,1... | collective-permute-start | bytes 200 | tf_op jit(solution)/shard_map/ppermute | solution.py:101
  (14 other events, 186.1 us)

commit v15 on v14

--- a/solution.py
+++ b/solution.py
@@ -174,7 +174,7 @@
     outer = lax.axis_size("c0")
     inner = lax.axis_size(INNER)
     rows_each = out_weight.shape[0]
-    weight_rows = ring_gather(out_weight, "c0")
+    weight_rows = ring_pieces(out_weight, "c0")
     arrival = (lax.axis_index("c0") - jnp.arange(outer, dtype=jnp.int32)) % outer
     half = kv_local // 2
     splits = [(0, half, ("c0", "c2", "c1")), (half, kv_local, ("c0", "c1", "c2"))]
@@ -206,13 +206,12 @@
     attended = (numerator / denominator[..., None]).astype(jnp.bfloat16)
     attended = attended.transpose(2, 0, 1, 3).reshape(tok_dev, kv_local * group_repeat * HEAD_WIDTH)
     all_heads = ring_all_gather(attended, "head").transpose(1, 0, 2).reshape(tok_dev, -1)
-    weight_rows = weight_rows.reshape(outer * rows_each, out_weight.shape[1])
     blocks = all_heads.reshape(tok_dev, outer, inner, rows_each).transpose(2, 0, 1, 3)
     regrouped = permute_all_to_all(blocks, INNER)
     regrouped = jnp.take(regrouped.reshape(inner * tok_dev, outer, rows_each), arrival, axis=1)
-    partial = jnp.dot(
-        regrouped.reshape(inner * tok_dev, outer * rows_each), weight_rows, preferred_element_type=jnp.float32
-    )
+    partial = jnp.dot(regrouped[:, 0], weight_rows[0], preferred_element_type=jnp.float32)
+    for t in range(1, outer):
+        partial = partial + jnp.dot(regrouped[:, t], weight_rows[t], preferred_element_type=jnp.float32)
     by_dest = partial.reshape(2, 2, tok_dev, -1)
     cut = by_dest.shape[-1] // 2
     mixed = jnp.concatenate([

time: 256 us -> 235 us (0.918)
  waiting for transfers between devices: 170 us -> 155 us
  other arithmetic: 19.2 us -> 11.6 us
    ppermute x14, waiting for transfers between devices: 108 us -> 92.7 us  [ring_pieces(): lax.ppermute(pieces[-1], axis, [(k, (k + 1) % n) for k in range(n)])]
    another operation x8 -> x7, other arithmetic: 9.85 us -> 2.23 us  [ring_gather(): return jnp.stack(ring_pieces(x, axis))]
    dot_general x1 -> x4, matrix products: 4.94 us -> 7.17 us  [the longest x3 6.18 us: shards(): jnp.dot(regrouped[:, t], weight_rows[t], preferred_element_type=jnp.float32)]
    unnamed x38 -> x34, local copies, waits for them, and re-layouts: 3.53 us -> 5.6 us
  transfers between devices with their start and end apart: 25 -> 25, of which waited for: 21 -> 20; matrix products, arithmetic and copies ran while one was open for 11% -> 11% of each run, Pallas kernels for 0% -> 0%
where the time goes in v15:
time: 235 us; the launch traced here: 234 us
  waiting for transfers between devices  155 us (66%)
  local copies, waits for them, and re-layouts  25.3 us (11%)
  starting transfers between devices  20.3 us (9%)
  matrix products  18.3 us (8%)
  other arithmetic  11.6 us (5%)
  blocking collectives  2.47 us (1%)
    ppermute x14, waiting for transfers between devices, ring_pieces(): lax.ppermute(pieces[-1], axis, [(k, (k + 1) % n) for k in range(n)])  92.7 us
    ppermute x2, waiting for transfers between devices, swap_reduce_scatter(): keep = keep + lax.ppermute(sent, first, [(0, 1), (1, 0)])  24.1 us
    ppermute x4, waiting for transfers between devices, butterfly_sum(): x = x + lax.ppermute(x, axis, [(i, i ^ bit) for i in range(size)])  13.3 us
    reshape x4, local copies, waits for them, and re-layouts, shards(): gathered.append((got.reshape(key_rows.shape[0], -1), key_rows))  13.3 us
    ppermute x14, starting transfers between devices, ring_pieces(): lax.ppermute(pieces[-1], axis, [(k, (k + 1) % n) for k in range(n)])  13.2 us
    ppermute x2, waiting for transfers between devices, swap_reduce_scatter(): return mine + lax.ppermute(sent, second, [(0, 1), (1, 0)])  13.1 us
    ppermute x3, waiting for transfers between devices, permute_all_to_all(): lax.ppermute(sent, axes, [(k, (k + shift) % n) for k in range(n)])  12.2 us
    dot_general x3, matrix products, shards(): jnp.dot(regrouped[:, t], weight_rows[t], preferred_element_type=jnp.float32)  6.18 us
  transfers between devices with their start and end apart: 25, of which 20 were waited for; matrix products, arithmetic and copies ran while one was open for 11% of the time, Pallas kernels for 0%

profile of v15, /device:TPU:0, one launch (start us, length us, event | category | flops | bytes accessed | tf_op | source)
XLA Modules:
  0.0 234.5 jit_solution(9069501297658023585)
XLA Ops:
  1.9 3.1 %collective-permute-start = (bf16[128,1024]{1,0:T(8,128)(2,1)S(1)}, bf16[128,1024]{1,0:T(8,128)(2,1)S(1)}, u32[]{:S(2)}, u32[]{:S(2)}) collective-permute-start(bf16[128,1024]{1,0:T(8,128)(2,1)S(1)} %get-tuple-element.57), channel_id=1, source_target_pairs={{0,8},{8,16},{16,24},{24,0},{1,9},{9,17},{17,25},{25,1},{2,10},{10... | collective-permute-start | bytes 786440 | tf_op jit(solution)/shard_map/ppermute | solution.py:34
  6.7 7.5 %collective-permute-done = bf16[128,1024]{1,0:T(8,128)(2,1)S(1)} collective-permute-done((bf16[128,1024]{1,0:T(8,128)(2,1)S(1)}, bf16[128,1024]{1,0:T(8,128)(2,1)S(1)}, u32[]{:S(2)}, u32[]{:S(2)}) %collective-permute-start) | collective-permute-done | bytes 262176 | tf_op jit(solution)/shard_map/ppermute | solution.py:34
  14.2 5.6 %collective-permute-done.5 = bf16[128,1024]{1,0:T(8,128)(2,1)S(1)} collective-permute-done((bf16[128,1024]{1,0:T(8,128)(2,1)S(1)}, bf16[128,1024]{1,0:T(8,128)(2,1)S(1)}, u32[]{:S(2)}, u32[]{:S(2)}) %collective-permute-start.5) | collective-permute-done | bytes 262176 | tf_op jit(solution)/shard_map/ppermute | solution.py:34
  19.8 5.6 %collective-permute-done.1 = bf16[128,1024]{1,0:T(8,128)(2,1)S(1)} collective-permute-done((bf16[128,1024]{1,0:T(8,128)(2,1)S(1)}, bf16[128,1024]{1,0:T(8,128)(2,1)S(1)}, u32[]{:S(2)}, u32[]{:S(2)}) %collective-permute-start.1) | collective-permute-done | bytes 262176 | tf_op jit(solution)/shard_map/ppermute | solution.py:34
  25.4 5.6 %collective-permute-done.6 = bf16[128,1024]{1,0:T(8,128)(2,1)S(1)} collective-permute-done((bf16[128,1024]{1,0:T(8,128)(2,1)S(1)}, bf16[128,1024]{1,0:T(8,128)(2,1)S(1)}, u32[]{:S(2)}, u32[]{:S(2)}) %collective-permute-start.6) | collective-permute-done | bytes 262176 | tf_op jit(solution)/shard_map/ppermute | solution.py:34
  32.6 4.0 %collective-permute-done.2 = bf16[128,1024]{1,0:T(8,128)(2,1)S(1)} collective-permute-done((bf16[128,1024]{1,0:T(8,128)(2,1)S(1)}, bf16[128,1024]{1,0:T(8,128)(2,1)S(1)}, u32[]{:S(2)}, u32[]{:S(2)}) %collective-permute-start.2) | collective-permute-done | bytes 262176 | tf_op jit(solution)/shard_map/ppermute | solution.py:34
  38.6 3.6 %collective-permute-done.7 = bf16[128,1024]{1,0:T(8,128)(2,1)S(1)} collective-permute-done((bf16[128,1024]{1,0:T(8,128)(2,1)S(1)}, bf16[128,1024]{1,0:T(8,128)(2,1)S(1)}, u32[]{:S(2)}, u32[]{:S(2)}) %collective-permute-start.7) | collective-permute-done | bytes 262176 | tf_op jit(solution)/shard_map/ppermute | solution.py:34
  44.3 22.5 %collective-permute-done.10 = bf16[256,2304]{1,0:T(8,128)(2,1)} collective-permute-done((bf16[256,2304]{1,0:T(8,128)(2,1)S(1)}, bf16[256,2304]{1,0:T(8,128)(2,1)}, u32[]{:S(2)}, u32[]{:S(2)}) %collective-permute-start.10) | collective-permute-done | bytes 1179680 | tf_op jit(solution)/shard_map/ppermute | solution.py:34
  71.6 24.5 %collective-permute-done.11 = bf16[256,2304]{1,0:T(8,128)(2,1)} collective-permute-done((bf16[256,2304]{1,0:T(8,128)(2,1)}, bf16[256,2304]{1,0:T(8,128)(2,1)}, u32[]{:S(2)}, u32[]{:S(2)}) %collective-permute-start.11) | collective-permute-done | bytes 1179680 | tf_op jit(solution)/shard_map/ppermute | solution.py:34
  99.2 2.5 %copy.71 = bf16[1024,1024]{0,1:T(8,128)(2,1)} copy(bf16[1024,1024]{1,0:T(8,128)(2,1)S(1)} %bitcast.180) | data formatting | bytes 4194304 | tf_op jit(solution)/shard_map/reshape | solution.py:188
  101.7 4.0 %copy.73 = bf16[1024,1024]{0,1:T(8,128)(2,1)} copy(bf16[1024,1024]{1,0:T(8,128)(2,1)} %bitcast.17) | data formatting | bytes 4194304 | tf_op jit(solution)/shard_map/reshape | solution.py:188
  105.7 8.3 %collective-permute-done.4 = bf16[2,4,128,1024]{3,2,1,0:T(8,128)(2,1)} collective-permute-done((bf16[2,4,128,1024]{3,2,1,0:T(8,128)(2,1)S(1)}, bf16[2,4,128,1024]{3,2,1,0:T(8,128)(2,1)}, u32[]{:S(2)}, u32[]{:S(2)}) %collective-permute-start.4) | collective-permute-done | bytes 2097184 | tf_op jit(solution)/shard_map/ppermute | solution.py:34
  114.0 2.9 %copy.72 = bf16[1024,1024]{0,1:T(8,128)(2,1)S(1)} copy(bf16[1024,1024]{1,0:T(8,128)(2,1)} %bitcast.9) | data formatting | bytes 4194304 | tf_op jit(solution)/shard_map/reshape | solution.py:188
  116.9 3.9 %copy.74 = bf16[1024,1024]{0,1:T(8,128)(2,1)} copy(bf16[1024,1024]{1,0:T(8,128)(2,1)} %bitcast.19) | data formatting | bytes 4194304 | tf_op jit(solution)/shard_map/reshape | solution.py:188
  120.8 3.6 %collective-permute-done.12 = bf16[256,2304]{1,0:T(8,128)(2,1)} collective-permute-done((bf16[256,2304]{1,0:T(8,128)(2,1)}, bf16[256,2304]{1,0:T(8,128)(2,1)}, u32[]{:S(2)}, u32[]{:S(2)}) %collective-permute-start.12) | collective-permute-done | bytes 1179680 | tf_op jit(solution)/shard_map/ppermute | solution.py:34
  148.0 5.5 %collective-permute-done.14 = bf16[128,4,256]{2,0,1:T(8,128)(2,1)S(1)} collective-permute-done((bf16[128,4,256]{2,0,1:T(8,128)(2,1)S(1)}, bf16[128,4,256]{2,0,1:T(8,128)(2,1)S(1)}, u32[]{:S(2)}, u32[]{:S(2)}) %collective-permute-start.14) | collective-permute-done | bytes 262176 | tf_op jit(solution)/shard_map/ppermute | solution.py:71
  153.6 6.7 %collective-permute-done.15 = bf16[128,4,256]{2,0,1:T(8,128)(2,1)S(1)} collective-permute-done((bf16[128,4,256]{2,0,1:T(8,128)(2,1)S(1)}, bf16[128,4,256]{2,0,1:T(8,128)(2,1)S(1)}, u32[]{:S(2)}, u32[]{:S(2)}) %collective-permute-start.15) | collective-permute-done | bytes 262176 | tf_op jit(solution)/shard_map/ppermute | solution.py:71
  173.4 24.1 %collective-permute-done.19 = f32[2,128,1152]{2,1,0:T(8,128)} collective-permute-done((f32[2,128,1152]{2,1,0:T(8,128)S(1)}, f32[2,128,1152]{2,1,0:T(8,128)}, u32[]{:S(2)}, u32[]{:S(2)}) %collective-permute-start.19) | collective-permute-done | bytes 1179680 | tf_op jit(solution)/shard_map/ppermute | solution.py:90
  202.7 10.2 %collective-permute-done.20 = f32[128,1152]{1,0:T(8,128)S(1)} collective-permute-done((f32[128,1152]{1,0:T(8,128)S(1)}, f32[128,1152]{1,0:T(8,128)S(1)}, u32[]{:S(2)}, u32[]{:S(2)}) %collective-permute-start.20) | collective-permute-done | bytes 589856 | tf_op jit(solution)/shard_map/ppermute | solution.py:93
  213.0 2.9 %collective-permute-done.18 = f32[128,1152]{1,0:T(8,128)S(1)} collective-permute-done((f32[128,1152]{1,0:T(8,128)S(1)}, f32[128,1152]{1,0:T(8,128)S(1)}, u32[]{:S(2)}, u32[]{:S(2)}) %collective-permute-start.18) | collective-permute-done | bytes 589856 | tf_op jit(solution)/shard_map/ppermute | solution.py:93
  216.2 2.5 %psum.7 = f32[3,128]{1,0:T(4,128)S(1)} all-reduce(f32[3,128]{1,0:T(4,128)S(1)} %pad_maximum_fusion.9), channel_id=1, replica_groups=mesh['c0'=4,'c1'=2,'c2'=2,'head'=2] {'head'}, use_global_device_ids=true, to_apply=%region_13.14 | all-reduce | flops 384 | bytes 3072 | tf_op jit(solution)/shard_map/psum | solution.py:222
  218.9 3.5 %collective-permute-done.21 = f32[16]{0:T(128)S(1)} collective-permute-done((f32[16]{0:T(128)S(1)}, f32[16]{0:T(128)S(1)}, u32[]{:S(2)}, u32[]{:S(2)}) %collective-permute-start.21) | collective-permute-done | bytes 96 | tf_op jit(solution)/shard_map/ppermute | solution.py:101
  222.4 4.4 %collective-permute-done.22 = f32[16]{0:T(128)S(1)} collective-permute-done((f32[16]{0:T(128)S(1)}, f32[16]{0:T(128)S(1)}, u32[]{:S(2)}, u32[]{:S(2)}) %collective-permute-start.22) | collective-permute-done | bytes 96 | tf_op jit(solution)/shard_map/ppermute | solution.py:101
  227.2 3.3 %collective-permute-done.23 = f32[16]{0:T(128)S(1)} collective-permute-done((f32[16]{0:T(128)S(1)}, f32[16]{0:T(128)S(1)}, u32[]{:S(2)}, u32[]{:S(2)}) %collective-permute-start.23) | collective-permute-done | bytes 96 | tf_op jit(solution)/shard_map/ppermute | solution.py:101
  (145 shorter events, 63.1 us)
Async XLA Ops:
  1.9 12.2 %collective-permute-start = (bf16[128,1024]{1,0:T(8,128)(2,1)S(1)}, bf16[128,1024]{1,0:T(8,128)(2,1)S(1)}, u32[]{:S(2)}, u32[]{:S(2)}) collective-permute-start(bf16[128,1024]{1,0:T(8,128)(2,1)S(1)} %get-tuple-element.57), channel_id=1, source_target_pairs={{0,8},{8,16},{16,24},{24,0},{1,9},{9,17},{17,25},{25,1},{2,10},{10... | collective-permute-start | bytes 786440 | tf_op jit(solution)/shard_map/ppermute | solution.py:34
  5.1 14.7 %collective-permute-start.5 = (bf16[128,1024]{1,0:T(8,128)(2,1)S(1)}, bf16[128,1024]{1,0:T(8,128)(2,1)S(1)}, u32[]{:S(2)}, u32[]{:S(2)}) collective-permute-start(bf16[128,1024]{1,0:T(8,128)(2,1)S(1)} %get-tuple-element.51), channel_id=1, source_target_pairs={{0,8},{8,16},{16,24},{24,0},{1,9},{9,17},{17,25},{25,1},{2,10},{10... | collective-permute-start | bytes 786440 | tf_op jit(solution)/shard_map/ppermute | solution.py:34
  14.2 11.2 %collective-permute-start.1 = (bf16[128,1024]{1,0:T(8,128)(2,1)S(1)}, bf16[128,1024]{1,0:T(8,128)(2,1)S(1)}, u32[]{:S(2)}, u32[]{:S(2)}) collective-permute-start(bf16[128,1024]{1,0:T(8,128)(2,1)S(1)} %collective-permute-done), channel_id=1, source_target_pairs={{0,8},{8,16},{16,24},{24,0},{1,9},{9,17},{17,25},{25,1},{2,10},{10... | collective-permute-start | bytes 786440 | tf_op jit(solution)/shard_map/ppermute | solution.py:34
  19.8 11.2 %collective-permute-start.6 = (bf16[128,1024]{1,0:T(8,128)(2,1)S(1)}, bf16[128,1024]{1,0:T(8,128)(2,1)S(1)}, u32[]{:S(2)}, u32[]{:S(2)}) collective-permute-start(bf16[128,1024]{1,0:T(8,128)(2,1)S(1)} %collective-permute-done.5), channel_id=1, source_target_pairs={{0,8},{8,16},{16,24},{24,0},{1,9},{9,17},{17,25},{25,1},{2,10},{10... | collective-permute-start | bytes 786440 | tf_op jit(solution)/shard_map/ppermute | solution.py:34
  25.4 11.2 %collective-permute-start.2 = (bf16[128,1024]{1,0:T(8,128)(2,1)S(1)}, bf16[128,1024]{1,0:T(8,128)(2,1)S(1)}, u32[]{:S(2)}, u32[]{:S(2)}) collective-permute-start(bf16[128,1024]{1,0:T(8,128)(2,1)S(1)} %collective-permute-done.1), channel_id=1, source_target_pairs={{0,8},{8,16},{16,24},{24,0},{1,9},{9,17},{17,25},{25,1},{2,10},{10... | collective-permute-start | bytes 786440 | tf_op jit(solution)/shard_map/ppermute | solution.py:34
  31.0 11.2 %collective-permute-start.7 = (bf16[128,1024]{1,0:T(8,128)(2,1)S(1)}, bf16[128,1024]{1,0:T(8,128)(2,1)S(1)}, u32[]{:S(2)}, u32[]{:S(2)}) collective-permute-start(bf16[128,1024]{1,0:T(8,128)(2,1)S(1)} %collective-permute-done.6), channel_id=1, source_target_pairs={{0,8},{8,16},{16,24},{24,0},{1,9},{9,17},{17,25},{25,1},{2,10},{10... | collective-permute-start | bytes 786440 | tf_op jit(solution)/shard_map/ppermute | solution.py:34
  31.1 35.8 %collective-permute-start.10 = (bf16[256,2304]{1,0:T(8,128)(2,1)S(1)}, bf16[256,2304]{1,0:T(8,128)(2,1)}, u32[]{:S(2)}, u32[]{:S(2)}) collective-permute-start(bf16[256,2304]{1,0:T(8,128)(2,1)S(1)} %copy-done.4), channel_id=1, source_target_pairs={{0,8},{8,16},{16,24},{24,0},{1,9},{9,17},{17,25},{25,1},{2,10},{10... | collective-permute-start | bytes 3538952 | tf_op jit(solution)/shard_map/ppermute | solution.py:34
  36.8 30.0 %collective-permute-start.3 = (bf16[4,128,1024]{2,1,0:T(8,128)(2,1)S(1)}, bf16[4,128,1024]{2,1,0:T(8,128)(2,1)S(1)}, u32[]{:S(2)}, u32[]{:S(2)}) collective-permute-start(bf16[4,128,1024]{2,1,0:T(8,128)(2,1)S(1)} %get-tuple-element.49), channel_id=1, source_target_pairs={{0,2},{2,0},{1,3},{3,1},{4,6},{6,4},{5,7},{7,5},{8,10},{10,8},{9,1... | collective-permute-start | bytes 3145736 | tf_op jit(solution)/shard_map/ppermute | solution.py:34
  42.4 26.2 %collective-permute-start.8 = (bf16[4,128,1024]{2,1,0:T(8,128)(2,1)S(1)}, bf16[4,128,1024]{2,1,0:T(8,128)(2,1)S(1)}, u32[]{:S(2)}, u32[]{:S(2)}) collective-permute-start(bf16[4,128,1024]{2,1,0:T(8,128)(2,1)S(1)} %get-tuple-element.47), channel_id=1, source_target_pairs={{0,4},{4,0},{1,5},{5,1},{2,6},{6,2},{3,7},{7,3},{8,12},{12,8},{9,1... | collective-permute-start | bytes 3145736 | tf_op jit(solution)/shard_map/ppermute | solution.py:34
  66.8 29.3 %collective-permute-start.11 = (bf16[256,2304]{1,0:T(8,128)(2,1)}, bf16[256,2304]{1,0:T(8,128)(2,1)}, u32[]{:S(2)}, u32[]{:S(2)}) collective-permute-start(bf16[256,2304]{1,0:T(8,128)(2,1)} %collective-permute-done.10), channel_id=1, source_target_pairs={{0,8},{8,16},{16,24},{24,0},{1,9},{9,17},{17,25},{25,1},{2,10},{10... | collective-permute-start | bytes 3538952 | tf_op jit(solution)/shard_map/ppermute | solution.py:34
  67.0 47.0 %collective-permute-start.4 = (bf16[2,4,128,1024]{3,2,1,0:T(8,128)(2,1)S(1)}, bf16[2,4,128,1024]{3,2,1,0:T(8,128)(2,1)}, u32[]{:S(2)}, u32[]{:S(2)}) collective-permute-start(bf16[2,4,128,1024]{3,2,1,0:T(8,128)(2,1)S(1)} %pad_maximum_fusion), channel_id=1, source_target_pairs={{0,4},{4,0},{1,5},{5,1},{2,6},{6,2},{3,7},{7,3},{8,12},{12,8},{9,1... | collective-permute-start | bytes 6291464 | tf_op jit(solution)/shard_map/ppermute | solution.py:34
  70.1 46.8 %collective-permute-start.9 = (bf16[2,4,128,1024]{3,2,1,0:T(8,128)(2,1)}, bf16[2,4,128,1024]{3,2,1,0:T(8,128)(2,1)}, u32[]{:S(2)}, u32[]{:S(2)}) collective-permute-start(bf16[2,4,128,1024]{3,2,1,0:T(8,128)(2,1)} %pad_maximum_fusion.1), channel_id=1, source_target_pairs={{0,2},{2,0},{1,3},{3,1},{4,6},{6,4},{5,7},{7,5},{8,10},{10,8},{9,1... | collective-permute-start | bytes 6291464 | tf_op jit(solution)/shard_map/ppermute | solution.py:34
  96.1 28.3 %collective-permute-start.12 = (bf16[256,2304]{1,0:T(8,128)(2,1)}, bf16[256,2304]{1,0:T(8,128)(2,1)}, u32[]{:S(2)}, u32[]{:S(2)}) collective-permute-start(bf16[256,2304]{1,0:T(8,128)(2,1)} %collective-permute-done.11), channel_id=1, source_target_pairs={{0,8},{8,16},{16,24},{24,0},{1,9},{9,17},{17,25},{25,1},{2,10},{10... | collective-permute-start | bytes 3538952 | tf_op jit(solution)/shard_map/ppermute | solution.py:34
  144.1 9.4 %collective-permute-start.14 = (bf16[128,4,256]{2,0,1:T(8,128)(2,1)S(1)}, bf16[128,4,256]{2,0,1:T(8,128)(2,1)S(1)}, u32[]{:S(2)}, u32[]{:S(2)}) collective-permute-start(bf16[128,4,256]{2,0,1:T(8,128)(2,1)S(1)} %bitcast.206), channel_id=1, source_target_pairs={{0,6},{2,0},{4,2},{6,4},{1,7},{3,1},{5,3},{7,5},{8,14},{10,8},{12,... | collective-permute-start | bytes 786440 | tf_op jit(solution)/shard_map/ppermute | solution.py:71
  146.5 13.8 %collective-permute-start.15 = (bf16[128,4,256]{2,0,1:T(8,128)(2,1)S(1)}, bf16[128,4,256]{2,0,1:T(8,128)(2,1)S(1)}, u32[]{:S(2)}, u32[]{:S(2)}) collective-permute-start(bf16[128,4,256]{2,0,1:T(8,128)(2,1)S(1)} %bitcast.207), channel_id=1, source_target_pairs={{0,4},{2,6},{4,0},{6,2},{1,5},{3,7},{5,1},{7,3},{8,12},{10,14},{12... | collective-permute-start | bytes 786440 | tf_op jit(solution)/shard_map/ppermute | solution.py:71
  147.3 13.0 %collective-permute-start.16 = (bf16[128,4,256]{2,0,1:T(8,128)(2,1)S(1)}, bf16[128,4,256]{2,0,1:T(8,128)(2,1)S(1)}, u32[]{:S(2)}, u32[]{:S(2)}) collective-permute-start(bf16[128,4,256]{2,0,1:T(8,128)(2,1)S(1)} %bitcast.208), channel_id=1, source_target_pairs={{0,2},{2,4},{4,6},{6,0},{1,3},{3,5},{5,7},{7,1},{8,10},{10,12},{12... | collective-permute-start | bytes 786440 | tf_op jit(solution)/shard_map/ppermute | solution.py:71
  170.4 27.0 %collective-permute-start.19 = (f32[2,128,1152]{2,1,0:T(8,128)S(1)}, f32[2,128,1152]{2,1,0:T(8,128)}, u32[]{:S(2)}, u32[]{:S(2)}) collective-permute-start(f32[2,128,1152]{2,1,0:T(8,128)S(1)} %dynamic-slice_bitcast_fusion), channel_id=1, source_target_pairs={{0,4},{4,0},{1,5},{5,1},{2,6},{6,2},{3,7},{7,3},{8,12},{12,8},{9,1... | collective-permute-start | bytes 3538952 | tf_op jit(solution)/shard_map/ppermute | solution.py:90
  172.1 28.2 %collective-permute-start.17 = (f32[2,128,1152]{2,1,0:T(8,128)}, f32[2,128,1152]{2,1,0:T(8,128)}, u32[]{:S(2)}, u32[]{:S(2)}) collective-permute-start(f32[2,128,1152]{2,1,0:T(8,128)} %dynamic-slice_bitcast_fusion.1), channel_id=1, source_target_pairs={{0,2},{2,0},{1,3},{3,1},{4,6},{6,4},{5,7},{7,5},{8,10},{10,8},{9,1... | collective-permute-start | bytes 3538952 | tf_op jit(solution)/shard_map/ppermute | solution.py:90
  199.2 13.7 %collective-permute-start.20 = (f32[128,1152]{1,0:T(8,128)S(1)}, f32[128,1152]{1,0:T(8,128)S(1)}, u32[]{:S(2)}, u32[]{:S(2)}) collective-permute-start(f32[128,1152]{1,0:T(8,128)S(1)} %dynamic-slice_bitcast_fusion.2), channel_id=1, source_target_pairs={{0,2},{2,0},{1,3},{3,1},{4,6},{6,4},{5,7},{7,5},{8,10},{10,8},{9,1... | collective-permute-start | bytes 1769480 | tf_op jit(solution)/shard_map/ppermute | solution.py:93
  201.8 14.1 %collective-permute-start.18 = (f32[128,1152]{1,0:T(8,128)S(1)}, f32[128,1152]{1,0:T(8,128)S(1)}, u32[]{:S(2)}, u32[]{:S(2)}) collective-permute-start(f32[128,1152]{1,0:T(8,128)S(1)} %dynamic-slice_bitcast_fusion.3), channel_id=1, source_target_pairs={{0,4},{4,0},{1,5},{5,1},{2,6},{6,2},{3,7},{7,3},{8,12},{12,8},{9,1... | collective-permute-start | bytes 1769480 | tf_op jit(solution)/shard_map/ppermute | solution.py:93
  218.8 3.6 %collective-permute-start.21 = (f32[16]{0:T(128)S(1)}, f32[16]{0:T(128)S(1)}, u32[]{:S(2)}, u32[]{:S(2)}) collective-permute-start(f32[16]{0:T(128)S(1)} %select_reduce_fusion), channel_id=1, source_target_pairs={{0,8},{8,0},{16,24},{24,16},{1,9},{9,1},{17,25},{25,17},{2,10},{10... | collective-permute-start | bytes 200 | tf_op jit(solution)/shard_map/ppermute | solution.py:101
  222.4 4.4 %collective-permute-start.22 = (f32[16]{0:T(128)S(1)}, f32[16]{0:T(128)S(1)}, u32[]{:S(2)}, u32[]{:S(2)}) collective-permute-start(f32[16]{0:T(128)S(1)} %add.564), channel_id=1, source_target_pairs={{0,16},{8,24},{16,0},{24,8},{1,17},{9,25},{17,1},{25,9},{2,18},{10... | collective-permute-start | bytes 200 | tf_op jit(solution)/shard_map/ppermute | solution.py:101
  226.9 3.5 %collective-permute-start.23 = (f32[16]{0:T(128)S(1)}, f32[16]{0:T(128)S(1)}, u32[]{:S(2)}, u32[]{:S(2)}) collective-permute-start(f32[16]{0:T(128)S(1)} %add.565), channel_id=1, source_target_pairs={{0,4},{4,0},{1,5},{5,1},{2,6},{6,2},{3,7},{7,3},{8,12},{12,8},{9,1... | collective-permute-start | bytes 200 | tf_op jit(solution)/shard_map/ppermute | solution.py:101
  230.4 3.5 %collective-permute-start.24 = (f32[16]{0:T(128)S(1)}, f32[16]{0:T(128)S(1)}, u32[]{:S(2)}, u32[]{:S(2)}) collective-permute-start(f32[16]{0:T(128)S(1)} %add.566), channel_id=1, source_target_pairs={{0,2},{2,0},{1,3},{3,1},{4,6},{6,4},{5,7},{7,5},{8,10},{10,8},{9,1... | collective-permute-start | bytes 200 | tf_op jit(solution)/shard_map/ppermute | solution.py:101
  (12 other events, 149.8 us)

commit v16 on v15

--- a/solution.py
+++ b/solution.py
@@ -187,7 +187,10 @@
             key_rows = (source[:, None] * tok_dev + jnp.arange(tok_dev, dtype=jnp.int32)[None, :]).reshape(-1)
             gathered.append((got.reshape(key_rows.shape[0], -1), key_rows))
             bounds.append((first, last))
-    gathered, weight_rows = lax.optimization_barrier((gathered, weight_rows))
+    late = [len(gathered) - 1 - k for k in range(len(gathered)) if k % 2 == 0]
+    held, weight_rows = lax.optimization_barrier(([gathered[k] for k in late], weight_rows))
+    for k, piece in zip(late, held):
+        gathered[k] = piece
     numerators, denominators = [], []
     states = {}
     for (first, last), (got, key_rows) in zip(bounds, gathered):

time: 235 us -> 233 us (level)
  waiting for transfers between devices: 155 us -> 151 us
  local copies, waits for them, and re-layouts: 25.3 us -> 28.6 us
    reshape x4 -> x2, local copies, waits for them, and re-layouts: 13.3 us -> 6.83 us  [shards(): gathered.append((got.reshape(key_rows.shape[0], -1), key_rows))]
    unnamed x34 -> x48, local copies, waits for them, and re-layouts: 5.6 us -> 11.9 us
    ppermute x14, waiting for transfers between devices: 92.7 us -> 87.9 us  [ring_pieces(): lax.ppermute(pieces[-1], axis, [(k, (k + 1) % n) for k in range(n)])]
    slice x4, local copies, waits for them, and re-layouts: 2.23 us -> 5.73 us  [shards(): got[:, :width]]
  transfers between devices with their start and end apart: 25 -> 25, of which waited for: 20 -> 20; matrix products, arithmetic and copies ran while one was open for 11% -> 13% of each run, Pallas kernels for 0% -> 0%
where the time goes in v16:
time: 233 us; the launch traced here: 232 us
  waiting for transfers between devices  151 us (65%)
  local copies, waits for them, and re-layouts  28.6 us (12%)
  starting transfers between devices  20.4 us (9%)
  matrix products  17.2 us (7%)
  other arithmetic  11.5 us (5%)
  blocking collectives  2.47 us (1%)
    ppermute x14, waiting for transfers between devices, ring_pieces(): lax.ppermute(pieces[-1], axis, [(k, (k + 1) % n) for k in range(n)])  87.9 us
    ppermute x2, waiting for transfers between devices, swap_reduce_scatter(): keep = keep + lax.ppermute(sent, first, [(0, 1), (1, 0)])  24 us
    ppermute x4, waiting for transfers between devices, butterfly_sum(): x = x + lax.ppermute(x, axis, [(i, i ^ bit) for i in range(size)])  13.3 us
    ppermute x14, starting transfers between devices, ring_pieces(): lax.ppermute(pieces[-1], axis, [(k, (k + 1) % n) for k in range(n)])  13.2 us
    ppermute x2, waiting for transfers between devices, swap_reduce_scatter(): return mine + lax.ppermute(sent, second, [(0, 1), (1, 0)])  13.1 us
    ppermute x3, waiting for transfers between devices, permute_all_to_all(): lax.ppermute(sent, axes, [(k, (k + shift) % n) for k in range(n)])  12.2 us
    unnamed x48, local copies, waits for them, and re-layouts  11.9 us
    reshape x2, local copies, waits for them, and re-layouts, shards(): gathered.append((got.reshape(key_rows.shape[0], -1), key_rows))  6.83 us
  transfers between devices with their start and end apart: 25, of which 20 were waited for; matrix products, arithmetic and copies ran while one was open for 13% of the time, Pallas kernels for 0%

profile of v16, /device:TPU:0, one launch (start us, length us, event | category | flops | bytes accessed | tf_op | source)
XLA Modules:
  0.0 231.9 jit_solution(13605636639668840692)
XLA Ops:
  1.9 3.1 %collective-permute-start.4 = (bf16[128,1024]{1,0:T(8,128)(2,1)S(1)}, bf16[128,1024]{1,0:T(8,128)(2,1)S(1)}, u32[]{:S(2)}, u32[]{:S(2)}) collective-permute-start(bf16[128,1024]{1,0:T(8,128)(2,1)S(1)} %get-tuple-element.49), channel_id=1, source_target_pairs={{0,8},{8,16},{16,24},{24,0},{1,9},{9,17},{17,25},{25,1},{2,10},{10... | collective-permute-start | bytes 786440 | tf_op jit(solution)/shard_map/ppermute | solution.py:34
  6.7 7.5 %collective-permute-done.4 = bf16[128,1024]{1,0:T(8,128)(2,1)S(1)} collective-permute-done((bf16[128,1024]{1,0:T(8,128)(2,1)S(1)}, bf16[128,1024]{1,0:T(8,128)(2,1)S(1)}, u32[]{:S(2)}, u32[]{:S(2)}) %collective-permute-start.4) | collective-permute-done | bytes 262176 | tf_op jit(solution)/shard_map/ppermute | solution.py:34
  14.2 5.6 %collective-permute-done = bf16[128,1024]{1,0:T(8,128)(2,1)S(1)} collective-permute-done((bf16[128,1024]{1,0:T(8,128)(2,1)S(1)}, bf16[128,1024]{1,0:T(8,128)(2,1)S(1)}, u32[]{:S(2)}, u32[]{:S(2)}) %collective-permute-start) | collective-permute-done | bytes 262176 | tf_op jit(solution)/shard_map/ppermute | solution.py:34
  19.8 5.6 %collective-permute-done.5 = bf16[128,1024]{1,0:T(8,128)(2,1)S(1)} collective-permute-done((bf16[128,1024]{1,0:T(8,128)(2,1)S(1)}, bf16[128,1024]{1,0:T(8,128)(2,1)S(1)}, u32[]{:S(2)}, u32[]{:S(2)}) %collective-permute-start.5) | collective-permute-done | bytes 262176 | tf_op jit(solution)/shard_map/ppermute | solution.py:34
  25.4 5.6 %collective-permute-done.1 = bf16[128,1024]{1,0:T(8,128)(2,1)S(1)} collective-permute-done((bf16[128,1024]{1,0:T(8,128)(2,1)S(1)}, bf16[128,1024]{1,0:T(8,128)(2,1)S(1)}, u32[]{:S(2)}, u32[]{:S(2)}) %collective-permute-start.1) | collective-permute-done | bytes 262176 | tf_op jit(solution)/shard_map/ppermute | solution.py:34
  32.6 4.0 %collective-permute-done.6 = bf16[128,1024]{1,0:T(8,128)(2,1)S(1)} collective-permute-done((bf16[128,1024]{1,0:T(8,128)(2,1)S(1)}, bf16[128,1024]{1,0:T(8,128)(2,1)S(1)}, u32[]{:S(2)}, u32[]{:S(2)}) %collective-permute-start.6) | collective-permute-done | bytes 262176 | tf_op jit(solution)/shard_map/ppermute | solution.py:34
  38.6 3.6 %collective-permute-done.2 = bf16[128,1024]{1,0:T(8,128)(2,1)S(1)} collective-permute-done((bf16[128,1024]{1,0:T(8,128)(2,1)S(1)}, bf16[128,1024]{1,0:T(8,128)(2,1)S(1)}, u32[]{:S(2)}, u32[]{:S(2)}) %collective-permute-start.2) | collective-permute-done | bytes 262176 | tf_op jit(solution)/shard_map/ppermute | solution.py:34
  44.2 22.5 %collective-permute-done.10 = bf16[256,2304]{1,0:T(8,128)(2,1)S(1)} collective-permute-done((bf16[256,2304]{1,0:T(8,128)(2,1)S(1)}, bf16[256,2304]{1,0:T(8,128)(2,1)S(1)}, u32[]{:S(2)}, u32[]{:S(2)}) %collective-permute-start.10) | collective-permute-done | bytes 1179680 | tf_op jit(solution)/shard_map/ppermute | solution.py:34
  71.6 24.1 %collective-permute-done.11 = bf16[256,2304]{1,0:T(8,128)(2,1)} collective-permute-done((bf16[256,2304]{1,0:T(8,128)(2,1)S(1)}, bf16[256,2304]{1,0:T(8,128)(2,1)}, u32[]{:S(2)}, u32[]{:S(2)}) %collective-permute-start.11) | collective-permute-done | bytes 1179680 | tf_op jit(solution)/shard_map/ppermute | solution.py:34
  99.8 2.3 copy.86
  103.4 2.7 %fusion.98 = (bf16[1024,512]{1,0:T(8,128)(2,1)S(1)}, bf16[1024,512]{1,0:T(8,128)(2,1)}) fusion(bf16[1024,1024]{1,0:T(8,128)(2,1)} %bitcast.8), kind=kLoop, calls=%fused_computation.231 | loop fusion | bytes 4194304 | tf_op jit(solution)/shard_map/slice | solution.py:203
  109.7 4.2 %collective-permute-done.8 = bf16[2,4,128,1024]{3,2,1,0:T(8,128)(2,1)} collective-permute-done((bf16[2,4,128,1024]{3,2,1,0:T(8,128)(2,1)S(1)}, bf16[2,4,128,1024]{3,2,1,0:T(8,128)(2,1)}, u32[]{:S(2)}, u32[]{:S(2)}) %collective-permute-start.8) | collective-permute-done | bytes 2097184 | tf_op jit(solution)/shard_map/ppermute | solution.py:34
  113.9 4.0 %copy.74 = bf16[1024,1024]{0,1:T(8,128)(2,1)} copy(bf16[1024,1024]{1,0:T(8,128)(2,1)} %bitcast.22) | data formatting | bytes 4194304 | tf_op jit(solution)/shard_map/reshape | solution.py:188
  117.9 2.9 %copy.75 = bf16[1024,1024]{0,1:T(8,128)(2,1)S(1)} copy(bf16[1024,1024]{1,0:T(8,128)(2,1)} %bitcast.24) | data formatting | bytes 4194304 | tf_op jit(solution)/shard_map/reshape | solution.py:188
  120.8 3.3 %collective-permute-done.12 = bf16[256,2304]{1,0:T(8,128)(2,1)} collective-permute-done((bf16[256,2304]{1,0:T(8,128)(2,1)}, bf16[256,2304]{1,0:T(8,128)(2,1)}, u32[]{:S(2)}, u32[]{:S(2)}) %collective-permute-start.12) | collective-permute-done | bytes 1179680 | tf_op jit(solution)/shard_map/ppermute | solution.py:34
  146.2 5.5 %collective-permute-done.14 = bf16[128,4,256]{2,0,1:T(8,128)(2,1)S(1)} collective-permute-done((bf16[128,4,256]{2,0,1:T(8,128)(2,1)S(1)}, bf16[128,4,256]{2,0,1:T(8,128)(2,1)S(1)}, u32[]{:S(2)}, u32[]{:S(2)}) %collective-permute-start.14) | collective-permute-done | bytes 262176 | tf_op jit(solution)/shard_map/ppermute | solution.py:71
  151.6 6.7 %collective-permute-done.15 = bf16[128,4,256]{2,0,1:T(8,128)(2,1)S(1)} collective-permute-done((bf16[128,4,256]{2,0,1:T(8,128)(2,1)S(1)}, bf16[128,4,256]{2,0,1:T(8,128)(2,1)S(1)}, u32[]{:S(2)}, u32[]{:S(2)}) %collective-permute-start.15) | collective-permute-done | bytes 262176 | tf_op jit(solution)/shard_map/ppermute | solution.py:71
  170.8 24.0 %collective-permute-done.19 = f32[2,128,1152]{2,1,0:T(8,128)} collective-permute-done((f32[2,128,1152]{2,1,0:T(8,128)S(1)}, f32[2,128,1152]{2,1,0:T(8,128)}, u32[]{:S(2)}, u32[]{:S(2)}) %collective-permute-start.19) | collective-permute-done | bytes 1179680 | tf_op jit(solution)/shard_map/ppermute | solution.py:90
  200.1 10.2 %collective-permute-done.20 = f32[128,1152]{1,0:T(8,128)S(1)} collective-permute-done((f32[128,1152]{1,0:T(8,128)S(1)}, f32[128,1152]{1,0:T(8,128)S(1)}, u32[]{:S(2)}, u32[]{:S(2)}) %collective-permute-start.20) | collective-permute-done | bytes 589856 | tf_op jit(solution)/shard_map/ppermute | solution.py:93
  210.4 2.9 %collective-permute-done.18 = f32[128,1152]{1,0:T(8,128)S(1)} collective-permute-done((f32[128,1152]{1,0:T(8,128)S(1)}, f32[128,1152]{1,0:T(8,128)S(1)}, u32[]{:S(2)}, u32[]{:S(2)}) %collective-permute-start.18) | collective-permute-done | bytes 589856 | tf_op jit(solution)/shard_map/ppermute | solution.py:93
  213.6 2.5 %psum.7 = f32[3,128]{1,0:T(4,128)S(1)} all-reduce(f32[3,128]{1,0:T(4,128)S(1)} %pad_maximum_fusion.9), channel_id=1, replica_groups=mesh['c0'=4,'c1'=2,'c2'=2,'head'=2] {'head'}, use_global_device_ids=true, to_apply=%region_13.14 | all-reduce | flops 384 | bytes 3072 | tf_op jit(solution)/shard_map/psum | solution.py:225
  216.3 3.5 %collective-permute-done.21 = f32[16]{0:T(128)S(1)} collective-permute-done((f32[16]{0:T(128)S(1)}, f32[16]{0:T(128)S(1)}, u32[]{:S(2)}, u32[]{:S(2)}) %collective-permute-start.21) | collective-permute-done | bytes 96 | tf_op jit(solution)/shard_map/ppermute | solution.py:101
  219.8 4.4 %collective-permute-done.22 = f32[16]{0:T(128)S(1)} collective-permute-done((f32[16]{0:T(128)S(1)}, f32[16]{0:T(128)S(1)}, u32[]{:S(2)}, u32[]{:S(2)}) %collective-permute-start.22) | collective-permute-done | bytes 96 | tf_op jit(solution)/shard_map/ppermute | solution.py:101
  224.6 3.3 %collective-permute-done.23 = f32[16]{0:T(128)S(1)} collective-permute-done((f32[16]{0:T(128)S(1)}, f32[16]{0:T(128)S(1)}, u32[]{:S(2)}, u32[]{:S(2)}) %collective-permute-start.23) | collective-permute-done | bytes 96 | tf_op jit(solution)/shard_map/ppermute | solution.py:101
  (154 shorter events, 66.7 us)
Async XLA Ops:
  1.9 12.2 %collective-permute-start.4 = (bf16[128,1024]{1,0:T(8,128)(2,1)S(1)}, bf16[128,1024]{1,0:T(8,128)(2,1)S(1)}, u32[]{:S(2)}, u32[]{:S(2)}) collective-permute-start(bf16[128,1024]{1,0:T(8,128)(2,1)S(1)} %get-tuple-element.49), channel_id=1, source_target_pairs={{0,8},{8,16},{16,24},{24,0},{1,9},{9,17},{17,25},{25,1},{2,10},{10... | collective-permute-start | bytes 786440 | tf_op jit(solution)/shard_map/ppermute | solution.py:34
  5.1 14.7 %collective-permute-start = (bf16[128,1024]{1,0:T(8,128)(2,1)S(1)}, bf16[128,1024]{1,0:T(8,128)(2,1)S(1)}, u32[]{:S(2)}, u32[]{:S(2)}) collective-permute-start(bf16[128,1024]{1,0:T(8,128)(2,1)S(1)} %get-tuple-element.43), channel_id=1, source_target_pairs={{0,8},{8,16},{16,24},{24,0},{1,9},{9,17},{17,25},{25,1},{2,10},{10... | collective-permute-start | bytes 786440 | tf_op jit(solution)/shard_map/ppermute | solution.py:34
  14.2 11.2 %collective-permute-start.5 = (bf16[128,1024]{1,0:T(8,128)(2,1)S(1)}, bf16[128,1024]{1,0:T(8,128)(2,1)S(1)}, u32[]{:S(2)}, u32[]{:S(2)}) collective-permute-start(bf16[128,1024]{1,0:T(8,128)(2,1)S(1)} %collective-permute-done.4), channel_id=1, source_target_pairs={{0,8},{8,16},{16,24},{24,0},{1,9},{9,17},{17,25},{25,1},{2,10},{10... | collective-permute-start | bytes 786440 | tf_op jit(solution)/shard_map/ppermute | solution.py:34
  19.8 11.2 %collective-permute-start.1 = (bf16[128,1024]{1,0:T(8,128)(2,1)S(1)}, bf16[128,1024]{1,0:T(8,128)(2,1)S(1)}, u32[]{:S(2)}, u32[]{:S(2)}) collective-permute-start(bf16[128,1024]{1,0:T(8,128)(2,1)S(1)} %collective-permute-done), channel_id=1, source_target_pairs={{0,8},{8,16},{16,24},{24,0},{1,9},{9,17},{17,25},{25,1},{2,10},{10... | collective-permute-start | bytes 786440 | tf_op jit(solution)/shard_map/ppermute | solution.py:34
  25.4 11.2 %collective-permute-start.6 = (bf16[128,1024]{1,0:T(8,128)(2,1)S(1)}, bf16[128,1024]{1,0:T(8,128)(2,1)S(1)}, u32[]{:S(2)}, u32[]{:S(2)}) collective-permute-start(bf16[128,1024]{1,0:T(8,128)(2,1)S(1)} %collective-permute-done.5), channel_id=1, source_target_pairs={{0,8},{8,16},{16,24},{24,0},{1,9},{9,17},{17,25},{25,1},{2,10},{10... | collective-permute-start | bytes 786440 | tf_op jit(solution)/shard_map/ppermute | solution.py:34
  31.0 11.2 %collective-permute-start.2 = (bf16[128,1024]{1,0:T(8,128)(2,1)S(1)}, bf16[128,1024]{1,0:T(8,128)(2,1)S(1)}, u32[]{:S(2)}, u32[]{:S(2)}) collective-permute-start(bf16[128,1024]{1,0:T(8,128)(2,1)S(1)} %collective-permute-done.1), channel_id=1, source_target_pairs={{0,8},{8,16},{16,24},{24,0},{1,9},{9,17},{17,25},{25,1},{2,10},{10... | collective-permute-start | bytes 786440 | tf_op jit(solution)/shard_map/ppermute | solution.py:34
  31.1 35.6 %collective-permute-start.10 = (bf16[256,2304]{1,0:T(8,128)(2,1)S(1)}, bf16[256,2304]{1,0:T(8,128)(2,1)S(1)}, u32[]{:S(2)}, u32[]{:S(2)}) collective-permute-start(bf16[256,2304]{1,0:T(8,128)(2,1)S(1)} %copy-done.2), channel_id=1, source_target_pairs={{0,8},{8,16},{16,24},{24,0},{1,9},{9,17},{17,25},{25,1},{2,10},{10... | collective-permute-start | bytes 3538952 | tf_op jit(solution)/shard_map/ppermute | solution.py:34
  36.8 29.9 %collective-permute-start.7 = (bf16[4,128,1024]{2,1,0:T(8,128)(2,1)S(1)}, bf16[4,128,1024]{2,1,0:T(8,128)(2,1)S(1)}, u32[]{:S(2)}, u32[]{:S(2)}) collective-permute-start(bf16[4,128,1024]{2,1,0:T(8,128)(2,1)S(1)} %get-tuple-element.41), channel_id=1, source_target_pairs={{0,4},{4,0},{1,5},{5,1},{2,6},{6,2},{3,7},{7,3},{8,12},{12,8},{9,1... | collective-permute-start | bytes 3145736 | tf_op jit(solution)/shard_map/ppermute | solution.py:34
  42.4 26.1 %collective-permute-start.3 = (bf16[4,128,1024]{2,1,0:T(8,128)(2,1)S(1)}, bf16[4,128,1024]{2,1,0:T(8,128)(2,1)S(1)}, u32[]{:S(2)}, u32[]{:S(2)}) collective-permute-start(bf16[4,128,1024]{2,1,0:T(8,128)(2,1)S(1)} %get-tuple-element.39), channel_id=1, source_target_pairs={{0,2},{2,0},{1,3},{3,1},{4,6},{6,4},{5,7},{7,5},{8,10},{10,8},{9,1... | collective-permute-start | bytes 3145736 | tf_op jit(solution)/shard_map/ppermute | solution.py:34
  66.7 29.1 %collective-permute-start.11 = (bf16[256,2304]{1,0:T(8,128)(2,1)S(1)}, bf16[256,2304]{1,0:T(8,128)(2,1)}, u32[]{:S(2)}, u32[]{:S(2)}) collective-permute-start(bf16[256,2304]{1,0:T(8,128)(2,1)S(1)} %collective-permute-done.10), channel_id=1, source_target_pairs={{0,8},{8,16},{16,24},{24,0},{1,9},{9,17},{17,25},{25,1},{2,10},{10... | collective-permute-start | bytes 3538952 | tf_op jit(solution)/shard_map/ppermute | solution.py:34
  66.9 47.0 %collective-permute-start.8 = (bf16[2,4,128,1024]{3,2,1,0:T(8,128)(2,1)S(1)}, bf16[2,4,128,1024]{3,2,1,0:T(8,128)(2,1)}, u32[]{:S(2)}, u32[]{:S(2)}) collective-permute-start(bf16[2,4,128,1024]{3,2,1,0:T(8,128)(2,1)S(1)} %pad_maximum_fusion.1), channel_id=1, source_target_pairs={{0,2},{2,0},{1,3},{3,1},{4,6},{6,4},{5,7},{7,5},{8,10},{10,8},{9,1... | collective-permute-start | bytes 6291464 | tf_op jit(solution)/shard_map/ppermute | solution.py:34
  70.0 47.9 %collective-permute-start.9 = (bf16[2,4,128,1024]{3,2,1,0:T(8,128)(2,1)}, bf16[2,4,128,1024]{3,2,1,0:T(8,128)(2,1)}, u32[]{:S(2)}, u32[]{:S(2)}) collective-permute-start(bf16[2,4,128,1024]{3,2,1,0:T(8,128)(2,1)} %pad_maximum_fusion), channel_id=1, source_target_pairs={{0,4},{4,0},{1,5},{5,1},{2,6},{6,2},{3,7},{7,3},{8,12},{12,8},{9,1... | collective-permute-start | bytes 6291464 | tf_op jit(solution)/shard_map/ppermute | solution.py:34
  95.8 28.3 %collective-permute-start.12 = (bf16[256,2304]{1,0:T(8,128)(2,1)}, bf16[256,2304]{1,0:T(8,128)(2,1)}, u32[]{:S(2)}, u32[]{:S(2)}) collective-permute-start(bf16[256,2304]{1,0:T(8,128)(2,1)} %collective-permute-done.11), channel_id=1, source_target_pairs={{0,8},{8,16},{16,24},{24,0},{1,9},{9,17},{17,25},{25,1},{2,10},{10... | collective-permute-start | bytes 3538952 | tf_op jit(solution)/shard_map/ppermute | solution.py:34
  142.2 9.4 %collective-permute-start.14 = (bf16[128,4,256]{2,0,1:T(8,128)(2,1)S(1)}, bf16[128,4,256]{2,0,1:T(8,128)(2,1)S(1)}, u32[]{:S(2)}, u32[]{:S(2)}) collective-permute-start(bf16[128,4,256]{2,0,1:T(8,128)(2,1)S(1)} %bitcast.274), channel_id=1, source_target_pairs={{0,6},{2,0},{4,2},{6,4},{1,7},{3,1},{5,3},{7,5},{8,14},{10,8},{12,... | collective-permute-start | bytes 786440 | tf_op jit(solution)/shard_map/ppermute | solution.py:71
  144.6 13.8 %collective-permute-start.15 = (bf16[128,4,256]{2,0,1:T(8,128)(2,1)S(1)}, bf16[128,4,256]{2,0,1:T(8,128)(2,1)S(1)}, u32[]{:S(2)}, u32[]{:S(2)}) collective-permute-start(bf16[128,4,256]{2,0,1:T(8,128)(2,1)S(1)} %bitcast.275), channel_id=1, source_target_pairs={{0,4},{2,6},{4,0},{6,2},{1,5},{3,7},{5,1},{7,3},{8,12},{10,14},{12... | collective-permute-start | bytes 786440 | tf_op jit(solution)/shard_map/ppermute | solution.py:71
  145.4 13.0 %collective-permute-start.16 = (bf16[128,4,256]{2,0,1:T(8,128)(2,1)S(1)}, bf16[128,4,256]{2,0,1:T(8,128)(2,1)S(1)}, u32[]{:S(2)}, u32[]{:S(2)}) collective-permute-start(bf16[128,4,256]{2,0,1:T(8,128)(2,1)S(1)} %bitcast.276), channel_id=1, source_target_pairs={{0,2},{2,4},{4,6},{6,0},{1,3},{3,5},{5,7},{7,1},{8,10},{10,12},{12... | collective-permute-start | bytes 786440 | tf_op jit(solution)/shard_map/ppermute | solution.py:71
  167.8 27.0 %collective-permute-start.19 = (f32[2,128,1152]{2,1,0:T(8,128)S(1)}, f32[2,128,1152]{2,1,0:T(8,128)}, u32[]{:S(2)}, u32[]{:S(2)}) collective-permute-start(f32[2,128,1152]{2,1,0:T(8,128)S(1)} %dynamic-slice_bitcast_fusion), channel_id=1, source_target_pairs={{0,4},{4,0},{1,5},{5,1},{2,6},{6,2},{3,7},{7,3},{8,12},{12,8},{9,1... | collective-permute-start | bytes 3538952 | tf_op jit(solution)/shard_map/ppermute | solution.py:90
  169.5 28.3 %collective-permute-start.17 = (f32[2,128,1152]{2,1,0:T(8,128)}, f32[2,128,1152]{2,1,0:T(8,128)}, u32[]{:S(2)}, u32[]{:S(2)}) collective-permute-start(f32[2,128,1152]{2,1,0:T(8,128)} %dynamic-slice_bitcast_fusion.1), channel_id=1, source_target_pairs={{0,2},{2,0},{1,3},{3,1},{4,6},{6,4},{5,7},{7,5},{8,10},{10,8},{9,1... | collective-permute-start | bytes 3538952 | tf_op jit(solution)/shard_map/ppermute | solution.py:90
  196.6 13.7 %collective-permute-start.20 = (f32[128,1152]{1,0:T(8,128)S(1)}, f32[128,1152]{1,0:T(8,128)S(1)}, u32[]{:S(2)}, u32[]{:S(2)}) collective-permute-start(f32[128,1152]{1,0:T(8,128)S(1)} %dynamic-slice_bitcast_fusion.2), channel_id=1, source_target_pairs={{0,2},{2,0},{1,3},{3,1},{4,6},{6,4},{5,7},{7,5},{8,10},{10,8},{9,1... | collective-permute-start | bytes 1769480 | tf_op jit(solution)/shard_map/ppermute | solution.py:93
  199.2 14.1 %collective-permute-start.18 = (f32[128,1152]{1,0:T(8,128)S(1)}, f32[128,1152]{1,0:T(8,128)S(1)}, u32[]{:S(2)}, u32[]{:S(2)}) collective-permute-start(f32[128,1152]{1,0:T(8,128)S(1)} %dynamic-slice_bitcast_fusion.3), channel_id=1, source_target_pairs={{0,4},{4,0},{1,5},{5,1},{2,6},{6,2},{3,7},{7,3},{8,12},{12,8},{9,1... | collective-permute-start | bytes 1769480 | tf_op jit(solution)/shard_map/ppermute | solution.py:93
  216.2 3.6 %collective-permute-start.21 = (f32[16]{0:T(128)S(1)}, f32[16]{0:T(128)S(1)}, u32[]{:S(2)}, u32[]{:S(2)}) collective-permute-start(f32[16]{0:T(128)S(1)} %select_reduce_fusion), channel_id=1, source_target_pairs={{0,8},{8,0},{16,24},{24,16},{1,9},{9,1},{17,25},{25,17},{2,10},{10... | collective-permute-start | bytes 200 | tf_op jit(solution)/shard_map/ppermute | solution.py:101
  219.8 4.4 %collective-permute-start.22 = (f32[16]{0:T(128)S(1)}, f32[16]{0:T(128)S(1)}, u32[]{:S(2)}, u32[]{:S(2)}) collective-permute-start(f32[16]{0:T(128)S(1)} %add.644), channel_id=1, source_target_pairs={{0,16},{8,24},{16,0},{24,8},{1,17},{9,25},{17,1},{25,9},{2,18},{10... | collective-permute-start | bytes 200 | tf_op jit(solution)/shard_map/ppermute | solution.py:101
  224.3 3.5 %collective-permute-start.23 = (f32[16]{0:T(128)S(1)}, f32[16]{0:T(128)S(1)}, u32[]{:S(2)}, u32[]{:S(2)}) collective-permute-start(f32[16]{0:T(128)S(1)} %add.645), channel_id=1, source_target_pairs={{0,4},{4,0},{1,5},{5,1},{2,6},{6,2},{3,7},{7,3},{8,12},{12,8},{9,1... | collective-permute-start | bytes 200 | tf_op jit(solution)/shard_map/ppermute | solution.py:101
  227.8 3.5 %collective-permute-start.24 = (f32[16]{0:T(128)S(1)}, f32[16]{0:T(128)S(1)}, u32[]{:S(2)}, u32[]{:S(2)}) collective-permute-start(f32[16]{0:T(128)S(1)} %add.646), channel_id=1, source_target_pairs={{0,2},{2,0},{1,3},{3,1},{4,6},{6,4},{5,7},{7,5},{8,10},{10,8},{9,1... | collective-permute-start | bytes 200 | tf_op jit(solution)/shard_map/ppermute | solution.py:101
  (17 other events, 154.7 us)

commit v17 on v16

--- a/solution.py
+++ b/solution.py
@@ -50,9 +50,10 @@
     last = order[-1]
     n = lax.axis_size(last)
     own = lax.axis_index(last)
+    flat = x.reshape(-1, x.shape[-1])
     return [
-        (piece, (((own - t) % n) * stride[last] + source).reshape(-1))
-        for t, piece in enumerate(ring_pieces(x, last))
+        (piece.T, (((own - t) % n) * stride[last] + source).reshape(-1))
+        for t, piece in enumerate(ring_pieces(flat.T, last))
     ]
 
 

time: 233 us -> 235 us (level)
  local copies, waits for them, and re-layouts: 28.6 us -> 20.1 us
  starting transfers between devices: 20.4 us -> 25.9 us
  other arithmetic: 11.5 us -> 15 us
    ppermute x14, waiting for transfers between devices: 87.9 us -> 95.9 us  [ring_pieces(): lax.ppermute(pieces[-1], axis, [(k, (k + 1) % n) for k in range(n)])]
    unnamed x48 -> x34, local copies, waits for them, and re-layouts: 11.9 us -> 5.36 us
    ppermute x4, starting transfers between devices: 0.72 us -> 4.4 us  [butterfly_sum(): x = x + lax.ppermute(x, axis, [(i, i ^ bit) for i in range(size)])]
    ppermute x4, waiting for transfers between devices: 13.3 us -> 9.66 us  [butterfly_sum(): x = x + lax.ppermute(x, axis, [(i, i ^ bit) for i in range(size)])]
    another operation x7, other arithmetic: 2.24 us -> 5.8 us  [ring_gather(): return jnp.stack(ring_pieces(x, axis))]
  transfers between devices with their start and end apart: 25 -> 25, of which waited for: 20 -> 20; matrix products, arithmetic and copies ran while one was open for 13% -> 10% of each run, Pallas kernels for 0% -> 0%
where the time goes in v17:
time: 235 us
  waiting for transfers between devices  153 us (65%)
  starting transfers between devices  25.9 us (11%)
  local copies, waits for them, and re-layouts  20.1 us (9%)
  matrix products  17.2 us (7%)
  other arithmetic  15 us (6%)
  blocking collectives  2.47 us (1%)
    ppermute x14, waiting for transfers between devices, ring_pieces(): lax.ppermute(pieces[-1], axis, [(k, (k + 1) % n) for k in range(n)])  95.9 us
    ppermute x2, waiting for transfers between devices, swap_reduce_scatter(): keep = keep + lax.ppermute(sent, first, [(0, 1), (1, 0)])  23.5 us
    ppermute x14, starting transfers between devices, ring_pieces(): lax.ppermute(pieces[-1], axis, [(k, (k + 1) % n) for k in range(n)])  13.1 us
    ppermute x2, waiting for transfers between devices, swap_reduce_scatter(): return mine + lax.ppermute(sent, second, [(0, 1), (1, 0)])  12.6 us
    ppermute x3, waiting for transfers between devices, permute_all_to_all(): lax.ppermute(sent, axes, [(k, (k + shift) % n) for k in range(n)])  11.2 us
    ppermute x4, waiting for transfers between devices, butterfly_sum(): x = x + lax.ppermute(x, axis, [(i, i ^ bit) for i in range(size)])  9.66 us
    reshape x2, local copies, waits for them, and re-layouts, gather_order(): flat = x.reshape(-1, x.shape[-1])  6.8 us
    another operation x7, other arithmetic, ring_gather(): return jnp.stack(ring_pieces(x, axis))  5.8 us
  transfers between devices with their start and end apart: 25, of which 20 were waited for; matrix products, arithmetic and copies ran while one was open for 10% of the time, Pallas kernels for 0%

profile of v17, /device:TPU:0, one launch (start us, length us, event | category | flops | bytes accessed | tf_op | source)
XLA Modules:
  0.0 234.7 jit_solution(10480685114577173399)
XLA Ops:
  1.9 3.1 %collective-permute-start.4 = (bf16[128,1024]{1,0:T(8,128)(2,1)S(1)}, bf16[128,1024]{1,0:T(8,128)(2,1)S(1)}, u32[]{:S(2)}, u32[]{:S(2)}) collective-permute-start(bf16[128,1024]{1,0:T(8,128)(2,1)S(1)} %get-tuple-element.49), channel_id=1, source_target_pairs={{0,8},{8,16},{16,24},{24,0},{1,9},{9,17},{17,25},{25,1},{2,10},{10... | collective-permute-start | bytes 786440 | tf_op jit(solution)/shard_map/ppermute | solution.py:34
  6.7 7.5 %collective-permute-done.4 = bf16[128,1024]{1,0:T(8,128)(2,1)S(1)} collective-permute-done((bf16[128,1024]{1,0:T(8,128)(2,1)S(1)}, bf16[128,1024]{1,0:T(8,128)(2,1)S(1)}, u32[]{:S(2)}, u32[]{:S(2)}) %collective-permute-start.4) | collective-permute-done | bytes 262176 | tf_op jit(solution)/shard_map/ppermute | solution.py:34
  14.2 5.6 %collective-permute-done = bf16[128,1024]{1,0:T(8,128)(2,1)S(1)} collective-permute-done((bf16[128,1024]{1,0:T(8,128)(2,1)S(1)}, bf16[128,1024]{1,0:T(8,128)(2,1)S(1)}, u32[]{:S(2)}, u32[]{:S(2)}) %collective-permute-start) | collective-permute-done | bytes 262176 | tf_op jit(solution)/shard_map/ppermute | solution.py:34
  19.8 5.6 %collective-permute-done.5 = bf16[128,1024]{1,0:T(8,128)(2,1)S(1)} collective-permute-done((bf16[128,1024]{1,0:T(8,128)(2,1)S(1)}, bf16[128,1024]{1,0:T(8,128)(2,1)S(1)}, u32[]{:S(2)}, u32[]{:S(2)}) %collective-permute-start.5) | collective-permute-done | bytes 262176 | tf_op jit(solution)/shard_map/ppermute | solution.py:34
  25.4 5.6 %collective-permute-done.1 = bf16[128,1024]{1,0:T(8,128)(2,1)S(1)} collective-permute-done((bf16[128,1024]{1,0:T(8,128)(2,1)S(1)}, bf16[128,1024]{1,0:T(8,128)(2,1)S(1)}, u32[]{:S(2)}, u32[]{:S(2)}) %collective-permute-start.1) | collective-permute-done | bytes 262176 | tf_op jit(solution)/shard_map/ppermute | solution.py:34
  32.6 4.0 %collective-permute-done.6 = bf16[128,1024]{1,0:T(8,128)(2,1)S(1)} collective-permute-done((bf16[128,1024]{1,0:T(8,128)(2,1)S(1)}, bf16[128,1024]{1,0:T(8,128)(2,1)S(1)}, u32[]{:S(2)}, u32[]{:S(2)}) %collective-permute-start.6) | collective-permute-done | bytes 262176 | tf_op jit(solution)/shard_map/ppermute | solution.py:34
  38.6 3.6 %collective-permute-done.2 = bf16[128,1024]{1,0:T(8,128)(2,1)S(1)} collective-permute-done((bf16[128,1024]{1,0:T(8,128)(2,1)S(1)}, bf16[128,1024]{1,0:T(8,128)(2,1)S(1)}, u32[]{:S(2)}, u32[]{:S(2)}) %collective-permute-start.2) | collective-permute-done | bytes 262176 | tf_op jit(solution)/shard_map/ppermute | solution.py:34
  45.2 21.6 %collective-permute-done.10 = bf16[256,2304]{1,0:T(8,128)(2,1)} collective-permute-done((bf16[256,2304]{1,0:T(8,128)(2,1)S(1)}, bf16[256,2304]{1,0:T(8,128)(2,1)}, u32[]{:S(2)}, u32[]{:S(2)}) %collective-permute-start.10) | collective-permute-done | bytes 1179680 | tf_op jit(solution)/shard_map/ppermute | solution.py:34
  68.3 2.9 %copy.70 = bf16[1024,1024]{0,1:T(8,128)(2,1)S(1)} copy(bf16[1024,1024]{1,0:T(8,128)(2,1)} %bitcast.252) | data formatting | bytes 4194304 | tf_op jit(solution)/shard_map/reshape | solution.py:53
  72.8 2.7 %pad_maximum_fusion = bf16[2,4,128,1024]{3,2,1,0:T(8,128)(2,1)} fusion(bf16[1,4,128,1024]{3,2,1,0:T(8,128)(2,1)} %bitcast.7, bf16[1,4,128,1024]{3,2,1,0:T(8,128)(2,1)S(1)} %get-tuple-element.38), kind=kLoop, calls=%fused_computation.16 | loop fusion | flops 1048576 | bytes 4194304 | tf_op jit(solution)/shard_map/stack | solution.py:39
  75.5 3.9 %copy.67 = bf16[1024,1024]{0,1:T(8,128)(2,1)} copy(bf16[1024,1024]{1,0:T(8,128)(2,1)} %bitcast.253) | data formatting | bytes 4194304 | tf_op jit(solution)/shard_map/reshape | solution.py:53
  81.1 15.0 %collective-permute-done.11 = bf16[256,2304]{1,0:T(8,128)(2,1)} collective-permute-done((bf16[256,2304]{1,0:T(8,128)(2,1)}, bf16[256,2304]{1,0:T(8,128)(2,1)}, u32[]{:S(2)}, u32[]{:S(2)}) %collective-permute-start.11) | collective-permute-done | bytes 1179680 | tf_op jit(solution)/shard_map/ppermute | solution.py:34
  100.5 23.8 %collective-permute-done.12 = bf16[256,2304]{1,0:T(8,128)(2,1)S(1)} collective-permute-done((bf16[256,2304]{1,0:T(8,128)(2,1)}, bf16[256,2304]{1,0:T(8,128)(2,1)S(1)}, u32[]{:S(2)}, u32[]{:S(2)}) %collective-permute-start.12) | collective-permute-done | bytes 1179680 | tf_op jit(solution)/shard_map/ppermute | solution.py:34
  150.1 5.0 %collective-permute-done.14 = bf16[128,4,256]{2,0,1:T(8,128)(2,1)S(1)} collective-permute-done((bf16[128,4,256]{2,0,1:T(8,128)(2,1)S(1)}, bf16[128,4,256]{2,0,1:T(8,128)(2,1)S(1)}, u32[]{:S(2)}, u32[]{:S(2)}) %collective-permute-start.14) | collective-permute-done | bytes 262176 | tf_op jit(solution)/shard_map/ppermute | solution.py:72
  155.1 6.2 %collective-permute-done.15 = bf16[128,4,256]{2,0,1:T(8,128)(2,1)S(1)} collective-permute-done((bf16[128,4,256]{2,0,1:T(8,128)(2,1)S(1)}, bf16[128,4,256]{2,0,1:T(8,128)(2,1)S(1)}, u32[]{:S(2)}, u32[]{:S(2)}) %collective-permute-start.15) | collective-permute-done | bytes 262176 | tf_op jit(solution)/shard_map/ppermute | solution.py:72
  165.3 2.1 fusion.34
  173.7 23.5 %collective-permute-done.19 = f32[2,128,1152]{2,1,0:T(8,128)} collective-permute-done((f32[2,128,1152]{2,1,0:T(8,128)S(1)}, f32[2,128,1152]{2,1,0:T(8,128)}, u32[]{:S(2)}, u32[]{:S(2)}) %collective-permute-start.19) | collective-permute-done | bytes 1179680 | tf_op jit(solution)/shard_map/ppermute | solution.py:91
  203.5 9.7 %collective-permute-done.20 = f32[128,1152]{1,0:T(8,128)S(1)} collective-permute-done((f32[128,1152]{1,0:T(8,128)S(1)}, f32[128,1152]{1,0:T(8,128)S(1)}, u32[]{:S(2)}, u32[]{:S(2)}) %collective-permute-start.20) | collective-permute-done | bytes 589856 | tf_op jit(solution)/shard_map/ppermute | solution.py:94
  213.2 2.9 %collective-permute-done.18 = f32[128,1152]{1,0:T(8,128)S(1)} collective-permute-done((f32[128,1152]{1,0:T(8,128)S(1)}, f32[128,1152]{1,0:T(8,128)S(1)}, u32[]{:S(2)}, u32[]{:S(2)}) %collective-permute-start.18) | collective-permute-done | bytes 589856 | tf_op jit(solution)/shard_map/ppermute | solution.py:94
  216.4 2.5 %psum.7 = f32[3,128]{1,0:T(4,128)S(1)} all-reduce(f32[3,128]{1,0:T(4,128)S(1)} %pad_maximum_fusion.9), channel_id=1, replica_groups=mesh['c0'=4,'c1'=2,'c2'=2,'head'=2] {'head'}, use_global_device_ids=true, to_apply=%region_13.14 | all-reduce | flops 384 | bytes 3072 | tf_op jit(solution)/shard_map/psum | solution.py:226
  219.7 2.9 %collective-permute-done.21 = f32[16]{0:T(128)S(1)} collective-permute-done((f32[16]{0:T(128)S(1)}, f32[16]{0:T(128)S(1)}, u32[]{:S(2)}, u32[]{:S(2)}) %collective-permute-start.21) | collective-permute-done | bytes 96 | tf_op jit(solution)/shard_map/ppermute | solution.py:102
  224.7 2.4 %collective-permute-done.22 = f32[16]{0:T(128)S(1)} collective-permute-done((f32[16]{0:T(128)S(1)}, f32[16]{0:T(128)S(1)}, u32[]{:S(2)}, u32[]{:S(2)}) %collective-permute-start.22) | collective-permute-done | bytes 96 | tf_op jit(solution)/shard_map/ppermute | solution.py:102
  228.4 2.3 collective-permute-done.23
  232.1 2.1 collective-permute-done.24
  (140 shorter events, 67.0 us)
Async XLA Ops:
  1.9 12.2 %collective-permute-start.4 = (bf16[128,1024]{1,0:T(8,128)(2,1)S(1)}, bf16[128,1024]{1,0:T(8,128)(2,1)S(1)}, u32[]{:S(2)}, u32[]{:S(2)}) collective-permute-start(bf16[128,1024]{1,0:T(8,128)(2,1)S(1)} %get-tuple-element.49), channel_id=1, source_target_pairs={{0,8},{8,16},{16,24},{24,0},{1,9},{9,17},{17,25},{25,1},{2,10},{10... | collective-permute-start | bytes 786440 | tf_op jit(solution)/shard_map/ppermute | solution.py:34
  5.1 14.7 %collective-permute-start = (bf16[128,1024]{1,0:T(8,128)(2,1)S(1)}, bf16[128,1024]{1,0:T(8,128)(2,1)S(1)}, u32[]{:S(2)}, u32[]{:S(2)}) collective-permute-start(bf16[128,1024]{1,0:T(8,128)(2,1)S(1)} %get-tuple-element.43), channel_id=1, source_target_pairs={{0,8},{8,16},{16,24},{24,0},{1,9},{9,17},{17,25},{25,1},{2,10},{10... | collective-permute-start | bytes 786440 | tf_op jit(solution)/shard_map/ppermute | solution.py:34
  14.2 11.2 %collective-permute-start.5 = (bf16[128,1024]{1,0:T(8,128)(2,1)S(1)}, bf16[128,1024]{1,0:T(8,128)(2,1)S(1)}, u32[]{:S(2)}, u32[]{:S(2)}) collective-permute-start(bf16[128,1024]{1,0:T(8,128)(2,1)S(1)} %collective-permute-done.4), channel_id=1, source_target_pairs={{0,8},{8,16},{16,24},{24,0},{1,9},{9,17},{17,25},{25,1},{2,10},{10... | collective-permute-start | bytes 786440 | tf_op jit(solution)/shard_map/ppermute | solution.py:34
  19.8 11.2 %collective-permute-start.1 = (bf16[128,1024]{1,0:T(8,128)(2,1)S(1)}, bf16[128,1024]{1,0:T(8,128)(2,1)S(1)}, u32[]{:S(2)}, u32[]{:S(2)}) collective-permute-start(bf16[128,1024]{1,0:T(8,128)(2,1)S(1)} %collective-permute-done), channel_id=1, source_target_pairs={{0,8},{8,16},{16,24},{24,0},{1,9},{9,17},{17,25},{25,1},{2,10},{10... | collective-permute-start | bytes 786440 | tf_op jit(solution)/shard_map/ppermute | solution.py:34
  25.4 11.2 %collective-permute-start.6 = (bf16[128,1024]{1,0:T(8,128)(2,1)S(1)}, bf16[128,1024]{1,0:T(8,128)(2,1)S(1)}, u32[]{:S(2)}, u32[]{:S(2)}) collective-permute-start(bf16[128,1024]{1,0:T(8,128)(2,1)S(1)} %collective-permute-done.5), channel_id=1, source_target_pairs={{0,8},{8,16},{16,24},{24,0},{1,9},{9,17},{17,25},{25,1},{2,10},{10... | collective-permute-start | bytes 786440 | tf_op jit(solution)/shard_map/ppermute | solution.py:34
  31.0 11.2 %collective-permute-start.2 = (bf16[128,1024]{1,0:T(8,128)(2,1)S(1)}, bf16[128,1024]{1,0:T(8,128)(2,1)S(1)}, u32[]{:S(2)}, u32[]{:S(2)}) collective-permute-start(bf16[128,1024]{1,0:T(8,128)(2,1)S(1)} %collective-permute-done.1), channel_id=1, source_target_pairs={{0,8},{8,16},{16,24},{24,0},{1,9},{9,17},{17,25},{25,1},{2,10},{10... | collective-permute-start | bytes 786440 | tf_op jit(solution)/shard_map/ppermute | solution.py:34
  31.1 35.8 %collective-permute-start.10 = (bf16[256,2304]{1,0:T(8,128)(2,1)S(1)}, bf16[256,2304]{1,0:T(8,128)(2,1)}, u32[]{:S(2)}, u32[]{:S(2)}) collective-permute-start(bf16[256,2304]{1,0:T(8,128)(2,1)S(1)} %copy-done.3), channel_id=1, source_target_pairs={{0,8},{8,16},{16,24},{24,0},{1,9},{9,17},{17,25},{25,1},{2,10},{10... | collective-permute-start | bytes 3538952 | tf_op jit(solution)/shard_map/ppermute | solution.py:34
  36.8 30.0 %collective-permute-start.7 = (bf16[4,128,1024]{2,1,0:T(8,128)(2,1)S(1)}, bf16[4,128,1024]{2,1,0:T(8,128)(2,1)S(1)}, u32[]{:S(2)}, u32[]{:S(2)}) collective-permute-start(bf16[4,128,1024]{2,1,0:T(8,128)(2,1)S(1)} %get-tuple-element.41), channel_id=1, source_target_pairs={{0,4},{4,0},{1,5},{5,1},{2,6},{6,2},{3,7},{7,3},{8,12},{12,8},{9,1... | collective-permute-start | bytes 3145736 | tf_op jit(solution)/shard_map/ppermute | solution.py:34
  43.4 29.3 %collective-permute-start.3 = (bf16[4,128,1024]{2,1,0:T(8,128)(2,1)}, bf16[4,128,1024]{2,1,0:T(8,128)(2,1)}, u32[]{:S(2)}, u32[]{:S(2)}) collective-permute-start(bf16[4,128,1024]{2,1,0:T(8,128)(2,1)} %get-tuple-element.39), channel_id=1, source_target_pairs={{0,2},{2,0},{1,3},{3,1},{4,6},{6,4},{5,7},{7,5},{8,10},{10,8},{9,1... | collective-permute-start | bytes 3145736 | tf_op jit(solution)/shard_map/ppermute | solution.py:34
  66.8 29.3 %collective-permute-start.11 = (bf16[256,2304]{1,0:T(8,128)(2,1)}, bf16[256,2304]{1,0:T(8,128)(2,1)}, u32[]{:S(2)}, u32[]{:S(2)}) collective-permute-start(bf16[256,2304]{1,0:T(8,128)(2,1)} %collective-permute-done.10), channel_id=1, source_target_pairs={{0,8},{8,16},{16,24},{24,0},{1,9},{9,17},{17,25},{25,1},{2,10},{10... | collective-permute-start | bytes 3538952 | tf_op jit(solution)/shard_map/ppermute | solution.py:34
  71.2 53.1 %collective-permute-start.8 = (bf16[1024,1024]{1,0:T(8,128)(2,1)S(1)}, bf16[1024,1024]{1,0:T(8,128)(2,1)}, u32[]{:S(2)}, u32[]{:S(2)}) collective-permute-start(bf16[1024,1024]{1,0:T(8,128)(2,1)S(1)} %bitcast.250), channel_id=1, source_target_pairs={{0,2},{2,0},{1,3},{3,1},{4,6},{6,4},{5,7},{7,5},{8,10},{10,8},{9,1... | collective-permute-start | bytes 6291464 | tf_op jit(solution)/shard_map/ppermute | solution.py:34
  79.4 46.6 %collective-permute-start.9 = (bf16[1024,1024]{1,0:T(8,128)(2,1)}, bf16[1024,1024]{1,0:T(8,128)(2,1)}, u32[]{:S(2)}, u32[]{:S(2)}) collective-permute-start(bf16[1024,1024]{1,0:T(8,128)(2,1)} %bitcast.251), channel_id=1, source_target_pairs={{0,4},{4,0},{1,5},{5,1},{2,6},{6,2},{3,7},{7,3},{8,12},{12,8},{9,1... | collective-permute-start | bytes 6291464 | tf_op jit(solution)/shard_map/ppermute | solution.py:34
  96.1 28.2 %collective-permute-start.12 = (bf16[256,2304]{1,0:T(8,128)(2,1)}, bf16[256,2304]{1,0:T(8,128)(2,1)S(1)}, u32[]{:S(2)}, u32[]{:S(2)}) collective-permute-start(bf16[256,2304]{1,0:T(8,128)(2,1)} %collective-permute-done.11), channel_id=1, source_target_pairs={{0,8},{8,16},{16,24},{24,0},{1,9},{9,17},{17,25},{25,1},{2,10},{10... | collective-permute-start | bytes 3538952 | tf_op jit(solution)/shard_map/ppermute | solution.py:34
  145.7 9.4 %collective-permute-start.14 = (bf16[128,4,256]{2,0,1:T(8,128)(2,1)S(1)}, bf16[128,4,256]{2,0,1:T(8,128)(2,1)S(1)}, u32[]{:S(2)}, u32[]{:S(2)}) collective-permute-start(bf16[128,4,256]{2,0,1:T(8,128)(2,1)S(1)} %bitcast.278), channel_id=1, source_target_pairs={{0,6},{2,0},{4,2},{6,4},{1,7},{3,1},{5,3},{7,5},{8,14},{10,8},{12,... | collective-permute-start | bytes 786440 | tf_op jit(solution)/shard_map/ppermute | solution.py:72
  147.6 13.8 %collective-permute-start.15 = (bf16[128,4,256]{2,0,1:T(8,128)(2,1)S(1)}, bf16[128,4,256]{2,0,1:T(8,128)(2,1)S(1)}, u32[]{:S(2)}, u32[]{:S(2)}) collective-permute-start(bf16[128,4,256]{2,0,1:T(8,128)(2,1)S(1)} %bitcast.279), channel_id=1, source_target_pairs={{0,4},{2,6},{4,0},{6,2},{1,5},{3,7},{5,1},{7,3},{8,12},{10,14},{12... | collective-permute-start | bytes 786440 | tf_op jit(solution)/shard_map/ppermute | solution.py:72
  148.6 12.8 %collective-permute-start.16 = (bf16[128,4,256]{2,0,1:T(8,128)(2,1)S(1)}, bf16[128,4,256]{2,0,1:T(8,128)(2,1)S(1)}, u32[]{:S(2)}, u32[]{:S(2)}) collective-permute-start(bf16[128,4,256]{2,0,1:T(8,128)(2,1)S(1)} %bitcast.280), channel_id=1, source_target_pairs={{0,2},{2,4},{4,6},{6,0},{1,3},{3,5},{5,7},{7,1},{8,10},{10,12},{12... | collective-permute-start | bytes 786440 | tf_op jit(solution)/shard_map/ppermute | solution.py:72
  170.3 26.9 %collective-permute-start.19 = (f32[2,128,1152]{2,1,0:T(8,128)S(1)}, f32[2,128,1152]{2,1,0:T(8,128)}, u32[]{:S(2)}, u32[]{:S(2)}) collective-permute-start(f32[2,128,1152]{2,1,0:T(8,128)S(1)} %dynamic-slice_bitcast_fusion), channel_id=1, source_target_pairs={{0,4},{4,0},{1,5},{5,1},{2,6},{6,2},{3,7},{7,3},{8,12},{12,8},{9,1... | collective-permute-start | bytes 3538952 | tf_op jit(solution)/shard_map/ppermute | solution.py:91
  172.2 28.3 %collective-permute-start.17 = (f32[2,128,1152]{2,1,0:T(8,128)}, f32[2,128,1152]{2,1,0:T(8,128)}, u32[]{:S(2)}, u32[]{:S(2)}) collective-permute-start(f32[2,128,1152]{2,1,0:T(8,128)} %dynamic-slice_bitcast_fusion.1), channel_id=1, source_target_pairs={{0,2},{2,0},{1,3},{3,1},{4,6},{6,4},{5,7},{7,5},{8,10},{10,8},{9,1... | collective-permute-start | bytes 3538952 | tf_op jit(solution)/shard_map/ppermute | solution.py:91
  198.9 14.2 %collective-permute-start.20 = (f32[128,1152]{1,0:T(8,128)S(1)}, f32[128,1152]{1,0:T(8,128)S(1)}, u32[]{:S(2)}, u32[]{:S(2)}) collective-permute-start(f32[128,1152]{1,0:T(8,128)S(1)} %dynamic-slice_bitcast_fusion.2), channel_id=1, source_target_pairs={{0,2},{2,0},{1,3},{3,1},{4,6},{6,4},{5,7},{7,5},{8,10},{10,8},{9,1... | collective-permute-start | bytes 1769480 | tf_op jit(solution)/shard_map/ppermute | solution.py:94
  201.9 14.2 %collective-permute-start.18 = (f32[128,1152]{1,0:T(8,128)S(1)}, f32[128,1152]{1,0:T(8,128)S(1)}, u32[]{:S(2)}, u32[]{:S(2)}) collective-permute-start(f32[128,1152]{1,0:T(8,128)S(1)} %dynamic-slice_bitcast_fusion.3), channel_id=1, source_target_pairs={{0,4},{4,0},{1,5},{5,1},{2,6},{6,2},{3,7},{7,3},{8,12},{12,8},{9,1... | collective-permute-start | bytes 1769480 | tf_op jit(solution)/shard_map/ppermute | solution.py:94
  219.0 3.6 %collective-permute-start.21 = (f32[16]{0:T(128)S(1)}, f32[16]{0:T(128)S(1)}, u32[]{:S(2)}, u32[]{:S(2)}) collective-permute-start(f32[16]{0:T(128)S(1)} %select_reduce_fusion), channel_id=1, source_target_pairs={{0,8},{8,0},{16,24},{24,16},{1,9},{9,1},{17,25},{25,17},{2,10},{10... | collective-permute-start | bytes 200 | tf_op jit(solution)/shard_map/ppermute | solution.py:102
  222.6 4.4 %collective-permute-start.22 = (f32[16]{0:T(128)S(1)}, f32[16]{0:T(128)S(1)}, u32[]{:S(2)}, u32[]{:S(2)}) collective-permute-start(f32[16]{0:T(128)S(1)} %add.644), channel_id=1, source_target_pairs={{0,16},{8,24},{16,0},{24,8},{1,17},{9,25},{17,1},{25,9},{2,18},{10... | collective-permute-start | bytes 200 | tf_op jit(solution)/shard_map/ppermute | solution.py:102
  227.1 3.5 %collective-permute-start.23 = (f32[16]{0:T(128)S(1)}, f32[16]{0:T(128)S(1)}, u32[]{:S(2)}, u32[]{:S(2)}) collective-permute-start(f32[16]{0:T(128)S(1)} %add.645), channel_id=1, source_target_pairs={{0,4},{4,0},{1,5},{5,1},{2,6},{6,2},{3,7},{7,3},{8,12},{12,8},{9,1... | collective-permute-start | bytes 200 | tf_op jit(solution)/shard_map/ppermute | solution.py:102
  230.6 3.5 %collective-permute-start.24 = (f32[16]{0:T(128)S(1)}, f32[16]{0:T(128)S(1)}, u32[]{:S(2)}, u32[]{:S(2)}) collective-permute-start(f32[16]{0:T(128)S(1)} %add.646), channel_id=1, source_target_pairs={{0,2},{2,0},{1,3},{3,1},{4,6},{6,4},{5,7},{7,5},{8,10},{10,8},{9,1... | collective-permute-start | bytes 200 | tf_op jit(solution)/shard_map/ppermute | solution.py:102
  (12 other events, 143.0 us)

commit v18 on v16

--- a/solution.py
+++ b/solution.py
@@ -42,8 +42,9 @@
 def gather_order(x, order):
     stride = {"c2": 1, "c1": lax.axis_size("c2"), "c0": lax.axis_size("c1") * lax.axis_size("c2")}
     source = jnp.zeros((), jnp.int32)
+    x = x.T
     for axis in order[:-1]:
-        x = ring_gather(x, axis)
+        x = jnp.concatenate(ring_pieces(x, axis), axis=1)
         n = lax.axis_size(axis)
         came = (lax.axis_index(axis) - jnp.arange(n, dtype=jnp.int32)) % n
         source = came.reshape((n,) + (1,) * source.ndim) * stride[axis] + source[None]
@@ -51,7 +52,7 @@
     n = lax.axis_size(last)
     own = lax.axis_index(last)
     return [
-        (piece, (((own - t) % n) * stride[last] + source).reshape(-1))
+        (piece.T, (((own - t) % n) * stride[last] + source).reshape(-1))
         for t, piece in enumerate(ring_pieces(x, last))
     ]
 

time: 233 us -> 235 us (level)
  waiting for transfers between devices: 151 us -> 162 us
  local copies, waits for them, and re-layouts: 28.6 us -> 18.9 us
    ppermute x14, waiting for transfers between devices: 87.9 us -> 99.3 us  [ring_pieces(): lax.ppermute(pieces[-1], axis, [(k, (k + 1) % n) for k in range(n)])]
    reshape x2 -> x0, local copies, waits for them, and re-layouts: 6.83 us -> none  [shards(): gathered.append((got.reshape(key_rows.shape[0], -1), key_rows))]
    unnamed x48 -> x46, local copies, waits for them, and re-layouts: 11.9 us -> 8.12 us
    slice x4 -> x3, local copies, waits for them, and re-layouts: 5.73 us -> 4.56 us  [shards(): got[:, :width]]
  transfers between devices with their start and end apart: 25 -> 25, of which waited for: 20 -> 19; matrix products, arithmetic and copies ran while one was open for 13% -> 8% of each run, Pallas kernels for 0% -> 0%
where the time goes in v18:
time: 235 us
  waiting for transfers between devices  162 us (69%)
  starting transfers between devices  20.3 us (9%)
  local copies, waits for them, and re-layouts  18.9 us (8%)
  matrix products  18.3 us (8%)
  other arithmetic  11.5 us (5%)
  blocking collectives  2.47 us (1%)
    ppermute x14, waiting for transfers between devices, ring_pieces(): lax.ppermute(pieces[-1], axis, [(k, (k + 1) % n) for k in range(n)])  99.3 us
    ppermute x2, waiting for transfers between devices, swap_reduce_scatter(): keep = keep + lax.ppermute(sent, first, [(0, 1), (1, 0)])  24.1 us
    ppermute x4, waiting for transfers between devices, butterfly_sum(): x = x + lax.ppermute(x, axis, [(i, i ^ bit) for i in range(size)])  13.3 us
    ppermute x14, starting transfers between devices, ring_pieces(): lax.ppermute(pieces[-1], axis, [(k, (k + 1) % n) for k in range(n)])  13.2 us
    ppermute x2, waiting for transfers between devices, swap_reduce_scatter(): return mine + lax.ppermute(sent, second, [(0, 1), (1, 0)])  13.1 us
    ppermute x3, waiting for transfers between devices, permute_all_to_all(): lax.ppermute(sent, axes, [(k, (k + shift) % n) for k in range(n)])  12.2 us
    unnamed x46, local copies, waits for them, and re-layouts  8.12 us
    dot_general x3, matrix products, shards(): jnp.dot(regrouped[:, t], weight_rows[t], preferred_element_type=jnp.float32)  6.18 us
  transfers between devices with their start and end apart: 25, of which 19 were waited for; matrix products, arithmetic and copies ran while one was open for 8% of the time, Pallas kernels for 0%

profile of v18, /device:TPU:0, one launch (start us, length us, event | category | flops | bytes accessed | tf_op | source)
XLA Modules:
  0.0 234.6 jit_solution(16779409169202614489)
XLA Ops:
  3.0 3.1 %collective-permute-start.4 = (bf16[1024,128]{1,0:T(8,128)(2,1)S(1)}, bf16[1024,128]{1,0:T(8,128)(2,1)S(1)}, u32[]{:S(2)}, u32[]{:S(2)}) collective-permute-start(bf16[1024,128]{1,0:T(8,128)(2,1)S(1)} %maximum_bitcast_fusion.1), channel_id=1, source_target_pairs={{0,8},{8,16},{16,24},{24,0},{1,9},{9,17},{17,25},{25,1},{2,10},{10... | collective-permute-start | bytes 786440 | tf_op jit(solution)/shard_map/ppermute | solution.py:34
  8.0 7.2 %collective-permute-done.4 = bf16[1024,128]{1,0:T(8,128)(2,1)S(1)} collective-permute-done((bf16[1024,128]{1,0:T(8,128)(2,1)S(1)}, bf16[1024,128]{1,0:T(8,128)(2,1)S(1)}, u32[]{:S(2)}, u32[]{:S(2)}) %collective-permute-start.4) | collective-permute-done | bytes 262176 | tf_op jit(solution)/shard_map/ppermute | solution.py:34
  15.3 5.6 %collective-permute-done = bf16[1024,128]{1,0:T(8,128)(2,1)S(1)} collective-permute-done((bf16[1024,128]{1,0:T(8,128)(2,1)S(1)}, bf16[1024,128]{1,0:T(8,128)(2,1)S(1)}, u32[]{:S(2)}, u32[]{:S(2)}) %collective-permute-start) | collective-permute-done | bytes 262176 | tf_op jit(solution)/shard_map/ppermute | solution.py:34
  20.9 5.6 %collective-permute-done.5 = bf16[1024,128]{1,0:T(8,128)(2,1)S(1)} collective-permute-done((bf16[1024,128]{1,0:T(8,128)(2,1)S(1)}, bf16[1024,128]{1,0:T(8,128)(2,1)S(1)}, u32[]{:S(2)}, u32[]{:S(2)}) %collective-permute-start.5) | collective-permute-done | bytes 262176 | tf_op jit(solution)/shard_map/ppermute | solution.py:34
  26.5 5.6 %collective-permute-done.1 = bf16[1024,128]{1,0:T(8,128)(2,1)S(1)} collective-permute-done((bf16[1024,128]{1,0:T(8,128)(2,1)S(1)}, bf16[1024,128]{1,0:T(8,128)(2,1)S(1)}, u32[]{:S(2)}, u32[]{:S(2)}) %collective-permute-start.1) | collective-permute-done | bytes 262176 | tf_op jit(solution)/shard_map/ppermute | solution.py:34
  33.7 4.0 %collective-permute-done.6 = bf16[1024,128]{1,0:T(8,128)(2,1)S(1)} collective-permute-done((bf16[1024,128]{1,0:T(8,128)(2,1)S(1)}, bf16[1024,128]{1,0:T(8,128)(2,1)S(1)}, u32[]{:S(2)}, u32[]{:S(2)}) %collective-permute-start.6) | collective-permute-done | bytes 262176 | tf_op jit(solution)/shard_map/ppermute | solution.py:34
  39.7 3.7 %collective-permute-done.2 = bf16[1024,128]{1,0:T(8,128)(2,1)S(1)} collective-permute-done((bf16[1024,128]{1,0:T(8,128)(2,1)S(1)}, bf16[1024,128]{1,0:T(8,128)(2,1)S(1)}, u32[]{:S(2)}, u32[]{:S(2)}) %collective-permute-start.2) | collective-permute-done | bytes 262176 | tf_op jit(solution)/shard_map/ppermute | solution.py:34
  49.8 18.1 %collective-permute-done.10 = bf16[256,2304]{1,0:T(8,128)(2,1)} collective-permute-done((bf16[256,2304]{1,0:T(8,128)(2,1)S(1)}, bf16[256,2304]{1,0:T(8,128)(2,1)}, u32[]{:S(2)}, u32[]{:S(2)}) %collective-permute-start.10) | collective-permute-done | bytes 1179680 | tf_op jit(solution)/shard_map/ppermute | solution.py:34
  73.1 24.1 %collective-permute-done.11 = bf16[256,2304]{1,0:T(8,128)(2,1)} collective-permute-done((bf16[256,2304]{1,0:T(8,128)(2,1)}, bf16[256,2304]{1,0:T(8,128)(2,1)}, u32[]{:S(2)}, u32[]{:S(2)}) %collective-permute-start.11) | collective-permute-done | bytes 1179680 | tf_op jit(solution)/shard_map/ppermute | solution.py:34
  101.9 23.6 %collective-permute-done.12 = bf16[256,2304]{1,0:T(8,128)(2,1)} collective-permute-done((bf16[256,2304]{1,0:T(8,128)(2,1)}, bf16[256,2304]{1,0:T(8,128)(2,1)}, u32[]{:S(2)}, u32[]{:S(2)}) %collective-permute-start.12) | collective-permute-done | bytes 1179680 | tf_op jit(solution)/shard_map/ppermute | solution.py:34
  125.5 2.7 %fusion.95 = (bf16[1024,512]{0,1:T(8,128)(2,1)S(1)}, bf16[1024,512]{0,1:T(8,128)(2,1)S(1)}, bf16[1024,512]{0,1:T(8,128)(2,1)S(1)}, bf16[1024,512]{0,1:T(8,128)(2,1)S(1)}) fusion(bf16[1024,1024]{0,1:T(8,128)(2,1)} %bitcast.14, bf16[1024,1024]{0,1:T(8,128)(2,1)} %bitcast.12), kind=kLoop, calls=%fused_computation.236 | loop fusion | bytes 8388608 | tf_op jit(solution)/shard_map/slice | solution.py:204
  144.3 2.2 collective-permute-start.14
  148.2 5.5 %collective-permute-done.14 = bf16[128,4,256]{2,0,1:T(8,128)(2,1)S(1)} collective-permute-done((bf16[128,4,256]{2,0,1:T(8,128)(2,1)S(1)}, bf16[128,4,256]{2,0,1:T(8,128)(2,1)S(1)}, u32[]{:S(2)}, u32[]{:S(2)}) %collective-permute-start.14) | collective-permute-done | bytes 262176 | tf_op jit(solution)/shard_map/ppermute | solution.py:72
  153.7 6.7 %collective-permute-done.15 = bf16[128,4,256]{2,0,1:T(8,128)(2,1)S(1)} collective-permute-done((bf16[128,4,256]{2,0,1:T(8,128)(2,1)S(1)}, bf16[128,4,256]{2,0,1:T(8,128)(2,1)S(1)}, u32[]{:S(2)}, u32[]{:S(2)}) %collective-permute-start.15) | collective-permute-done | bytes 262176 | tf_op jit(solution)/shard_map/ppermute | solution.py:72
  163.6 2.1 fusion.33
  165.6 2.1 fusion.34
  173.5 24.1 %collective-permute-done.19 = f32[2,128,1152]{2,1,0:T(8,128)} collective-permute-done((f32[2,128,1152]{2,1,0:T(8,128)S(1)}, f32[2,128,1152]{2,1,0:T(8,128)}, u32[]{:S(2)}, u32[]{:S(2)}) %collective-permute-start.19) | collective-permute-done | bytes 1179680 | tf_op jit(solution)/shard_map/ppermute | solution.py:91
  202.9 10.2 %collective-permute-done.20 = f32[128,1152]{1,0:T(8,128)S(1)} collective-permute-done((f32[128,1152]{1,0:T(8,128)S(1)}, f32[128,1152]{1,0:T(8,128)S(1)}, u32[]{:S(2)}, u32[]{:S(2)}) %collective-permute-start.20) | collective-permute-done | bytes 589856 | tf_op jit(solution)/shard_map/ppermute | solution.py:94
  213.1 2.9 %collective-permute-done.18 = f32[128,1152]{1,0:T(8,128)S(1)} collective-permute-done((f32[128,1152]{1,0:T(8,128)S(1)}, f32[128,1152]{1,0:T(8,128)S(1)}, u32[]{:S(2)}, u32[]{:S(2)}) %collective-permute-start.18) | collective-permute-done | bytes 589856 | tf_op jit(solution)/shard_map/ppermute | solution.py:94
  216.4 2.5 %psum.7 = f32[3,128]{1,0:T(4,128)S(1)} all-reduce(f32[3,128]{1,0:T(4,128)S(1)} %pad_maximum_fusion.5), channel_id=1, replica_groups=mesh['c0'=4,'c1'=2,'c2'=2,'head'=2] {'head'}, use_global_device_ids=true, to_apply=%region_13.14 | all-reduce | flops 384 | bytes 3072 | tf_op jit(solution)/shard_map/psum | solution.py:226
  219.0 3.5 %collective-permute-done.21 = f32[16]{0:T(128)S(1)} collective-permute-done((f32[16]{0:T(128)S(1)}, f32[16]{0:T(128)S(1)}, u32[]{:S(2)}, u32[]{:S(2)}) %collective-permute-start.21) | collective-permute-done | bytes 96 | tf_op jit(solution)/shard_map/ppermute | solution.py:102
  222.6 4.4 %collective-permute-done.22 = f32[16]{0:T(128)S(1)} collective-permute-done((f32[16]{0:T(128)S(1)}, f32[16]{0:T(128)S(1)}, u32[]{:S(2)}, u32[]{:S(2)}) %collective-permute-start.22) | collective-permute-done | bytes 96 | tf_op jit(solution)/shard_map/ppermute | solution.py:102
  227.3 3.3 %collective-permute-done.23 = f32[16]{0:T(128)S(1)} collective-permute-done((f32[16]{0:T(128)S(1)}, f32[16]{0:T(128)S(1)}, u32[]{:S(2)}, u32[]{:S(2)}) %collective-permute-start.23) | collective-permute-done | bytes 96 | tf_op jit(solution)/shard_map/ppermute | solution.py:102
  232.0 2.1 collective-permute-done.24
  (152 shorter events, 58.7 us)
Async XLA Ops:
  3.0 12.2 %collective-permute-start.4 = (bf16[1024,128]{1,0:T(8,128)(2,1)S(1)}, bf16[1024,128]{1,0:T(8,128)(2,1)S(1)}, u32[]{:S(2)}, u32[]{:S(2)}) collective-permute-start(bf16[1024,128]{1,0:T(8,128)(2,1)S(1)} %maximum_bitcast_fusion.1), channel_id=1, source_target_pairs={{0,8},{8,16},{16,24},{24,0},{1,9},{9,17},{17,25},{25,1},{2,10},{10... | collective-permute-start | bytes 786440 | tf_op jit(solution)/shard_map/ppermute | solution.py:34
  6.4 14.5 %collective-permute-start = (bf16[1024,128]{1,0:T(8,128)(2,1)S(1)}, bf16[1024,128]{1,0:T(8,128)(2,1)S(1)}, u32[]{:S(2)}, u32[]{:S(2)}) collective-permute-start(bf16[1024,128]{1,0:T(8,128)(2,1)S(1)} %maximum_bitcast_fusion), channel_id=1, source_target_pairs={{0,8},{8,16},{16,24},{24,0},{1,9},{9,17},{17,25},{25,1},{2,10},{10... | collective-permute-start | bytes 786440 | tf_op jit(solution)/shard_map/ppermute | solution.py:34
  15.2 11.2 %collective-permute-start.5 = (bf16[1024,128]{1,0:T(8,128)(2,1)S(1)}, bf16[1024,128]{1,0:T(8,128)(2,1)S(1)}, u32[]{:S(2)}, u32[]{:S(2)}) collective-permute-start(bf16[1024,128]{1,0:T(8,128)(2,1)S(1)} %collective-permute-done.4), channel_id=1, source_target_pairs={{0,8},{8,16},{16,24},{24,0},{1,9},{9,17},{17,25},{25,1},{2,10},{10... | collective-permute-start | bytes 786440 | tf_op jit(solution)/shard_map/ppermute | solution.py:34
  20.8 11.2 %collective-permute-start.1 = (bf16[1024,128]{1,0:T(8,128)(2,1)S(1)}, bf16[1024,128]{1,0:T(8,128)(2,1)S(1)}, u32[]{:S(2)}, u32[]{:S(2)}) collective-permute-start(bf16[1024,128]{1,0:T(8,128)(2,1)S(1)} %collective-permute-done), channel_id=1, source_target_pairs={{0,8},{8,16},{16,24},{24,0},{1,9},{9,17},{17,25},{25,1},{2,10},{10... | collective-permute-start | bytes 786440 | tf_op jit(solution)/shard_map/ppermute | solution.py:34
  26.5 11.2 %collective-permute-start.6 = (bf16[1024,128]{1,0:T(8,128)(2,1)S(1)}, bf16[1024,128]{1,0:T(8,128)(2,1)S(1)}, u32[]{:S(2)}, u32[]{:S(2)}) collective-permute-start(bf16[1024,128]{1,0:T(8,128)(2,1)S(1)} %collective-permute-done.5), channel_id=1, source_target_pairs={{0,8},{8,16},{16,24},{24,0},{1,9},{9,17},{17,25},{25,1},{2,10},{10... | collective-permute-start | bytes 786440 | tf_op jit(solution)/shard_map/ppermute | solution.py:34
  32.1 11.2 %collective-permute-start.2 = (bf16[1024,128]{1,0:T(8,128)(2,1)S(1)}, bf16[1024,128]{1,0:T(8,128)(2,1)S(1)}, u32[]{:S(2)}, u32[]{:S(2)}) collective-permute-start(bf16[1024,128]{1,0:T(8,128)(2,1)S(1)} %collective-permute-done.1), channel_id=1, source_target_pairs={{0,8},{8,16},{16,24},{24,0},{1,9},{9,17},{17,25},{25,1},{2,10},{10... | collective-permute-start | bytes 786440 | tf_op jit(solution)/shard_map/ppermute | solution.py:34
  32.1 35.8 %collective-permute-start.10 = (bf16[256,2304]{1,0:T(8,128)(2,1)S(1)}, bf16[256,2304]{1,0:T(8,128)(2,1)}, u32[]{:S(2)}, u32[]{:S(2)}) collective-permute-start(bf16[256,2304]{1,0:T(8,128)(2,1)S(1)} %copy-done.2), channel_id=1, source_target_pairs={{0,8},{8,16},{16,24},{24,0},{1,9},{9,17},{17,25},{25,1},{2,10},{10... | collective-permute-start | bytes 3538952 | tf_op jit(solution)/shard_map/ppermute | solution.py:34
  37.8 30.8 %collective-permute-start.7 = (bf16[1024,512]{1,0:T(8,128)(2,1)S(1)}, bf16[1024,512]{1,0:T(8,128)(2,1)S(1)}, u32[]{:S(2)}, u32[]{:S(2)}) collective-permute-start(bf16[1024,512]{1,0:T(8,128)(2,1)S(1)} %pad_maximum_fusion.2), channel_id=1, source_target_pairs={{0,4},{4,0},{1,5},{5,1},{2,6},{6,2},{3,7},{7,3},{8,12},{12,8},{9,1... | collective-permute-start | bytes 3145736 | tf_op jit(solution)/shard_map/ppermute | solution.py:34
  43.5 26.9 %collective-permute-start.3 = (bf16[1024,512]{1,0:T(8,128)(2,1)S(1)}, bf16[1024,512]{1,0:T(8,128)(2,1)S(1)}, u32[]{:S(2)}, u32[]{:S(2)}) collective-permute-start(bf16[1024,512]{1,0:T(8,128)(2,1)S(1)} %pad_maximum_fusion.1), channel_id=1, source_target_pairs={{0,2},{2,0},{1,3},{3,1},{4,6},{6,4},{5,7},{7,5},{8,10},{10,8},{9,1... | collective-permute-start | bytes 3145736 | tf_op jit(solution)/shard_map/ppermute | solution.py:34
  67.9 29.3 %collective-permute-start.11 = (bf16[256,2304]{1,0:T(8,128)(2,1)}, bf16[256,2304]{1,0:T(8,128)(2,1)}, u32[]{:S(2)}, u32[]{:S(2)}) collective-permute-start(bf16[256,2304]{1,0:T(8,128)(2,1)} %collective-permute-done.10), channel_id=1, source_target_pairs={{0,8},{8,16},{16,24},{24,0},{1,9},{9,17},{17,25},{25,1},{2,10},{10... | collective-permute-start | bytes 3538952 | tf_op jit(solution)/shard_map/ppermute | solution.py:34
  68.8 56.7 %collective-permute-start.8 = (bf16[1024,1024]{1,0:T(8,128)(2,1)S(1)}, bf16[1024,1024]{1,0:T(8,128)(2,1)}, u32[]{:S(2)}, u32[]{:S(2)}) collective-permute-start(bf16[1024,1024]{1,0:T(8,128)(2,1)S(1)} %constant_dynamic-update-slice_fusion.5), channel_id=1, source_target_pairs={{0,2},{2,0},{1,3},{3,1},{4,6},{6,4},{5,7},{7,5},{8,10},{10,8},{9,1... | collective-permute-start | bytes 6291464 | tf_op jit(solution)/shard_map/ppermute | solution.py:34
  71.4 54.1 %collective-permute-start.9 = (bf16[1024,1024]{1,0:T(8,128)(2,1)}, bf16[1024,1024]{1,0:T(8,128)(2,1)}, u32[]{:S(2)}, u32[]{:S(2)}) collective-permute-start(bf16[1024,1024]{1,0:T(8,128)(2,1)} %constant_dynamic-update-slice_fusion), channel_id=1, source_target_pairs={{0,4},{4,0},{1,5},{5,1},{2,6},{6,2},{3,7},{7,3},{8,12},{12,8},{9,1... | collective-permute-start | bytes 6291464 | tf_op jit(solution)/shard_map/ppermute | solution.py:34
  97.1 28.3 %collective-permute-start.12 = (bf16[256,2304]{1,0:T(8,128)(2,1)}, bf16[256,2304]{1,0:T(8,128)(2,1)}, u32[]{:S(2)}, u32[]{:S(2)}) collective-permute-start(bf16[256,2304]{1,0:T(8,128)(2,1)} %collective-permute-done.11), channel_id=1, source_target_pairs={{0,8},{8,16},{16,24},{24,0},{1,9},{9,17},{17,25},{25,1},{2,10},{10... | collective-permute-start | bytes 3538952 | tf_op jit(solution)/shard_map/ppermute | solution.py:34
  144.3 9.4 %collective-permute-start.14 = (bf16[128,4,256]{2,0,1:T(8,128)(2,1)S(1)}, bf16[128,4,256]{2,0,1:T(8,128)(2,1)S(1)}, u32[]{:S(2)}, u32[]{:S(2)}) collective-permute-start(bf16[128,4,256]{2,0,1:T(8,128)(2,1)S(1)} %bitcast.258), channel_id=1, source_target_pairs={{0,6},{2,0},{4,2},{6,4},{1,7},{3,1},{5,3},{7,5},{8,14},{10,8},{12,... | collective-permute-start | bytes 786440 | tf_op jit(solution)/shard_map/ppermute | solution.py:72
  146.7 13.8 %collective-permute-start.15 = (bf16[128,4,256]{2,0,1:T(8,128)(2,1)S(1)}, bf16[128,4,256]{2,0,1:T(8,128)(2,1)S(1)}, u32[]{:S(2)}, u32[]{:S(2)}) collective-permute-start(bf16[128,4,256]{2,0,1:T(8,128)(2,1)S(1)} %bitcast.259), channel_id=1, source_target_pairs={{0,4},{2,6},{4,0},{6,2},{1,5},{3,7},{5,1},{7,3},{8,12},{10,14},{12... | collective-permute-start | bytes 786440 | tf_op jit(solution)/shard_map/ppermute | solution.py:72
  147.4 13.0 %collective-permute-start.16 = (bf16[128,4,256]{2,0,1:T(8,128)(2,1)S(1)}, bf16[128,4,256]{2,0,1:T(8,128)(2,1)S(1)}, u32[]{:S(2)}, u32[]{:S(2)}) collective-permute-start(bf16[128,4,256]{2,0,1:T(8,128)(2,1)S(1)} %bitcast.260), channel_id=1, source_target_pairs={{0,2},{2,4},{4,6},{6,0},{1,3},{3,5},{5,7},{7,1},{8,10},{10,12},{12... | collective-permute-start | bytes 786440 | tf_op jit(solution)/shard_map/ppermute | solution.py:72
  170.5 27.0 %collective-permute-start.19 = (f32[2,128,1152]{2,1,0:T(8,128)S(1)}, f32[2,128,1152]{2,1,0:T(8,128)}, u32[]{:S(2)}, u32[]{:S(2)}) collective-permute-start(f32[2,128,1152]{2,1,0:T(8,128)S(1)} %dynamic-slice_bitcast_fusion), channel_id=1, source_target_pairs={{0,4},{4,0},{1,5},{5,1},{2,6},{6,2},{3,7},{7,3},{8,12},{12,8},{9,1... | collective-permute-start | bytes 3538952 | tf_op jit(solution)/shard_map/ppermute | solution.py:91
  172.2 28.2 %collective-permute-start.17 = (f32[2,128,1152]{2,1,0:T(8,128)}, f32[2,128,1152]{2,1,0:T(8,128)}, u32[]{:S(2)}, u32[]{:S(2)}) collective-permute-start(f32[2,128,1152]{2,1,0:T(8,128)} %dynamic-slice_bitcast_fusion.1), channel_id=1, source_target_pairs={{0,2},{2,0},{1,3},{3,1},{4,6},{6,4},{5,7},{7,5},{8,10},{10,8},{9,1... | collective-permute-start | bytes 3538952 | tf_op jit(solution)/shard_map/ppermute | solution.py:91
  199.4 13.7 %collective-permute-start.20 = (f32[128,1152]{1,0:T(8,128)S(1)}, f32[128,1152]{1,0:T(8,128)S(1)}, u32[]{:S(2)}, u32[]{:S(2)}) collective-permute-start(f32[128,1152]{1,0:T(8,128)S(1)} %dynamic-slice_bitcast_fusion.2), channel_id=1, source_target_pairs={{0,2},{2,0},{1,3},{3,1},{4,6},{6,4},{5,7},{7,5},{8,10},{10,8},{9,1... | collective-permute-start | bytes 1769480 | tf_op jit(solution)/shard_map/ppermute | solution.py:94
  201.9 14.1 %collective-permute-start.18 = (f32[128,1152]{1,0:T(8,128)S(1)}, f32[128,1152]{1,0:T(8,128)S(1)}, u32[]{:S(2)}, u32[]{:S(2)}) collective-permute-start(f32[128,1152]{1,0:T(8,128)S(1)} %dynamic-slice_bitcast_fusion.3), channel_id=1, source_target_pairs={{0,4},{4,0},{1,5},{5,1},{2,6},{6,2},{3,7},{7,3},{8,12},{12,8},{9,1... | collective-permute-start | bytes 1769480 | tf_op jit(solution)/shard_map/ppermute | solution.py:94
  219.0 3.6 %collective-permute-start.21 = (f32[16]{0:T(128)S(1)}, f32[16]{0:T(128)S(1)}, u32[]{:S(2)}, u32[]{:S(2)}) collective-permute-start(f32[16]{0:T(128)S(1)} %select_reduce_fusion), channel_id=1, source_target_pairs={{0,8},{8,0},{16,24},{24,16},{1,9},{9,1},{17,25},{25,17},{2,10},{10... | collective-permute-start | bytes 200 | tf_op jit(solution)/shard_map/ppermute | solution.py:102
  222.6 4.4 %collective-permute-start.22 = (f32[16]{0:T(128)S(1)}, f32[16]{0:T(128)S(1)}, u32[]{:S(2)}, u32[]{:S(2)}) collective-permute-start(f32[16]{0:T(128)S(1)} %add.644), channel_id=1, source_target_pairs={{0,16},{8,24},{16,0},{24,8},{1,17},{9,25},{17,1},{25,9},{2,18},{10... | collective-permute-start | bytes 200 | tf_op jit(solution)/shard_map/ppermute | solution.py:102
  227.0 3.5 %collective-permute-start.23 = (f32[16]{0:T(128)S(1)}, f32[16]{0:T(128)S(1)}, u32[]{:S(2)}, u32[]{:S(2)}) collective-permute-start(f32[16]{0:T(128)S(1)} %add.645), channel_id=1, source_target_pairs={{0,4},{4,0},{1,5},{5,1},{2,6},{6,2},{3,7},{7,3},{8,12},{12,8},{9,1... | collective-permute-start | bytes 200 | tf_op jit(solution)/shard_map/ppermute | solution.py:102
  230.6 3.5 %collective-permute-start.24 = (f32[16]{0:T(128)S(1)}, f32[16]{0:T(128)S(1)}, u32[]{:S(2)}, u32[]{:S(2)}) collective-permute-start(f32[16]{0:T(128)S(1)} %add.646), channel_id=1, source_target_pairs={{0,2},{2,0},{1,3},{3,1},{4,6},{6,4},{5,7},{7,5},{8,10},{10,8},{9,1... | collective-permute-start | bytes 200 | tf_op jit(solution)/shard_map/ppermute | solution.py:102
  (13 other events, 249.1 us)

commit v19 on v16

--- a/solution.py
+++ b/solution.py
@@ -212,15 +212,17 @@
     blocks = all_heads.reshape(tok_dev, outer, inner, rows_each).transpose(2, 0, 1, 3)
     regrouped = permute_all_to_all(blocks, INNER)
     regrouped = jnp.take(regrouped.reshape(inner * tok_dev, outer, rows_each), arrival, axis=1)
-    partial = jnp.dot(regrouped[:, 0], weight_rows[0], preferred_element_type=jnp.float32)
-    for t in range(1, outer):
-        partial = partial + jnp.dot(regrouped[:, t], weight_rows[t], preferred_element_type=jnp.float32)
-    by_dest = partial.reshape(2, 2, tok_dev, -1)
-    cut = by_dest.shape[-1] // 2
-    mixed = jnp.concatenate([
-        swap_reduce_scatter(by_dest[..., :cut], "c2", "c1"),
-        swap_reduce_scatter(by_dest[..., cut:].transpose(1, 0, 2, 3), "c1", "c2"),
-    ], axis=-1)
+    cut = out_weight.shape[1] // 2
+
+    def product(cols):
+        total = jnp.dot(regrouped[:, 0], weight_rows[0][:, cols], preferred_element_type=jnp.float32)
+        for t in range(1, outer):
+            total = total + jnp.dot(regrouped[:, t], weight_rows[t][:, cols], preferred_element_type=jnp.float32)
+        return total.reshape(2, 2, tok_dev, -1)
+
+    first_half = swap_reduce_scatter(product(slice(0, cut)), "c2", "c1")
+    second_half = swap_reduce_scatter(product(slice(cut, None)).transpose(1, 0, 2, 3), "c1", "c2")
+    mixed = jnp.concatenate([first_half, second_half], axis=-1)
     hidden = hidden_in.astype(jnp.float32)
     sums = lax.psum(
         jnp.stack([

time: 233 us -> 232 us (level)
  waiting for transfers between devices: 151 us -> 147 us
    ppermute x2, waiting for transfers between devices: 13.1 us -> 9.67 us  [swap_reduce_scatter(): return mine + lax.ppermute(sent, second, [(0, 1), (1, 0)])]
    dot_general x4 -> x8, matrix products: 5.93 us -> 8.3 us  [the longest x6 7.3 us: product(): jnp.dot(regrouped[:, t], weight_rows[t][:, cols], preferred_element_type=...]
  transfers between devices with their start and end apart: 25 -> 25, of which waited for: 20 -> 21; matrix products, arithmetic and copies ran while one was open for 13% -> 14% of each run, Pallas kernels for 0% -> 0%
where the time goes in v19:
time: 232 us
  waiting for transfers between devices  147 us (63%)
  local copies, waits for them, and re-layouts  27.9 us (12%)
  starting transfers between devices  22.5 us (10%)
  matrix products  19.5 us (8%)
  other arithmetic  11.5 us (5%)
  blocking collectives  2.47 us (1%)
    ppermute x14, waiting for transfers between devices, ring_pieces(): lax.ppermute(pieces[-1], axis, [(k, (k + 1) % n) for k in range(n)])  87.9 us
    ppermute x2, waiting for transfers between devices, swap_reduce_scatter(): keep = keep + lax.ppermute(sent, first, [(0, 1), (1, 0)])  25.2 us
    ppermute x14, starting transfers between devices, ring_pieces(): lax.ppermute(pieces[-1], axis, [(k, (k + 1) % n) for k in range(n)])  13.2 us
    ppermute x3, waiting for transfers between devices, permute_all_to_all(): lax.ppermute(sent, axes, [(k, (k + shift) % n) for k in range(n)])  12.2 us
    ppermute x4, waiting for transfers between devices, butterfly_sum(): x = x + lax.ppermute(x, axis, [(i, i ^ bit) for i in range(size)])  11.5 us
    unnamed x48, local copies, waits for them, and re-layouts  11.5 us
    ppermute x2, waiting for transfers between devices, swap_reduce_scatter(): return mine + lax.ppermute(sent, second, [(0, 1), (1, 0)])  9.67 us
    dot_general x6, matrix products, product(): jnp.dot(regrouped[:, t], weight_rows[t][:, cols], preferred_element_type=...  7.3 us
  transfers between devices with their start and end apart: 25, of which 21 were waited for; matrix products, arithmetic and copies ran while one was open for 14% of the time, Pallas kernels for 0%

profile of v19, /device:TPU:0, one launch (start us, length us, event | category | flops | bytes accessed | tf_op | source)
XLA Modules:
  0.0 231.7 jit_solution(12268679313851171215)
XLA Ops:
  1.9 3.1 %collective-permute-start.4 = (bf16[128,1024]{1,0:T(8,128)(2,1)S(1)}, bf16[128,1024]{1,0:T(8,128)(2,1)S(1)}, u32[]{:S(2)}, u32[]{:S(2)}) collective-permute-start(bf16[128,1024]{1,0:T(8,128)(2,1)S(1)} %get-tuple-element.47), channel_id=1, source_target_pairs={{0,8},{8,16},{16,24},{24,0},{1,9},{9,17},{17,25},{25,1},{2,10},{10... | collective-permute-start | bytes 786440 | tf_op jit(solution)/shard_map/ppermute | solution.py:34
  6.7 7.5 %collective-permute-done.4 = bf16[128,1024]{1,0:T(8,128)(2,1)S(1)} collective-permute-done((bf16[128,1024]{1,0:T(8,128)(2,1)S(1)}, bf16[128,1024]{1,0:T(8,128)(2,1)S(1)}, u32[]{:S(2)}, u32[]{:S(2)}) %collective-permute-start.4) | collective-permute-done | bytes 262176 | tf_op jit(solution)/shard_map/ppermute | solution.py:34
  14.2 5.6 %collective-permute-done = bf16[128,1024]{1,0:T(8,128)(2,1)S(1)} collective-permute-done((bf16[128,1024]{1,0:T(8,128)(2,1)S(1)}, bf16[128,1024]{1,0:T(8,128)(2,1)S(1)}, u32[]{:S(2)}, u32[]{:S(2)}) %collective-permute-start) | collective-permute-done | bytes 262176 | tf_op jit(solution)/shard_map/ppermute | solution.py:34
  19.8 5.6 %collective-permute-done.5 = bf16[128,1024]{1,0:T(8,128)(2,1)S(1)} collective-permute-done((bf16[128,1024]{1,0:T(8,128)(2,1)S(1)}, bf16[128,1024]{1,0:T(8,128)(2,1)S(1)}, u32[]{:S(2)}, u32[]{:S(2)}) %collective-permute-start.5) | collective-permute-done | bytes 262176 | tf_op jit(solution)/shard_map/ppermute | solution.py:34
  25.4 5.6 %collective-permute-done.1 = bf16[128,1024]{1,0:T(8,128)(2,1)S(1)} collective-permute-done((bf16[128,1024]{1,0:T(8,128)(2,1)S(1)}, bf16[128,1024]{1,0:T(8,128)(2,1)S(1)}, u32[]{:S(2)}, u32[]{:S(2)}) %collective-permute-start.1) | collective-permute-done | bytes 262176 | tf_op jit(solution)/shard_map/ppermute | solution.py:34
  32.6 4.0 %collective-permute-done.6 = bf16[128,1024]{1,0:T(8,128)(2,1)S(1)} collective-permute-done((bf16[128,1024]{1,0:T(8,128)(2,1)S(1)}, bf16[128,1024]{1,0:T(8,128)(2,1)S(1)}, u32[]{:S(2)}, u32[]{:S(2)}) %collective-permute-start.6) | collective-permute-done | bytes 262176 | tf_op jit(solution)/shard_map/ppermute | solution.py:34
  38.6 3.6 %collective-permute-done.2 = bf16[128,1024]{1,0:T(8,128)(2,1)S(1)} collective-permute-done((bf16[128,1024]{1,0:T(8,128)(2,1)S(1)}, bf16[128,1024]{1,0:T(8,128)(2,1)S(1)}, u32[]{:S(2)}, u32[]{:S(2)}) %collective-permute-start.2) | collective-permute-done | bytes 262176 | tf_op jit(solution)/shard_map/ppermute | solution.py:34
  44.2 22.5 %collective-permute-done.10 = bf16[256,2304]{1,0:T(8,128)(2,1)S(1)} collective-permute-done((bf16[256,2304]{1,0:T(8,128)(2,1)S(1)}, bf16[256,2304]{1,0:T(8,128)(2,1)S(1)}, u32[]{:S(2)}, u32[]{:S(2)}) %collective-permute-start.10) | collective-permute-done | bytes 1179680 | tf_op jit(solution)/shard_map/ppermute | solution.py:34
  71.6 24.1 %collective-permute-done.11 = bf16[256,2304]{1,0:T(8,128)(2,1)} collective-permute-done((bf16[256,2304]{1,0:T(8,128)(2,1)S(1)}, bf16[256,2304]{1,0:T(8,128)(2,1)}, u32[]{:S(2)}, u32[]{:S(2)}) %collective-permute-start.11) | collective-permute-done | bytes 1179680 | tf_op jit(solution)/shard_map/ppermute | solution.py:34
  99.8 2.3 copy.86
  103.4 2.7 %fusion.102 = (bf16[1024,512]{1,0:T(8,128)(2,1)S(1)}, bf16[1024,512]{1,0:T(8,128)(2,1)}) fusion(bf16[1024,1024]{1,0:T(8,128)(2,1)} %bitcast.8), kind=kLoop, calls=%fused_computation.240 | loop fusion | bytes 4194304 | tf_op jit(solution)/shard_map/slice | solution.py:203
  109.7 4.2 %collective-permute-done.8 = bf16[2,4,128,1024]{3,2,1,0:T(8,128)(2,1)} collective-permute-done((bf16[2,4,128,1024]{3,2,1,0:T(8,128)(2,1)S(1)}, bf16[2,4,128,1024]{3,2,1,0:T(8,128)(2,1)}, u32[]{:S(2)}, u32[]{:S(2)}) %collective-permute-start.8) | collective-permute-done | bytes 2097184 | tf_op jit(solution)/shard_map/ppermute | solution.py:34
  113.9 4.0 %copy.74 = bf16[1024,1024]{0,1:T(8,128)(2,1)} copy(bf16[1024,1024]{1,0:T(8,128)(2,1)} %bitcast.22) | data formatting | bytes 4194304 | tf_op jit(solution)/shard_map/reshape | solution.py:188
  117.9 2.9 %copy.75 = bf16[1024,1024]{0,1:T(8,128)(2,1)S(1)} copy(bf16[1024,1024]{1,0:T(8,128)(2,1)} %bitcast.24) | data formatting | bytes 4194304 | tf_op jit(solution)/shard_map/reshape | solution.py:188
  120.8 3.4 %collective-permute-done.12 = bf16[256,2304]{1,0:T(8,128)(2,1)} collective-permute-done((bf16[256,2304]{1,0:T(8,128)(2,1)}, bf16[256,2304]{1,0:T(8,128)(2,1)}, u32[]{:S(2)}, u32[]{:S(2)}) %collective-permute-start.12) | collective-permute-done | bytes 1179680 | tf_op jit(solution)/shard_map/ppermute | solution.py:34
  146.2 5.5 %collective-permute-done.14 = bf16[128,4,256]{2,0,1:T(8,128)(2,1)S(1)} collective-permute-done((bf16[128,4,256]{2,0,1:T(8,128)(2,1)S(1)}, bf16[128,4,256]{2,0,1:T(8,128)(2,1)S(1)}, u32[]{:S(2)}, u32[]{:S(2)}) %collective-permute-start.14) | collective-permute-done | bytes 262176 | tf_op jit(solution)/shard_map/ppermute | solution.py:71
  151.6 6.7 %collective-permute-done.15 = bf16[128,4,256]{2,0,1:T(8,128)(2,1)S(1)} collective-permute-done((bf16[128,4,256]{2,0,1:T(8,128)(2,1)S(1)}, bf16[128,4,256]{2,0,1:T(8,128)(2,1)S(1)}, u32[]{:S(2)}, u32[]{:S(2)}) %collective-permute-start.15) | collective-permute-done | bytes 262176 | tf_op jit(solution)/shard_map/ppermute | solution.py:71
  172.2 20.3 %collective-permute-done.19 = f32[2,128,1152]{2,1,0:T(8,128)} collective-permute-done((f32[2,128,1152]{2,1,0:T(8,128)S(1)}, f32[2,128,1152]{2,1,0:T(8,128)}, u32[]{:S(2)}, u32[]{:S(2)}) %collective-permute-start.19) | collective-permute-done | bytes 1179680 | tf_op jit(solution)/shard_map/ppermute | solution.py:90
  195.4 4.9 %collective-permute-done.17 = f32[2,128,1152]{2,1,0:T(8,128)} collective-permute-done((f32[2,128,1152]{2,1,0:T(8,128)}, f32[2,128,1152]{2,1,0:T(8,128)}, u32[]{:S(2)}, u32[]{:S(2)}) %collective-permute-start.17) | collective-permute-done | bytes 1179680 | tf_op jit(solution)/shard_map/ppermute | solution.py:90
  203.3 7.5 %collective-permute-done.20 = f32[128,1152]{1,0:T(8,128)S(1)} collective-permute-done((f32[128,1152]{1,0:T(8,128)S(1)}, f32[128,1152]{1,0:T(8,128)S(1)}, u32[]{:S(2)}, u32[]{:S(2)}) %collective-permute-start.20) | collective-permute-done | bytes 589856 | tf_op jit(solution)/shard_map/ppermute | solution.py:93
  213.4 2.5 %psum.7 = f32[3,128]{1,0:T(4,128)S(1)} all-reduce(f32[3,128]{1,0:T(4,128)S(1)} %pad_maximum_fusion.9), channel_id=1, replica_groups=mesh['c0'=4,'c1'=2,'c2'=2,'head'=2] {'head'}, use_global_device_ids=true, to_apply=%region_13.14 | all-reduce | flops 384 | bytes 3072 | tf_op jit(solution)/shard_map/psum | solution.py:227
  216.1 3.5 %collective-permute-done.21 = f32[16]{0:T(128)S(1)} collective-permute-done((f32[16]{0:T(128)S(1)}, f32[16]{0:T(128)S(1)}, u32[]{:S(2)}, u32[]{:S(2)}) %collective-permute-start.21) | collective-permute-done | bytes 96 | tf_op jit(solution)/shard_map/ppermute | solution.py:101
  219.6 4.4 %collective-permute-done.22 = f32[16]{0:T(128)S(1)} collective-permute-done((f32[16]{0:T(128)S(1)}, f32[16]{0:T(128)S(1)}, u32[]{:S(2)}, u32[]{:S(2)}) %collective-permute-start.22) | collective-permute-done | bytes 96 | tf_op jit(solution)/shard_map/ppermute | solution.py:101
  224.8 2.8 %collective-permute-done.23 = f32[16]{0:T(128)S(1)} collective-permute-done((f32[16]{0:T(128)S(1)}, f32[16]{0:T(128)S(1)}, u32[]{:S(2)}, u32[]{:S(2)}) %collective-permute-start.23) | collective-permute-done | bytes 96 | tf_op jit(solution)/shard_map/ppermute | solution.py:101
  (157 shorter events, 71.4 us)
Async XLA Ops:
  1.9 12.2 %collective-permute-start.4 = (bf16[128,1024]{1,0:T(8,128)(2,1)S(1)}, bf16[128,1024]{1,0:T(8,128)(2,1)S(1)}, u32[]{:S(2)}, u32[]{:S(2)}) collective-permute-start(bf16[128,1024]{1,0:T(8,128)(2,1)S(1)} %get-tuple-element.47), channel_id=1, source_target_pairs={{0,8},{8,16},{16,24},{24,0},{1,9},{9,17},{17,25},{25,1},{2,10},{10... | collective-permute-start | bytes 786440 | tf_op jit(solution)/shard_map/ppermute | solution.py:34
  5.1 14.7 %collective-permute-start = (bf16[128,1024]{1,0:T(8,128)(2,1)S(1)}, bf16[128,1024]{1,0:T(8,128)(2,1)S(1)}, u32[]{:S(2)}, u32[]{:S(2)}) collective-permute-start(bf16[128,1024]{1,0:T(8,128)(2,1)S(1)} %get-tuple-element.41), channel_id=1, source_target_pairs={{0,8},{8,16},{16,24},{24,0},{1,9},{9,17},{17,25},{25,1},{2,10},{10... | collective-permute-start | bytes 786440 | tf_op jit(solution)/shard_map/ppermute | solution.py:34
  14.2 11.2 %collective-permute-start.5 = (bf16[128,1024]{1,0:T(8,128)(2,1)S(1)}, bf16[128,1024]{1,0:T(8,128)(2,1)S(1)}, u32[]{:S(2)}, u32[]{:S(2)}) collective-permute-start(bf16[128,1024]{1,0:T(8,128)(2,1)S(1)} %collective-permute-done.4), channel_id=1, source_target_pairs={{0,8},{8,16},{16,24},{24,0},{1,9},{9,17},{17,25},{25,1},{2,10},{10... | collective-permute-start | bytes 786440 | tf_op jit(solution)/shard_map/ppermute | solution.py:34
  19.8 11.2 %collective-permute-start.1 = (bf16[128,1024]{1,0:T(8,128)(2,1)S(1)}, bf16[128,1024]{1,0:T(8,128)(2,1)S(1)}, u32[]{:S(2)}, u32[]{:S(2)}) collective-permute-start(bf16[128,1024]{1,0:T(8,128)(2,1)S(1)} %collective-permute-done), channel_id=1, source_target_pairs={{0,8},{8,16},{16,24},{24,0},{1,9},{9,17},{17,25},{25,1},{2,10},{10... | collective-permute-start | bytes 786440 | tf_op jit(solution)/shard_map/ppermute | solution.py:34
  25.4 11.2 %collective-permute-start.6 = (bf16[128,1024]{1,0:T(8,128)(2,1)S(1)}, bf16[128,1024]{1,0:T(8,128)(2,1)S(1)}, u32[]{:S(2)}, u32[]{:S(2)}) collective-permute-start(bf16[128,1024]{1,0:T(8,128)(2,1)S(1)} %collective-permute-done.5), channel_id=1, source_target_pairs={{0,8},{8,16},{16,24},{24,0},{1,9},{9,17},{17,25},{25,1},{2,10},{10... | collective-permute-start | bytes 786440 | tf_op jit(solution)/shard_map/ppermute | solution.py:34
  31.0 11.2 %collective-permute-start.2 = (bf16[128,1024]{1,0:T(8,128)(2,1)S(1)}, bf16[128,1024]{1,0:T(8,128)(2,1)S(1)}, u32[]{:S(2)}, u32[]{:S(2)}) collective-permute-start(bf16[128,1024]{1,0:T(8,128)(2,1)S(1)} %collective-permute-done.1), channel_id=1, source_target_pairs={{0,8},{8,16},{16,24},{24,0},{1,9},{9,17},{17,25},{25,1},{2,10},{10... | collective-permute-start | bytes 786440 | tf_op jit(solution)/shard_map/ppermute | solution.py:34
  31.1 35.6 %collective-permute-start.10 = (bf16[256,2304]{1,0:T(8,128)(2,1)S(1)}, bf16[256,2304]{1,0:T(8,128)(2,1)S(1)}, u32[]{:S(2)}, u32[]{:S(2)}) collective-permute-start(bf16[256,2304]{1,0:T(8,128)(2,1)S(1)} %copy-done.2), channel_id=1, source_target_pairs={{0,8},{8,16},{16,24},{24,0},{1,9},{9,17},{17,25},{25,1},{2,10},{10... | collective-permute-start | bytes 3538952 | tf_op jit(solution)/shard_map/ppermute | solution.py:34
  36.8 29.9 %collective-permute-start.7 = (bf16[4,128,1024]{2,1,0:T(8,128)(2,1)S(1)}, bf16[4,128,1024]{2,1,0:T(8,128)(2,1)S(1)}, u32[]{:S(2)}, u32[]{:S(2)}) collective-permute-start(bf16[4,128,1024]{2,1,0:T(8,128)(2,1)S(1)} %get-tuple-element.39), channel_id=1, source_target_pairs={{0,4},{4,0},{1,5},{5,1},{2,6},{6,2},{3,7},{7,3},{8,12},{12,8},{9,1... | collective-permute-start | bytes 3145736 | tf_op jit(solution)/shard_map/ppermute | solution.py:34
  42.4 26.1 %collective-permute-start.3 = (bf16[4,128,1024]{2,1,0:T(8,128)(2,1)S(1)}, bf16[4,128,1024]{2,1,0:T(8,128)(2,1)S(1)}, u32[]{:S(2)}, u32[]{:S(2)}) collective-permute-start(bf16[4,128,1024]{2,1,0:T(8,128)(2,1)S(1)} %get-tuple-element.37), channel_id=1, source_target_pairs={{0,2},{2,0},{1,3},{3,1},{4,6},{6,4},{5,7},{7,5},{8,10},{10,8},{9,1... | collective-permute-start | bytes 3145736 | tf_op jit(solution)/shard_map/ppermute | solution.py:34
  66.7 29.1 %collective-permute-start.11 = (bf16[256,2304]{1,0:T(8,128)(2,1)S(1)}, bf16[256,2304]{1,0:T(8,128)(2,1)}, u32[]{:S(2)}, u32[]{:S(2)}) collective-permute-start(bf16[256,2304]{1,0:T(8,128)(2,1)S(1)} %collective-permute-done.10), channel_id=1, source_target_pairs={{0,8},{8,16},{16,24},{24,0},{1,9},{9,17},{17,25},{25,1},{2,10},{10... | collective-permute-start | bytes 3538952 | tf_op jit(solution)/shard_map/ppermute | solution.py:34
  66.9 47.0 %collective-permute-start.8 = (bf16[2,4,128,1024]{3,2,1,0:T(8,128)(2,1)S(1)}, bf16[2,4,128,1024]{3,2,1,0:T(8,128)(2,1)}, u32[]{:S(2)}, u32[]{:S(2)}) collective-permute-start(bf16[2,4,128,1024]{3,2,1,0:T(8,128)(2,1)S(1)} %pad_maximum_fusion.1), channel_id=1, source_target_pairs={{0,2},{2,0},{1,3},{3,1},{4,6},{6,4},{5,7},{7,5},{8,10},{10,8},{9,1... | collective-permute-start | bytes 6291464 | tf_op jit(solution)/shard_map/ppermute | solution.py:34
  70.0 47.9 %collective-permute-start.9 = (bf16[2,4,128,1024]{3,2,1,0:T(8,128)(2,1)}, bf16[2,4,128,1024]{3,2,1,0:T(8,128)(2,1)}, u32[]{:S(2)}, u32[]{:S(2)}) collective-permute-start(bf16[2,4,128,1024]{3,2,1,0:T(8,128)(2,1)} %pad_maximum_fusion), channel_id=1, source_target_pairs={{0,4},{4,0},{1,5},{5,1},{2,6},{6,2},{3,7},{7,3},{8,12},{12,8},{9,1... | collective-permute-start | bytes 6291464 | tf_op jit(solution)/shard_map/ppermute | solution.py:34
  95.8 28.3 %collective-permute-start.12 = (bf16[256,2304]{1,0:T(8,128)(2,1)}, bf16[256,2304]{1,0:T(8,128)(2,1)}, u32[]{:S(2)}, u32[]{:S(2)}) collective-permute-start(bf16[256,2304]{1,0:T(8,128)(2,1)} %collective-permute-done.11), channel_id=1, source_target_pairs={{0,8},{8,16},{16,24},{24,0},{1,9},{9,17},{17,25},{25,1},{2,10},{10... | collective-permute-start | bytes 3538952 | tf_op jit(solution)/shard_map/ppermute | solution.py:34
  142.2 9.4 %collective-permute-start.14 = (bf16[128,4,256]{2,0,1:T(8,128)(2,1)S(1)}, bf16[128,4,256]{2,0,1:T(8,128)(2,1)S(1)}, u32[]{:S(2)}, u32[]{:S(2)}) collective-permute-start(bf16[128,4,256]{2,0,1:T(8,128)(2,1)S(1)} %bitcast.278), channel_id=1, source_target_pairs={{0,6},{2,0},{4,2},{6,4},{1,7},{3,1},{5,3},{7,5},{8,14},{10,8},{12,... | collective-permute-start | bytes 786440 | tf_op jit(solution)/shard_map/ppermute | solution.py:71
  144.6 13.8 %collective-permute-start.15 = (bf16[128,4,256]{2,0,1:T(8,128)(2,1)S(1)}, bf16[128,4,256]{2,0,1:T(8,128)(2,1)S(1)}, u32[]{:S(2)}, u32[]{:S(2)}) collective-permute-start(bf16[128,4,256]{2,0,1:T(8,128)(2,1)S(1)} %bitcast.279), channel_id=1, source_target_pairs={{0,4},{2,6},{4,0},{6,2},{1,5},{3,7},{5,1},{7,3},{8,12},{10,14},{12... | collective-permute-start | bytes 786440 | tf_op jit(solution)/shard_map/ppermute | solution.py:71
  145.4 13.0 %collective-permute-start.16 = (bf16[128,4,256]{2,0,1:T(8,128)(2,1)S(1)}, bf16[128,4,256]{2,0,1:T(8,128)(2,1)S(1)}, u32[]{:S(2)}, u32[]{:S(2)}) collective-permute-start(bf16[128,4,256]{2,0,1:T(8,128)(2,1)S(1)} %bitcast.280), channel_id=1, source_target_pairs={{0,2},{2,4},{4,6},{6,0},{1,3},{3,5},{5,7},{7,1},{8,10},{10,12},{12... | collective-permute-start | bytes 786440 | tf_op jit(solution)/shard_map/ppermute | solution.py:71
  165.5 27.0 %collective-permute-start.19 = (f32[2,128,1152]{2,1,0:T(8,128)S(1)}, f32[2,128,1152]{2,1,0:T(8,128)}, u32[]{:S(2)}, u32[]{:S(2)}) collective-permute-start(f32[2,128,1152]{2,1,0:T(8,128)S(1)} %dynamic-slice_bitcast_fusion), channel_id=1, source_target_pairs={{0,4},{4,0},{1,5},{5,1},{2,6},{6,2},{3,7},{7,3},{8,12},{12,8},{9,1... | collective-permute-start | bytes 3538952 | tf_op jit(solution)/shard_map/ppermute | solution.py:90
  171.1 29.2 %collective-permute-start.17 = (f32[2,128,1152]{2,1,0:T(8,128)}, f32[2,128,1152]{2,1,0:T(8,128)}, u32[]{:S(2)}, u32[]{:S(2)}) collective-permute-start(f32[2,128,1152]{2,1,0:T(8,128)} %dynamic-slice_bitcast_fusion.1), channel_id=1, source_target_pairs={{0,2},{2,0},{1,3},{3,1},{4,6},{6,4},{5,7},{7,5},{8,10},{10,8},{9,1... | collective-permute-start | bytes 3538952 | tf_op jit(solution)/shard_map/ppermute | solution.py:90
  194.3 16.5 %collective-permute-start.20 = (f32[128,1152]{1,0:T(8,128)S(1)}, f32[128,1152]{1,0:T(8,128)S(1)}, u32[]{:S(2)}, u32[]{:S(2)}) collective-permute-start(f32[128,1152]{1,0:T(8,128)S(1)} %dynamic-slice_bitcast_fusion.2), channel_id=1, source_target_pairs={{0,2},{2,0},{1,3},{3,1},{4,6},{6,4},{5,7},{7,5},{8,10},{10,8},{9,1... | collective-permute-start | bytes 1769480 | tf_op jit(solution)/shard_map/ppermute | solution.py:93
  201.8 11.3 %collective-permute-start.18 = (f32[128,1152]{1,0:T(8,128)S(1)}, f32[128,1152]{1,0:T(8,128)S(1)}, u32[]{:S(2)}, u32[]{:S(2)}) collective-permute-start(f32[128,1152]{1,0:T(8,128)S(1)} %dynamic-slice_bitcast_fusion.3), channel_id=1, source_target_pairs={{0,4},{4,0},{1,5},{5,1},{2,6},{6,2},{3,7},{7,3},{8,12},{12,8},{9,1... | collective-permute-start | bytes 1769480 | tf_op jit(solution)/shard_map/ppermute | solution.py:93
  216.0 3.6 %collective-permute-start.21 = (f32[16]{0:T(128)S(1)}, f32[16]{0:T(128)S(1)}, u32[]{:S(2)}, u32[]{:S(2)}) collective-permute-start(f32[16]{0:T(128)S(1)} %select_reduce_fusion), channel_id=1, source_target_pairs={{0,8},{8,0},{16,24},{24,16},{1,9},{9,1},{17,25},{25,17},{2,10},{10... | collective-permute-start | bytes 200 | tf_op jit(solution)/shard_map/ppermute | solution.py:101
  219.6 4.4 %collective-permute-start.22 = (f32[16]{0:T(128)S(1)}, f32[16]{0:T(128)S(1)}, u32[]{:S(2)}, u32[]{:S(2)}) collective-permute-start(f32[16]{0:T(128)S(1)} %add.656), channel_id=1, source_target_pairs={{0,16},{8,24},{16,0},{24,8},{1,17},{9,25},{17,1},{25,9},{2,18},{10... | collective-permute-start | bytes 200 | tf_op jit(solution)/shard_map/ppermute | solution.py:101
  224.1 3.5 %collective-permute-start.23 = (f32[16]{0:T(128)S(1)}, f32[16]{0:T(128)S(1)}, u32[]{:S(2)}, u32[]{:S(2)}) collective-permute-start(f32[16]{0:T(128)S(1)} %add.657), channel_id=1, source_target_pairs={{0,4},{4,0},{1,5},{5,1},{2,6},{6,2},{3,7},{7,3},{8,12},{12,8},{9,1... | collective-permute-start | bytes 200 | tf_op jit(solution)/shard_map/ppermute | solution.py:101
  227.6 3.5 %collective-permute-start.24 = (f32[16]{0:T(128)S(1)}, f32[16]{0:T(128)S(1)}, u32[]{:S(2)}, u32[]{:S(2)}) collective-permute-start(f32[16]{0:T(128)S(1)} %add.658), channel_id=1, source_target_pairs={{0,2},{2,0},{1,3},{3,1},{4,6},{6,4},{5,7},{7,5},{8,10},{10,8},{9,1... | collective-permute-start | bytes 200 | tf_op jit(solution)/shard_map/ppermute | solution.py:101
  (17 other events, 152.9 us)

commit v20 on v16

--- a/solution.py
+++ b/solution.py
@@ -27,11 +27,14 @@
     return jnp.sum((positions[:, None] >= doc_ends[None, :]).astype(jnp.int32), axis=1)
 
 
-def ring_pieces(x, axis):
+def ring_pieces(x, axis, direct=False):
     n = lax.axis_size(axis)
     pieces = [x]
-    for _ in range(n - 1):
-        pieces.append(lax.ppermute(pieces[-1], axis, [(k, (k + 1) % n) for k in range(n)]))
+    for t in range(1, n):
+        if direct:
+            pieces.append(lax.ppermute(x, axis, [(k, (k + t) % n) for k in range(n)]))
+        else:
+            pieces.append(lax.ppermute(pieces[-1], axis, [(k, (k + 1) % n) for k in range(n)]))
     return pieces
 
 
@@ -42,8 +45,8 @@
 def gather_order(x, order):
     stride = {"c2": 1, "c1": lax.axis_size("c2"), "c0": lax.axis_size("c1") * lax.axis_size("c2")}
     source = jnp.zeros((), jnp.int32)
-    for axis in order[:-1]:
-        x = ring_gather(x, axis)
+    for stage, axis in enumerate(order[:-1]):
+        x = jnp.stack(ring_pieces(x, axis, direct=stage == 0))
         n = lax.axis_size(axis)
         came = (lax.axis_index(axis) - jnp.arange(n, dtype=jnp.int32)) % n
         source = came.reshape((n,) + (1,) * source.ndim) * stride[axis] + source[None]

time: 233 us -> 261 us (1.12)
  starting transfers between devices: 20.4 us -> 36.3 us
  waiting for transfers between devices: 151 us -> 163 us
    ppermute x0 -> x6, waiting for transfers between devices: none -> 52.7 us  [ring_pieces(): pieces.append(lax.ppermute(x, axis, [(k, (k + t) % n) for k in range(n)]))]
    ppermute x14 -> x8, waiting for transfers between devices: 87.9 us -> 51.4 us  [ring_pieces(): lax.ppermute(pieces[-1], axis, [(k, (k + 1) % n) for k in range(n)])]
    ppermute x0 -> x6, starting transfers between devices: none -> 20.7 us  [ring_pieces(): pieces.append(lax.ppermute(x, axis, [(k, (k + t) % n) for k in range(n)]))]
    ppermute x14 -> x8, starting transfers between devices: 13.2 us -> 5.51 us  [ring_pieces(): lax.ppermute(pieces[-1], axis, [(k, (k + 1) % n) for k in range(n)])]
  transfers between devices with their start and end apart: 25 -> 25, of which waited for: 20 -> 16; matrix products, arithmetic and copies ran while one was open for 13% -> 11% of each run, Pallas kernels for 0% -> 0%
where the time goes in v20:
time: 261 us; the launch traced here: 260 us
  waiting for transfers between devices  163 us (62%)
  starting transfers between devices  36.3 us (14%)
  local copies, waits for them, and re-layouts  28.6 us (11%)
  matrix products  17.2 us (7%)
  other arithmetic  11.4 us (4%)
    ppermute x6, waiting for transfers between devices, ring_pieces(): pieces.append(lax.ppermute(x, axis, [(k, (k + t) % n) for k in range(n)]))  52.7 us
    ppermute x8, waiting for transfers between devices, ring_pieces(): lax.ppermute(pieces[-1], axis, [(k, (k + 1) % n) for k in range(n)])  51.4 us
    ppermute x2, waiting for transfers between devices, swap_reduce_scatter(): keep = keep + lax.ppermute(sent, first, [(0, 1), (1, 0)])  24 us
    ppermute x6, starting transfers between devices, ring_pieces(): pieces.append(lax.ppermute(x, axis, [(k, (k + t) % n) for k in range(n)]))  20.7 us
    ppermute x3, waiting for transfers between devices, permute_all_to_all(): lax.ppermute(sent, axes, [(k, (k + shift) % n) for k in range(n)])  12.2 us
    unnamed x48, local copies, waits for them, and re-layouts  11.9 us
    ppermute x2, waiting for transfers between devices, swap_reduce_scatter(): return mine + lax.ppermute(sent, second, [(0, 1), (1, 0)])  11.7 us
    ppermute x4, waiting for transfers between devices, butterfly_sum(): x = x + lax.ppermute(x, axis, [(i, i ^ bit) for i in range(size)])  10.9 us
  transfers between devices with their start and end apart: 25, of which 16 were waited for; matrix products, arithmetic and copies ran while one was open for 11% of the time, Pallas kernels for 0%

profile of v20, /device:TPU:0, one launch (start us, length us, event | category | flops | bytes accessed | tf_op | source)
XLA Modules:
  0.0 260.1 jit_solution(14084416945287415626)
XLA Ops:
  1.9 5.1 %collective-permute-start.6 = (bf16[128,1024]{1,0:T(8,128)(2,1)S(1)}, bf16[128,1024]{1,0:T(8,128)(2,1)S(1)}, u32[]{:S(2)}, u32[]{:S(2)}) collective-permute-start(bf16[128,1024]{1,0:T(8,128)(2,1)S(1)} %get-tuple-element.49), channel_id=1, source_target_pairs={{0,24},{8,0},{16,8},{24,16},{1,25},{9,1},{17,9},{25,17},{2,26},{10... | collective-permute-start | bytes 786440 | tf_op jit(solution)/shard_map/ppermute | solution.py:35
  8.1 2.9 %collective-permute-start.2 = (bf16[128,1024]{1,0:T(8,128)(2,1)S(1)}, bf16[128,1024]{1,0:T(8,128)(2,1)S(1)}, u32[]{:S(2)}, u32[]{:S(2)}) collective-permute-start(bf16[128,1024]{1,0:T(8,128)(2,1)S(1)} %get-tuple-element.43), channel_id=1, source_target_pairs={{0,24},{8,0},{16,8},{24,16},{1,25},{9,1},{17,9},{25,17},{2,26},{10... | collective-permute-start | bytes 786440 | tf_op jit(solution)/shard_map/ppermute | solution.py:35
  13.8 10.6 %collective-permute-start = (bf16[128,1024]{1,0:T(8,128)(2,1)S(1)}, bf16[128,1024]{1,0:T(8,128)(2,1)S(1)}, u32[]{:S(2)}, u32[]{:S(2)}) collective-permute-start(bf16[128,1024]{1,0:T(8,128)(2,1)S(1)} %get-tuple-element.43), channel_id=1, source_target_pairs={{0,8},{8,16},{16,24},{24,0},{1,9},{9,17},{17,25},{25,1},{2,10},{10... | collective-permute-start | bytes 786440 | tf_op jit(solution)/shard_map/ppermute | solution.py:35
  24.4 7.3 %collective-permute-done.5 = bf16[128,1024]{1,0:T(8,128)(2,1)S(1)} collective-permute-done((bf16[128,1024]{1,0:T(8,128)(2,1)S(1)}, bf16[128,1024]{1,0:T(8,128)(2,1)S(1)}, u32[]{:S(2)}, u32[]{:S(2)}) %collective-permute-start.5) | collective-permute-done | bytes 262176 | tf_op jit(solution)/shard_map/ppermute | solution.py:35
  33.4 43.7 %collective-permute-done.1 = bf16[128,1024]{1,0:T(8,128)(2,1)S(1)} collective-permute-done((bf16[128,1024]{1,0:T(8,128)(2,1)S(1)}, bf16[128,1024]{1,0:T(8,128)(2,1)S(1)}, u32[]{:S(2)}, u32[]{:S(2)}) %collective-permute-start.1) | collective-permute-done | bytes 262176 | tf_op jit(solution)/shard_map/ppermute | solution.py:35
  79.8 23.6 %collective-permute-done.3 = bf16[4,128,1024]{2,1,0:T(8,128)(2,1)S(1)} collective-permute-done((bf16[4,128,1024]{2,1,0:T(8,128)(2,1)S(1)}, bf16[4,128,1024]{2,1,0:T(8,128)(2,1)S(1)}, u32[]{:S(2)}, u32[]{:S(2)}) %collective-permute-start.3) | collective-permute-done | bytes 1048608 | tf_op jit(solution)/shard_map/ppermute | solution.py:37
  107.9 2.0 copy.41
  111.4 2.3 copy.86
  115.0 2.7 %fusion.98 = (bf16[1024,512]{1,0:T(8,128)(2,1)S(1)}, bf16[1024,512]{1,0:T(8,128)(2,1)}) fusion(bf16[1024,1024]{1,0:T(8,128)(2,1)} %bitcast.8), kind=kLoop, calls=%fused_computation.231 | loop fusion | bytes 4194304 | tf_op jit(solution)/shard_map/slice | solution.py:206
  117.6 2.3 copy.83
  121.2 25.2 %collective-permute-done.8 = bf16[2,4,128,1024]{3,2,1,0:T(8,128)(2,1)} collective-permute-done((bf16[2,4,128,1024]{3,2,1,0:T(8,128)(2,1)S(1)}, bf16[2,4,128,1024]{3,2,1,0:T(8,128)(2,1)}, u32[]{:S(2)}, u32[]{:S(2)}) %collective-permute-start.8) | collective-permute-done | bytes 2097184 | tf_op jit(solution)/shard_map/ppermute | solution.py:37
  146.4 4.0 %copy.74 = bf16[1024,1024]{0,1:T(8,128)(2,1)} copy(bf16[1024,1024]{1,0:T(8,128)(2,1)} %bitcast.22) | data formatting | bytes 4194304 | tf_op jit(solution)/shard_map/reshape | solution.py:191
  150.4 2.9 %copy.75 = bf16[1024,1024]{0,1:T(8,128)(2,1)S(1)} copy(bf16[1024,1024]{1,0:T(8,128)(2,1)} %bitcast.24) | data formatting | bytes 4194304 | tf_op jit(solution)/shard_map/reshape | solution.py:191
  171.4 2.7 %collective-permute-start.14 = (bf16[128,4,256]{2,0,1:T(8,128)(2,1)S(1)}, bf16[128,4,256]{2,0,1:T(8,128)(2,1)S(1)}, u32[]{:S(2)}, u32[]{:S(2)}) collective-permute-start(bf16[128,4,256]{2,0,1:T(8,128)(2,1)S(1)} %bitcast.274), channel_id=1, source_target_pairs={{0,6},{2,0},{4,2},{6,4},{1,7},{3,1},{5,3},{7,5},{8,14},{10,8},{12,... | collective-permute-start | bytes 786440 | tf_op jit(solution)/shard_map/ppermute | solution.py:74
  175.8 5.0 %collective-permute-done.14 = bf16[128,4,256]{2,0,1:T(8,128)(2,1)S(1)} collective-permute-done((bf16[128,4,256]{2,0,1:T(8,128)(2,1)S(1)}, bf16[128,4,256]{2,0,1:T(8,128)(2,1)S(1)}, u32[]{:S(2)}, u32[]{:S(2)}) %collective-permute-start.14) | collective-permute-done | bytes 262176 | tf_op jit(solution)/shard_map/ppermute | solution.py:74
  180.8 7.2 %collective-permute-done.15 = bf16[128,4,256]{2,0,1:T(8,128)(2,1)S(1)} collective-permute-done((bf16[128,4,256]{2,0,1:T(8,128)(2,1)S(1)}, bf16[128,4,256]{2,0,1:T(8,128)(2,1)S(1)}, u32[]{:S(2)}, u32[]{:S(2)}) %collective-permute-start.15) | collective-permute-done | bytes 262176 | tf_op jit(solution)/shard_map/ppermute | solution.py:74
  189.1 2.1 fusion.32
  191.2 2.2 fusion.33
  200.4 24.0 %collective-permute-done.19 = f32[2,128,1152]{2,1,0:T(8,128)} collective-permute-done((f32[2,128,1152]{2,1,0:T(8,128)S(1)}, f32[2,128,1152]{2,1,0:T(8,128)}, u32[]{:S(2)}, u32[]{:S(2)}) %collective-permute-start.19) | collective-permute-done | bytes 1179680 | tf_op jit(solution)/shard_map/ppermute | solution.py:93
  229.8 9.8 %collective-permute-done.20 = f32[128,1152]{1,0:T(8,128)S(1)} collective-permute-done((f32[128,1152]{1,0:T(8,128)S(1)}, f32[128,1152]{1,0:T(8,128)S(1)}, u32[]{:S(2)}, u32[]{:S(2)}) %collective-permute-start.20) | collective-permute-done | bytes 589856 | tf_op jit(solution)/shard_map/ppermute | solution.py:96
  241.9 2.5 psum.7
  244.5 3.5 %collective-permute-done.21 = f32[16]{0:T(128)S(1)} collective-permute-done((f32[16]{0:T(128)S(1)}, f32[16]{0:T(128)S(1)}, u32[]{:S(2)}, u32[]{:S(2)}) %collective-permute-start.21) | collective-permute-done | bytes 96 | tf_op jit(solution)/shard_map/ppermute | solution.py:104
  248.1 4.4 %collective-permute-done.22 = f32[16]{0:T(128)S(1)} collective-permute-done((f32[16]{0:T(128)S(1)}, f32[16]{0:T(128)S(1)}, u32[]{:S(2)}, u32[]{:S(2)}) %collective-permute-start.22) | collective-permute-done | bytes 96 | tf_op jit(solution)/shard_map/ppermute | solution.py:104
  254.2 1.9 collective-permute-done.23
  (154 shorter events, 59.2 us)
Async XLA Ops:
  1.9 11.9 %collective-permute-start.6 = (bf16[128,1024]{1,0:T(8,128)(2,1)S(1)}, bf16[128,1024]{1,0:T(8,128)(2,1)S(1)}, u32[]{:S(2)}, u32[]{:S(2)}) collective-permute-start(bf16[128,1024]{1,0:T(8,128)(2,1)S(1)} %get-tuple-element.49), channel_id=1, source_target_pairs={{0,24},{8,0},{16,8},{24,16},{1,25},{9,1},{17,9},{25,17},{2,26},{10... | collective-permute-start | bytes 786440 | tf_op jit(solution)/shard_map/ppermute | solution.py:35
  7.0 24.6 %collective-permute-start.5 = (bf16[128,1024]{1,0:T(8,128)(2,1)S(1)}, bf16[128,1024]{1,0:T(8,128)(2,1)S(1)}, u32[]{:S(2)}, u32[]{:S(2)}) collective-permute-start(bf16[128,1024]{1,0:T(8,128)(2,1)S(1)} %get-tuple-element.49), channel_id=1, source_target_pairs={{0,16},{8,24},{16,0},{24,8},{1,17},{9,25},{17,1},{25,9},{2,18},{10... | collective-permute-start | bytes 786440 | tf_op jit(solution)/shard_map/ppermute | solution.py:35
  7.0 24.6 %collective-permute-start.4 = (bf16[128,1024]{1,0:T(8,128)(2,1)S(1)}, bf16[128,1024]{1,0:T(8,128)(2,1)S(1)}, u32[]{:S(2)}, u32[]{:S(2)}) collective-permute-start(bf16[128,1024]{1,0:T(8,128)(2,1)S(1)} %get-tuple-element.49), channel_id=1, source_target_pairs={{0,8},{8,16},{16,24},{24,0},{1,9},{9,17},{17,25},{25,1},{2,10},{10... | collective-permute-start | bytes 786440 | tf_op jit(solution)/shard_map/ppermute | solution.py:35
  8.1 25.3 %collective-permute-start.2 = (bf16[128,1024]{1,0:T(8,128)(2,1)S(1)}, bf16[128,1024]{1,0:T(8,128)(2,1)S(1)}, u32[]{:S(2)}, u32[]{:S(2)}) collective-permute-start(bf16[128,1024]{1,0:T(8,128)(2,1)S(1)} %get-tuple-element.43), channel_id=1, source_target_pairs={{0,24},{8,0},{16,8},{24,16},{1,25},{9,1},{17,9},{25,17},{2,26},{10... | collective-permute-start | bytes 786440 | tf_op jit(solution)/shard_map/ppermute | solution.py:35
  11.0 66.1 %collective-permute-start.1 = (bf16[128,1024]{1,0:T(8,128)(2,1)S(1)}, bf16[128,1024]{1,0:T(8,128)(2,1)S(1)}, u32[]{:S(2)}, u32[]{:S(2)}) collective-permute-start(bf16[128,1024]{1,0:T(8,128)(2,1)S(1)} %get-tuple-element.43), channel_id=1, source_target_pairs={{0,16},{8,24},{16,0},{24,8},{1,17},{9,25},{17,1},{25,9},{2,18},{10... | collective-permute-start | bytes 786440 | tf_op jit(solution)/shard_map/ppermute | solution.py:35
  13.8 63.3 %collective-permute-start = (bf16[128,1024]{1,0:T(8,128)(2,1)S(1)}, bf16[128,1024]{1,0:T(8,128)(2,1)S(1)}, u32[]{:S(2)}, u32[]{:S(2)}) collective-permute-start(bf16[128,1024]{1,0:T(8,128)(2,1)S(1)} %get-tuple-element.43), channel_id=1, source_target_pairs={{0,8},{8,16},{16,24},{24,0},{1,9},{9,17},{17,25},{25,1},{2,10},{10... | collective-permute-start | bytes 786440 | tf_op jit(solution)/shard_map/ppermute | solution.py:35
  31.6 47.2 %collective-permute-start.10 = (bf16[256,2304]{1,0:T(8,128)(2,1)S(1)}, bf16[256,2304]{1,0:T(8,128)(2,1)S(1)}, u32[]{:S(2)}, u32[]{:S(2)}) collective-permute-start(bf16[256,2304]{1,0:T(8,128)(2,1)S(1)} %copy-done.2), channel_id=1, source_target_pairs={{0,8},{8,16},{16,24},{24,0},{1,9},{9,17},{17,25},{25,1},{2,10},{10... | collective-permute-start | bytes 3538952 | tf_op jit(solution)/shard_map/ppermute | solution.py:37
  31.8 47.0 %collective-permute-start.7 = (bf16[4,128,1024]{2,1,0:T(8,128)(2,1)S(1)}, bf16[4,128,1024]{2,1,0:T(8,128)(2,1)S(1)}, u32[]{:S(2)}, u32[]{:S(2)}) collective-permute-start(bf16[4,128,1024]{2,1,0:T(8,128)(2,1)S(1)} %get-tuple-element.41), channel_id=1, source_target_pairs={{0,4},{4,0},{1,5},{5,1},{2,6},{6,2},{3,7},{7,3},{8,12},{12,8},{9,1... | collective-permute-start | bytes 3145736 | tf_op jit(solution)/shard_map/ppermute | solution.py:37
  77.3 26.2 %collective-permute-start.3 = (bf16[4,128,1024]{2,1,0:T(8,128)(2,1)S(1)}, bf16[4,128,1024]{2,1,0:T(8,128)(2,1)S(1)}, u32[]{:S(2)}, u32[]{:S(2)}) collective-permute-start(bf16[4,128,1024]{2,1,0:T(8,128)(2,1)S(1)} %get-tuple-element.39), channel_id=1, source_target_pairs={{0,2},{2,0},{1,3},{3,1},{4,6},{6,4},{5,7},{7,5},{8,10},{10,8},{9,1... | collective-permute-start | bytes 3145736 | tf_op jit(solution)/shard_map/ppermute | solution.py:37
  78.8 28.5 %collective-permute-start.11 = (bf16[256,2304]{1,0:T(8,128)(2,1)S(1)}, bf16[256,2304]{1,0:T(8,128)(2,1)}, u32[]{:S(2)}, u32[]{:S(2)}) collective-permute-start(bf16[256,2304]{1,0:T(8,128)(2,1)S(1)} %collective-permute-done.10), channel_id=1, source_target_pairs={{0,8},{8,16},{16,24},{24,0},{1,9},{9,17},{17,25},{25,1},{2,10},{10... | collective-permute-start | bytes 3538952 | tf_op jit(solution)/shard_map/ppermute | solution.py:37
  79.1 67.3 %collective-permute-start.8 = (bf16[2,4,128,1024]{3,2,1,0:T(8,128)(2,1)S(1)}, bf16[2,4,128,1024]{3,2,1,0:T(8,128)(2,1)}, u32[]{:S(2)}, u32[]{:S(2)}) collective-permute-start(bf16[2,4,128,1024]{3,2,1,0:T(8,128)(2,1)S(1)} %pad_maximum_fusion.1), channel_id=1, source_target_pairs={{0,2},{2,0},{1,3},{3,1},{4,6},{6,4},{5,7},{7,5},{8,10},{10,8},{9,1... | collective-permute-start | bytes 6291464 | tf_op jit(solution)/shard_map/ppermute | solution.py:37
  104.9 45.5 %collective-permute-start.9 = (bf16[2,4,128,1024]{3,2,1,0:T(8,128)(2,1)}, bf16[2,4,128,1024]{3,2,1,0:T(8,128)(2,1)}, u32[]{:S(2)}, u32[]{:S(2)}) collective-permute-start(bf16[2,4,128,1024]{3,2,1,0:T(8,128)(2,1)} %pad_maximum_fusion), channel_id=1, source_target_pairs={{0,4},{4,0},{1,5},{5,1},{2,6},{6,2},{3,7},{7,3},{8,12},{12,8},{9,1... | collective-permute-start | bytes 6291464 | tf_op jit(solution)/shard_map/ppermute | solution.py:37
  107.3 46.0 %collective-permute-start.12 = (bf16[256,2304]{1,0:T(8,128)(2,1)}, bf16[256,2304]{1,0:T(8,128)(2,1)}, u32[]{:S(2)}, u32[]{:S(2)}) collective-permute-start(bf16[256,2304]{1,0:T(8,128)(2,1)} %collective-permute-done.11), channel_id=1, source_target_pairs={{0,8},{8,16},{16,24},{24,0},{1,9},{9,17},{17,25},{25,1},{2,10},{10... | collective-permute-start | bytes 3538952 | tf_op jit(solution)/shard_map/ppermute | solution.py:37
  171.4 9.4 %collective-permute-start.14 = (bf16[128,4,256]{2,0,1:T(8,128)(2,1)S(1)}, bf16[128,4,256]{2,0,1:T(8,128)(2,1)S(1)}, u32[]{:S(2)}, u32[]{:S(2)}) collective-permute-start(bf16[128,4,256]{2,0,1:T(8,128)(2,1)S(1)} %bitcast.274), channel_id=1, source_target_pairs={{0,6},{2,0},{4,2},{6,4},{1,7},{3,1},{5,3},{7,5},{8,14},{10,8},{12,... | collective-permute-start | bytes 786440 | tf_op jit(solution)/shard_map/ppermute | solution.py:74
  174.3 13.8 %collective-permute-start.15 = (bf16[128,4,256]{2,0,1:T(8,128)(2,1)S(1)}, bf16[128,4,256]{2,0,1:T(8,128)(2,1)S(1)}, u32[]{:S(2)}, u32[]{:S(2)}) collective-permute-start(bf16[128,4,256]{2,0,1:T(8,128)(2,1)S(1)} %bitcast.275), channel_id=1, source_target_pairs={{0,4},{2,6},{4,0},{6,2},{1,5},{3,7},{5,1},{7,3},{8,12},{10,14},{12... | collective-permute-start | bytes 786440 | tf_op jit(solution)/shard_map/ppermute | solution.py:74
  175.0 13.0 %collective-permute-start.16 = (bf16[128,4,256]{2,0,1:T(8,128)(2,1)S(1)}, bf16[128,4,256]{2,0,1:T(8,128)(2,1)S(1)}, u32[]{:S(2)}, u32[]{:S(2)}) collective-permute-start(bf16[128,4,256]{2,0,1:T(8,128)(2,1)S(1)} %bitcast.276), channel_id=1, source_target_pairs={{0,2},{2,4},{4,6},{6,0},{1,3},{3,5},{5,7},{7,1},{8,10},{10,12},{12... | collective-permute-start | bytes 786440 | tf_op jit(solution)/shard_map/ppermute | solution.py:74
  197.4 27.0 %collective-permute-start.19 = (f32[2,128,1152]{2,1,0:T(8,128)S(1)}, f32[2,128,1152]{2,1,0:T(8,128)}, u32[]{:S(2)}, u32[]{:S(2)}) collective-permute-start(f32[2,128,1152]{2,1,0:T(8,128)S(1)} %dynamic-slice_bitcast_fusion), channel_id=1, source_target_pairs={{0,4},{4,0},{1,5},{5,1},{2,6},{6,2},{3,7},{7,3},{8,12},{12,8},{9,1... | collective-permute-start | bytes 3538952 | tf_op jit(solution)/shard_map/ppermute | solution.py:93
  199.1 27.6 %collective-permute-start.17 = (f32[2,128,1152]{2,1,0:T(8,128)}, f32[2,128,1152]{2,1,0:T(8,128)}, u32[]{:S(2)}, u32[]{:S(2)}) collective-permute-start(f32[2,128,1152]{2,1,0:T(8,128)} %dynamic-slice_bitcast_fusion.1), channel_id=1, source_target_pairs={{0,2},{2,0},{1,3},{3,1},{4,6},{6,4},{5,7},{7,5},{8,10},{10,8},{9,1... | collective-permute-start | bytes 3538952 | tf_op jit(solution)/shard_map/ppermute | solution.py:93
  226.3 13.4 %collective-permute-start.20 = (f32[128,1152]{1,0:T(8,128)S(1)}, f32[128,1152]{1,0:T(8,128)S(1)}, u32[]{:S(2)}, u32[]{:S(2)}) collective-permute-start(f32[128,1152]{1,0:T(8,128)S(1)} %dynamic-slice_bitcast_fusion.2), channel_id=1, source_target_pairs={{0,2},{2,0},{1,3},{3,1},{4,6},{6,4},{5,7},{7,5},{8,10},{10,8},{9,1... | collective-permute-start | bytes 1769480 | tf_op jit(solution)/shard_map/ppermute | solution.py:96
  228.1 13.4 %collective-permute-start.18 = (f32[128,1152]{1,0:T(8,128)S(1)}, f32[128,1152]{1,0:T(8,128)S(1)}, u32[]{:S(2)}, u32[]{:S(2)}) collective-permute-start(f32[128,1152]{1,0:T(8,128)S(1)} %dynamic-slice_bitcast_fusion.3), channel_id=1, source_target_pairs={{0,4},{4,0},{1,5},{5,1},{2,6},{6,2},{3,7},{7,3},{8,12},{12,8},{9,1... | collective-permute-start | bytes 1769480 | tf_op jit(solution)/shard_map/ppermute | solution.py:96
  244.5 3.6 %collective-permute-start.21 = (f32[16]{0:T(128)S(1)}, f32[16]{0:T(128)S(1)}, u32[]{:S(2)}, u32[]{:S(2)}) collective-permute-start(f32[16]{0:T(128)S(1)} %select_reduce_fusion), channel_id=1, source_target_pairs={{0,8},{8,0},{16,24},{24,16},{1,9},{9,1},{17,25},{25,17},{2,10},{10... | collective-permute-start | bytes 200 | tf_op jit(solution)/shard_map/ppermute | solution.py:104
  248.1 4.4 %collective-permute-start.22 = (f32[16]{0:T(128)S(1)}, f32[16]{0:T(128)S(1)}, u32[]{:S(2)}, u32[]{:S(2)}) collective-permute-start(f32[16]{0:T(128)S(1)} %add.644), channel_id=1, source_target_pairs={{0,16},{8,24},{16,0},{24,8},{1,17},{9,25},{17,1},{25,9},{2,18},{10... | collective-permute-start | bytes 200 | tf_op jit(solution)/shard_map/ppermute | solution.py:104
  252.5 3.5 %collective-permute-start.23 = (f32[16]{0:T(128)S(1)}, f32[16]{0:T(128)S(1)}, u32[]{:S(2)}, u32[]{:S(2)}) collective-permute-start(f32[16]{0:T(128)S(1)} %add.645), channel_id=1, source_target_pairs={{0,4},{4,0},{1,5},{5,1},{2,6},{6,2},{3,7},{7,3},{8,12},{12,8},{9,1... | collective-permute-start | bytes 200 | tf_op jit(solution)/shard_map/ppermute | solution.py:104
  256.1 3.5 %collective-permute-start.24 = (f32[16]{0:T(128)S(1)}, f32[16]{0:T(128)S(1)}, u32[]{:S(2)}, u32[]{:S(2)}) collective-permute-start(f32[16]{0:T(128)S(1)} %add.646), channel_id=1, source_target_pairs={{0,2},{2,0},{1,3},{3,1},{4,6},{6,4},{5,7},{7,5},{8,10},{10,8},{9,1... | collective-permute-start | bytes 200 | tf_op jit(solution)/shard_map/ppermute | solution.py:104
  (17 other events, 193.3 us)
